TPU v7x, 32 devices: a whole 2x2x4 slice. The times are simulated.
32 devices in a mesh: row: 8 (over z, y), rep: 4 (over x, core).
Axes of the slice: x: 2, y: 2, z: 4, core: 2. Of those that a mesh axis runs over, the one named last changes fastest.
Arguments:
- features: bfloat16 [2048, 256], P('row'), may hold values from -6 to 6
- cotangent: bfloat16 [2048, 256], P('row'), may hold values from -0.3125 to 0.3125
- weight_one: bfloat16 [256, 256], replicated, may hold values from -0.375 to 0.375
- weight_two: bfloat16 [256, 256], replicated, may hold values from -0.375 to 0.375
- block_index: int32 [8, 4, 2, 4], P('row', 'rep'), may hold values from 0 to 15, as said below
- block_count: int32 [8, 4, 2], P('row', 'rep'), may hold values from 0 to 4
- block_values: bfloat16 [8, 4, 2, 4, 128, 128], P('row', 'rep'), as said below
Outputs:
- logits: bfloat16 [2048, 256], P(('row', 'rep'))
- grad_one: float32 [256, 256], replicated
- grad_two: float32 [256, 256], replicated
Inputs may be any that keep to these rules, and one draw needn't show every extreme that they name: block_index[i, j, a, s] lies in [j * 4, (j + 1) * 4); for s < block_count[i, j, a] the entries rise strictly; later entries equal j * 4 and are not part of A. `block_values`: A is symmetric: block (r, c) is listed exactly when block (c, r) is, and its entries are the transpose of those of block (c, r). Entries are normal with standard deviation (0.5 * 128 * 16) ** -0.5, cut at five such deviations; blocks on the diagonal are symmetric.
All inputs are finite; a program needn't handle non-finite values.
Results may differ from a plain program's by a relative error of at most 0.0059.
Values may be sent and summed in bfloat16 or wider, within the bound.
No kernel may reach another device: no remote copies, remote signals or barrier semaphores. Data moves between devices by JAX's collectives and lax.ppermute only.
A program may use at most 64 MiB of HBM per device.

v0:
```python
import jax
import jax.numpy as jnp
from jax import lax
from jax.sharding import PartitionSpec as P


def broadcast(array, axis, root):
    mine = lax.axis_index(axis) == root
    return lax.psum(jnp.where(mine, array, jnp.zeros_like(array)), axis)


def aggregate(source, block_index, block_count, block_values):
    copies = lax.axis_size("rep")
    sections = lax.axis_size("row") // copies
    copy_index = lax.axis_index("rep")
    node_rows, feature_width = source.shape
    block_rows = block_values.shape[2]
    slot_count = block_values.shape[3]
    block_side = block_values.shape[-1]

    def fetch(state_unused, section_index):
        panel = broadcast(source, "row", copy_index * sections + section_index)
        return (state_unused, panel)

    state_unused, panels = lax.scan(fetch, jnp.int32(0), jnp.arange(sections, dtype=jnp.int32))
    panels = panels.reshape(sections * block_rows, block_side, feature_width)
    columns = block_index[0, 0] - copy_index * slot_count
    live_slots = jnp.arange(slot_count, dtype=jnp.int32)[None, :] < block_count[0, 0][:, None]
    picked = jnp.take(panels, columns.reshape(-1), axis=0).reshape(
        block_rows, slot_count, block_side, feature_width
    )
    picked = jnp.where(live_slots[:, :, None, None], picked, jnp.zeros((), picked.dtype))
    partial_value = lax.dot_general(
        block_values[0, 0],
        picked,
        (((1, 3), (1, 2)), ((0,), (0,))),
        preferred_element_type=jnp.float32,
    )
    partial_value = partial_value.reshape(node_rows, feature_width)
    result = lax.psum(partial_value, "rep")
    return result


def shards(features, cotangent, weight_one, weight_two, block_index, block_count, block_values):
    copies = lax.axis_size("rep")
    copy_index = lax.axis_index("rep")
    node_rows = features.shape[0]
    share_rows = node_rows // copies
    first_row = copy_index * share_rows

    def own_rows(array):
        return lax.dynamic_slice_in_dim(array, first_row, share_rows, 0)

    agg_one = aggregate(features, block_index, block_count, block_values).astype(jnp.bfloat16)
    pre_one = jnp.dot(agg_one, weight_one, preferred_element_type=jnp.float32)
    hidden = jax.nn.silu(pre_one).astype(jnp.bfloat16)
    agg_two = aggregate(hidden, block_index, block_count, block_values).astype(jnp.bfloat16)
    agg_two_own = own_rows(agg_two)
    logits = jnp.dot(agg_two_own, weight_two, preferred_element_type=jnp.float32).astype(
        jnp.bfloat16
    )
    cotangent_own = own_rows(cotangent)
    grad_two = lax.dot_general(
        agg_two_own, cotangent_own, (((0,), (0,)), ((), ())), preferred_element_type=jnp.float32
    )
    grad_two = lax.psum(grad_two, ("row", "rep"))
    back_signal = lax.dot_general(
        cotangent, weight_two, (((1,), (1,)), ((), ())), preferred_element_type=jnp.float32
    ).astype(jnp.bfloat16)
    carried = aggregate(back_signal, block_index, block_count, block_values)
    carried = own_rows(carried)
    pre_own = own_rows(pre_one)
    agg_one_own = own_rows(agg_one)
    gate_value = jax.nn.sigmoid(pre_own)
    pre_grad = (carried * (gate_value + pre_own * gate_value * (1.0 - gate_value))).astype(
        jnp.bfloat16
    )
    grad_one = lax.dot_general(
        agg_one_own, pre_grad, (((0,), (0,)), ((), ())), preferred_element_type=jnp.float32
    )
    grad_one = lax.psum(grad_one, ("row", "rep"))
    return (logits, grad_one, grad_two)


def solution(mesh):
    in_specs = (
        P("row", None),
        P("row", None),
        P(),
        P(),
        P("row", "rep", None, None),
        P("row", "rep", None),
        P("row", "rep", None, None, None, None),
    )
    out_specs = (P(("row", "rep"), None), P(), P())
    return jax.shard_map(shards, mesh=mesh, in_specs=in_specs, out_specs=out_specs, check_vma=False)
```

profile of v0, /device:TPU:0, one launch (start us, length us, event | category | flops | bytes accessed | tf_op | source)
XLA Modules:
  0.0 661.8 jit_solution(11847135036822304722)
XLA Ops:
  8.0 0.7 copy-done.4
  8.9 1.2 convolution_convert_fusion
  10.1 154.0 %while.38 = (s32[]{:T(128)}, bf16[2,256,256]{2,1,0:T(8,128)(2,1)S(1)}, s32[2]{0:T(128)S(1)}, s32[]{:T(128)}, bf16[256,256]{1,0:T(8,128)(2,1)S(1)}, /*index=5*/s32[]{:T(128)}, u32[]{:T(128)}, u32[]{:T(128)}) while((s32[]{:T(128)}, bf16[2,256,256]{2,1,0:T(8,128)(2,1)S(1)}, s32[2]{0:T(128)S(1)}, s32[]{:T(128)}, ...), condition=%wide.region_10.12_spmd, body=%wide.region_8.11_spmd.sunk | while | flops 131079 | bytes 1310923 | solution.py:25
  10.2 0.6 dynamic_slice.53
  11.4 0.7 select_bitcast_fusion.8
  12.1 75.9 %all-reduce.17.cloned.1.call-done = bf16[1,256,256]{2,1,0:T(8,128)(2,1)} async-done(((bf16[1,256,256]{2,1,0:T(8,128)(2,1)}), bf16[1,256,256]{2,1,0:T(8,128)(2,1)}) %all-reduce.17.cloned.1.call-update) | async-done | bytes 131088 | tf_op jit(solution)/shard_map/while/body/eval_jaxpr/psum | solution.py:9
  88.0 0.9 constant_dynamic-update-slice_fusion.8
  89.0 0.6 dynamic_slice.53
  90.2 0.7 select_bitcast_fusion.8
  90.9 72.3 %all-reduce.17.cloned.1.call-done = bf16[1,256,256]{2,1,0:T(8,128)(2,1)} async-done(((bf16[1,256,256]{2,1,0:T(8,128)(2,1)}), bf16[1,256,256]{2,1,0:T(8,128)(2,1)}) %all-reduce.17.cloned.1.call-update) | async-done | bytes 131088 | tf_op jit(solution)/shard_map/while/body/eval_jaxpr/psum | solution.py:9
  163.2 0.9 constant_dynamic-update-slice_fusion.8
  164.1 0.6 gather_fusion.2
  164.7 0.9 copy-done.1
  165.6 150.0 %while.36 = (s32[]{:T(128)}, bf16[2,256,256]{2,1,0:T(8,128)(2,1)S(1)}, s32[2]{0:T(128)S(1)}, s32[]{:T(128)}, bf16[256,256]{1,0:T(8,128)(2,1)S(1)}, /*index=5*/s32[]{:T(128)}, u32[]{:T(128)}, u32[]{:T(128)}) while((s32[]{:T(128)}, bf16[2,256,256]{2,1,0:T(8,128)(2,1)S(1)}, s32[2]{0:T(128)S(1)}, s32[]{:T(128)}, bf16[256,256]{1,0:T(8,128)(2,1)S(1)}, ...), condition=%wide.region_2.3_spmd, body=%wide.region_0.2_spmd.sunk | while | flops 131079 | bytes 1310923 | solution.py:25
  165.6 0.6 dynamic_slice.51
  166.8 0.7 select_bitcast_fusion.6
  167.5 72.3 %all-reduce.13.cloned.1.call-done = bf16[1,256,256]{2,1,0:T(8,128)(2,1)} async-done(((bf16[1,256,256]{2,1,0:T(8,128)(2,1)}), bf16[1,256,256]{2,1,0:T(8,128)(2,1)}) %all-reduce.13.cloned.1.call-update) | async-done | bytes 131088 | tf_op jit(solution)/shard_map/while/body/eval_jaxpr/psum | solution.py:9
  239.8 0.9 constant_dynamic-update-slice_fusion.6
  240.8 0.6 dynamic_slice.51
  242.1 0.7 select_bitcast_fusion.6
  242.8 71.9 %all-reduce.13.cloned.1.call-done = bf16[1,256,256]{2,1,0:T(8,128)(2,1)} async-done(((bf16[1,256,256]{2,1,0:T(8,128)(2,1)}), bf16[1,256,256]{2,1,0:T(8,128)(2,1)}) %all-reduce.13.cloned.1.call-update) | async-done | bytes 131088 | tf_op jit(solution)/shard_map/while/body/eval_jaxpr/psum | solution.py:9
  314.7 0.9 constant_dynamic-update-slice_fusion.6
  315.6 0.6 gather_fusion
  316.2 0.6 copy-done.6
  317.1 0.3 fusion.4
  317.4 13.1 %all-reduce.18 = bf16[256,256]{1,0:T(8,128)(2,1)S(1)} all-reduce(f32[256,256]{1,0:T(8,128)S(1)} %bitcast.65), channel_id=1, replica_groups=mesh['row'=8,'rep'=4] {'rep'}, use_global_device_ids=true, to_apply=%region_3.5 | all-reduce | flops 65536 | bytes 393216 | tf_op jit(solution)/shard_map/psum | solution.py:40
  330.5 1.0 fusion
  331.8 150.5 %while.37 = (s32[]{:T(128)}, bf16[2,256,256]{2,1,0:T(8,128)(2,1)S(1)}, s32[2]{0:T(128)S(1)}, s32[]{:T(128)}, bf16[256,256]{1,0:T(8,128)(2,1)S(1)}, /*index=5*/s32[]{:T(128)}, u32[]{:T(128)}, u32[]{:T(128)}) while((s32[]{:T(128)}, bf16[2,256,256]{2,1,0:T(8,128)(2,1)S(1)}, s32[2]{0:T(128)S(1)}, s32[]{:T(128)}, bf16[256,256]{1,0:T(8,128)(2,1)S(1)}, ...), condition=%wide.region_6.8_spmd, body=%wide.region_4.7_spmd.sunk | while | flops 131079 | bytes 1310923 | solution.py:25
  331.9 0.6 dynamic_slice.52
  333.1 0.7 select_bitcast_fusion.7
  333.8 72.7 %all-reduce.15.cloned.1.call-done = bf16[1,256,256]{2,1,0:T(8,128)(2,1)} async-done(((bf16[1,256,256]{2,1,0:T(8,128)(2,1)}), bf16[1,256,256]{2,1,0:T(8,128)(2,1)}) %all-reduce.15.cloned.1.call-update) | async-done | bytes 131088 | tf_op jit(solution)/shard_map/while/body/eval_jaxpr/psum | solution.py:9
  406.5 0.9 constant_dynamic-update-slice_fusion.7
  407.5 0.6 dynamic_slice.52
  408.8 0.7 select_bitcast_fusion.7
  409.5 71.9 %all-reduce.15.cloned.1.call-done = bf16[1,256,256]{2,1,0:T(8,128)(2,1)} async-done(((bf16[1,256,256]{2,1,0:T(8,128)(2,1)}), bf16[1,256,256]{2,1,0:T(8,128)(2,1)}) %all-reduce.15.cloned.1.call-update) | async-done | bytes 131088 | tf_op jit(solution)/shard_map/while/body/eval_jaxpr/psum | solution.py:9
  481.4 0.9 constant_dynamic-update-slice_fusion.7
  482.4 0.5 all-reduce.9.cloned.1.call-update
  483.0 0.6 gather_fusion.1
  483.7 0.3 fusion.2
  484.0 13.8 %all-reduce.19 = bf16[256,256]{1,0:T(8,128)(2,1)S(1)} all-reduce(f32[256,256]{1,0:T(8,128)S(1)} %bitcast.64), channel_id=1, replica_groups=mesh['row'=8,'rep'=4] {'rep'}, use_global_device_ids=true, to_apply=%region_7.9 | all-reduce | flops 65536 | bytes 393216 | tf_op jit(solution)/shard_map/psum | solution.py:40
  497.7 1.7 fusion.16
  499.4 17.9 %all-reduce.9.cloned.1.call-done = f32[256,256]{1,0:T(8,128)} async-done(((f32[256,256]{1,0:T(8,128)}), f32[256,256]{1,0:T(8,128)}) %all-reduce.9.cloned.1.call-update) | async-done | bytes 262160 | tf_op jit(solution)/shard_map/psum | solution.py:40
  517.3 1.8 fusion.15
  519.1 0.9 copy-done.2
  519.9 0.8 convolution_convert_fusion.1
  520.7 131.2 %all-reduce.11.cloned.1.call-done = (f32[256,256]{1,0:T(8,128)}, f32[256,256]{1,0:T(8,128)}) async-done(((f32[256,256]{1,0:T(8,128)}, f32[256,256]{1,0:T(8,128)}), (f32[256,256]{1,0:T(8,128)}, f32[256,256]{1,0:T(8,128)})) %all-reduce.11.cloned.1.call-update) | async-done | bytes 524304 | tf_op jit(solution)/shard_map/psum | solution.py:81
  651.9 1.7 copy.44
  653.6 0.7 copy.45
  (40 shorter events, 1.2 us)
Async XLA Ops:
  8.0 309.1 %copy-start = (bf16[1,1,2,4,128,128]{5,4,3,2,1,0:T(8,128)(2,1)S(1)}, bf16[1,1,2,4,128,128]{5,4,3,2,1,0:T(8,128)(2,1)}, u32[]{:S(2)}) copy-start(bf16[1,1,2,4,128,128]{5,4,3,2,1,0:T(8,128)(2,1)} %param.21) | copy-start | bytes 786436
  8.0 0.7 copy-start.4
  10.1 77.9 %all-reduce.17.cloned.1.call-start = ((), (), s32[]{:S(2)}) async-start(), calls=%async_computation.4 | async-start | bytes 262144 | tf_op jit(solution)/shard_map/while/body/eval_jaxpr/psum | solution.py:9
  88.9 74.3 %all-reduce.17.cloned.1.call-start = ((), (), s32[]{:S(2)}) async-start(), calls=%async_computation.4 | async-start | bytes 262144 | tf_op jit(solution)/shard_map/while/body/eval_jaxpr/psum | solution.py:9
  164.7 0.9 copy-start.1
  165.6 74.2 %all-reduce.13.cloned.1.call-start = ((), (), s32[]{:S(2)}) async-start(), calls=%async_computation.2 | async-start | bytes 262144 | tf_op jit(solution)/shard_map/while/body/eval_jaxpr/psum | solution.py:9
  240.8 73.9 %all-reduce.13.cloned.1.call-start = ((), (), s32[]{:S(2)}) async-start(), calls=%async_computation.2 | async-start | bytes 262144 | tf_op jit(solution)/shard_map/while/body/eval_jaxpr/psum | solution.py:9
  316.2 0.7 copy-start.6
  330.5 1.0 copy-start.5
  331.8 74.7 %all-reduce.15.cloned.1.call-start = ((), (), s32[]{:S(2)}) async-start(), calls=%async_computation.3 | async-start | bytes 262144 | tf_op jit(solution)/shard_map/while/body/eval_jaxpr/psum | solution.py:9
  407.5 73.9 %all-reduce.15.cloned.1.call-start = ((), (), s32[]{:S(2)}) async-start(), calls=%async_computation.3 | async-start | bytes 262144 | tf_op jit(solution)/shard_map/while/body/eval_jaxpr/psum | solution.py:9
  482.3 35.0 %all-reduce.9.cloned.1.call-start = ((), (), s32[]{:S(2)}) async-start(), calls=%async_computation | async-start | bytes 524288 | tf_op jit(solution)/shard_map/psum | solution.py:40
  482.9 169.0 %all-reduce.11.cloned.1.call-start = ((), (), s32[]{:S(2)}) async-start(), calls=%async_computation.1 | async-start | bytes 1048576 | tf_op jit(solution)/shard_map/psum | solution.py:81
  519.0 0.9 copy-start.2
  651.9 1.7 copy-start.3
Sparse Core Ops, SparseCore 0:
  14.8 73.1 all-reduce.16
  93.6 69.4 all-reduce.16
  170.3 69.4 all-reduce.12
  245.2 69.4 all-reduce.12
  336.2 70.2 all-reduce.14
  411.9 69.4 all-reduce.14
Sparse Core Ops, SparseCore 1:
  485.7 31.5 all-reduce.8
  523.2 128.7 all-reduce.10
where the time goes:
time: 662 us
  waiting for transfers between devices  587 us (89%)
  blocking collectives  26.8 us (4%)
  local copies, waits for them, and re-layouts  16.4 us (2%)
  between operations  15.7 us (2%)
  matrix products  7.22 us (1%)
    psum x6, waiting for transfers between devices, broadcast(): return lax.psum(jnp.where(mine, array, jnp.zeros_like(array)), axis)  437 us
    psum x1, waiting for transfers between devices, shards(): grad_one = lax.psum(grad_one, ('row', 'rep'))  131 us
    psum x2, blocking collectives, aggregate(): result = lax.psum(partial_value, 'rep')  26.8 us
    psum x1, waiting for transfers between devices, aggregate(): result = lax.psum(partial_value, 'rep')  17.9 us
  transfers between devices with their start and end apart: 8, of which 8 were waited for; matrix products, arithmetic and copies ran while one was open for 1% of the time, Pallas kernels for 0%

commit v1 on v0

v1 whole, which is shorter than its diff:
```python
import jax
import jax.numpy as jnp
from jax import lax
from jax.sharding import PartitionSpec as P

AXES = ("row", "rep")


def is_pow2(n):
    return n > 0 and (n & (n - 1)) == 0


def bit_pairs(devices, bit):
    return [(d, d ^ (1 << bit)) for d in range(devices)]


def reduce_scatter_bits(y, me, bits, devices):
    for step, bit in enumerate(bits):
        axis = len(bits) - 1 - step
        mine = (me >> bit) & 1
        keep = lax.dynamic_index_in_dim(y, mine, axis, keepdims=False)
        send = lax.dynamic_index_in_dim(y, 1 - mine, axis, keepdims=False)
        y = keep + lax.ppermute(send, AXES, bit_pairs(devices, bit))
    return y


def all_gather_bits(z, me, bits, devices):
    for step, bit in enumerate(reversed(bits)):
        mine = (me >> bit) & 1
        other = lax.ppermute(z, AXES, bit_pairs(devices, bit))
        low = jnp.where(mine == 0, z, other)
        high = jnp.where(mine == 0, other, z)
        z = jnp.stack([low, high], axis=step)
    return z


def gather_rounds(x, rows, copies):
    sections = rows // copies
    pieces = []
    for t in range(sections):
        pairs = []
        for r in range(rows):
            for c in range(copies):
                q = c * sections + (r + t) % sections
                pairs.append((q * copies + r // sections, r * copies + c))
        pieces.append(lax.ppermute(x, AXES, pairs))
    return jnp.stack(pieces)


def local_product(pieces, block_index, block_count, block_values, row_index, copy_index):
    sections = pieces.shape[0]
    block_rows = block_values.shape[2]
    slot_count = block_values.shape[3]
    block_side = block_values.shape[-1]
    width = pieces.shape[-1]
    panels = pieces.reshape(sections * block_rows, block_side, width)
    local = block_index[0, 0] - copy_index * slot_count
    shard = local // block_rows
    arrival = (shard - row_index) % sections
    columns = arrival * block_rows + local % block_rows
    live_slots = jnp.arange(slot_count, dtype=jnp.int32)[None, :] < block_count[0, 0][:, None]
    picked = jnp.take(panels, columns.reshape(-1), axis=0).reshape(
        block_rows, slot_count, block_side, width
    )
    picked = jnp.where(live_slots[:, :, None, None], picked, jnp.zeros((), picked.dtype))
    partial_value = lax.dot_general(
        block_values[0, 0],
        picked,
        (((1, 3), (1, 2)), ((0,), (0,))),
        preferred_element_type=jnp.float32,
    )
    return partial_value.reshape(block_rows * block_side, width)


def shards(features, cotangent, weight_one, weight_two, block_index, block_count, block_values):
    rows = lax.axis_size("row")
    copies = lax.axis_size("rep")
    row_index = lax.axis_index("row")
    copy_index = lax.axis_index("rep")
    devices = rows * copies
    me = row_index * copies + copy_index
    node_rows, feature_width = features.shape
    share_rows = node_rows // copies
    rep_levels = copies.bit_length() - 1
    rep_bits = list(range(rep_levels))
    all_bits = list(range(devices.bit_length() - 1))

    def reduce_rep(partial_value):
        y = partial_value.reshape([2] * rep_levels + [share_rows, partial_value.shape[-1]])
        return reduce_scatter_bits(y, me, rep_bits, devices)

    def gather_rep(z):
        return all_gather_bits(z, me, rep_bits, devices).reshape(node_rows, z.shape[-1])

    back_signal = lax.dot_general(
        cotangent, weight_two, (((1,), (1,)), ((), ())), preferred_element_type=jnp.float32
    ).astype(jnp.bfloat16)
    stage_in = jnp.concatenate([features, back_signal], axis=1)
    pieces = gather_rounds(stage_in, rows, copies)
    both = reduce_rep(
        local_product(pieces, block_index, block_count, block_values, row_index, copy_index)
    )
    agg_one = both[:, :feature_width].astype(jnp.bfloat16)
    carried = both[:, feature_width:]
    pre_one = jnp.dot(agg_one, weight_one, preferred_element_type=jnp.float32)
    hidden = jax.nn.silu(pre_one).astype(jnp.bfloat16)
    gate_value = jax.nn.sigmoid(pre_one)
    pre_grad = (carried * (gate_value + pre_one * gate_value * (1.0 - gate_value))).astype(
        jnp.bfloat16
    )
    grad_one = lax.dot_general(
        agg_one, pre_grad, (((0,), (0,)), ((), ())), preferred_element_type=jnp.float32
    )

    hidden_full = gather_rep(hidden)
    pieces_two = gather_rounds(hidden_full, rows, copies)
    agg_two = reduce_rep(
        local_product(pieces_two, block_index, block_count, block_values, row_index, copy_index)
    ).astype(jnp.bfloat16)
    logits = jnp.dot(agg_two, weight_two, preferred_element_type=jnp.float32).astype(jnp.bfloat16)
    cotangent_own = lax.dynamic_slice_in_dim(cotangent, copy_index * share_rows, share_rows, 0)
    grad_two = lax.dot_general(
        agg_two, cotangent_own, (((0,), (0,)), ((), ())), preferred_element_type=jnp.float32
    )

    grads = jnp.stack([grad_one, grad_two])
    total = grads.size
    levels = len(all_bits)
    segment = grads.reshape([2] * levels + [total // devices])
    summed = reduce_scatter_bits(segment, me, all_bits, devices)
    grads = all_gather_bits(summed, me, all_bits, devices).reshape(grads.shape)
    return (logits, grads[0], grads[1])


def solution(mesh):
    rows = mesh.shape["row"]
    copies = mesh.shape["rep"]
    if not (is_pow2(rows) and is_pow2(copies) and rows % copies == 0):
        raise ValueError("unsupported mesh")
    in_specs = (
        P("row", None),
        P("row", None),
        P(),
        P(),
        P("row", "rep", None, None),
        P("row", "rep", None),
        P("row", "rep", None, None, None, None),
    )
    out_specs = (P(("row", "rep"), None), P(), P())
    return jax.shard_map(shards, mesh=mesh, in_specs=in_specs, out_specs=out_specs, check_vma=False)
```

time: 662 us -> 114 us (0.17)
  waiting for transfers between devices: 587 us -> 52.3 us
  starting transfers between devices: 0.3 us -> 48 us
  blocking collectives: 26.8 us -> 0 us
  between operations: 15.7 us -> 1.18 us
  local copies, waits for them, and re-layouts: 16.4 us -> 7.95 us
    psum x8 -> x0, waiting for transfers between devices: 586 us -> none  [the longest x6 437 us: broadcast(): return lax.psum(jnp.where(mine, array, jnp.zeros_like(array)), axis)]
    ppermute x0 -> x20, waiting for transfers between devices: none -> 52.3 us  [the longest x9 23.7 us: reduce_scatter_bits(): y = keep + lax.ppermute(send, AXES, bit_pairs(devices, bit))]
    ppermute x0 -> x20, starting transfers between devices: none -> 48 us  [the longest x9 36.7 us: reduce_scatter_bits(): y = keep + lax.ppermute(send, AXES, bit_pairs(devices, bit))]
    psum x2 -> x0, blocking collectives: 26.8 us -> none  [aggregate(): result = lax.psum(partial_value, 'rep')]
  transfers between devices with their start and end apart: 8 -> 20, of which waited for: 8 -> 18; matrix products, arithmetic and copies ran while one was open for 1% -> 1% of each run, Pallas kernels for 0% -> 0%
where the time goes in v1:
time: 114 us
  waiting for transfers between devices  52.3 us (46%)
  starting transfers between devices  48 us (42%)
  local copies, waits for them, and re-layouts  7.95 us (7%)
  other arithmetic  2.42 us (2%)
  matrix products  2.3 us (2%)
  between operations  1.18 us (1%)
    ppermute x9, starting transfers between devices, reduce_scatter_bits(): y = keep + lax.ppermute(send, AXES, bit_pairs(devices, bit))  36.7 us
    ppermute x9, waiting for transfers between devices, reduce_scatter_bits(): y = keep + lax.ppermute(send, AXES, bit_pairs(devices, bit))  23.7 us
    ppermute x7, waiting for transfers between devices, all_gather_bits(): other = lax.ppermute(z, AXES, bit_pairs(devices, bit))  17.8 us
    ppermute x4, waiting for transfers between devices, gather_rounds(): pieces.append(lax.ppermute(x, AXES, pairs))  10.8 us
    ppermute x7, starting transfers between devices, all_gather_bits(): other = lax.ppermute(z, AXES, bit_pairs(devices, bit))  6.31 us
    ppermute x4, starting transfers between devices, gather_rounds(): pieces.append(lax.ppermute(x, AXES, pairs))  4.96 us
  transfers between devices with their start and end apart: 20, of which 18 were waited for; matrix products, arithmetic and copies ran while one was open for 1% of the time, Pallas kernels for 0%

profile of v1, /device:TPU:0, one launch (start us, length us, event | category | flops | bytes accessed | tf_op | source)
XLA Modules:
  0.0 114.1 jit_solution(10359106851162910429)
XLA Ops:
  0.7 1.1 copy.15
  2.0 3.1 %collective-permute-start.1 = (bf16[256,512]{0,1:T(8,128)(2,1)S(1)}, bf16[256,512]{0,1:T(8,128)(2,1)S(1)}, u32[]{:S(2)}, u32[]{:S(2)}) collective-permute-start(bf16[256,512]{0,1:T(8,128)(2,1)S(1)} %pad_maximum_fusion.2), channel_id=1, source_target_pairs={{4,0},{12,1},{20,2},{28,3},{0,4},{8,5},{16,6},{24,7},{5,8},{13,9},... | collective-permute-start | bytes 786440 | tf_op jit(solution)/shard_map/ppermute | solution.py:46
  5.1 0.7 collective-permute-start
  5.8 0.7 copy-done.3
  6.6 5.6 %collective-permute-done.1 = bf16[256,512]{0,1:T(8,128)(2,1)S(1)} collective-permute-done((bf16[256,512]{0,1:T(8,128)(2,1)S(1)}, bf16[256,512]{0,1:T(8,128)(2,1)S(1)}, u32[]{:S(2)}, u32[]{:S(2)}) %collective-permute-start.1) | collective-permute-done | bytes 262176 | tf_op jit(solution)/shard_map/ppermute | solution.py:46
  12.5 0.6 gather_fusion
  13.1 0.4 fusion
  13.6 4.4 %collective-permute-start.2 = (f32[2,64,512]{2,1,0:T(8,128)S(1)}, f32[2,64,512]{2,1,0:T(8,128)S(1)}, u32[]{:S(2)}, u32[]{:S(2)}) collective-permute-start(f32[2,64,512]{2,1,0:T(8,128)S(1)} %dynamic-slice_bitcast_fusion), channel_id=1, source_target_pairs={{0,1},{1,0},{2,3},{3,2},{4,5},{5,4},{6,7},{7,6},{8,9},{9,8},{10,11... | collective-permute-start | bytes 786440 | tf_op jit(solution)/shard_map/ppermute | solution.py:23
  18.0 1.2 %collective-permute-done.2 = f32[2,64,512]{2,1,0:T(8,128)S(1)} collective-permute-done((f32[2,64,512]{2,1,0:T(8,128)S(1)}, f32[2,64,512]{2,1,0:T(8,128)S(1)}, u32[]{:S(2)}, u32[]{:S(2)}) %collective-permute-start.2) | collective-permute-done | bytes 262176 | tf_op jit(solution)/shard_map/ppermute | solution.py:23
  19.3 17.2 %collective-permute-start.3 = (f32[64,512]{1,0:T(8,128)S(1)}, f32[64,512]{1,0:T(8,128)S(1)}, u32[]{:S(2)}, u32[]{:S(2)}) collective-permute-start(f32[64,512]{1,0:T(8,128)S(1)} %dynamic-slice_bitcast_fusion.2), channel_id=1, source_target_pairs={{0,2},{1,3},{2,0},{3,1},{4,6},{5,7},{6,4},{7,5},{8,10},{9,11},{10,... | collective-permute-start | bytes 393224 | tf_op jit(solution)/shard_map/ppermute | solution.py:23
  36.4 3.8 %collective-permute-done.3 = f32[64,512]{1,0:T(8,128)S(1)} collective-permute-done((f32[64,512]{1,0:T(8,128)S(1)}, f32[64,512]{1,0:T(8,128)S(1)}, u32[]{:S(2)}, u32[]{:S(2)}) %collective-permute-start.3) | collective-permute-done | bytes 131104 | tf_op jit(solution)/shard_map/ppermute | solution.py:23
  40.5 1.8 %collective-permute-start.4 = (bf16[64,256]{1,0:T(8,128)(2,1)S(1)}, bf16[64,256]{1,0:T(8,128)(2,1)S(1)}, u32[]{:S(2)}, u32[]{:S(2)}) collective-permute-start(bf16[64,256]{1,0:T(8,128)(2,1)S(1)} %get-tuple-element.31), channel_id=1, source_target_pairs={{0,2},{1,3},{2,0},{3,1},{4,6},{5,7},{6,4},{7,5},{8,10},{9,11},{10,... | collective-permute-start | bytes 98312 | tf_op jit(solution)/shard_map/ppermute | solution.py:30
  42.3 2.2 %collective-permute-done.4 = bf16[64,256]{1,0:T(8,128)(2,1)S(1)} collective-permute-done((bf16[64,256]{1,0:T(8,128)(2,1)S(1)}, bf16[64,256]{1,0:T(8,128)(2,1)S(1)}, u32[]{:S(2)}, u32[]{:S(2)}) %collective-permute-start.4) | collective-permute-done | bytes 32800 | tf_op jit(solution)/shard_map/ppermute | solution.py:30
  44.5 1.2 %collective-permute-done.5 = bf16[2,64,256]{2,1,0:T(8,128)(2,1)S(1)} collective-permute-done((bf16[2,64,256]{2,1,0:T(8,128)(2,1)S(1)}, bf16[2,64,256]{2,1,0:T(8,128)(2,1)S(1)}, u32[]{:S(2)}, u32[]{:S(2)}) %collective-permute-start.5) | collective-permute-done | bytes 65568 | tf_op jit(solution)/shard_map/ppermute | solution.py:30
  45.8 0.6 collective-permute-start.7
  46.4 0.7 collective-permute-start.6
  47.1 5.2 %collective-permute-done.7 = bf16[256,256]{1,0:T(8,128)(2,1)S(1)} collective-permute-done((bf16[256,256]{1,0:T(8,128)(2,1)S(1)}, bf16[256,256]{1,0:T(8,128)(2,1)S(1)}, u32[]{:S(2)}, u32[]{:S(2)}) %collective-permute-start.7) | collective-permute-done | bytes 131104 | tf_op jit(solution)/shard_map/ppermute | solution.py:46
  52.3 0.6 gather_fusion.1
  52.9 0.3 fusion.5
  53.3 2.2 %collective-permute-start.8 = (f32[2,64,256]{2,1,0:T(8,128)S(1)}, f32[2,64,256]{2,1,0:T(8,128)S(1)}, u32[]{:S(2)}, u32[]{:S(2)}) collective-permute-start(f32[2,64,256]{2,1,0:T(8,128)S(1)} %dynamic-slice_bitcast_fusion.1), channel_id=1, source_target_pairs={{0,1},{1,0},{2,3},{3,2},{4,5},{5,4},{6,7},{7,6},{8,9},{9,8},{10,11... | collective-permute-start | bytes 393224 | tf_op jit(solution)/shard_map/ppermute | solution.py:23
  55.9 0.6 collective-permute-done.8
  56.5 8.3 %collective-permute-start.9 = (f32[64,256]{1,0:T(8,128)S(1)}, f32[64,256]{1,0:T(8,128)S(1)}, u32[]{:S(2)}, u32[]{:S(2)}) collective-permute-start(f32[64,256]{1,0:T(8,128)S(1)} %dynamic-slice_bitcast_fusion.3), channel_id=1, source_target_pairs={{0,2},{1,3},{2,0},{3,1},{4,6},{5,7},{6,4},{7,5},{8,10},{9,11},{10,... | collective-permute-start | bytes 196616 | tf_op jit(solution)/shard_map/ppermute | solution.py:23
  64.8 2.4 %collective-permute-done.9 = f32[64,256]{1,0:T(8,128)S(1)} collective-permute-done((f32[64,256]{1,0:T(8,128)S(1)}, f32[64,256]{1,0:T(8,128)S(1)}, u32[]{:S(2)}, u32[]{:S(2)}) %collective-permute-start.9) | collective-permute-done | bytes 65568 | tf_op jit(solution)/shard_map/ppermute | solution.py:23
  67.7 0.6 constant_dynamic-slice_fusion.9
  68.5 1.5 %collective-permute-done.10 = f32[2,2,2,2,4096]{4,3,2,1,0:T(2,128)S(1)} collective-permute-done((f32[2,2,2,2,4096]{4,3,2,1,0:T(2,128)S(1)}, f32[2,2,2,2,4096]{4,3,2,1,0:T(2,128)S(1)}, u32[]{:S(2)}, u32[]{:S(2)}) %collective-permute-start.10) | collective-permute-done | bytes 262176 | tf_op jit(solution)/shard_map/ppermute | solution.py:23
  70.1 0.3 bitcast_add_fusion
  70.3 0.3 constant_dynamic-slice_fusion.7
  70.7 1.9 %collective-permute-start.11 = (f32[2,2,2,4096]{3,2,1,0:T(2,128)S(1)}, f32[2,2,2,4096]{3,2,1,0:T(2,128)S(1)}, u32[]{:S(2)}, u32[]{:S(2)}) collective-permute-start(f32[2,2,2,4096]{3,2,1,0:T(2,128)S(1)} %bitcast.126), channel_id=1, source_target_pairs={{0,2},{1,3},{2,0},{3,1},{4,6},{5,7},{6,4},{7,5},{8,10},{9,11},{10,... | collective-permute-start | bytes 393224 | tf_op jit(solution)/shard_map/ppermute | solution.py:23
  72.7 3.8 %collective-permute-done.11 = f32[2,2,2,4096]{3,2,1,0:T(2,128)S(1)} collective-permute-done((f32[2,2,2,4096]{3,2,1,0:T(2,128)S(1)}, f32[2,2,2,4096]{3,2,1,0:T(2,128)S(1)}, u32[]{:S(2)}, u32[]{:S(2)}) %collective-permute-start.11) | collective-permute-done | bytes 131104 | tf_op jit(solution)/shard_map/ppermute | solution.py:23
  76.8 1.6 %collective-permute-start.12 = (f32[2,2,4096]{2,1,0:T(2,128)S(1)}, f32[2,2,4096]{2,1,0:T(2,128)S(1)}, u32[]{:S(2)}, u32[]{:S(2)}) collective-permute-start(f32[2,2,4096]{2,1,0:T(2,128)S(1)} %bitcast.129), channel_id=1, source_target_pairs={{0,4},{1,5},{2,6},{3,7},{4,0},{5,1},{6,2},{7,3},{8,12},{9,13},{10,... | collective-permute-start | bytes 196616 | tf_op jit(solution)/shard_map/ppermute | solution.py:23
  78.4 2.7 %collective-permute-done.12 = f32[2,2,4096]{2,1,0:T(2,128)S(1)} collective-permute-done((f32[2,2,4096]{2,1,0:T(2,128)S(1)}, f32[2,2,4096]{2,1,0:T(2,128)S(1)}, u32[]{:S(2)}, u32[]{:S(2)}) %collective-permute-start.12) | collective-permute-done | bytes 65568 | tf_op jit(solution)/shard_map/ppermute | solution.py:23
  81.4 3.9 %collective-permute-done.13 = f32[2,4096]{1,0:T(2,128)S(1)} collective-permute-done((f32[2,4096]{1,0:T(2,128)S(1)}, f32[2,4096]{1,0:T(2,128)S(1)}, u32[]{:S(2)}, u32[]{:S(2)}) %collective-permute-start.13) | collective-permute-done | bytes 32800 | tf_op jit(solution)/shard_map/ppermute | solution.py:23
  85.4 0.9 collective-permute-start.14
  86.3 3.8 %collective-permute-done.14 = f32[4096]{0:T(1024)S(1)} collective-permute-done((f32[4096]{0:T(1024)S(1)}, f32[4096]{0:T(1024)S(1)}, u32[]{:S(2)}, u32[]{:S(2)}) %collective-permute-start.14) | collective-permute-done | bytes 16416 | tf_op jit(solution)/shard_map/ppermute | solution.py:23
  90.1 0.8 collective-permute-start.15
  90.9 3.8 %collective-permute-done.15 = f32[4096]{0:T(1024)S(1)} collective-permute-done((f32[4096]{0:T(1024)S(1)}, f32[4096]{0:T(1024)S(1)}, u32[]{:S(2)}, u32[]{:S(2)}) %collective-permute-start.15) | collective-permute-done | bytes 16416 | tf_op jit(solution)/shard_map/ppermute | solution.py:30
  94.9 3.8 %collective-permute-done.16 = f32[2,4096]{1,0:T(2,128)S(1)} collective-permute-done((f32[2,4096]{1,0:T(2,128)S(1)}, f32[2,4096]{1,0:T(2,128)S(1)}, u32[]{:S(2)}, u32[]{:S(2)}) %collective-permute-start.16) | collective-permute-done | bytes 32800 | tf_op jit(solution)/shard_map/ppermute | solution.py:30
  98.9 1.6 %collective-permute-start.17 = (f32[2,2,4096]{2,1,0:T(2,128)S(1)}, f32[2,2,4096]{2,1,0:T(2,128)S(1)}, u32[]{:S(2)}, u32[]{:S(2)}) collective-permute-start(f32[2,2,4096]{2,1,0:T(2,128)S(1)} %pad_maximum_fusion.8), channel_id=1, source_target_pairs={{0,4},{1,5},{2,6},{3,7},{4,0},{5,1},{6,2},{7,3},{8,12},{9,13},{10,... | collective-permute-start | bytes 196616 | tf_op jit(solution)/shard_map/ppermute | solution.py:30
  100.5 2.7 %collective-permute-done.17 = f32[2,2,4096]{2,1,0:T(2,128)S(1)} collective-permute-done((f32[2,2,4096]{2,1,0:T(2,128)S(1)}, f32[2,2,4096]{2,1,0:T(2,128)S(1)}, u32[]{:S(2)}, u32[]{:S(2)}) %collective-permute-start.17) | collective-permute-done | bytes 65568 | tf_op jit(solution)/shard_map/ppermute | solution.py:30
  103.6 1.8 %collective-permute-start.18 = (f32[2,2,2,4096]{3,2,1,0:T(2,128)S(1)}, f32[2,2,2,4096]{3,2,1,0:T(2,128)S(1)}, u32[]{:S(2)}, u32[]{:S(2)}) collective-permute-start(f32[2,2,2,4096]{3,2,1,0:T(2,128)S(1)} %pad_maximum_fusion.6), channel_id=1, source_target_pairs={{0,2},{1,3},{2,0},{3,1},{4,6},{5,7},{6,4},{7,5},{8,10},{9,11},{10,... | collective-permute-start | bytes 393224 | tf_op jit(solution)/shard_map/ppermute | solution.py:30
  105.4 3.2 %collective-permute-done.18 = f32[2,2,2,4096]{3,2,1,0:T(2,128)S(1)} collective-permute-done((f32[2,2,2,4096]{3,2,1,0:T(2,128)S(1)}, f32[2,2,2,4096]{3,2,1,0:T(2,128)S(1)}, u32[]{:S(2)}, u32[]{:S(2)}) %collective-permute-start.18) | collective-permute-done | bytes 131104 | tf_op jit(solution)/shard_map/ppermute | solution.py:30
  109.4 0.8 convolution_convert_fusion.1
  110.2 0.8 collective-permute-done.19
  110.9 0.3 broadcast_select_fusion
  111.5 0.3 copy.21
  111.8 0.5 pad_maximum_fusion.1
  112.3 0.9 squeeze.94
  113.2 0.9 squeeze.95
  (73 shorter events, 4.6 us)
Async XLA Ops:
  0.6 12.5 %copy-start = (bf16[1,1,2,4,128,128]{5,4,3,2,1,0:T(8,128)(2,1)S(1)}, bf16[1,1,2,4,128,128]{5,4,3,2,1,0:T(8,128)(2,1)}, u32[]{:S(2)}) copy-start(bf16[1,1,2,4,128,128]{5,4,3,2,1,0:T(8,128)(2,1)} %param.13) | copy-start | bytes 786436
  0.6 1.1 copy-start.2
  0.7 1.1 copy-start.1
  2.0 10.2 %collective-permute-start.1 = (bf16[256,512]{0,1:T(8,128)(2,1)S(1)}, bf16[256,512]{0,1:T(8,128)(2,1)S(1)}, u32[]{:S(2)}, u32[]{:S(2)}) collective-permute-start(bf16[256,512]{0,1:T(8,128)(2,1)S(1)} %pad_maximum_fusion.2), channel_id=1, source_target_pairs={{4,0},{12,1},{20,2},{28,3},{0,4},{8,5},{16,6},{24,7},{5,8},{13,9},... | collective-permute-start | bytes 786440 | tf_op jit(solution)/shard_map/ppermute | solution.py:46
  5.1 7.2 %collective-permute-start = (bf16[256,512]{0,1:T(8,128)(2,1)S(1)}, bf16[256,512]{0,1:T(8,128)(2,1)S(1)}, u32[]{:S(2)}, u32[]{:S(2)}) collective-permute-start(bf16[256,512]{0,1:T(8,128)(2,1)S(1)} %pad_maximum_fusion.2), channel_id=1, source_target_pairs={{0,0},{8,1},{16,2},{24,3},{4,4},{12,5},{20,6},{28,7},{1,8},{9,9},{... | collective-permute-start | bytes 786440 | tf_op jit(solution)/shard_map/ppermute | solution.py:46
  5.7 0.7 copy-start.3
  5.8 0.7 copy-start.4
  13.6 5.6 %collective-permute-start.2 = (f32[2,64,512]{2,1,0:T(8,128)S(1)}, f32[2,64,512]{2,1,0:T(8,128)S(1)}, u32[]{:S(2)}, u32[]{:S(2)}) collective-permute-start(f32[2,64,512]{2,1,0:T(8,128)S(1)} %dynamic-slice_bitcast_fusion), channel_id=1, source_target_pairs={{0,1},{1,0},{2,3},{3,2},{4,5},{5,4},{6,7},{7,6},{8,9},{9,8},{10,11... | collective-permute-start | bytes 786440 | tf_op jit(solution)/shard_map/ppermute | solution.py:23
  19.3 21.0 %collective-permute-start.3 = (f32[64,512]{1,0:T(8,128)S(1)}, f32[64,512]{1,0:T(8,128)S(1)}, u32[]{:S(2)}, u32[]{:S(2)}) collective-permute-start(f32[64,512]{1,0:T(8,128)S(1)} %dynamic-slice_bitcast_fusion.2), channel_id=1, source_target_pairs={{0,2},{1,3},{2,0},{3,1},{4,6},{5,7},{6,4},{7,5},{8,10},{9,11},{10,... | collective-permute-start | bytes 393224 | tf_op jit(solution)/shard_map/ppermute | solution.py:23
  36.4 3.8 %copy-start.5 = (bf16[256,256]{1,0:T(8,128)(2,1)S(1)}, bf16[256,256]{1,0:T(8,128)(2,1)}, u32[]{:S(2)}) copy-start(bf16[256,256]{1,0:T(8,128)(2,1)} %param.9) | copy-start | bytes 393220
  40.5 4.0 %collective-permute-start.4 = (bf16[64,256]{1,0:T(8,128)(2,1)S(1)}, bf16[64,256]{1,0:T(8,128)(2,1)S(1)}, u32[]{:S(2)}, u32[]{:S(2)}) collective-permute-start(bf16[64,256]{1,0:T(8,128)(2,1)S(1)} %get-tuple-element.31), channel_id=1, source_target_pairs={{0,2},{1,3},{2,0},{3,1},{4,6},{5,7},{6,4},{7,5},{8,10},{9,11},{10,... | collective-permute-start | bytes 98312 | tf_op jit(solution)/shard_map/ppermute | solution.py:30
  44.5 1.3 %collective-permute-start.5 = (bf16[2,64,256]{2,1,0:T(8,128)(2,1)S(1)}, bf16[2,64,256]{2,1,0:T(8,128)(2,1)S(1)}, u32[]{:S(2)}, u32[]{:S(2)}) collective-permute-start(bf16[2,64,256]{2,1,0:T(8,128)(2,1)S(1)} %pad_maximum_fusion.7), channel_id=1, source_target_pairs={{0,1},{1,0},{2,3},{3,2},{4,5},{5,4},{6,7},{7,6},{8,9},{9,8},{10,11... | collective-permute-start | bytes 196616 | tf_op jit(solution)/shard_map/ppermute | solution.py:30
  45.8 6.4 %collective-permute-start.7 = (bf16[256,256]{1,0:T(8,128)(2,1)S(1)}, bf16[256,256]{1,0:T(8,128)(2,1)S(1)}, u32[]{:S(2)}, u32[]{:S(2)}) collective-permute-start(bf16[256,256]{1,0:T(8,128)(2,1)S(1)} %bitcast.124), channel_id=1, source_target_pairs={{4,0},{12,1},{20,2},{28,3},{0,4},{8,5},{16,6},{24,7},{5,8},{13,9},... | collective-permute-start | bytes 393224 | tf_op jit(solution)/shard_map/ppermute | solution.py:46
  46.4 5.9 %collective-permute-start.6 = (bf16[256,256]{1,0:T(8,128)(2,1)S(1)}, bf16[256,256]{1,0:T(8,128)(2,1)S(1)}, u32[]{:S(2)}, u32[]{:S(2)}) collective-permute-start(bf16[256,256]{1,0:T(8,128)(2,1)S(1)} %bitcast.125), channel_id=1, source_target_pairs={{0,0},{8,1},{16,2},{24,3},{4,4},{12,5},{20,6},{28,7},{1,8},{9,9},{... | collective-permute-start | bytes 393224 | tf_op jit(solution)/shard_map/ppermute | solution.py:46
  53.3 3.2 %collective-permute-start.8 = (f32[2,64,256]{2,1,0:T(8,128)S(1)}, f32[2,64,256]{2,1,0:T(8,128)S(1)}, u32[]{:S(2)}, u32[]{:S(2)}) collective-permute-start(f32[2,64,256]{2,1,0:T(8,128)S(1)} %dynamic-slice_bitcast_fusion.1), channel_id=1, source_target_pairs={{0,1},{1,0},{2,3},{3,2},{4,5},{5,4},{6,7},{7,6},{8,9},{9,8},{10,11... | collective-permute-start | bytes 393224 | tf_op jit(solution)/shard_map/ppermute | solution.py:23
  56.5 10.7 %collective-permute-start.9 = (f32[64,256]{1,0:T(8,128)S(1)}, f32[64,256]{1,0:T(8,128)S(1)}, u32[]{:S(2)}, u32[]{:S(2)}) collective-permute-start(f32[64,256]{1,0:T(8,128)S(1)} %dynamic-slice_bitcast_fusion.3), channel_id=1, source_target_pairs={{0,2},{1,3},{2,0},{3,1},{4,6},{5,7},{6,4},{7,5},{8,10},{9,11},{10,... | collective-permute-start | bytes 196616 | tf_op jit(solution)/shard_map/ppermute | solution.py:23
  68.5 1.6 %collective-permute-start.10 = (f32[2,2,2,2,4096]{4,3,2,1,0:T(2,128)S(1)}, f32[2,2,2,2,4096]{4,3,2,1,0:T(2,128)S(1)}, u32[]{:S(2)}, u32[]{:S(2)}) collective-permute-start(f32[2,2,2,2,4096]{4,3,2,1,0:T(2,128)S(1)} %bitcast.117), channel_id=1, source_target_pairs={{0,1},{1,0},{2,3},{3,2},{4,5},{5,4},{6,7},{7,6},{8,9},{9,8},{10,11... | collective-permute-start | bytes 786440 | tf_op jit(solution)/shard_map/ppermute | solution.py:23
  70.7 5.7 %collective-permute-start.11 = (f32[2,2,2,4096]{3,2,1,0:T(2,128)S(1)}, f32[2,2,2,4096]{3,2,1,0:T(2,128)S(1)}, u32[]{:S(2)}, u32[]{:S(2)}) collective-permute-start(f32[2,2,2,4096]{3,2,1,0:T(2,128)S(1)} %bitcast.126), channel_id=1, source_target_pairs={{0,2},{1,3},{2,0},{3,1},{4,6},{5,7},{6,4},{7,5},{8,10},{9,11},{10,... | collective-permute-start | bytes 393224 | tf_op jit(solution)/shard_map/ppermute | solution.py:23
  76.8 4.3 %collective-permute-start.12 = (f32[2,2,4096]{2,1,0:T(2,128)S(1)}, f32[2,2,4096]{2,1,0:T(2,128)S(1)}, u32[]{:S(2)}, u32[]{:S(2)}) collective-permute-start(f32[2,2,4096]{2,1,0:T(2,128)S(1)} %bitcast.129), channel_id=1, source_target_pairs={{0,4},{1,5},{2,6},{3,7},{4,0},{5,1},{6,2},{7,3},{8,12},{9,13},{10,... | collective-permute-start | bytes 196616 | tf_op jit(solution)/shard_map/ppermute | solution.py:23
  81.3 4.0 %collective-permute-start.13 = (f32[2,4096]{1,0:T(2,128)S(1)}, f32[2,4096]{1,0:T(2,128)S(1)}, u32[]{:S(2)}, u32[]{:S(2)}) collective-permute-start(f32[2,4096]{1,0:T(2,128)S(1)} %bitcast.131), channel_id=1, source_target_pairs={{0,8},{1,9},{2,10},{3,11},{4,12},{5,13},{6,14},{7,15},{8,0},{9,1},... | collective-permute-start | bytes 98312 | tf_op jit(solution)/shard_map/ppermute | solution.py:23
  85.4 4.7 %collective-permute-start.14 = (f32[4096]{0:T(1024)S(1)}, f32[4096]{0:T(1024)S(1)}, u32[]{:S(2)}, u32[]{:S(2)}) collective-permute-start(f32[4096]{0:T(1024)S(1)} %bitcast.132), channel_id=1, source_target_pairs={{0,16},{1,17},{2,18},{3,19},{4,20},{5,21},{6,22},{7,23},{8,24},{9,... | collective-permute-start | bytes 49160 | tf_op jit(solution)/shard_map/ppermute | solution.py:23
  90.1 4.6 %collective-permute-start.15 = (f32[4096]{0:T(1024)S(1)}, f32[4096]{0:T(1024)S(1)}, u32[]{:S(2)}, u32[]{:S(2)}) collective-permute-start(f32[4096]{0:T(1024)S(1)} %add.210), channel_id=1, source_target_pairs={{0,16},{1,17},{2,18},{3,19},{4,20},{5,21},{6,22},{7,23},{8,24},{9,... | collective-permute-start | bytes 49160 | tf_op jit(solution)/shard_map/ppermute | solution.py:30
  94.8 4.0 %collective-permute-start.16 = (f32[2,4096]{1,0:T(2,128)S(1)}, f32[2,4096]{1,0:T(2,128)S(1)}, u32[]{:S(2)}, u32[]{:S(2)}) collective-permute-start(f32[2,4096]{1,0:T(2,128)S(1)} %pad_maximum_fusion.9), channel_id=1, source_target_pairs={{0,8},{1,9},{2,10},{3,11},{4,12},{5,13},{6,14},{7,15},{8,0},{9,1},... | collective-permute-start | bytes 98312 | tf_op jit(solution)/shard_map/ppermute | solution.py:30
  98.9 4.3 %collective-permute-start.17 = (f32[2,2,4096]{2,1,0:T(2,128)S(1)}, f32[2,2,4096]{2,1,0:T(2,128)S(1)}, u32[]{:S(2)}, u32[]{:S(2)}) collective-permute-start(f32[2,2,4096]{2,1,0:T(2,128)S(1)} %pad_maximum_fusion.8), channel_id=1, source_target_pairs={{0,4},{1,5},{2,6},{3,7},{4,0},{5,1},{6,2},{7,3},{8,12},{9,13},{10,... | collective-permute-start | bytes 196616 | tf_op jit(solution)/shard_map/ppermute | solution.py:30
  103.6 5.0 %collective-permute-start.18 = (f32[2,2,2,4096]{3,2,1,0:T(2,128)S(1)}, f32[2,2,2,4096]{3,2,1,0:T(2,128)S(1)}, u32[]{:S(2)}, u32[]{:S(2)}) collective-permute-start(f32[2,2,2,4096]{3,2,1,0:T(2,128)S(1)} %pad_maximum_fusion.6), channel_id=1, source_target_pairs={{0,2},{1,3},{2,0},{3,1},{4,6},{5,7},{6,4},{7,5},{8,10},{9,11},{10,... | collective-permute-start | bytes 393224 | tf_op jit(solution)/shard_map/ppermute | solution.py:30
  109.3 1.6 %collective-permute-start.19 = (f32[2,2,2,2,4096]{4,3,2,1,0:T(2,128)S(1)}, f32[2,2,2,2,4096]{4,3,2,1,0:T(2,128)S(1)}, u32[]{:S(2)}, u32[]{:S(2)}) collective-permute-start(f32[2,2,2,2,4096]{4,3,2,1,0:T(2,128)S(1)} %pad_maximum_fusion.4), channel_id=1, source_target_pairs={{0,1},{1,0},{2,3},{3,2},{4,5},{5,4},{6,7},{7,6},{8,9},{9,8},{10,11... | collective-permute-start | bytes 786440 | tf_op jit(solution)/shard_map/ppermute | solution.py:30

commit v2 on v1

--- a/solution.py
+++ b/solution.py
@@ -95,13 +95,14 @@
     back_signal = lax.dot_general(
         cotangent, weight_two, (((1,), (1,)), ((), ())), preferred_element_type=jnp.float32
     ).astype(jnp.bfloat16)
-    stage_in = jnp.concatenate([features, back_signal], axis=1)
+    stage_in = jnp.concatenate([features, back_signal, cotangent], axis=1)
     pieces = gather_rounds(stage_in, rows, copies)
     both = reduce_rep(
         local_product(pieces, block_index, block_count, block_values, row_index, copy_index)
     )
     agg_one = both[:, :feature_width].astype(jnp.bfloat16)
-    carried = both[:, feature_width:]
+    carried = both[:, feature_width : 2 * feature_width]
+    spread_cotangent = both[:, 2 * feature_width :]
     pre_one = jnp.dot(agg_one, weight_one, preferred_element_type=jnp.float32)
     hidden = jax.nn.silu(pre_one).astype(jnp.bfloat16)
     gate_value = jax.nn.sigmoid(pre_one)
@@ -111,6 +112,19 @@
     grad_one = lax.dot_general(
         agg_one, pre_grad, (((0,), (0,)), ((), ())), preferred_element_type=jnp.float32
     )
+    grad_two = lax.dot_general(
+        hidden.astype(jnp.float32),
+        spread_cotangent,
+        (((0,), (0,)), ((), ())),
+        precision=lax.Precision.HIGHEST,
+        preferred_element_type=jnp.float32,
+    )
+    grads = jnp.stack([grad_one, grad_two])
+    total = grads.size
+    levels = len(all_bits)
+    segment = grads.reshape([2] * levels + [total // devices])
+    summed = reduce_scatter_bits(segment, me, all_bits, devices)
+    grads = all_gather_bits(summed, me, all_bits, devices).reshape(grads.shape)
 
     hidden_full = gather_rep(hidden)
     pieces_two = gather_rounds(hidden_full, rows, copies)
@@ -118,17 +132,6 @@
         local_product(pieces_two, block_index, block_count, block_values, row_index, copy_index)
     ).astype(jnp.bfloat16)
     logits = jnp.dot(agg_two, weight_two, preferred_element_type=jnp.float32).astype(jnp.bfloat16)
-    cotangent_own = lax.dynamic_slice_in_dim(cotangent, copy_index * share_rows, share_rows, 0)
-    grad_two = lax.dot_general(
-        agg_two, cotangent_own, (((0,), (0,)), ((), ())), preferred_element_type=jnp.float32
-    )
-
-    grads = jnp.stack([grad_one, grad_two])
-    total = grads.size
-    levels = len(all_bits)
-    segment = grads.reshape([2] * levels + [total // devices])
-    summed = reduce_scatter_bits(segment, me, all_bits, devices)
-    grads = all_gather_bits(summed, me, all_bits, devices).reshape(grads.shape)
     return (logits, grads[0], grads[1])
 
 

time: 114 us -> 111 us (0.974)
  waiting for transfers between devices: 52.3 us -> 47.6 us
  matrix products: 2.3 us -> 3.47 us
    ppermute x7, waiting for transfers between devices: 17.8 us -> 14.1 us  [all_gather_bits(): other = lax.ppermute(z, AXES, bit_pairs(devices, bit))]
    ppermute x7, starting transfers between devices: 6.31 us -> 3.32 us  [all_gather_bits(): other = lax.ppermute(z, AXES, bit_pairs(devices, bit))]
    ppermute x9, starting transfers between devices: 36.7 us -> 39.2 us  [reduce_scatter_bits(): y = keep + lax.ppermute(send, AXES, bit_pairs(devices, bit))]
    ppermute x4, waiting for transfers between devices: 10.8 us -> 9.08 us  [gather_rounds(): pieces.append(lax.ppermute(x, AXES, pairs))]
    unnamed x18 -> x17, local copies, waits for them, and re-layouts: 2.15 us -> 2.48 us
  transfers between devices with their start and end apart: 20 -> 20, of which waited for: 18 -> 12; matrix products, arithmetic and copies ran while one was open for 1% -> 4% of each run, Pallas kernels for 0% -> 0%
where the time goes in v2:
time: 111 us
  waiting for transfers between devices  47.6 us (43%)
  starting transfers between devices  47.4 us (43%)
  local copies, waits for them, and re-layouts  8.38 us (8%)
  matrix products  3.47 us (3%)
  other arithmetic  2.45 us (2%)
  between operations  1.23 us (1%)
    ppermute x9, starting transfers between devices, reduce_scatter_bits(): y = keep + lax.ppermute(send, AXES, bit_pairs(devices, bit))  39.2 us
    ppermute x9, waiting for transfers between devices, reduce_scatter_bits(): y = keep + lax.ppermute(send, AXES, bit_pairs(devices, bit))  24.4 us
    ppermute x7, waiting for transfers between devices, all_gather_bits(): other = lax.ppermute(z, AXES, bit_pairs(devices, bit))  14.1 us
    ppermute x4, waiting for transfers between devices, gather_rounds(): pieces.append(lax.ppermute(x, AXES, pairs))  9.08 us
    ppermute x4, starting transfers between devices, gather_rounds(): pieces.append(lax.ppermute(x, AXES, pairs))  4.97 us
    ppermute x7, starting transfers between devices, all_gather_bits(): other = lax.ppermute(z, AXES, bit_pairs(devices, bit))  3.32 us
    unnamed x17, local copies, waits for them, and re-layouts  2.48 us
  transfers between devices with their start and end apart: 20, of which 12 were waited for; matrix products, arithmetic and copies ran while one was open for 4% of the time, Pallas kernels for 0%

profile of v2, /device:TPU:0, one launch (start us, length us, event | category | flops | bytes accessed | tf_op | source)
XLA Modules:
  0.0 110.5 jit_solution(15431550739343062846)
XLA Ops:
  0.7 1.0 copy.17
  1.7 1.2 %convolution_convert_fusion = bf16[256,256]{0,1:T(8,128)(2,1)S(1)} fusion(bf16[256,256]{1,0:T(8,128)(2,1)} %param.8, bf16[256,256]{1,0:T(8,128)(2,1)} %param.10), kind=kOutput, calls=%fused_computation.7 | convolution fusion | flops 33619968 | bytes 393216 | tf_op jit(solution)/shard_map/dot_general | solution.py:95
  2.9 1.0 copy.16
  4.0 3.1 %collective-permute-start.1 = (bf16[256,768]{0,1:T(8,128)(2,1)S(1)}, bf16[256,768]{0,1:T(8,128)(2,1)S(1)}, u32[]{:S(2)}, u32[]{:S(2)}) collective-permute-start(bf16[256,768]{0,1:T(8,128)(2,1)S(1)} %pad_maximum_fusion.1), channel_id=1, source_target_pairs={{4,0},{12,1},{20,2},{28,3},{0,4},{8,5},{16,6},{24,7},{5,8},{13,9},... | collective-permute-start | bytes 1179656 | tf_op jit(solution)/shard_map/ppermute | solution.py:46
  7.0 0.7 collective-permute-start
  7.9 9.1 %collective-permute-done.1 = bf16[256,768]{0,1:T(8,128)(2,1)S(1)} collective-permute-done((bf16[256,768]{0,1:T(8,128)(2,1)S(1)}, bf16[256,768]{0,1:T(8,128)(2,1)S(1)}, u32[]{:S(2)}, u32[]{:S(2)}) %collective-permute-start.1) | collective-permute-done | bytes 393248 | tf_op jit(solution)/shard_map/ppermute | solution.py:46
  17.1 0.3 copy.18
  17.3 0.6 gather_fusion
  18.0 0.5 fusion
  18.6 6.5 %collective-permute-start.2 = (f32[2,64,768]{2,1,0:T(8,128)S(1)}, f32[2,64,768]{2,1,0:T(8,128)S(1)}, u32[]{:S(2)}, u32[]{:S(2)}) collective-permute-start(f32[2,64,768]{2,1,0:T(8,128)S(1)} %dynamic-slice_bitcast_fusion), channel_id=1, source_target_pairs={{0,1},{1,0},{2,3},{3,2},{4,5},{5,4},{6,7},{7,6},{8,9},{9,8},{10,11... | collective-permute-start | bytes 1179656 | tf_op jit(solution)/shard_map/ppermute | solution.py:23
  25.0 1.3 %collective-permute-done.2 = f32[2,64,768]{2,1,0:T(8,128)S(1)} collective-permute-done((f32[2,64,768]{2,1,0:T(8,128)S(1)}, f32[2,64,768]{2,1,0:T(8,128)S(1)}, u32[]{:S(2)}, u32[]{:S(2)}) %collective-permute-start.2) | collective-permute-done | bytes 393248 | tf_op jit(solution)/shard_map/ppermute | solution.py:23
  26.5 23.6 %collective-permute-start.3 = (f32[64,768]{1,0:T(8,128)S(1)}, f32[64,768]{1,0:T(8,128)S(1)}, u32[]{:S(2)}, u32[]{:S(2)}) collective-permute-start(f32[64,768]{1,0:T(8,128)S(1)} %dynamic-slice_bitcast_fusion.1), channel_id=1, source_target_pairs={{0,2},{1,3},{2,0},{3,1},{4,6},{5,7},{6,4},{7,5},{8,10},{9,11},{10,... | collective-permute-start | bytes 589832 | tf_op jit(solution)/shard_map/ppermute | solution.py:23
  50.1 5.2 %collective-permute-done.3 = f32[64,768]{1,0:T(8,128)S(1)} collective-permute-done((f32[64,768]{1,0:T(8,128)S(1)}, f32[64,768]{1,0:T(8,128)S(1)}, u32[]{:S(2)}, u32[]{:S(2)}) %collective-permute-start.3) | collective-permute-done | bytes 196640 | tf_op jit(solution)/shard_map/ppermute | solution.py:23
  55.3 0.2 fusion.22
  55.5 0.2 fusion.23
  55.9 0.3 fusion.17
  56.4 0.6 constant_dynamic-slice_fusion.9
  57.0 0.2 copy.42
  57.3 1.8 %collective-permute-start.4 = (bf16[64,256]{1,0:T(8,128)(2,1)S(1)}, bf16[64,256]{1,0:T(8,128)(2,1)S(1)}, u32[]{:S(2)}, u32[]{:S(2)}) collective-permute-start(bf16[64,256]{1,0:T(8,128)(2,1)S(1)} %get-tuple-element.31), channel_id=1, source_target_pairs={{0,2},{1,3},{2,0},{3,1},{4,6},{5,7},{6,4},{7,5},{8,10},{9,11},{10,... | collective-permute-start | bytes 98312 | tf_op jit(solution)/shard_map/ppermute | solution.py:30
  59.1 0.3 bitcast_add_fusion.1
  59.4 0.3 constant_dynamic-slice_fusion.7
  59.8 1.5 %collective-permute-start.11 = (f32[2,2,2,4096]{3,2,1,0:T(2,128)S(1)}, f32[2,2,2,4096]{3,2,1,0:T(2,128)S(1)}, u32[]{:S(2)}, u32[]{:S(2)}) collective-permute-start(f32[2,2,2,4096]{3,2,1,0:T(2,128)S(1)} %bitcast.126), channel_id=1, source_target_pairs={{0,2},{1,3},{2,0},{3,1},{4,6},{5,7},{6,4},{7,5},{8,10},{9,11},{10,... | collective-permute-start | bytes 393224 | tf_op jit(solution)/shard_map/ppermute | solution.py:23
  61.4 4.0 %collective-permute-done.11 = f32[2,2,2,4096]{3,2,1,0:T(2,128)S(1)} collective-permute-done((f32[2,2,2,4096]{3,2,1,0:T(2,128)S(1)}, f32[2,2,2,4096]{3,2,1,0:T(2,128)S(1)}, u32[]{:S(2)}, u32[]{:S(2)}) %collective-permute-start.11) | collective-permute-done | bytes 131104 | tf_op jit(solution)/shard_map/ppermute | solution.py:23
  65.8 0.6 collective-permute-start.12
  66.4 3.7 %collective-permute-done.12 = f32[2,2,4096]{2,1,0:T(2,128)S(1)} collective-permute-done((f32[2,2,4096]{2,1,0:T(2,128)S(1)}, f32[2,2,4096]{2,1,0:T(2,128)S(1)}, u32[]{:S(2)}, u32[]{:S(2)}) %collective-permute-start.12) | collective-permute-done | bytes 65568 | tf_op jit(solution)/shard_map/ppermute | solution.py:23
  70.3 0.2 collective-permute-start.13
  70.5 0.6 collective-permute-start.7
  71.1 0.7 collective-permute-start.6
  71.7 2.5 %collective-permute-done.13 = f32[2,4096]{1,0:T(2,128)S(1)} collective-permute-done((f32[2,4096]{1,0:T(2,128)S(1)}, f32[2,4096]{1,0:T(2,128)S(1)}, u32[]{:S(2)}, u32[]{:S(2)}) %collective-permute-start.13) | collective-permute-done | bytes 32800 | tf_op jit(solution)/shard_map/ppermute | solution.py:23
  74.3 4.6 %collective-permute-start.14 = (f32[4096]{0:T(1024)S(1)}, f32[4096]{0:T(1024)S(1)}, u32[]{:S(2)}, u32[]{:S(2)}) collective-permute-start(f32[4096]{0:T(1024)S(1)} %bitcast.132), channel_id=1, source_target_pairs={{0,16},{1,17},{2,18},{3,19},{4,20},{5,21},{6,22},{7,23},{8,24},{9,... | collective-permute-start | bytes 49160 | tf_op jit(solution)/shard_map/ppermute | solution.py:23
  79.0 7.6 %collective-permute-done.14 = f32[4096]{0:T(1024)S(1)} collective-permute-done((f32[4096]{0:T(1024)S(1)}, f32[4096]{0:T(1024)S(1)}, u32[]{:S(2)}, u32[]{:S(2)}) %collective-permute-start.14) | collective-permute-done | bytes 16416 | tf_op jit(solution)/shard_map/ppermute | solution.py:23
  86.6 0.6 gather_fusion.1
  87.2 4.0 %collective-permute-done.15 = f32[4096]{0:T(1024)S(1)} collective-permute-done((f32[4096]{0:T(1024)S(1)}, f32[4096]{0:T(1024)S(1)}, u32[]{:S(2)}, u32[]{:S(2)}) %collective-permute-start.15) | collective-permute-done | bytes 16416 | tf_op jit(solution)/shard_map/ppermute | solution.py:30
  91.3 0.3 fusion.7
  91.6 3.6 %collective-permute-done.16 = f32[2,4096]{1,0:T(2,128)S(1)} collective-permute-done((f32[2,4096]{1,0:T(2,128)S(1)}, f32[2,4096]{1,0:T(2,128)S(1)}, u32[]{:S(2)}, u32[]{:S(2)}) %collective-permute-start.16) | collective-permute-done | bytes 32800 | tf_op jit(solution)/shard_map/ppermute | solution.py:30
  95.4 1.2 %collective-permute-start.17 = (f32[2,2,4096]{2,1,0:T(2,128)S(1)}, f32[2,2,4096]{2,1,0:T(2,128)S(1)}, u32[]{:S(2)}, u32[]{:S(2)}) collective-permute-start(f32[2,2,4096]{2,1,0:T(2,128)S(1)} %pad_maximum_fusion.8), channel_id=1, source_target_pairs={{0,4},{1,5},{2,6},{3,7},{4,0},{5,1},{6,2},{7,3},{8,12},{9,13},{10,... | collective-permute-start | bytes 196616 | tf_op jit(solution)/shard_map/ppermute | solution.py:30
  96.7 3.0 %collective-permute-done.17 = f32[2,2,4096]{2,1,0:T(2,128)S(1)} collective-permute-done((f32[2,2,4096]{2,1,0:T(2,128)S(1)}, f32[2,2,4096]{2,1,0:T(2,128)S(1)}, u32[]{:S(2)}, u32[]{:S(2)}) %collective-permute-start.17) | collective-permute-done | bytes 65568 | tf_op jit(solution)/shard_map/ppermute | solution.py:30
  100.2 2.1 %collective-permute-start.9 = (f32[64,256]{1,0:T(8,128)S(1)}, f32[64,256]{1,0:T(8,128)S(1)}, u32[]{:S(2)}, u32[]{:S(2)}) collective-permute-start(f32[64,256]{1,0:T(8,128)S(1)} %dynamic-slice_bitcast_fusion.3), channel_id=1, source_target_pairs={{0,2},{1,3},{2,0},{3,1},{4,6},{5,7},{6,4},{7,5},{8,10},{9,11},{10,... | collective-permute-start | bytes 196616 | tf_op jit(solution)/shard_map/ppermute | solution.py:23
  102.3 2.8 %collective-permute-done.18 = f32[2,2,2,4096]{3,2,1,0:T(2,128)S(1)} collective-permute-done((f32[2,2,2,4096]{3,2,1,0:T(2,128)S(1)}, f32[2,2,2,4096]{3,2,1,0:T(2,128)S(1)}, u32[]{:S(2)}, u32[]{:S(2)}) %collective-permute-start.18) | collective-permute-done | bytes 131104 | tf_op jit(solution)/shard_map/ppermute | solution.py:30
  105.5 0.2 pad_maximum_fusion.4
  105.9 0.8 convolution_convert_fusion.1
  106.6 0.7 collective-permute-done.19
  107.4 0.3 broadcast_select_fusion
  107.7 0.2 stack.118
  107.9 0.3 copy.23
  108.2 0.5 pad_maximum_fusion.2
  108.7 0.9 squeeze.94
  109.6 0.9 squeeze.95
  (71 shorter events, 3.0 us)
Async XLA Ops:
  0.6 17.4 %copy-start = (bf16[1,1,2,4,128,128]{5,4,3,2,1,0:T(8,128)(2,1)S(1)}, bf16[1,1,2,4,128,128]{5,4,3,2,1,0:T(8,128)(2,1)}, u32[]{:S(2)}) copy-start(bf16[1,1,2,4,128,128]{5,4,3,2,1,0:T(8,128)(2,1)} %param.13) | copy-start | bytes 786436
  0.6 7.1 %copy-start.2 = (s32[1,1,2,4]{3,2,1,0:T(2,128)S(1)}, s32[1,1,2,4]{3,2,1,0:T(2,128)}, u32[]{:S(2)}) copy-start(s32[1,1,2,4]{3,2,1,0:T(2,128)} %param.11) | copy-start | bytes 100
  0.7 7.1 %copy-start.3 = (s32[1,1,2]{2,1,0:T(1,128)S(1)}, s32[1,1,2]{2,1,0:T(1,128)}, u32[]{:S(2)}) copy-start(s32[1,1,2]{2,1,0:T(1,128)} %param.12) | copy-start | bytes 28
  4.0 13.0 %collective-permute-start.1 = (bf16[256,768]{0,1:T(8,128)(2,1)S(1)}, bf16[256,768]{0,1:T(8,128)(2,1)S(1)}, u32[]{:S(2)}, u32[]{:S(2)}) collective-permute-start(bf16[256,768]{0,1:T(8,128)(2,1)S(1)} %pad_maximum_fusion.1), channel_id=1, source_target_pairs={{4,0},{12,1},{20,2},{28,3},{0,4},{8,5},{16,6},{24,7},{5,8},{13,9},... | collective-permute-start | bytes 1179656 | tf_op jit(solution)/shard_map/ppermute | solution.py:46
  7.0 10.0 %collective-permute-start = (bf16[256,768]{0,1:T(8,128)(2,1)S(1)}, bf16[256,768]{0,1:T(8,128)(2,1)S(1)}, u32[]{:S(2)}, u32[]{:S(2)}) collective-permute-start(bf16[256,768]{0,1:T(8,128)(2,1)S(1)} %pad_maximum_fusion.1), channel_id=1, source_target_pairs={{0,0},{8,1},{16,2},{24,3},{4,4},{12,5},{20,6},{28,7},{1,8},{9,9},{... | collective-permute-start | bytes 1179656 | tf_op jit(solution)/shard_map/ppermute | solution.py:46
  18.5 36.8 %copy-start.4 = (bf16[256,256]{1,0:T(8,128)(2,1)S(1)}, bf16[256,256]{1,0:T(8,128)(2,1)}, u32[]{:S(2)}) copy-start(bf16[256,256]{1,0:T(8,128)(2,1)} %param.9) | copy-start | bytes 393220
  18.6 7.8 %collective-permute-start.2 = (f32[2,64,768]{2,1,0:T(8,128)S(1)}, f32[2,64,768]{2,1,0:T(8,128)S(1)}, u32[]{:S(2)}, u32[]{:S(2)}) collective-permute-start(f32[2,64,768]{2,1,0:T(8,128)S(1)} %dynamic-slice_bitcast_fusion), channel_id=1, source_target_pairs={{0,1},{1,0},{2,3},{3,2},{4,5},{5,4},{6,7},{7,6},{8,9},{9,8},{10,11... | collective-permute-start | bytes 1179656 | tf_op jit(solution)/shard_map/ppermute | solution.py:23
  26.5 28.8 %collective-permute-start.3 = (f32[64,768]{1,0:T(8,128)S(1)}, f32[64,768]{1,0:T(8,128)S(1)}, u32[]{:S(2)}, u32[]{:S(2)}) collective-permute-start(f32[64,768]{1,0:T(8,128)S(1)} %dynamic-slice_bitcast_fusion.1), channel_id=1, source_target_pairs={{0,2},{1,3},{2,0},{3,1},{4,6},{5,7},{6,4},{7,5},{8,10},{9,11},{10,... | collective-permute-start | bytes 589832 | tf_op jit(solution)/shard_map/ppermute | solution.py:23
  57.2 1.9 %collective-permute-start.10 = (f32[2,2,2,2,4096]{4,3,2,1,0:T(2,128)S(1)}, f32[2,2,2,2,4096]{4,3,2,1,0:T(2,128)S(1)}, u32[]{:S(2)}, u32[]{:S(2)}) collective-permute-start(f32[2,2,2,2,4096]{4,3,2,1,0:T(2,128)S(1)} %bitcast.117), channel_id=1, source_target_pairs={{0,1},{1,0},{2,3},{3,2},{4,5},{5,4},{6,7},{7,6},{8,9},{9,8},{10,11... | collective-permute-start | bytes 786440 | tf_op jit(solution)/shard_map/ppermute | solution.py:23
  57.3 4.0 %collective-permute-start.4 = (bf16[64,256]{1,0:T(8,128)(2,1)S(1)}, bf16[64,256]{1,0:T(8,128)(2,1)S(1)}, u32[]{:S(2)}, u32[]{:S(2)}) collective-permute-start(bf16[64,256]{1,0:T(8,128)(2,1)S(1)} %get-tuple-element.31), channel_id=1, source_target_pairs={{0,2},{1,3},{2,0},{3,1},{4,6},{5,7},{6,4},{7,5},{8,10},{9,11},{10,... | collective-permute-start | bytes 98312 | tf_op jit(solution)/shard_map/ppermute | solution.py:30
  59.8 5.6 %collective-permute-start.11 = (f32[2,2,2,4096]{3,2,1,0:T(2,128)S(1)}, f32[2,2,2,4096]{3,2,1,0:T(2,128)S(1)}, u32[]{:S(2)}, u32[]{:S(2)}) collective-permute-start(f32[2,2,2,4096]{3,2,1,0:T(2,128)S(1)} %bitcast.126), channel_id=1, source_target_pairs={{0,2},{1,3},{2,0},{3,1},{4,6},{5,7},{6,4},{7,5},{8,10},{9,11},{10,... | collective-permute-start | bytes 393224 | tf_op jit(solution)/shard_map/ppermute | solution.py:23
  61.4 5.0 %collective-permute-start.5 = (bf16[2,64,256]{2,1,0:T(8,128)(2,1)S(1)}, bf16[2,64,256]{2,1,0:T(8,128)(2,1)S(1)}, u32[]{:S(2)}, u32[]{:S(2)}) collective-permute-start(bf16[2,64,256]{2,1,0:T(8,128)(2,1)S(1)} %pad_maximum_fusion.7), channel_id=1, source_target_pairs={{0,1},{1,0},{2,3},{3,2},{4,5},{5,4},{6,7},{7,6},{8,9},{9,8},{10,11... | collective-permute-start | bytes 196616 | tf_op jit(solution)/shard_map/ppermute | solution.py:30
  65.8 4.3 %collective-permute-start.12 = (f32[2,2,4096]{2,1,0:T(2,128)S(1)}, f32[2,2,4096]{2,1,0:T(2,128)S(1)}, u32[]{:S(2)}, u32[]{:S(2)}) collective-permute-start(f32[2,2,4096]{2,1,0:T(2,128)S(1)} %bitcast.129), channel_id=1, source_target_pairs={{0,4},{1,5},{2,6},{3,7},{4,0},{5,1},{6,2},{7,3},{8,12},{9,13},{10,... | collective-permute-start | bytes 196616 | tf_op jit(solution)/shard_map/ppermute | solution.py:23
  70.3 4.0 %collective-permute-start.13 = (f32[2,4096]{1,0:T(2,128)S(1)}, f32[2,4096]{1,0:T(2,128)S(1)}, u32[]{:S(2)}, u32[]{:S(2)}) collective-permute-start(f32[2,4096]{1,0:T(2,128)S(1)} %bitcast.131), channel_id=1, source_target_pairs={{0,8},{1,9},{2,10},{3,11},{4,12},{5,13},{6,14},{7,15},{8,0},{9,1},... | collective-permute-start | bytes 98312 | tf_op jit(solution)/shard_map/ppermute | solution.py:23
  70.5 16.0 %collective-permute-start.7 = (bf16[256,256]{1,0:T(8,128)(2,1)S(1)}, bf16[256,256]{1,0:T(8,128)(2,1)S(1)}, u32[]{:S(2)}, u32[]{:S(2)}) collective-permute-start(bf16[256,256]{1,0:T(8,128)(2,1)S(1)} %bitcast.124), channel_id=1, source_target_pairs={{4,0},{12,1},{20,2},{28,3},{0,4},{8,5},{16,6},{24,7},{5,8},{13,9},... | collective-permute-start | bytes 393224 | tf_op jit(solution)/shard_map/ppermute | solution.py:46
  71.1 15.5 %collective-permute-start.6 = (bf16[256,256]{1,0:T(8,128)(2,1)S(1)}, bf16[256,256]{1,0:T(8,128)(2,1)S(1)}, u32[]{:S(2)}, u32[]{:S(2)}) collective-permute-start(bf16[256,256]{1,0:T(8,128)(2,1)S(1)} %bitcast.125), channel_id=1, source_target_pairs={{0,0},{8,1},{16,2},{24,3},{4,4},{12,5},{20,6},{28,7},{1,8},{9,9},{... | collective-permute-start | bytes 393224 | tf_op jit(solution)/shard_map/ppermute | solution.py:46
  74.3 12.2 %collective-permute-start.14 = (f32[4096]{0:T(1024)S(1)}, f32[4096]{0:T(1024)S(1)}, u32[]{:S(2)}, u32[]{:S(2)}) collective-permute-start(f32[4096]{0:T(1024)S(1)} %bitcast.132), channel_id=1, source_target_pairs={{0,16},{1,17},{2,18},{3,19},{4,20},{5,21},{6,22},{7,23},{8,24},{9,... | collective-permute-start | bytes 49160 | tf_op jit(solution)/shard_map/ppermute | solution.py:23
  86.5 4.6 %collective-permute-start.15 = (f32[4096]{0:T(1024)S(1)}, f32[4096]{0:T(1024)S(1)}, u32[]{:S(2)}, u32[]{:S(2)}) collective-permute-start(f32[4096]{0:T(1024)S(1)} %add.206), channel_id=1, source_target_pairs={{0,16},{1,17},{2,18},{3,19},{4,20},{5,21},{6,22},{7,23},{8,24},{9,... | collective-permute-start | bytes 49160 | tf_op jit(solution)/shard_map/ppermute | solution.py:30
  91.2 4.0 %collective-permute-start.16 = (f32[2,4096]{1,0:T(2,128)S(1)}, f32[2,4096]{1,0:T(2,128)S(1)}, u32[]{:S(2)}, u32[]{:S(2)}) collective-permute-start(f32[2,4096]{1,0:T(2,128)S(1)} %pad_maximum_fusion.9), channel_id=1, source_target_pairs={{0,8},{1,9},{2,10},{3,11},{4,12},{5,13},{6,14},{7,15},{8,0},{9,1},... | collective-permute-start | bytes 98312 | tf_op jit(solution)/shard_map/ppermute | solution.py:30
  95.4 4.3 %collective-permute-start.17 = (f32[2,2,4096]{2,1,0:T(2,128)S(1)}, f32[2,2,4096]{2,1,0:T(2,128)S(1)}, u32[]{:S(2)}, u32[]{:S(2)}) collective-permute-start(f32[2,2,4096]{2,1,0:T(2,128)S(1)} %pad_maximum_fusion.8), channel_id=1, source_target_pairs={{0,4},{1,5},{2,6},{3,7},{4,0},{5,1},{6,2},{7,3},{8,12},{9,13},{10,... | collective-permute-start | bytes 196616 | tf_op jit(solution)/shard_map/ppermute | solution.py:30
  96.6 9.2 %copy-start.1 = (bf16[256,256]{1,0:T(8,128)(2,1)S(1)}, bf16[256,256]{1,0:T(8,128)(2,1)}, u32[]{:S(2)}) copy-start(bf16[256,256]{1,0:T(8,128)(2,1)} %param.10) | copy-start | bytes 393220
  96.6 3.5 %collective-permute-start.8 = (f32[2,64,256]{2,1,0:T(8,128)S(1)}, f32[2,64,256]{2,1,0:T(8,128)S(1)}, u32[]{:S(2)}, u32[]{:S(2)}) collective-permute-start(f32[2,64,256]{2,1,0:T(8,128)S(1)} %dynamic-slice_bitcast_fusion.2), channel_id=1, source_target_pairs={{0,1},{1,0},{2,3},{3,2},{4,5},{5,4},{6,7},{7,6},{8,9},{9,8},{10,11... | collective-permute-start | bytes 393224 | tf_op jit(solution)/shard_map/ppermute | solution.py:23
  100.1 5.0 %collective-permute-start.18 = (f32[2,2,2,4096]{3,2,1,0:T(2,128)S(1)}, f32[2,2,2,4096]{3,2,1,0:T(2,128)S(1)}, u32[]{:S(2)}, u32[]{:S(2)}) collective-permute-start(f32[2,2,2,4096]{3,2,1,0:T(2,128)S(1)} %pad_maximum_fusion.6), channel_id=1, source_target_pairs={{0,2},{1,3},{2,0},{3,1},{4,6},{5,7},{6,4},{7,5},{8,10},{9,11},{10,... | collective-permute-start | bytes 393224 | tf_op jit(solution)/shard_map/ppermute | solution.py:30
  100.2 5.6 %collective-permute-start.9 = (f32[64,256]{1,0:T(8,128)S(1)}, f32[64,256]{1,0:T(8,128)S(1)}, u32[]{:S(2)}, u32[]{:S(2)}) collective-permute-start(f32[64,256]{1,0:T(8,128)S(1)} %dynamic-slice_bitcast_fusion.3), channel_id=1, source_target_pairs={{0,2},{1,3},{2,0},{3,1},{4,6},{5,7},{6,4},{7,5},{8,10},{9,11},{10,... | collective-permute-start | bytes 196616 | tf_op jit(solution)/shard_map/ppermute | solution.py:23
  105.8 1.6 %collective-permute-start.19 = (f32[2,2,2,2,4096]{4,3,2,1,0:T(2,128)S(1)}, f32[2,2,2,2,4096]{4,3,2,1,0:T(2,128)S(1)}, u32[]{:S(2)}, u32[]{:S(2)}) collective-permute-start(f32[2,2,2,2,4096]{4,3,2,1,0:T(2,128)S(1)} %pad_maximum_fusion.4), channel_id=1, source_target_pairs={{0,1},{1,0},{2,3},{3,2},{4,5},{5,4},{6,7},{7,6},{8,9},{9,8},{10,11... | collective-permute-start | bytes 786440 | tf_op jit(solution)/shard_map/ppermute | solution.py:30

commit v3 on v2

--- a/solution.py
+++ b/solution.py
@@ -92,17 +92,20 @@
     def gather_rep(z):
         return all_gather_bits(z, me, rep_bits, devices).reshape(node_rows, z.shape[-1])
 
-    back_signal = lax.dot_general(
-        cotangent, weight_two, (((1,), (1,)), ((), ())), preferred_element_type=jnp.float32
-    ).astype(jnp.bfloat16)
-    stage_in = jnp.concatenate([features, back_signal, cotangent], axis=1)
+    stage_in = jnp.concatenate([features, cotangent], axis=1)
     pieces = gather_rounds(stage_in, rows, copies)
     both = reduce_rep(
         local_product(pieces, block_index, block_count, block_values, row_index, copy_index)
     )
     agg_one = both[:, :feature_width].astype(jnp.bfloat16)
-    carried = both[:, feature_width : 2 * feature_width]
-    spread_cotangent = both[:, 2 * feature_width :]
+    spread_cotangent = both[:, feature_width:]
+    carried = lax.dot_general(
+        spread_cotangent,
+        weight_two.astype(jnp.float32),
+        (((1,), (1,)), ((), ())),
+        precision=lax.Precision.HIGHEST,
+        preferred_element_type=jnp.float32,
+    )
     pre_one = jnp.dot(agg_one, weight_one, preferred_element_type=jnp.float32)
     hidden = jax.nn.silu(pre_one).astype(jnp.bfloat16)
     gate_value = jax.nn.sigmoid(pre_one)

time: 111 us -> 96.2 us (0.87)
  starting transfers between devices: 47.4 us -> 39 us
  waiting for transfers between devices: 47.6 us -> 42.5 us
    ppermute x9, starting transfers between devices: 39.2 us -> 30.7 us  [reduce_scatter_bits(): y = keep + lax.ppermute(send, AXES, bit_pairs(devices, bit))]
    ppermute x4, waiting for transfers between devices: 9.08 us -> 5.61 us  [gather_rounds(): pieces.append(lax.ppermute(x, AXES, pairs))]
    ppermute x9, waiting for transfers between devices: 24.4 us -> 22.8 us  [reduce_scatter_bits(): y = keep + lax.ppermute(send, AXES, bit_pairs(devices, bit))]
    unnamed x17 -> x18, local copies, waits for them, and re-layouts: 2.48 us -> 2.81 us
where the time goes in v3:
time: 96.2 us; the launch traced here: 96 us
  waiting for transfers between devices  42.5 us (44%)
  starting transfers between devices  39 us (41%)
  local copies, waits for them, and re-layouts  8.4 us (9%)
  matrix products  2.47 us (3%)
  other arithmetic  2.38 us (2%)
  between operations  1.2 us (1%)
    ppermute x9, starting transfers between devices, reduce_scatter_bits(): y = keep + lax.ppermute(send, AXES, bit_pairs(devices, bit))  30.7 us
    ppermute x9, waiting for transfers between devices, reduce_scatter_bits(): y = keep + lax.ppermute(send, AXES, bit_pairs(devices, bit))  22.8 us
    ppermute x7, waiting for transfers between devices, all_gather_bits(): other = lax.ppermute(z, AXES, bit_pairs(devices, bit))  14.1 us
    ppermute x4, waiting for transfers between devices, gather_rounds(): pieces.append(lax.ppermute(x, AXES, pairs))  5.61 us
    ppermute x4, starting transfers between devices, gather_rounds(): pieces.append(lax.ppermute(x, AXES, pairs))  4.96 us
    ppermute x7, starting transfers between devices, all_gather_bits(): other = lax.ppermute(z, AXES, bit_pairs(devices, bit))  3.32 us
    unnamed x18, local copies, waits for them, and re-layouts  2.81 us
  transfers between devices with their start and end apart: 20, of which 12 were waited for; matrix products, arithmetic and copies ran while one was open for 4% of the time, Pallas kernels for 0%

profile of v3, /device:TPU:0, one launch (start us, length us, event | category | flops | bytes accessed | tf_op | source)
XLA Modules:
  0.0 96.0 jit_solution(3132001462303250692)
XLA Ops:
  0.7 1.0 %constant_dynamic-update-slice_fusion.1 = bf16[256,512]{1,0:T(8,128)(2,1)S(1)} fusion(bf16[256,256]{1,0:T(8,128)(2,1)} %param.7), kind=kLoop, calls=%fused_computation.72 | loop fusion | bytes 262144
  1.7 3.1 %collective-permute-start.1 = (bf16[256,512]{1,0:T(8,128)(2,1)S(1)}, bf16[256,512]{1,0:T(8,128)(2,1)S(1)}, u32[]{:S(2)}, u32[]{:S(2)}) collective-permute-start(bf16[256,512]{1,0:T(8,128)(2,1)S(1)} %constant_dynamic-update-slice_fusion), channel_id=1, source_target_pairs={{4,0},{12,1},{20,2},{28,3},{0,4},{8,5},{16,6},{24,7},{5,8},{13,9},... | collective-permute-start | bytes 786440 | tf_op jit(solution)/shard_map/ppermute | solution.py:46
  4.7 0.7 collective-permute-start
  5.4 0.7 copy-done.3
  6.3 5.6 %collective-permute-done.1 = bf16[256,512]{1,0:T(8,128)(2,1)S(1)} collective-permute-done((bf16[256,512]{1,0:T(8,128)(2,1)S(1)}, bf16[256,512]{1,0:T(8,128)(2,1)S(1)}, u32[]{:S(2)}, u32[]{:S(2)}) %collective-permute-start.1) | collective-permute-done | bytes 262176 | tf_op jit(solution)/shard_map/ppermute | solution.py:46
  11.9 0.6 gather_fusion
  12.6 0.4 fusion.1
  13.0 4.4 %collective-permute-start.2 = (f32[2,64,512]{2,1,0:T(8,128)S(1)}, f32[2,64,512]{2,1,0:T(8,128)S(1)}, u32[]{:S(2)}, u32[]{:S(2)}) collective-permute-start(f32[2,64,512]{2,1,0:T(8,128)S(1)} %dynamic-slice_bitcast_fusion), channel_id=1, source_target_pairs={{0,1},{1,0},{2,3},{3,2},{4,5},{5,4},{6,7},{7,6},{8,9},{9,8},{10,11... | collective-permute-start | bytes 786440 | tf_op jit(solution)/shard_map/ppermute | solution.py:23
  17.5 1.2 %collective-permute-done.2 = f32[2,64,512]{2,1,0:T(8,128)S(1)} collective-permute-done((f32[2,64,512]{2,1,0:T(8,128)S(1)}, f32[2,64,512]{2,1,0:T(8,128)S(1)}, u32[]{:S(2)}, u32[]{:S(2)}) %collective-permute-start.2) | collective-permute-done | bytes 262176 | tf_op jit(solution)/shard_map/ppermute | solution.py:23
  18.7 17.2 %collective-permute-start.3 = (f32[64,512]{1,0:T(8,128)S(1)}, f32[64,512]{1,0:T(8,128)S(1)}, u32[]{:S(2)}, u32[]{:S(2)}) collective-permute-start(f32[64,512]{1,0:T(8,128)S(1)} %dynamic-slice_bitcast_fusion.2), channel_id=1, source_target_pairs={{0,2},{1,3},{2,0},{3,1},{4,6},{5,7},{6,4},{7,5},{8,10},{9,11},{10,... | collective-permute-start | bytes 393224 | tf_op jit(solution)/shard_map/ppermute | solution.py:23
  35.9 3.8 %collective-permute-done.3 = f32[64,512]{1,0:T(8,128)S(1)} collective-permute-done((f32[64,512]{1,0:T(8,128)S(1)}, f32[64,512]{1,0:T(8,128)S(1)}, u32[]{:S(2)}, u32[]{:S(2)}) %collective-permute-start.3) | collective-permute-done | bytes 131104 | tf_op jit(solution)/shard_map/ppermute | solution.py:23
  39.7 0.2 fusion.23
  39.9 0.7 copy-done.2
  40.6 0.3 fusion
  40.9 0.2 fusion.26
  41.3 0.3 fusion.19
  41.9 0.6 constant_dynamic-slice_fusion.9
  42.5 0.2 copy.37
  42.8 1.8 %collective-permute-start.4 = (bf16[64,256]{1,0:T(8,128)(2,1)S(1)}, bf16[64,256]{1,0:T(8,128)(2,1)S(1)}, u32[]{:S(2)}, u32[]{:S(2)}) collective-permute-start(bf16[64,256]{1,0:T(8,128)(2,1)S(1)} %get-tuple-element.31), channel_id=1, source_target_pairs={{0,2},{1,3},{2,0},{3,1},{4,6},{5,7},{6,4},{7,5},{8,10},{9,11},{10,... | collective-permute-start | bytes 98312 | tf_op jit(solution)/shard_map/ppermute | solution.py:30
  44.6 0.3 bitcast_add_fusion
  44.8 0.3 constant_dynamic-slice_fusion.7
  45.3 1.5 %collective-permute-start.11 = (f32[2,2,2,4096]{3,2,1,0:T(2,128)S(1)}, f32[2,2,2,4096]{3,2,1,0:T(2,128)S(1)}, u32[]{:S(2)}, u32[]{:S(2)}) collective-permute-start(f32[2,2,2,4096]{3,2,1,0:T(2,128)S(1)} %bitcast.126), channel_id=1, source_target_pairs={{0,2},{1,3},{2,0},{3,1},{4,6},{5,7},{6,4},{7,5},{8,10},{9,11},{10,... | collective-permute-start | bytes 393224 | tf_op jit(solution)/shard_map/ppermute | solution.py:23
  46.9 4.0 %collective-permute-done.11 = f32[2,2,2,4096]{3,2,1,0:T(2,128)S(1)} collective-permute-done((f32[2,2,2,4096]{3,2,1,0:T(2,128)S(1)}, f32[2,2,2,4096]{3,2,1,0:T(2,128)S(1)}, u32[]{:S(2)}, u32[]{:S(2)}) %collective-permute-start.11) | collective-permute-done | bytes 131104 | tf_op jit(solution)/shard_map/ppermute | solution.py:23
  51.2 0.6 collective-permute-start.12
  51.8 3.7 %collective-permute-done.12 = f32[2,2,4096]{2,1,0:T(2,128)S(1)} collective-permute-done((f32[2,2,4096]{2,1,0:T(2,128)S(1)}, f32[2,2,4096]{2,1,0:T(2,128)S(1)}, u32[]{:S(2)}, u32[]{:S(2)}) %collective-permute-start.12) | collective-permute-done | bytes 65568 | tf_op jit(solution)/shard_map/ppermute | solution.py:23
  55.7 0.2 collective-permute-start.13
  55.9 0.6 collective-permute-start.7
  56.5 0.7 collective-permute-start.6
  57.2 2.5 %collective-permute-done.13 = f32[2,4096]{1,0:T(2,128)S(1)} collective-permute-done((f32[2,4096]{1,0:T(2,128)S(1)}, f32[2,4096]{1,0:T(2,128)S(1)}, u32[]{:S(2)}, u32[]{:S(2)}) %collective-permute-start.13) | collective-permute-done | bytes 32800 | tf_op jit(solution)/shard_map/ppermute | solution.py:23
  59.8 4.6 %collective-permute-start.14 = (f32[4096]{0:T(1024)S(1)}, f32[4096]{0:T(1024)S(1)}, u32[]{:S(2)}, u32[]{:S(2)}) collective-permute-start(f32[4096]{0:T(1024)S(1)} %bitcast.132), channel_id=1, source_target_pairs={{0,16},{1,17},{2,18},{3,19},{4,20},{5,21},{6,22},{7,23},{8,24},{9,... | collective-permute-start | bytes 49160 | tf_op jit(solution)/shard_map/ppermute | solution.py:23
  64.4 7.6 %collective-permute-done.14 = f32[4096]{0:T(1024)S(1)} collective-permute-done((f32[4096]{0:T(1024)S(1)}, f32[4096]{0:T(1024)S(1)}, u32[]{:S(2)}, u32[]{:S(2)}) %collective-permute-start.14) | collective-permute-done | bytes 16416 | tf_op jit(solution)/shard_map/ppermute | solution.py:23
  72.0 0.6 gather_fusion.1
  72.6 4.0 %collective-permute-done.15 = f32[4096]{0:T(1024)S(1)} collective-permute-done((f32[4096]{0:T(1024)S(1)}, f32[4096]{0:T(1024)S(1)}, u32[]{:S(2)}, u32[]{:S(2)}) %collective-permute-start.15) | collective-permute-done | bytes 16416 | tf_op jit(solution)/shard_map/ppermute | solution.py:30
  76.7 0.3 fusion.6
  77.1 3.6 %collective-permute-done.16 = f32[2,4096]{1,0:T(2,128)S(1)} collective-permute-done((f32[2,4096]{1,0:T(2,128)S(1)}, f32[2,4096]{1,0:T(2,128)S(1)}, u32[]{:S(2)}, u32[]{:S(2)}) %collective-permute-start.16) | collective-permute-done | bytes 32800 | tf_op jit(solution)/shard_map/ppermute | solution.py:30
  80.8 1.2 %collective-permute-start.17 = (f32[2,2,4096]{2,1,0:T(2,128)S(1)}, f32[2,2,4096]{2,1,0:T(2,128)S(1)}, u32[]{:S(2)}, u32[]{:S(2)}) collective-permute-start(f32[2,2,4096]{2,1,0:T(2,128)S(1)} %pad_maximum_fusion.7), channel_id=1, source_target_pairs={{0,4},{1,5},{2,6},{3,7},{4,0},{5,1},{6,2},{7,3},{8,12},{9,13},{10,... | collective-permute-start | bytes 196616 | tf_op jit(solution)/shard_map/ppermute | solution.py:30
  82.1 3.0 %collective-permute-done.17 = f32[2,2,4096]{2,1,0:T(2,128)S(1)} collective-permute-done((f32[2,2,4096]{2,1,0:T(2,128)S(1)}, f32[2,2,4096]{2,1,0:T(2,128)S(1)}, u32[]{:S(2)}, u32[]{:S(2)}) %collective-permute-start.17) | collective-permute-done | bytes 65568 | tf_op jit(solution)/shard_map/ppermute | solution.py:30
  85.7 2.1 %collective-permute-start.9 = (f32[64,256]{1,0:T(8,128)S(1)}, f32[64,256]{1,0:T(8,128)S(1)}, u32[]{:S(2)}, u32[]{:S(2)}) collective-permute-start(f32[64,256]{1,0:T(8,128)S(1)} %dynamic-slice_bitcast_fusion.3), channel_id=1, source_target_pairs={{0,2},{1,3},{2,0},{3,1},{4,6},{5,7},{6,4},{7,5},{8,10},{9,11},{10,... | collective-permute-start | bytes 196616 | tf_op jit(solution)/shard_map/ppermute | solution.py:23
  87.7 2.8 %collective-permute-done.18 = f32[2,2,2,4096]{3,2,1,0:T(2,128)S(1)} collective-permute-done((f32[2,2,2,4096]{3,2,1,0:T(2,128)S(1)}, f32[2,2,2,4096]{3,2,1,0:T(2,128)S(1)}, u32[]{:S(2)}, u32[]{:S(2)}) %collective-permute-start.18) | collective-permute-done | bytes 131104 | tf_op jit(solution)/shard_map/ppermute | solution.py:30
  91.0 0.2 pad_maximum_fusion.3
  91.3 0.8 convolution_convert_fusion
  92.1 0.7 collective-permute-done.19
  92.8 0.3 broadcast_select_fusion
  93.1 0.2 stack.118
  93.4 0.3 copy.18
  93.7 0.5 pad_maximum_fusion.1
  94.1 0.9 squeeze.94
  95.1 0.9 squeeze.95
  (71 shorter events, 2.9 us)
Async XLA Ops:
  0.6 11.9 %copy-start = (bf16[1,1,2,4,128,128]{5,4,3,2,1,0:T(8,128)(2,1)S(1)}, bf16[1,1,2,4,128,128]{5,4,3,2,1,0:T(8,128)(2,1)}, u32[]{:S(2)}) copy-start(bf16[1,1,2,4,128,128]{5,4,3,2,1,0:T(8,128)(2,1)} %param.13) | copy-start | bytes 786436
  0.6 1.0 %copy-start.1 = (bf16[256,256]{1,0:T(8,128)(2,1)S(1)}, bf16[256,256]{1,0:T(8,128)(2,1)}, u32[]{:S(2)}) copy-start(bf16[256,256]{1,0:T(8,128)(2,1)} %param.8) | copy-start | bytes 393220
  1.7 10.2 %collective-permute-start.1 = (bf16[256,512]{1,0:T(8,128)(2,1)S(1)}, bf16[256,512]{1,0:T(8,128)(2,1)S(1)}, u32[]{:S(2)}, u32[]{:S(2)}) collective-permute-start(bf16[256,512]{1,0:T(8,128)(2,1)S(1)} %constant_dynamic-update-slice_fusion), channel_id=1, source_target_pairs={{4,0},{12,1},{20,2},{28,3},{0,4},{8,5},{16,6},{24,7},{5,8},{13,9},... | collective-permute-start | bytes 786440 | tf_op jit(solution)/shard_map/ppermute | solution.py:46
  4.7 7.2 %collective-permute-start = (bf16[256,512]{1,0:T(8,128)(2,1)S(1)}, bf16[256,512]{1,0:T(8,128)(2,1)S(1)}, u32[]{:S(2)}, u32[]{:S(2)}) collective-permute-start(bf16[256,512]{1,0:T(8,128)(2,1)S(1)} %constant_dynamic-update-slice_fusion), channel_id=1, source_target_pairs={{0,0},{8,1},{16,2},{24,3},{4,4},{12,5},{20,6},{28,7},{1,8},{9,9},{... | collective-permute-start | bytes 786440 | tf_op jit(solution)/shard_map/ppermute | solution.py:46
  5.4 0.7 copy-start.3
  5.4 0.7 copy-start.4
  13.0 5.6 %collective-permute-start.2 = (f32[2,64,512]{2,1,0:T(8,128)S(1)}, f32[2,64,512]{2,1,0:T(8,128)S(1)}, u32[]{:S(2)}, u32[]{:S(2)}) collective-permute-start(f32[2,64,512]{2,1,0:T(8,128)S(1)} %dynamic-slice_bitcast_fusion), channel_id=1, source_target_pairs={{0,1},{1,0},{2,3},{3,2},{4,5},{5,4},{6,7},{7,6},{8,9},{9,8},{10,11... | collective-permute-start | bytes 786440 | tf_op jit(solution)/shard_map/ppermute | solution.py:23
  18.7 21.0 %collective-permute-start.3 = (f32[64,512]{1,0:T(8,128)S(1)}, f32[64,512]{1,0:T(8,128)S(1)}, u32[]{:S(2)}, u32[]{:S(2)}) collective-permute-start(f32[64,512]{1,0:T(8,128)S(1)} %dynamic-slice_bitcast_fusion.2), channel_id=1, source_target_pairs={{0,2},{1,3},{2,0},{3,1},{4,6},{5,7},{6,4},{7,5},{8,10},{9,11},{10,... | collective-permute-start | bytes 393224 | tf_op jit(solution)/shard_map/ppermute | solution.py:23
  35.9 3.8 %copy-start.5 = (bf16[256,256]{1,0:T(8,128)(2,1)S(1)}, bf16[256,256]{1,0:T(8,128)(2,1)}, u32[]{:S(2)}) copy-start(bf16[256,256]{1,0:T(8,128)(2,1)} %param.9) | copy-start | bytes 393220
  39.7 0.9 copy-start.2
  42.7 1.9 %collective-permute-start.10 = (f32[2,2,2,2,4096]{4,3,2,1,0:T(2,128)S(1)}, f32[2,2,2,2,4096]{4,3,2,1,0:T(2,128)S(1)}, u32[]{:S(2)}, u32[]{:S(2)}) collective-permute-start(f32[2,2,2,2,4096]{4,3,2,1,0:T(2,128)S(1)} %bitcast.115), channel_id=1, source_target_pairs={{0,1},{1,0},{2,3},{3,2},{4,5},{5,4},{6,7},{7,6},{8,9},{9,8},{10,11... | collective-permute-start | bytes 786440 | tf_op jit(solution)/shard_map/ppermute | solution.py:23
  42.8 4.0 %collective-permute-start.4 = (bf16[64,256]{1,0:T(8,128)(2,1)S(1)}, bf16[64,256]{1,0:T(8,128)(2,1)S(1)}, u32[]{:S(2)}, u32[]{:S(2)}) collective-permute-start(bf16[64,256]{1,0:T(8,128)(2,1)S(1)} %get-tuple-element.31), channel_id=1, source_target_pairs={{0,2},{1,3},{2,0},{3,1},{4,6},{5,7},{6,4},{7,5},{8,10},{9,11},{10,... | collective-permute-start | bytes 98312 | tf_op jit(solution)/shard_map/ppermute | solution.py:30
  45.3 5.6 %collective-permute-start.11 = (f32[2,2,2,4096]{3,2,1,0:T(2,128)S(1)}, f32[2,2,2,4096]{3,2,1,0:T(2,128)S(1)}, u32[]{:S(2)}, u32[]{:S(2)}) collective-permute-start(f32[2,2,2,4096]{3,2,1,0:T(2,128)S(1)} %bitcast.126), channel_id=1, source_target_pairs={{0,2},{1,3},{2,0},{3,1},{4,6},{5,7},{6,4},{7,5},{8,10},{9,11},{10,... | collective-permute-start | bytes 393224 | tf_op jit(solution)/shard_map/ppermute | solution.py:23
  46.8 5.0 %collective-permute-start.5 = (bf16[2,64,256]{2,1,0:T(8,128)(2,1)S(1)}, bf16[2,64,256]{2,1,0:T(8,128)(2,1)S(1)}, u32[]{:S(2)}, u32[]{:S(2)}) collective-permute-start(bf16[2,64,256]{2,1,0:T(8,128)(2,1)S(1)} %pad_maximum_fusion.6), channel_id=1, source_target_pairs={{0,1},{1,0},{2,3},{3,2},{4,5},{5,4},{6,7},{7,6},{8,9},{9,8},{10,11... | collective-permute-start | bytes 196616 | tf_op jit(solution)/shard_map/ppermute | solution.py:30
  51.2 4.3 %collective-permute-start.12 = (f32[2,2,4096]{2,1,0:T(2,128)S(1)}, f32[2,2,4096]{2,1,0:T(2,128)S(1)}, u32[]{:S(2)}, u32[]{:S(2)}) collective-permute-start(f32[2,2,4096]{2,1,0:T(2,128)S(1)} %bitcast.129), channel_id=1, source_target_pairs={{0,4},{1,5},{2,6},{3,7},{4,0},{5,1},{6,2},{7,3},{8,12},{9,13},{10,... | collective-permute-start | bytes 196616 | tf_op jit(solution)/shard_map/ppermute | solution.py:23
  55.7 4.0 %collective-permute-start.13 = (f32[2,4096]{1,0:T(2,128)S(1)}, f32[2,4096]{1,0:T(2,128)S(1)}, u32[]{:S(2)}, u32[]{:S(2)}) collective-permute-start(f32[2,4096]{1,0:T(2,128)S(1)} %bitcast.131), channel_id=1, source_target_pairs={{0,8},{1,9},{2,10},{3,11},{4,12},{5,13},{6,14},{7,15},{8,0},{9,1},... | collective-permute-start | bytes 98312 | tf_op jit(solution)/shard_map/ppermute | solution.py:23
  55.9 16.1 %collective-permute-start.7 = (bf16[256,256]{1,0:T(8,128)(2,1)S(1)}, bf16[256,256]{1,0:T(8,128)(2,1)S(1)}, u32[]{:S(2)}, u32[]{:S(2)}) collective-permute-start(bf16[256,256]{1,0:T(8,128)(2,1)S(1)} %bitcast.124), channel_id=1, source_target_pairs={{4,0},{12,1},{20,2},{28,3},{0,4},{8,5},{16,6},{24,7},{5,8},{13,9},... | collective-permute-start | bytes 393224 | tf_op jit(solution)/shard_map/ppermute | solution.py:46
  56.5 15.5 %collective-permute-start.6 = (bf16[256,256]{1,0:T(8,128)(2,1)S(1)}, bf16[256,256]{1,0:T(8,128)(2,1)S(1)}, u32[]{:S(2)}, u32[]{:S(2)}) collective-permute-start(bf16[256,256]{1,0:T(8,128)(2,1)S(1)} %bitcast.125), channel_id=1, source_target_pairs={{0,0},{8,1},{16,2},{24,3},{4,4},{12,5},{20,6},{28,7},{1,8},{9,9},{... | collective-permute-start | bytes 393224 | tf_op jit(solution)/shard_map/ppermute | solution.py:46
  59.8 12.2 %collective-permute-start.14 = (f32[4096]{0:T(1024)S(1)}, f32[4096]{0:T(1024)S(1)}, u32[]{:S(2)}, u32[]{:S(2)}) collective-permute-start(f32[4096]{0:T(1024)S(1)} %bitcast.132), channel_id=1, source_target_pairs={{0,16},{1,17},{2,18},{3,19},{4,20},{5,21},{6,22},{7,23},{8,24},{9,... | collective-permute-start | bytes 49160 | tf_op jit(solution)/shard_map/ppermute | solution.py:23
  72.0 4.6 %collective-permute-start.15 = (f32[4096]{0:T(1024)S(1)}, f32[4096]{0:T(1024)S(1)}, u32[]{:S(2)}, u32[]{:S(2)}) collective-permute-start(f32[4096]{0:T(1024)S(1)} %add.206), channel_id=1, source_target_pairs={{0,16},{1,17},{2,18},{3,19},{4,20},{5,21},{6,22},{7,23},{8,24},{9,... | collective-permute-start | bytes 49160 | tf_op jit(solution)/shard_map/ppermute | solution.py:30
  76.7 4.0 %collective-permute-start.16 = (f32[2,4096]{1,0:T(2,128)S(1)}, f32[2,4096]{1,0:T(2,128)S(1)}, u32[]{:S(2)}, u32[]{:S(2)}) collective-permute-start(f32[2,4096]{1,0:T(2,128)S(1)} %pad_maximum_fusion.8), channel_id=1, source_target_pairs={{0,8},{1,9},{2,10},{3,11},{4,12},{5,13},{6,14},{7,15},{8,0},{9,1},... | collective-permute-start | bytes 98312 | tf_op jit(solution)/shard_map/ppermute | solution.py:30
  80.8 4.3 %collective-permute-start.17 = (f32[2,2,4096]{2,1,0:T(2,128)S(1)}, f32[2,2,4096]{2,1,0:T(2,128)S(1)}, u32[]{:S(2)}, u32[]{:S(2)}) collective-permute-start(f32[2,2,4096]{2,1,0:T(2,128)S(1)} %pad_maximum_fusion.7), channel_id=1, source_target_pairs={{0,4},{1,5},{2,6},{3,7},{4,0},{5,1},{6,2},{7,3},{8,12},{9,13},{10,... | collective-permute-start | bytes 196616 | tf_op jit(solution)/shard_map/ppermute | solution.py:30
  82.1 3.5 %collective-permute-start.8 = (f32[2,64,256]{2,1,0:T(8,128)S(1)}, f32[2,64,256]{2,1,0:T(8,128)S(1)}, u32[]{:S(2)}, u32[]{:S(2)}) collective-permute-start(f32[2,64,256]{2,1,0:T(8,128)S(1)} %dynamic-slice_bitcast_fusion.1), channel_id=1, source_target_pairs={{0,1},{1,0},{2,3},{3,2},{4,5},{5,4},{6,7},{7,6},{8,9},{9,8},{10,11... | collective-permute-start | bytes 393224 | tf_op jit(solution)/shard_map/ppermute | solution.py:23
  85.5 5.0 %collective-permute-start.18 = (f32[2,2,2,4096]{3,2,1,0:T(2,128)S(1)}, f32[2,2,2,4096]{3,2,1,0:T(2,128)S(1)}, u32[]{:S(2)}, u32[]{:S(2)}) collective-permute-start(f32[2,2,2,4096]{3,2,1,0:T(2,128)S(1)} %pad_maximum_fusion.5), channel_id=1, source_target_pairs={{0,2},{1,3},{2,0},{3,1},{4,6},{5,7},{6,4},{7,5},{8,10},{9,11},{10,... | collective-permute-start | bytes 393224 | tf_op jit(solution)/shard_map/ppermute | solution.py:30
  85.7 5.6 %collective-permute-start.9 = (f32[64,256]{1,0:T(8,128)S(1)}, f32[64,256]{1,0:T(8,128)S(1)}, u32[]{:S(2)}, u32[]{:S(2)}) collective-permute-start(f32[64,256]{1,0:T(8,128)S(1)} %dynamic-slice_bitcast_fusion.3), channel_id=1, source_target_pairs={{0,2},{1,3},{2,0},{3,1},{4,6},{5,7},{6,4},{7,5},{8,10},{9,11},{10,... | collective-permute-start | bytes 196616 | tf_op jit(solution)/shard_map/ppermute | solution.py:23
  91.2 1.6 %collective-permute-start.19 = (f32[2,2,2,2,4096]{4,3,2,1,0:T(2,128)S(1)}, f32[2,2,2,2,4096]{4,3,2,1,0:T(2,128)S(1)}, u32[]{:S(2)}, u32[]{:S(2)}) collective-permute-start(f32[2,2,2,2,4096]{4,3,2,1,0:T(2,128)S(1)} %pad_maximum_fusion.3), channel_id=1, source_target_pairs={{0,1},{1,0},{2,3},{3,2},{4,5},{5,4},{6,7},{7,6},{8,9},{9,8},{10,11... | collective-permute-start | bytes 786440 | tf_op jit(solution)/shard_map/ppermute | solution.py:30

commit v4 on v3

--- a/solution.py
+++ b/solution.py
@@ -32,6 +32,51 @@
         high = jnp.where(mine == 0, other, z)
         z = jnp.stack([low, high], axis=step)
     return z
+
+
+def group_pairs(devices, mask):
+    return [(d, d ^ mask) for d in range(devices)]
+
+
+def reduce_scatter_groups(y, me, groups, devices):
+    levels = sum(len(group) for group in groups)
+    rest = y.shape[levels:]
+    for group in groups:
+        width = len(group)
+        size = 1 << width
+        low = group[0]
+        y = y.reshape(y.shape[: levels - width] + (size,) + rest)
+        axis = levels - width
+        mine = (me >> low) & (size - 1)
+        total = lax.dynamic_index_in_dim(y, mine, axis, keepdims=False)
+        for offset in range(1, size):
+            send = lax.dynamic_index_in_dim(y, mine ^ offset, axis, keepdims=False)
+            total = total + lax.ppermute(send, AXES, group_pairs(devices, offset << low))
+        y = total
+        levels -= width
+    return y
+
+
+def all_gather_groups(z, me, groups, devices):
+    done = 0
+    for group in reversed(groups):
+        width = len(group)
+        size = 1 << width
+        low = group[0]
+        mine = (me >> low) & (size - 1)
+        received = [z]
+        for offset in range(1, size):
+            received.append(lax.ppermute(z, AXES, group_pairs(devices, offset << low)))
+        stacked = jnp.stack(received, axis=done)
+        order = jnp.arange(size, dtype=jnp.int32) ^ mine
+        z = jnp.take(stacked, order, axis=done)
+        z = z.reshape(z.shape[:done] + (2,) * width + z.shape[done + 1 :])
+        done += width
+    return z
+
+
+def bit_groups(bits, widest):
+    return [bits[i : i + widest] for i in range(0, len(bits), widest)]
 
 
 def gather_rounds(x, rows, copies):
@@ -126,8 +171,9 @@
     total = grads.size
     levels = len(all_bits)
     segment = grads.reshape([2] * levels + [total // devices])
-    summed = reduce_scatter_bits(segment, me, all_bits, devices)
-    grads = all_gather_bits(summed, me, all_bits, devices).reshape(grads.shape)
+    groups = [[bit] for bit in rep_bits] + bit_groups(all_bits[rep_levels:], 3)
+    summed = reduce_scatter_groups(segment, me, groups, devices)
+    grads = all_gather_groups(summed, me, groups, devices).reshape(grads.shape)
 
     hidden_full = gather_rep(hidden)
     pieces_two = gather_rounds(hidden_full, rows, copies)

time: 96.2 us -> 104 us (1.081)
  starting transfers between devices: 39 us -> 61.3 us
  waiting for transfers between devices: 42.5 us -> 26.8 us
  local copies, waits for them, and re-layouts: 8.4 us -> 10 us
    ppermute x0 -> x18, starting transfers between devices: none -> 30.2 us  [the longest x9 18.1 us: reduce_scatter_groups(): lax.ppermute(send, AXES, group_pairs(devices, offset << low))]
    ppermute x9 -> x4, waiting for transfers between devices: 22.8 us -> 4.91 us  [reduce_scatter_bits(): y = keep + lax.ppermute(send, AXES, bit_pairs(devices, bit))]
    ppermute x0 -> x18, waiting for transfers between devices: none -> 15.4 us  [the longest x9 9.58 us: reduce_scatter_groups(): lax.ppermute(send, AXES, group_pairs(devices, offset << low))]
    ppermute x7 -> x2, waiting for transfers between devices: 14.1 us -> 0.93 us  [all_gather_bits(): other = lax.ppermute(z, AXES, bit_pairs(devices, bit))]
    ppermute x9 -> x4, starting transfers between devices: 30.7 us -> 24.3 us  [reduce_scatter_bits(): y = keep + lax.ppermute(send, AXES, bit_pairs(devices, bit))]
    gather x0 -> x5, local copies, waits for them, and re-layouts: none -> 2.7 us  [all_gather_groups(): z = jnp.take(stacked, order, axis=done)]
    ppermute x7 -> x2, starting transfers between devices: 3.32 us -> 1.88 us  [all_gather_bits(): other = lax.ppermute(z, AXES, bit_pairs(devices, bit))]
    another operation x12 -> x4, other arithmetic: 1.27 us -> 0.05 us  [all_gather_bits(): z = jnp.stack([low, high], axis=step)]
  transfers between devices with their start and end apart: 20 -> 28, of which waited for: 12 -> 11; matrix products, arithmetic and copies ran while one was open for 4% -> 6% of each run, Pallas kernels for 0% -> 0%
where the time goes in v4:
time: 104 us
  starting transfers between devices  61.3 us (59%)
  waiting for transfers between devices  26.8 us (26%)
  local copies, waits for them, and re-layouts  10 us (10%)
  matrix products  2.46 us (2%)
  other arithmetic  2.08 us (2%)
  between operations  1.19 us (1%)
    ppermute x4, starting transfers between devices, reduce_scatter_bits(): y = keep + lax.ppermute(send, AXES, bit_pairs(devices, bit))  24.3 us
    ppermute x9, starting transfers between devices, reduce_scatter_groups(): lax.ppermute(send, AXES, group_pairs(devices, offset << low))  18.1 us
    ppermute x9, starting transfers between devices, all_gather_groups(): received.append(lax.ppermute(z, AXES, group_pairs(devices, offset << low)))  12.1 us
    ppermute x9, waiting for transfers between devices, reduce_scatter_groups(): lax.ppermute(send, AXES, group_pairs(devices, offset << low))  9.58 us
    ppermute x9, waiting for transfers between devices, all_gather_groups(): received.append(lax.ppermute(z, AXES, group_pairs(devices, offset << low)))  5.82 us
    ppermute x4, waiting for transfers between devices, gather_rounds(): pieces.append(lax.ppermute(x, AXES, pairs))  5.56 us
    ppermute x4, starting transfers between devices, gather_rounds(): pieces.append(lax.ppermute(x, AXES, pairs))  4.95 us
    ppermute x4, waiting for transfers between devices, reduce_scatter_bits(): y = keep + lax.ppermute(send, AXES, bit_pairs(devices, bit))  4.91 us
  transfers between devices with their start and end apart: 28, of which 11 were waited for; matrix products, arithmetic and copies ran while one was open for 6% of the time, Pallas kernels for 0%

profile of v4, /device:TPU:0, one launch (start us, length us, event | category | flops | bytes accessed | tf_op | source)
XLA Modules:
  0.0 103.8 jit_solution(4081415233670340284)
XLA Ops:
  0.7 1.0 constant_dynamic-update-slice_fusion.1
  1.7 3.1 %collective-permute-start.1 = (bf16[256,512]{1,0:T(8,128)(2,1)S(1)}, bf16[256,512]{1,0:T(8,128)(2,1)S(1)}, u32[]{:S(2)}, u32[]{:S(2)}) collective-permute-start(bf16[256,512]{1,0:T(8,128)(2,1)S(1)} %constant_dynamic-update-slice_fusion), channel_id=1, source_target_pairs={{4,0},{12,1},{20,2},{28,3},{0,4},{8,5},{16,6},{24,7},{5,8},{13,9},... | collective-permute-start | bytes 786440 | tf_op jit(solution)/shard_map/ppermute | solution.py:91
  4.7 0.7 collective-permute-start
  5.4 0.7 copy-done.3
  6.3 5.5 %collective-permute-done.1 = bf16[256,512]{1,0:T(8,128)(2,1)S(1)} collective-permute-done((bf16[256,512]{1,0:T(8,128)(2,1)S(1)}, bf16[256,512]{1,0:T(8,128)(2,1)S(1)}, u32[]{:S(2)}, u32[]{:S(2)}) %collective-permute-start.1) | collective-permute-done | bytes 262176 | tf_op jit(solution)/shard_map/ppermute | solution.py:91
  11.9 0.6 gather_fusion
  12.6 0.4 fusion.1
  13.0 4.4 %collective-permute-start.2 = (f32[2,64,512]{2,1,0:T(8,128)S(1)}, f32[2,64,512]{2,1,0:T(8,128)S(1)}, u32[]{:S(2)}, u32[]{:S(2)}) collective-permute-start(f32[2,64,512]{2,1,0:T(8,128)S(1)} %dynamic-slice_bitcast_fusion), channel_id=1, source_target_pairs={{0,1},{1,0},{2,3},{3,2},{4,5},{5,4},{6,7},{7,6},{8,9},{9,8},{10,11... | collective-permute-start | bytes 786440 | tf_op jit(solution)/shard_map/ppermute | solution.py:23
  17.5 1.1 %collective-permute-done.2 = f32[2,64,512]{2,1,0:T(8,128)S(1)} collective-permute-done((f32[2,64,512]{2,1,0:T(8,128)S(1)}, f32[2,64,512]{2,1,0:T(8,128)S(1)}, u32[]{:S(2)}, u32[]{:S(2)}) %collective-permute-start.2) | collective-permute-done | bytes 262176 | tf_op jit(solution)/shard_map/ppermute | solution.py:23
  18.7 17.2 %collective-permute-start.3 = (f32[64,512]{1,0:T(8,128)S(1)}, f32[64,512]{1,0:T(8,128)S(1)}, u32[]{:S(2)}, u32[]{:S(2)}) collective-permute-start(f32[64,512]{1,0:T(8,128)S(1)} %dynamic-slice_bitcast_fusion.2), channel_id=1, source_target_pairs={{0,2},{1,3},{2,0},{3,1},{4,6},{5,7},{6,4},{7,5},{8,10},{9,11},{10,... | collective-permute-start | bytes 393224 | tf_op jit(solution)/shard_map/ppermute | solution.py:23
  35.9 3.8 %collective-permute-done.3 = f32[64,512]{1,0:T(8,128)S(1)} collective-permute-done((f32[64,512]{1,0:T(8,128)S(1)}, f32[64,512]{1,0:T(8,128)S(1)}, u32[]{:S(2)}, u32[]{:S(2)}) %collective-permute-start.3) | collective-permute-done | bytes 131104 | tf_op jit(solution)/shard_map/ppermute | solution.py:23
  39.9 1.8 %collective-permute-start.4 = (bf16[64,256]{1,0:T(8,128)(2,1)S(1)}, bf16[64,256]{1,0:T(8,128)(2,1)S(1)}, u32[]{:S(2)}, u32[]{:S(2)}) collective-permute-start(bf16[64,256]{1,0:T(8,128)(2,1)S(1)} %get-tuple-element.23), channel_id=1, source_target_pairs={{0,2},{1,3},{2,0},{3,1},{4,6},{5,7},{6,4},{7,5},{8,10},{9,11},{10,... | collective-permute-start | bytes 98312 | tf_op jit(solution)/shard_map/ppermute | solution.py:30
  41.7 0.3 fusion.18
  43.0 0.9 collective-permute-done.4
  44.0 0.6 constant_dynamic-slice_fusion.11
  44.8 0.6 collective-permute-start.10
  45.4 0.6 collective-permute-start.7
  46.0 0.7 collective-permute-start.6
  47.4 6.3 %collective-permute-start.11 = (f32[2,2,2,4096]{3,2,1,0:T(2,128)S(1)}, f32[2,2,2,4096]{3,2,1,0:T(2,128)S(1)}, u32[]{:S(2)}, u32[]{:S(2)}) collective-permute-start(f32[2,2,2,4096]{3,2,1,0:T(2,128)S(1)} %bitcast.132), channel_id=1, source_target_pairs={{0,2},{1,3},{2,0},{3,1},{4,6},{5,7},{6,4},{7,5},{8,10},{9,11},{10,... | collective-permute-start | bytes 393224 | tf_op jit(solution)/shard_map/ppermute | solution.py:54
  53.7 0.6 gather_fusion.1
  54.3 6.4 %collective-permute-done.11 = f32[2,2,2,4096]{3,2,1,0:T(2,128)S(1)} collective-permute-done((f32[2,2,2,4096]{3,2,1,0:T(2,128)S(1)}, f32[2,2,2,4096]{3,2,1,0:T(2,128)S(1)}, u32[]{:S(2)}, u32[]{:S(2)}) %collective-permute-start.11) | collective-permute-done | bytes 131104 | tf_op jit(solution)/shard_map/ppermute | solution.py:54
  61.1 3.0 %collective-permute-start.18 = (f32[4096]{0:T(1024)S(1)}, f32[4096]{0:T(1024)S(1)}, u32[]{:S(2)}, u32[]{:S(2)}) collective-permute-start(f32[4096]{0:T(1024)S(1)} %bitcast.148), channel_id=1, source_target_pairs={{0,28},{1,29},{2,30},{3,31},{4,24},{5,25},{6,26},{7,27},{8,20},{9,... | collective-permute-start | bytes 49160 | tf_op jit(solution)/shard_map/ppermute | solution.py:54
  64.2 1.8 %collective-permute-start.17 = (f32[4096]{0:T(1024)S(1)}, f32[4096]{0:T(1024)S(1)}, u32[]{:S(2)}, u32[]{:S(2)}) collective-permute-start(f32[4096]{0:T(1024)S(1)} %bitcast.145), channel_id=1, source_target_pairs={{0,24},{1,25},{2,26},{3,27},{4,28},{5,29},{6,30},{7,31},{8,16},{9,... | collective-permute-start | bytes 49160 | tf_op jit(solution)/shard_map/ppermute | solution.py:54
  66.0 0.3 fusion.6
  66.4 2.9 %collective-permute-start.15 = (f32[4096]{0:T(1024)S(1)}, f32[4096]{0:T(1024)S(1)}, u32[]{:S(2)}, u32[]{:S(2)}) collective-permute-start(f32[4096]{0:T(1024)S(1)} %bitcast.141), channel_id=1, source_target_pairs={{0,16},{1,17},{2,18},{3,19},{4,20},{5,21},{6,22},{7,23},{8,24},{9,... | collective-permute-start | bytes 49160 | tf_op jit(solution)/shard_map/ppermute | solution.py:54
  69.2 0.6 collective-permute-start.14
  69.8 2.4 %collective-permute-start.13 = (f32[4096]{0:T(1024)S(1)}, f32[4096]{0:T(1024)S(1)}, u32[]{:S(2)}, u32[]{:S(2)}) collective-permute-start(f32[4096]{0:T(1024)S(1)} %bitcast.139), channel_id=1, source_target_pairs={{0,8},{1,9},{2,10},{3,11},{4,12},{5,13},{6,14},{7,15},{8,0},{9,1},... | collective-permute-start | bytes 49160 | tf_op jit(solution)/shard_map/ppermute | solution.py:54
  72.2 0.5 collective-permute-start.12
  72.8 1.0 collective-permute-done.14
  74.1 1.9 %collective-permute-done.12 = f32[4096]{0:T(1024)S(1)} collective-permute-done((f32[4096]{0:T(1024)S(1)}, f32[4096]{0:T(1024)S(1)}, u32[]{:S(2)}, u32[]{:S(2)}) %collective-permute-start.12) | collective-permute-done | bytes 16416 | tf_op jit(solution)/shard_map/ppermute | solution.py:54
  76.0 0.6 collective-permute-start.19
  76.6 3.0 %collective-permute-start.21 = (f32[4096]{0:T(1024)S(1)}, f32[4096]{0:T(1024)S(1)}, u32[]{:S(2)}, u32[]{:S(2)}) collective-permute-start(f32[4096]{0:T(1024)S(1)} %add_add_fusion), channel_id=1, source_target_pairs={{0,12},{1,13},{2,14},{3,15},{4,8},{5,9},{6,10},{7,11},{8,4},{9,5},... | collective-permute-start | bytes 49160 | tf_op jit(solution)/shard_map/ppermute | solution.py:69
  79.6 0.6 collective-permute-start.22
  80.2 2.2 %collective-permute-start.23 = (f32[4096]{0:T(1024)S(1)}, f32[4096]{0:T(1024)S(1)}, u32[]{:S(2)}, u32[]{:S(2)}) collective-permute-start(f32[4096]{0:T(1024)S(1)} %add_add_fusion), channel_id=1, source_target_pairs={{0,20},{1,21},{2,22},{3,23},{4,16},{5,17},{6,18},{7,19},{8,28},{9,... | collective-permute-start | bytes 49160 | tf_op jit(solution)/shard_map/ppermute | solution.py:69
  82.5 2.0 %collective-permute-start.24 = (f32[4096]{0:T(1024)S(1)}, f32[4096]{0:T(1024)S(1)}, u32[]{:S(2)}, u32[]{:S(2)}) collective-permute-start(f32[4096]{0:T(1024)S(1)} %add_add_fusion), channel_id=1, source_target_pairs={{0,24},{1,25},{2,26},{3,27},{4,28},{5,29},{6,30},{7,31},{8,16},{9,... | collective-permute-start | bytes 49160 | tf_op jit(solution)/shard_map/ppermute | solution.py:69
  84.5 2.8 %collective-permute-start.25 = (f32[4096]{0:T(1024)S(1)}, f32[4096]{0:T(1024)S(1)}, u32[]{:S(2)}, u32[]{:S(2)}) collective-permute-start(f32[4096]{0:T(1024)S(1)} %add_add_fusion), channel_id=1, source_target_pairs={{0,28},{1,29},{2,30},{3,31},{4,24},{5,25},{6,26},{7,27},{8,20},{9,... | collective-permute-start | bytes 49160 | tf_op jit(solution)/shard_map/ppermute | solution.py:69
  87.3 2.5 %collective-permute-start.9 = (f32[64,256]{1,0:T(8,128)S(1)}, f32[64,256]{1,0:T(8,128)S(1)}, u32[]{:S(2)}, u32[]{:S(2)}) collective-permute-start(f32[64,256]{1,0:T(8,128)S(1)} %dynamic-slice_bitcast_fusion.3), channel_id=1, source_target_pairs={{0,2},{1,3},{2,0},{3,1},{4,6},{5,7},{6,4},{7,5},{8,10},{9,11},{10,... | collective-permute-start | bytes 196616 | tf_op jit(solution)/shard_map/ppermute | solution.py:23
  89.8 1.1 %collective-permute-done.25 = f32[4096]{0:T(1024)S(1)} collective-permute-done((f32[4096]{0:T(1024)S(1)}, f32[4096]{0:T(1024)S(1)}, u32[]{:S(2)}, u32[]{:S(2)}) %collective-permute-start.25) | collective-permute-done | bytes 16416 | tf_op jit(solution)/shard_map/ppermute | solution.py:69
  91.1 0.6 gather_fusion.2
  92.0 0.8 collective-permute-start.26
  92.9 0.8 convolution_convert_fusion
  93.7 3.4 %collective-permute-done.26 = f32[2,2,2,4096]{3,2,1,0:T(2,128)S(1)} collective-permute-done((f32[2,2,2,4096]{3,2,1,0:T(2,128)S(1)}, f32[2,2,2,4096]{3,2,1,0:T(2,128)S(1)}, u32[]{:S(2)}, u32[]{:S(2)}) %collective-permute-start.26) | collective-permute-done | bytes 131104 | tf_op jit(solution)/shard_map/ppermute | solution.py:69
  97.2 0.8 gather_fusion.3
  98.5 1.3 %collective-permute-done.27 = f32[2,2,2,2,4096]{4,2,1,0,3:T(2,128)S(1)} collective-permute-done((f32[2,2,2,2,4096]{4,2,1,0,3:T(2,128)S(1)}, f32[2,2,2,2,4096]{4,2,1,0,3:T(2,128)S(1)}, u32[]{:S(2)}, u32[]{:S(2)}) %collective-permute-start.27) | collective-permute-done | bytes 262176 | tf_op jit(solution)/shard_map/ppermute | solution.py:69
  100.1 1.1 %gather_fusion.4 = f32[2,2,2,2,2,4096]{5,3,2,1,4,0:T(2,128)S(1)} fusion(f32[2,2,2,2,2,4096]{5,2,1,0,3,4:T(2,128)S(1)} %pad_maximum_fusion.1, s32[1024]{0:T(1024)S(1)} %pad_clamp_fusion), kind=kCustom, calls=%fused_computation.4 | custom fusion | bytes 1048584 | tf_op jit(solution)/shard_map/jit(_take)/gather | solution.py:72
  101.2 0.3 select_bitcast_fusion
  101.8 0.9 squeeze.100
  102.9 0.9 squeeze.101
  (89 shorter events, 5.3 us)
Async XLA Ops:
  0.6 11.9 %copy-start = (bf16[1,1,2,4,128,128]{5,4,3,2,1,0:T(8,128)(2,1)S(1)}, bf16[1,1,2,4,128,128]{5,4,3,2,1,0:T(8,128)(2,1)}, u32[]{:S(2)}) copy-start(bf16[1,1,2,4,128,128]{5,4,3,2,1,0:T(8,128)(2,1)} %param.13) | copy-start | bytes 786436
  0.6 1.0 copy-start.1
  1.7 10.2 %collective-permute-start.1 = (bf16[256,512]{1,0:T(8,128)(2,1)S(1)}, bf16[256,512]{1,0:T(8,128)(2,1)S(1)}, u32[]{:S(2)}, u32[]{:S(2)}) collective-permute-start(bf16[256,512]{1,0:T(8,128)(2,1)S(1)} %constant_dynamic-update-slice_fusion), channel_id=1, source_target_pairs={{4,0},{12,1},{20,2},{28,3},{0,4},{8,5},{16,6},{24,7},{5,8},{13,9},... | collective-permute-start | bytes 786440 | tf_op jit(solution)/shard_map/ppermute | solution.py:91
  4.7 7.2 %collective-permute-start = (bf16[256,512]{1,0:T(8,128)(2,1)S(1)}, bf16[256,512]{1,0:T(8,128)(2,1)S(1)}, u32[]{:S(2)}, u32[]{:S(2)}) collective-permute-start(bf16[256,512]{1,0:T(8,128)(2,1)S(1)} %constant_dynamic-update-slice_fusion), channel_id=1, source_target_pairs={{0,0},{8,1},{16,2},{24,3},{4,4},{12,5},{20,6},{28,7},{1,8},{9,9},{... | collective-permute-start | bytes 786440 | tf_op jit(solution)/shard_map/ppermute | solution.py:91
  5.4 0.7 copy-start.3
  5.4 0.7 copy-start.4
  13.0 5.6 %collective-permute-start.2 = (f32[2,64,512]{2,1,0:T(8,128)S(1)}, f32[2,64,512]{2,1,0:T(8,128)S(1)}, u32[]{:S(2)}, u32[]{:S(2)}) collective-permute-start(f32[2,64,512]{2,1,0:T(8,128)S(1)} %dynamic-slice_bitcast_fusion), channel_id=1, source_target_pairs={{0,1},{1,0},{2,3},{3,2},{4,5},{5,4},{6,7},{7,6},{8,9},{9,8},{10,11... | collective-permute-start | bytes 786440 | tf_op jit(solution)/shard_map/ppermute | solution.py:23
  18.7 21.0 %collective-permute-start.3 = (f32[64,512]{1,0:T(8,128)S(1)}, f32[64,512]{1,0:T(8,128)S(1)}, u32[]{:S(2)}, u32[]{:S(2)}) collective-permute-start(f32[64,512]{1,0:T(8,128)S(1)} %dynamic-slice_bitcast_fusion.2), channel_id=1, source_target_pairs={{0,2},{1,3},{2,0},{3,1},{4,6},{5,7},{6,4},{7,5},{8,10},{9,11},{10,... | collective-permute-start | bytes 393224 | tf_op jit(solution)/shard_map/ppermute | solution.py:23
  35.9 3.8 %copy-start.5 = (bf16[256,256]{1,0:T(8,128)(2,1)S(1)}, bf16[256,256]{1,0:T(8,128)(2,1)}, u32[]{:S(2)}) copy-start(bf16[256,256]{1,0:T(8,128)(2,1)} %param.9) | copy-start | bytes 393220
  39.9 2.1 %copy-start.2 = (bf16[256,256]{1,0:T(8,128)(2,1)S(1)}, bf16[256,256]{1,0:T(8,128)(2,1)}, u32[]{:S(2)}) copy-start(bf16[256,256]{1,0:T(8,128)(2,1)} %param.10) | copy-start | bytes 393220
  39.9 4.0 %collective-permute-start.4 = (bf16[64,256]{1,0:T(8,128)(2,1)S(1)}, bf16[64,256]{1,0:T(8,128)(2,1)S(1)}, u32[]{:S(2)}, u32[]{:S(2)}) collective-permute-start(bf16[64,256]{1,0:T(8,128)(2,1)S(1)} %get-tuple-element.23), channel_id=1, source_target_pairs={{0,2},{1,3},{2,0},{3,1},{4,6},{5,7},{6,4},{7,5},{8,10},{9,11},{10,... | collective-permute-start | bytes 98312 | tf_op jit(solution)/shard_map/ppermute | solution.py:30
  43.9 1.4 %collective-permute-start.5 = (bf16[2,64,256]{2,1,0:T(8,128)(2,1)S(1)}, bf16[2,64,256]{2,1,0:T(8,128)(2,1)S(1)}, u32[]{:S(2)}, u32[]{:S(2)}) collective-permute-start(bf16[2,64,256]{2,1,0:T(8,128)(2,1)S(1)} %pad_maximum_fusion.5), channel_id=1, source_target_pairs={{0,1},{1,0},{2,3},{3,2},{4,5},{5,4},{6,7},{7,6},{8,9},{9,8},{10,11... | collective-permute-start | bytes 196616 | tf_op jit(solution)/shard_map/ppermute | solution.py:30
  44.8 1.9 %collective-permute-start.10 = (f32[2,2,2,2,4096]{4,3,2,1,0:T(2,128)S(1)}, f32[2,2,2,2,4096]{4,3,2,1,0:T(2,128)S(1)}, u32[]{:S(2)}, u32[]{:S(2)}) collective-permute-start(f32[2,2,2,2,4096]{4,3,2,1,0:T(2,128)S(1)} %bitcast.126), channel_id=1, source_target_pairs={{0,1},{1,0},{2,3},{3,2},{4,5},{5,4},{6,7},{7,6},{8,9},{9,8},{10,11... | collective-permute-start | bytes 786440 | tf_op jit(solution)/shard_map/ppermute | solution.py:54
  45.4 8.3 %collective-permute-start.7 = (bf16[256,256]{1,0:T(8,128)(2,1)S(1)}, bf16[256,256]{1,0:T(8,128)(2,1)S(1)}, u32[]{:S(2)}, u32[]{:S(2)}) collective-permute-start(bf16[256,256]{1,0:T(8,128)(2,1)S(1)} %bitcast.130), channel_id=1, source_target_pairs={{4,0},{12,1},{20,2},{28,3},{0,4},{8,5},{16,6},{24,7},{5,8},{13,9},... | collective-permute-start | bytes 393224 | tf_op jit(solution)/shard_map/ppermute | solution.py:91
  46.0 7.7 %collective-permute-start.6 = (bf16[256,256]{1,0:T(8,128)(2,1)S(1)}, bf16[256,256]{1,0:T(8,128)(2,1)S(1)}, u32[]{:S(2)}, u32[]{:S(2)}) collective-permute-start(bf16[256,256]{1,0:T(8,128)(2,1)S(1)} %bitcast.131), channel_id=1, source_target_pairs={{0,0},{8,1},{16,2},{24,3},{4,4},{12,5},{20,6},{28,7},{1,8},{9,9},{... | collective-permute-start | bytes 393224 | tf_op jit(solution)/shard_map/ppermute | solution.py:91
  47.4 13.4 %collective-permute-start.11 = (f32[2,2,2,4096]{3,2,1,0:T(2,128)S(1)}, f32[2,2,2,4096]{3,2,1,0:T(2,128)S(1)}, u32[]{:S(2)}, u32[]{:S(2)}) collective-permute-start(f32[2,2,2,4096]{3,2,1,0:T(2,128)S(1)} %bitcast.132), channel_id=1, source_target_pairs={{0,2},{1,3},{2,0},{3,1},{4,6},{5,7},{6,4},{7,5},{8,10},{9,11},{10,... | collective-permute-start | bytes 393224 | tf_op jit(solution)/shard_map/ppermute | solution.py:54
  61.1 8.7 %collective-permute-start.18 = (f32[4096]{0:T(1024)S(1)}, f32[4096]{0:T(1024)S(1)}, u32[]{:S(2)}, u32[]{:S(2)}) collective-permute-start(f32[4096]{0:T(1024)S(1)} %bitcast.148), channel_id=1, source_target_pairs={{0,28},{1,29},{2,30},{3,31},{4,24},{5,25},{6,26},{7,27},{8,20},{9,... | collective-permute-start | bytes 49160 | tf_op jit(solution)/shard_map/ppermute | solution.py:54
  64.2 8.1 %collective-permute-start.17 = (f32[4096]{0:T(1024)S(1)}, f32[4096]{0:T(1024)S(1)}, u32[]{:S(2)}, u32[]{:S(2)}) collective-permute-start(f32[4096]{0:T(1024)S(1)} %bitcast.145), channel_id=1, source_target_pairs={{0,24},{1,25},{2,26},{3,27},{4,28},{5,29},{6,30},{7,31},{8,16},{9,... | collective-permute-start | bytes 49160 | tf_op jit(solution)/shard_map/ppermute | solution.py:54
  66.3 6.4 %collective-permute-start.16 = (f32[4096]{0:T(1024)S(1)}, f32[4096]{0:T(1024)S(1)}, u32[]{:S(2)}, u32[]{:S(2)}) collective-permute-start(f32[4096]{0:T(1024)S(1)} %bitcast.144), channel_id=1, source_target_pairs={{0,20},{1,21},{2,22},{3,23},{4,16},{5,17},{6,18},{7,19},{8,28},{9,... | collective-permute-start | bytes 49160 | tf_op jit(solution)/shard_map/ppermute | solution.py:54
  66.4 6.5 %collective-permute-start.15 = (f32[4096]{0:T(1024)S(1)}, f32[4096]{0:T(1024)S(1)}, u32[]{:S(2)}, u32[]{:S(2)}) collective-permute-start(f32[4096]{0:T(1024)S(1)} %bitcast.141), channel_id=1, source_target_pairs={{0,16},{1,17},{2,18},{3,19},{4,20},{5,21},{6,22},{7,23},{8,24},{9,... | collective-permute-start | bytes 49160 | tf_op jit(solution)/shard_map/ppermute | solution.py:54
  69.2 4.6 %collective-permute-start.14 = (f32[4096]{0:T(1024)S(1)}, f32[4096]{0:T(1024)S(1)}, u32[]{:S(2)}, u32[]{:S(2)}) collective-permute-start(f32[4096]{0:T(1024)S(1)} %bitcast.140), channel_id=1, source_target_pairs={{0,12},{1,13},{2,14},{3,15},{4,8},{5,9},{6,10},{7,11},{8,4},{9,5},... | collective-permute-start | bytes 49160 | tf_op jit(solution)/shard_map/ppermute | solution.py:54
  69.8 4.3 %collective-permute-start.13 = (f32[4096]{0:T(1024)S(1)}, f32[4096]{0:T(1024)S(1)}, u32[]{:S(2)}, u32[]{:S(2)}) collective-permute-start(f32[4096]{0:T(1024)S(1)} %bitcast.139), channel_id=1, source_target_pairs={{0,8},{1,9},{2,10},{3,11},{4,12},{5,13},{6,14},{7,15},{8,0},{9,1},... | collective-permute-start | bytes 49160 | tf_op jit(solution)/shard_map/ppermute | solution.py:54
  72.2 3.7 %collective-permute-start.12 = (f32[4096]{0:T(1024)S(1)}, f32[4096]{0:T(1024)S(1)}, u32[]{:S(2)}, u32[]{:S(2)}) collective-permute-start(f32[4096]{0:T(1024)S(1)} %bitcast.138), channel_id=1, source_target_pairs={{0,4},{1,5},{2,6},{3,7},{4,0},{5,1},{6,2},{7,3},{8,12},{9,13},{10,... | collective-permute-start | bytes 49160 | tf_op jit(solution)/shard_map/ppermute | solution.py:54
  72.7 3.9 %collective-permute-start.8 = (f32[2,64,256]{2,1,0:T(8,128)S(1)}, f32[2,64,256]{2,1,0:T(8,128)S(1)}, u32[]{:S(2)}, u32[]{:S(2)}) collective-permute-start(f32[2,64,256]{2,1,0:T(8,128)S(1)} %dynamic-slice_bitcast_fusion.1), channel_id=1, source_target_pairs={{0,1},{1,0},{2,3},{3,2},{4,5},{5,4},{6,7},{7,6},{8,9},{9,8},{10,11... | collective-permute-start | bytes 393224 | tf_op jit(solution)/shard_map/ppermute | solution.py:23
  76.0 6.5 %collective-permute-start.19 = (f32[4096]{0:T(1024)S(1)}, f32[4096]{0:T(1024)S(1)}, u32[]{:S(2)}, u32[]{:S(2)}) collective-permute-start(f32[4096]{0:T(1024)S(1)} %add_add_fusion), channel_id=1, source_target_pairs={{0,4},{1,5},{2,6},{3,7},{4,0},{5,1},{6,2},{7,3},{8,12},{9,13},{10,... | collective-permute-start | bytes 49160 | tf_op jit(solution)/shard_map/ppermute | solution.py:69
  76.5 8.0 %collective-permute-start.20 = (f32[4096]{0:T(1024)S(1)}, f32[4096]{0:T(1024)S(1)}, u32[]{:S(2)}, u32[]{:S(2)}) collective-permute-start(f32[4096]{0:T(1024)S(1)} %add_add_fusion), channel_id=1, source_target_pairs={{0,8},{1,9},{2,10},{3,11},{4,12},{5,13},{6,14},{7,15},{8,0},{9,1},... | collective-permute-start | bytes 49160 | tf_op jit(solution)/shard_map/ppermute | solution.py:69
  76.6 10.6 %collective-permute-start.21 = (f32[4096]{0:T(1024)S(1)}, f32[4096]{0:T(1024)S(1)}, u32[]{:S(2)}, u32[]{:S(2)}) collective-permute-start(f32[4096]{0:T(1024)S(1)} %add_add_fusion), channel_id=1, source_target_pairs={{0,12},{1,13},{2,14},{3,15},{4,8},{5,9},{6,10},{7,11},{8,4},{9,5},... | collective-permute-start | bytes 49160 | tf_op jit(solution)/shard_map/ppermute | solution.py:69
  79.6 10.2 %collective-permute-start.22 = (f32[4096]{0:T(1024)S(1)}, f32[4096]{0:T(1024)S(1)}, u32[]{:S(2)}, u32[]{:S(2)}) collective-permute-start(f32[4096]{0:T(1024)S(1)} %add_add_fusion), channel_id=1, source_target_pairs={{0,16},{1,17},{2,18},{3,19},{4,20},{5,21},{6,22},{7,23},{8,24},{9,... | collective-permute-start | bytes 49160 | tf_op jit(solution)/shard_map/ppermute | solution.py:69
  80.2 9.6 %collective-permute-start.23 = (f32[4096]{0:T(1024)S(1)}, f32[4096]{0:T(1024)S(1)}, u32[]{:S(2)}, u32[]{:S(2)}) collective-permute-start(f32[4096]{0:T(1024)S(1)} %add_add_fusion), channel_id=1, source_target_pairs={{0,20},{1,21},{2,22},{3,23},{4,16},{5,17},{6,18},{7,19},{8,28},{9,... | collective-permute-start | bytes 49160 | tf_op jit(solution)/shard_map/ppermute | solution.py:69
  82.5 7.4 %collective-permute-start.24 = (f32[4096]{0:T(1024)S(1)}, f32[4096]{0:T(1024)S(1)}, u32[]{:S(2)}, u32[]{:S(2)}) collective-permute-start(f32[4096]{0:T(1024)S(1)} %add_add_fusion), channel_id=1, source_target_pairs={{0,24},{1,25},{2,26},{3,27},{4,28},{5,29},{6,30},{7,31},{8,16},{9,... | collective-permute-start | bytes 49160 | tf_op jit(solution)/shard_map/ppermute | solution.py:69
  84.5 6.4 %collective-permute-start.25 = (f32[4096]{0:T(1024)S(1)}, f32[4096]{0:T(1024)S(1)}, u32[]{:S(2)}, u32[]{:S(2)}) collective-permute-start(f32[4096]{0:T(1024)S(1)} %add_add_fusion), channel_id=1, source_target_pairs={{0,28},{1,29},{2,30},{3,31},{4,24},{5,25},{6,26},{7,27},{8,20},{9,... | collective-permute-start | bytes 49160 | tf_op jit(solution)/shard_map/ppermute | solution.py:69
  87.3 5.6 %collective-permute-start.9 = (f32[64,256]{1,0:T(8,128)S(1)}, f32[64,256]{1,0:T(8,128)S(1)}, u32[]{:S(2)}, u32[]{:S(2)}) collective-permute-start(f32[64,256]{1,0:T(8,128)S(1)} %dynamic-slice_bitcast_fusion.3), channel_id=1, source_target_pairs={{0,2},{1,3},{2,0},{3,1},{4,6},{5,7},{6,4},{7,5},{8,10},{9,11},{10,... | collective-permute-start | bytes 196616 | tf_op jit(solution)/shard_map/ppermute | solution.py:23
  92.0 5.0 %collective-permute-start.26 = (f32[2,2,2,4096]{3,2,1,0:T(2,128)S(1)}, f32[2,2,2,4096]{3,2,1,0:T(2,128)S(1)}, u32[]{:S(2)}, u32[]{:S(2)}) collective-permute-start(f32[2,2,2,4096]{3,2,1,0:T(2,128)S(1)} %broadcast_select_fusion), channel_id=1, source_target_pairs={{0,2},{1,3},{2,0},{3,1},{4,6},{5,7},{6,4},{7,5},{8,10},{9,11},{10,... | collective-permute-start | bytes 393224 | tf_op jit(solution)/shard_map/ppermute | solution.py:69
  98.2 1.6 %collective-permute-start.27 = (f32[2,2,2,2,4096]{4,2,1,0,3:T(2,128)S(1)}, f32[2,2,2,2,4096]{4,2,1,0,3:T(2,128)S(1)}, u32[]{:S(2)}, u32[]{:S(2)}) collective-permute-start(f32[2,2,2,2,4096]{4,2,1,0,3:T(2,128)S(1)} %bitcast_select_fusion.1), channel_id=1, source_target_pairs={{0,1},{1,0},{2,3},{3,2},{4,5},{5,4},{6,7},{7,6},{8,9},{9,8},{10,11... | collective-permute-start | bytes 786440 | tf_op jit(solution)/shard_map/ppermute | solution.py:69

commit v5 on v3

--- a/solution.py
+++ b/solution.py
@@ -12,6 +12,10 @@
 
 def bit_pairs(devices, bit):
     return [(d, d ^ (1 << bit)) for d in range(devices)]
+
+
+def group_pairs(devices, mask):
+    return [(d, d ^ mask) for d in range(devices)]
 
 
 def reduce_scatter_bits(y, me, bits, devices):
@@ -72,6 +76,32 @@
     return partial_value.reshape(block_rows * block_side, width)
 
 
+def halve(y, mine):
+    half = y.shape[0] // 2
+    keep = lax.dynamic_slice_in_dim(y, mine * half, half, 0)
+    send = lax.dynamic_slice_in_dim(y, (1 - mine) * half, half, 0)
+    return keep, send
+
+
+def join(z, other, mine, axis, stack):
+    low = jnp.where(mine == 0, z, other)
+    high = jnp.where(mine == 0, other, z)
+    if stack:
+        return jnp.stack([low, high], axis=axis)
+    return jnp.concatenate([low, high], axis=axis)
+
+
+def exchange(pieces, mask, devices, width):
+    flat = [p.reshape(-1, width) for p in pieces]
+    sizes = [f.shape[0] for f in flat]
+    got = lax.ppermute(jnp.concatenate(flat, axis=0), AXES, group_pairs(devices, mask))
+    out, at = [], 0
+    for p, n in zip(pieces, sizes):
+        out.append(got[at : at + n].reshape(p.shape))
+        at += n
+    return out
+
+
 def shards(features, cotangent, weight_one, weight_two, block_index, block_count, block_values):
     rows = lax.axis_size("row")
     copies = lax.axis_size("rep")
@@ -83,20 +113,16 @@
     share_rows = node_rows // copies
     rep_levels = copies.bit_length() - 1
     rep_bits = list(range(rep_levels))
-    all_bits = list(range(devices.bit_length() - 1))
-
-    def reduce_rep(partial_value):
-        y = partial_value.reshape([2] * rep_levels + [share_rows, partial_value.shape[-1]])
-        return reduce_scatter_bits(y, me, rep_bits, devices)
-
-    def gather_rep(z):
-        return all_gather_bits(z, me, rep_bits, devices).reshape(node_rows, z.shape[-1])
+    levels = devices.bit_length() - 1
+    grad_elems = feature_width * feature_width
+    width = feature_width if grad_elems // feature_width >= 8 * devices else grad_elems // (8 * devices)
+    my_bit = [(me >> b) & 1 for b in range(levels)]
 
     stage_in = jnp.concatenate([features, cotangent], axis=1)
     pieces = gather_rounds(stage_in, rows, copies)
-    both = reduce_rep(
-        local_product(pieces, block_index, block_count, block_values, row_index, copy_index)
-    )
+    partial_a = local_product(pieces, block_index, block_count, block_values, row_index, copy_index)
+    partial_a = partial_a.reshape([2] * rep_levels + [share_rows, partial_a.shape[-1]])
+    both = reduce_scatter_bits(partial_a, me, rep_bits, devices)
     agg_one = both[:, :feature_width].astype(jnp.bfloat16)
     spread_cotangent = both[:, feature_width:]
     carried = lax.dot_general(
@@ -122,20 +148,38 @@
         precision=lax.Precision.HIGHEST,
         preferred_element_type=jnp.float32,
     )
-    grads = jnp.stack([grad_one, grad_two])
-    total = grads.size
-    levels = len(all_bits)
-    segment = grads.reshape([2] * levels + [total // devices])
-    summed = reduce_scatter_bits(segment, me, all_bits, devices)
-    grads = all_gather_bits(summed, me, all_bits, devices).reshape(grads.shape)
-
-    hidden_full = gather_rep(hidden)
+    grads = [g.reshape(-1, width) for g in (grad_one, grad_two)]
+
+    grad_order = list(reversed(rep_bits)) + list(range(rep_levels, levels))
+    held = hidden.astype(jnp.float32)
+    for step, bit in enumerate(reversed(rep_bits)):
+        halves = [halve(g, my_bit[bit]) for g in grads]
+        got = exchange([held] + [h[1] for h in halves], 1 << bit, devices, width)
+        held = join(held, got[0], my_bit[bit], step, True)
+        grads = [h[0] + r for h, r in zip(halves, got[1:])]
+    hidden_full = held.reshape(node_rows, feature_width).astype(jnp.bfloat16)
+    for bit in grad_order[rep_levels:]:
+        halves = [halve(g, my_bit[bit]) for g in grads]
+        got = exchange([h[1] for h in halves], 1 << bit, devices, width)
+        grads = [h[0] + r for h, r in zip(halves, got)]
+    for bit in reversed(grad_order[rep_levels:]):
+        got = exchange(grads, 1 << bit, devices, width)
+        grads = [join(g, r, my_bit[bit], 0, False) for g, r in zip(grads, got)]
+
     pieces_two = gather_rounds(hidden_full, rows, copies)
-    agg_two = reduce_rep(
-        local_product(pieces_two, block_index, block_count, block_values, row_index, copy_index)
-    ).astype(jnp.bfloat16)
+    partial_b = local_product(pieces_two, block_index, block_count, block_values, row_index, copy_index)
+    partial_b = partial_b.reshape([2] * rep_levels + [share_rows, feature_width])
+    for step, bit in enumerate(rep_bits):
+        axis = rep_levels - 1 - step
+        keep = lax.dynamic_index_in_dim(partial_b, my_bit[bit], axis, keepdims=False)
+        send = lax.dynamic_index_in_dim(partial_b, 1 - my_bit[bit], axis, keepdims=False)
+        got = exchange([send] + grads, 1 << bit, devices, width)
+        partial_b = keep + got[0]
+        grads = [join(g, r, my_bit[bit], 0, False) for g, r in zip(grads, got[1:])]
+    agg_two = partial_b.astype(jnp.bfloat16)
     logits = jnp.dot(agg_two, weight_two, preferred_element_type=jnp.float32).astype(jnp.bfloat16)
-    return (logits, grads[0], grads[1])
+    grad_one, grad_two = [g.reshape(feature_width, feature_width) for g in grads]
+    return (logits, grad_one, grad_two)
 
 
 def solution(mesh):

time: 96.2 us -> 99.6 us (1.035)
  waiting for transfers between devices: 42.5 us -> 55.3 us
  local copies, waits for them, and re-layouts: 8.4 us -> 3.78 us
  starting transfers between devices: 39 us -> 34.6 us
    ppermute x7 -> x10, waiting for transfers between devices: 14.1 us -> 44.7 us  [exchange(): lax.ppermute(jnp.concatenate(flat, axis=0), AXES, group_pairs(devices, ma...]
    ppermute x9 -> x2, waiting for transfers between devices: 22.8 us -> 4.96 us  [reduce_scatter_bits(): y = keep + lax.ppermute(send, AXES, bit_pairs(devices, bit))]
    ppermute x9 -> x2, starting transfers between devices: 30.7 us -> 21.6 us  [reduce_scatter_bits(): y = keep + lax.ppermute(send, AXES, bit_pairs(devices, bit))]
    ppermute x7 -> x10, starting transfers between devices: 3.32 us -> 8.05 us  [exchange(): lax.ppermute(jnp.concatenate(flat, axis=0), AXES, group_pairs(devices, ma...]
    squeeze x2 -> x0, local copies, waits for them, and re-layouts: 1.86 us -> none  [shards(): return (logits, grads[0], grads[1])]
    concatenate x0 -> x12, other arithmetic: none -> 1.54 us  [the longest x2 1.44 us: join(): return jnp.concatenate([low, high], axis=axis)]
    another operation x12 -> x0, local copies, waits for them, and re-layouts: 1.29 us -> none  [the longest x9 0.91 us: all_gather_bits(): z = jnp.stack([low, high], axis=step)]
    another operation x12 -> x5, other arithmetic: 1.27 us -> 0.07 us  [the longest x4 0.05 us: join(): return jnp.stack([low, high], axis=axis)]
  transfers between devices with their start and end apart: 20 -> 16, of which waited for: 12 -> 13; matrix products, arithmetic and copies ran while one was open for 4% -> 1% of each run, Pallas kernels for 0% -> 0%
where the time goes in v5:
time: 99.6 us; the launch traced here: 99.4 us
  waiting for transfers between devices  55.3 us (56%)
  starting transfers between devices  34.6 us (35%)
  local copies, waits for them, and re-layouts  3.78 us (4%)
  matrix products  2.47 us (2%)
  other arithmetic  2.05 us (2%)
  between operations  1.14 us (1%)
    ppermute x10, waiting for transfers between devices, exchange(): lax.ppermute(jnp.concatenate(flat, axis=0), AXES, group_pairs(devices, ma...  44.7 us
    ppermute x2, starting transfers between devices, reduce_scatter_bits(): y = keep + lax.ppermute(send, AXES, bit_pairs(devices, bit))  21.6 us
    ppermute x10, starting transfers between devices, exchange(): lax.ppermute(jnp.concatenate(flat, axis=0), AXES, group_pairs(devices, ma...  8.05 us
    ppermute x4, waiting for transfers between devices, gather_rounds(): pieces.append(lax.ppermute(x, AXES, pairs))  5.61 us
    ppermute x4, starting transfers between devices, gather_rounds(): pieces.append(lax.ppermute(x, AXES, pairs))  4.96 us
    ppermute x2, waiting for transfers between devices, reduce_scatter_bits(): y = keep + lax.ppermute(send, AXES, bit_pairs(devices, bit))  4.96 us
    unnamed x15, local copies, waits for them, and re-layouts  2.28 us
  transfers between devices with their start and end apart: 16, of which 13 were waited for; matrix products, arithmetic and copies ran while one was open for 1% of the time, Pallas kernels for 0%

profile of v5, /device:TPU:0, one launch (start us, length us, event | category | flops | bytes accessed | tf_op | source)
XLA Modules:
  0.0 99.4 jit_solution(1951097479267588771)
XLA Ops:
  0.6 0.0 copy-start
  0.7 1.0 constant_dynamic-update-slice_fusion.1
  1.6 0.0 copy-done.1
  1.7 3.1 %collective-permute-start.1 = (bf16[256,512]{1,0:T(8,128)(2,1)S(1)}, bf16[256,512]{1,0:T(8,128)(2,1)S(1)}, u32[]{:S(2)}, u32[]{:S(2)}) collective-permute-start(bf16[256,512]{1,0:T(8,128)(2,1)S(1)} %constant_dynamic-update-slice_fusion), channel_id=1, source_target_pairs={{4,0},{12,1},{20,2},{28,3},{0,4},{8,5},{16,6},{24,7},{5,8},{13,9},... | collective-permute-start | bytes 786440 | tf_op jit(solution)/shard_map/ppermute | solution.py:50
  4.7 0.7 collective-permute-start
  5.4 0.7 copy-done.3
  6.1 0.1 compare_and_fusion
  6.2 0.1 sub.88
  6.3 5.6 %collective-permute-done.1 = bf16[256,512]{1,0:T(8,128)(2,1)S(1)} collective-permute-done((bf16[256,512]{1,0:T(8,128)(2,1)S(1)}, bf16[256,512]{1,0:T(8,128)(2,1)S(1)}, u32[]{:S(2)}, u32[]{:S(2)}) %collective-permute-start.1) | collective-permute-done | bytes 262176 | tf_op jit(solution)/shard_map/ppermute | solution.py:50
  11.9 0.1 pad_maximum_fusion
  11.9 0.6 gather_fusion
  12.6 0.4 fusion.1
  13.0 4.4 %collective-permute-start.2 = (f32[2,64,512]{2,1,0:T(8,128)S(1)}, f32[2,64,512]{2,1,0:T(8,128)S(1)}, u32[]{:S(2)}, u32[]{:S(2)}) collective-permute-start(f32[2,64,512]{2,1,0:T(8,128)S(1)} %dynamic-slice_bitcast_fusion), channel_id=1, source_target_pairs={{0,1},{1,0},{2,3},{3,2},{4,5},{5,4},{6,7},{7,6},{8,9},{9,8},{10,11... | collective-permute-start | bytes 786440 | tf_op jit(solution)/shard_map/ppermute | solution.py:27
  17.5 1.2 %collective-permute-done.2 = f32[2,64,512]{2,1,0:T(8,128)S(1)} collective-permute-done((f32[2,64,512]{2,1,0:T(8,128)S(1)}, f32[2,64,512]{2,1,0:T(8,128)S(1)}, u32[]{:S(2)}, u32[]{:S(2)}) %collective-permute-start.2) | collective-permute-done | bytes 262176 | tf_op jit(solution)/shard_map/ppermute | solution.py:27
  18.7 17.2 %collective-permute-start.3 = (f32[64,512]{1,0:T(8,128)S(1)}, f32[64,512]{1,0:T(8,128)S(1)}, u32[]{:S(2)}, u32[]{:S(2)}) collective-permute-start(f32[64,512]{1,0:T(8,128)S(1)} %dynamic-slice_bitcast_fusion.1), channel_id=1, source_target_pairs={{0,2},{1,3},{2,0},{3,1},{4,6},{5,7},{6,4},{7,5},{8,10},{9,11},{10,... | collective-permute-start | bytes 393224 | tf_op jit(solution)/shard_map/ppermute | solution.py:27
  35.9 3.8 %collective-permute-done.3 = f32[64,512]{1,0:T(8,128)S(1)} collective-permute-done((f32[64,512]{1,0:T(8,128)S(1)}, f32[64,512]{1,0:T(8,128)S(1)}, u32[]{:S(2)}, u32[]{:S(2)}) %collective-permute-start.3) | collective-permute-done | bytes 131104 | tf_op jit(solution)/shard_map/ppermute | solution.py:27
  39.7 0.2 fusion.42
  39.9 0.3 fusion.18
  40.2 0.6 copy-done.2
  40.8 0.3 fusion
  41.1 0.2 fusion.29
  41.4 1.8 %collective-permute-start.4 = (f32[320,256]{1,0:T(8,128)S(1)}, f32[320,256]{1,0:T(8,128)S(1)}, u32[]{:S(2)}, u32[]{:S(2)}) collective-permute-start(f32[320,256]{1,0:T(8,128)S(1)} %pad_maximum_fusion.1), channel_id=1, source_target_pairs={{0,2},{1,3},{2,0},{3,1},{4,6},{5,7},{6,4},{7,5},{8,10},{9,11},{10,... | collective-permute-start | bytes 983048 | tf_op jit(solution)/shard_map/ppermute | solution.py:97
  43.2 7.4 %collective-permute-done.4 = f32[320,256]{1,0:T(8,128)S(1)} collective-permute-done((f32[320,256]{1,0:T(8,128)S(1)}, f32[320,256]{1,0:T(8,128)S(1)}, u32[]{:S(2)}, u32[]{:S(2)}) %collective-permute-start.4) | collective-permute-done | bytes 327712 | tf_op jit(solution)/shard_map/ppermute | solution.py:97
  50.8 0.1 collective-permute-start.5
  50.9 1.5 %collective-permute-done.5 = f32[256,256]{1,0:T(8,128)S(1)} collective-permute-done((f32[256,256]{1,0:T(8,128)S(1)}, f32[256,256]{1,0:T(8,128)S(1)}, u32[]{:S(2)}, u32[]{:S(2)}) %collective-permute-start.5) | collective-permute-done | bytes 262176 | tf_op jit(solution)/shard_map/ppermute | solution.py:97
  52.5 0.6 collective-permute-start.8
  53.1 3.7 %collective-permute-done.8 = f32[64,256]{1,0:T(8,128)S(1)} collective-permute-done((f32[64,256]{1,0:T(8,128)S(1)}, f32[64,256]{1,0:T(8,128)S(1)}, u32[]{:S(2)}, u32[]{:S(2)}) %collective-permute-start.8) | collective-permute-done | bytes 65568 | tf_op jit(solution)/shard_map/ppermute | solution.py:97
  56.9 0.2 collective-permute-start.9
  57.1 3.8 %collective-permute-done.9 = f32[32,256]{1,0:T(8,128)S(1)} collective-permute-done((f32[32,256]{1,0:T(8,128)S(1)}, f32[32,256]{1,0:T(8,128)S(1)}, u32[]{:S(2)}, u32[]{:S(2)}) %collective-permute-start.9) | collective-permute-done | bytes 32800 | tf_op jit(solution)/shard_map/ppermute | solution.py:97
  60.9 1.1 %collective-permute-start.10 = (f32[16,256]{1,0:T(8,128)S(1)}, f32[16,256]{1,0:T(8,128)S(1)}, u32[]{:S(2)}, u32[]{:S(2)}) collective-permute-start(f32[16,256]{1,0:T(8,128)S(1)} %pad_maximum_fusion.19), channel_id=1, source_target_pairs={{0,16},{1,17},{2,18},{3,19},{4,20},{5,21},{6,22},{7,23},{8,24},{9,... | collective-permute-start | bytes 49160 | tf_op jit(solution)/shard_map/ppermute | solution.py:97
  62.0 0.6 collective-permute-start.7
  62.6 0.7 collective-permute-start.6
  63.3 6.0 %collective-permute-done.10 = f32[16,256]{1,0:T(8,128)S(1)} collective-permute-done((f32[16,256]{1,0:T(8,128)S(1)}, f32[16,256]{1,0:T(8,128)S(1)}, u32[]{:S(2)}, u32[]{:S(2)}) %collective-permute-start.10) | collective-permute-done | bytes 16416 | tf_op jit(solution)/shard_map/ppermute | solution.py:97
  69.2 0.5 collective-permute-start.11
  69.8 0.6 gather_fusion.1
  70.4 0.3 fusion.6
  70.7 6.0 %collective-permute-done.11 = f32[16,256]{1,0:T(8,128)S(1)} collective-permute-done((f32[16,256]{1,0:T(8,128)S(1)}, f32[16,256]{1,0:T(8,128)S(1)}, u32[]{:S(2)}, u32[]{:S(2)}) %collective-permute-start.11) | collective-permute-done | bytes 16416 | tf_op jit(solution)/shard_map/ppermute | solution.py:97
  76.7 0.1 collective-permute-start.12
  76.8 3.9 %collective-permute-done.12 = f32[32,256]{1,0:T(8,128)S(1)} collective-permute-done((f32[32,256]{1,0:T(8,128)S(1)}, f32[32,256]{1,0:T(8,128)S(1)}, u32[]{:S(2)}, u32[]{:S(2)}) %collective-permute-start.12) | collective-permute-done | bytes 32800 | tf_op jit(solution)/shard_map/ppermute | solution.py:97
  80.7 1.4 %collective-permute-start.13 = (f32[64,256]{1,0:T(8,128)S(1)}, f32[64,256]{1,0:T(8,128)S(1)}, u32[]{:S(2)}, u32[]{:S(2)}) collective-permute-start(f32[64,256]{1,0:T(8,128)S(1)} %pad_maximum_fusion.12), channel_id=1, source_target_pairs={{0,4},{1,5},{2,6},{3,7},{4,0},{5,1},{6,2},{7,3},{8,12},{9,13},{10,... | collective-permute-start | bytes 196616 | tf_op jit(solution)/shard_map/ppermute | solution.py:97
  82.1 2.9 %collective-permute-done.13 = f32[64,256]{1,0:T(8,128)S(1)} collective-permute-done((f32[64,256]{1,0:T(8,128)S(1)}, f32[64,256]{1,0:T(8,128)S(1)}, u32[]{:S(2)}, u32[]{:S(2)}) %collective-permute-start.13) | collective-permute-done | bytes 65568 | tf_op jit(solution)/shard_map/ppermute | solution.py:97
  85.1 0.1 collective-permute-start.14
  85.2 1.5 %collective-permute-done.14 = f32[256,256]{1,0:T(8,128)S(1)} collective-permute-done((f32[256,256]{1,0:T(8,128)S(1)}, f32[256,256]{1,0:T(8,128)S(1)}, u32[]{:S(2)}, u32[]{:S(2)}) %collective-permute-start.14) | collective-permute-done | bytes 262176 | tf_op jit(solution)/shard_map/ppermute | solution.py:97
  86.9 2.2 %collective-permute-start.15 = (f32[320,256]{1,0:T(8,128)S(1)}, f32[320,256]{1,0:T(8,128)S(1)}, u32[]{:S(2)}, u32[]{:S(2)}) collective-permute-start(f32[320,256]{1,0:T(8,128)S(1)} %get-tuple-element.3), channel_id=1, source_target_pairs={{0,2},{1,3},{2,0},{3,1},{4,6},{5,7},{6,4},{7,5},{8,10},{9,11},{10,... | collective-permute-start | bytes 983048 | tf_op jit(solution)/shard_map/ppermute | solution.py:97
  89.1 8.0 %collective-permute-done.15 = f32[320,256]{1,0:T(8,128)S(1)} collective-permute-done((f32[320,256]{1,0:T(8,128)S(1)}, f32[320,256]{1,0:T(8,128)S(1)}, u32[]{:S(2)}, u32[]{:S(2)}) %collective-permute-start.15) | collective-permute-done | bytes 327712 | tf_op jit(solution)/shard_map/ppermute | solution.py:97
  97.2 0.7 pad_maximum_fusion.4
  97.9 0.7 pad_maximum_fusion.5
  98.6 0.8 convolution_convert_fusion
  (64 shorter events, 0.8 us)
Async XLA Ops:
  0.6 11.9 %copy-start = (bf16[1,1,2,4,128,128]{5,4,3,2,1,0:T(8,128)(2,1)S(1)}, bf16[1,1,2,4,128,128]{5,4,3,2,1,0:T(8,128)(2,1)}, u32[]{:S(2)}) copy-start(bf16[1,1,2,4,128,128]{5,4,3,2,1,0:T(8,128)(2,1)} %param.13) | copy-start | bytes 786436
  0.6 1.0 %copy-start.1 = (bf16[256,256]{1,0:T(8,128)(2,1)S(1)}, bf16[256,256]{1,0:T(8,128)(2,1)}, u32[]{:S(2)}) copy-start(bf16[256,256]{1,0:T(8,128)(2,1)} %param.8) | copy-start | bytes 393220
  1.7 10.2 %collective-permute-start.1 = (bf16[256,512]{1,0:T(8,128)(2,1)S(1)}, bf16[256,512]{1,0:T(8,128)(2,1)S(1)}, u32[]{:S(2)}, u32[]{:S(2)}) collective-permute-start(bf16[256,512]{1,0:T(8,128)(2,1)S(1)} %constant_dynamic-update-slice_fusion), channel_id=1, source_target_pairs={{4,0},{12,1},{20,2},{28,3},{0,4},{8,5},{16,6},{24,7},{5,8},{13,9},... | collective-permute-start | bytes 786440 | tf_op jit(solution)/shard_map/ppermute | solution.py:50
  4.7 7.2 %collective-permute-start = (bf16[256,512]{1,0:T(8,128)(2,1)S(1)}, bf16[256,512]{1,0:T(8,128)(2,1)S(1)}, u32[]{:S(2)}, u32[]{:S(2)}) collective-permute-start(bf16[256,512]{1,0:T(8,128)(2,1)S(1)} %constant_dynamic-update-slice_fusion), channel_id=1, source_target_pairs={{0,0},{8,1},{16,2},{24,3},{4,4},{12,5},{20,6},{28,7},{1,8},{9,9},{... | collective-permute-start | bytes 786440 | tf_op jit(solution)/shard_map/ppermute | solution.py:50
  5.4 0.7 copy-start.3
  5.4 0.7 copy-start.4
  13.0 5.6 %collective-permute-start.2 = (f32[2,64,512]{2,1,0:T(8,128)S(1)}, f32[2,64,512]{2,1,0:T(8,128)S(1)}, u32[]{:S(2)}, u32[]{:S(2)}) collective-permute-start(f32[2,64,512]{2,1,0:T(8,128)S(1)} %dynamic-slice_bitcast_fusion), channel_id=1, source_target_pairs={{0,1},{1,0},{2,3},{3,2},{4,5},{5,4},{6,7},{7,6},{8,9},{9,8},{10,11... | collective-permute-start | bytes 786440 | tf_op jit(solution)/shard_map/ppermute | solution.py:27
  18.7 21.0 %collective-permute-start.3 = (f32[64,512]{1,0:T(8,128)S(1)}, f32[64,512]{1,0:T(8,128)S(1)}, u32[]{:S(2)}, u32[]{:S(2)}) collective-permute-start(f32[64,512]{1,0:T(8,128)S(1)} %dynamic-slice_bitcast_fusion.1), channel_id=1, source_target_pairs={{0,2},{1,3},{2,0},{3,1},{4,6},{5,7},{6,4},{7,5},{8,10},{9,11},{10,... | collective-permute-start | bytes 393224 | tf_op jit(solution)/shard_map/ppermute | solution.py:27
  35.9 3.8 %copy-start.5 = (bf16[256,256]{1,0:T(8,128)(2,1)S(1)}, bf16[256,256]{1,0:T(8,128)(2,1)}, u32[]{:S(2)}) copy-start(bf16[256,256]{1,0:T(8,128)(2,1)} %param.9) | copy-start | bytes 393220
  39.9 0.9 copy-start.2
  41.4 9.2 %collective-permute-start.4 = (f32[320,256]{1,0:T(8,128)S(1)}, f32[320,256]{1,0:T(8,128)S(1)}, u32[]{:S(2)}, u32[]{:S(2)}) collective-permute-start(f32[320,256]{1,0:T(8,128)S(1)} %pad_maximum_fusion.1), channel_id=1, source_target_pairs={{0,2},{1,3},{2,0},{3,1},{4,6},{5,7},{6,4},{7,5},{8,10},{9,11},{10,... | collective-permute-start | bytes 983048 | tf_op jit(solution)/shard_map/ppermute | solution.py:97
  50.8 1.6 %collective-permute-start.5 = (f32[256,256]{1,0:T(8,128)S(1)}, f32[256,256]{1,0:T(8,128)S(1)}, u32[]{:S(2)}, u32[]{:S(2)}) collective-permute-start(f32[256,256]{1,0:T(8,128)S(1)} %pad_maximum_fusion.2), channel_id=1, source_target_pairs={{0,1},{1,0},{2,3},{3,2},{4,5},{5,4},{6,7},{7,6},{8,9},{9,8},{10,11... | collective-permute-start | bytes 786440 | tf_op jit(solution)/shard_map/ppermute | solution.py:97
  52.5 4.3 %collective-permute-start.8 = (f32[64,256]{1,0:T(8,128)S(1)}, f32[64,256]{1,0:T(8,128)S(1)}, u32[]{:S(2)}, u32[]{:S(2)}) collective-permute-start(f32[64,256]{1,0:T(8,128)S(1)} %pad_maximum_fusion.11), channel_id=1, source_target_pairs={{0,4},{1,5},{2,6},{3,7},{4,0},{5,1},{6,2},{7,3},{8,12},{9,13},{10,... | collective-permute-start | bytes 196616 | tf_op jit(solution)/shard_map/ppermute | solution.py:97
  56.9 4.0 %collective-permute-start.9 = (f32[32,256]{1,0:T(8,128)S(1)}, f32[32,256]{1,0:T(8,128)S(1)}, u32[]{:S(2)}, u32[]{:S(2)}) collective-permute-start(f32[32,256]{1,0:T(8,128)S(1)} %pad_maximum_fusion.15), channel_id=1, source_target_pairs={{0,8},{1,9},{2,10},{3,11},{4,12},{5,13},{6,14},{7,15},{8,0},{9,1},... | collective-permute-start | bytes 98312 | tf_op jit(solution)/shard_map/ppermute | solution.py:97
  60.9 8.3 %collective-permute-start.10 = (f32[16,256]{1,0:T(8,128)S(1)}, f32[16,256]{1,0:T(8,128)S(1)}, u32[]{:S(2)}, u32[]{:S(2)}) collective-permute-start(f32[16,256]{1,0:T(8,128)S(1)} %pad_maximum_fusion.19), channel_id=1, source_target_pairs={{0,16},{1,17},{2,18},{3,19},{4,20},{5,21},{6,22},{7,23},{8,24},{9,... | collective-permute-start | bytes 49160 | tf_op jit(solution)/shard_map/ppermute | solution.py:97
  62.0 7.7 %collective-permute-start.7 = (bf16[256,256]{1,0:T(8,128)(2,1)S(1)}, bf16[256,256]{1,0:T(8,128)(2,1)S(1)}, u32[]{:S(2)}, u32[]{:S(2)}) collective-permute-start(bf16[256,256]{1,0:T(8,128)(2,1)S(1)} %bitcast.93), channel_id=1, source_target_pairs={{4,0},{12,1},{20,2},{28,3},{0,4},{8,5},{16,6},{24,7},{5,8},{13,9},... | collective-permute-start | bytes 393224 | tf_op jit(solution)/shard_map/ppermute | solution.py:50
  62.6 7.2 %collective-permute-start.6 = (bf16[256,256]{1,0:T(8,128)(2,1)S(1)}, bf16[256,256]{1,0:T(8,128)(2,1)S(1)}, u32[]{:S(2)}, u32[]{:S(2)}) collective-permute-start(bf16[256,256]{1,0:T(8,128)(2,1)S(1)} %bitcast.94), channel_id=1, source_target_pairs={{0,0},{8,1},{16,2},{24,3},{4,4},{12,5},{20,6},{28,7},{1,8},{9,9},{... | collective-permute-start | bytes 393224 | tf_op jit(solution)/shard_map/ppermute | solution.py:50
  69.2 7.5 %collective-permute-start.11 = (f32[16,256]{1,0:T(8,128)S(1)}, f32[16,256]{1,0:T(8,128)S(1)}, u32[]{:S(2)}, u32[]{:S(2)}) collective-permute-start(f32[16,256]{1,0:T(8,128)S(1)} %pad_maximum_fusion.20), channel_id=1, source_target_pairs={{0,16},{1,17},{2,18},{3,19},{4,20},{5,21},{6,22},{7,23},{8,24},{9,... | collective-permute-start | bytes 49160 | tf_op jit(solution)/shard_map/ppermute | solution.py:97
  76.7 4.0 %collective-permute-start.12 = (f32[32,256]{1,0:T(8,128)S(1)}, f32[32,256]{1,0:T(8,128)S(1)}, u32[]{:S(2)}, u32[]{:S(2)}) collective-permute-start(f32[32,256]{1,0:T(8,128)S(1)} %pad_maximum_fusion.16), channel_id=1, source_target_pairs={{0,8},{1,9},{2,10},{3,11},{4,12},{5,13},{6,14},{7,15},{8,0},{9,1},... | collective-permute-start | bytes 98312 | tf_op jit(solution)/shard_map/ppermute | solution.py:97
  80.7 4.3 %collective-permute-start.13 = (f32[64,256]{1,0:T(8,128)S(1)}, f32[64,256]{1,0:T(8,128)S(1)}, u32[]{:S(2)}, u32[]{:S(2)}) collective-permute-start(f32[64,256]{1,0:T(8,128)S(1)} %pad_maximum_fusion.12), channel_id=1, source_target_pairs={{0,4},{1,5},{2,6},{3,7},{4,0},{5,1},{6,2},{7,3},{8,12},{9,13},{10,... | collective-permute-start | bytes 196616 | tf_op jit(solution)/shard_map/ppermute | solution.py:97
  85.1 1.6 %collective-permute-start.14 = (f32[256,256]{1,0:T(8,128)S(1)}, f32[256,256]{1,0:T(8,128)S(1)}, u32[]{:S(2)}, u32[]{:S(2)}) collective-permute-start(f32[256,256]{1,0:T(8,128)S(1)} %get-tuple-element.11), channel_id=1, source_target_pairs={{0,1},{1,0},{2,3},{3,2},{4,5},{5,4},{6,7},{7,6},{8,9},{9,8},{10,11... | collective-permute-start | bytes 786440 | tf_op jit(solution)/shard_map/ppermute | solution.py:97
  86.9 10.2 %collective-permute-start.15 = (f32[320,256]{1,0:T(8,128)S(1)}, f32[320,256]{1,0:T(8,128)S(1)}, u32[]{:S(2)}, u32[]{:S(2)}) collective-permute-start(f32[320,256]{1,0:T(8,128)S(1)} %get-tuple-element.3), channel_id=1, source_target_pairs={{0,2},{1,3},{2,0},{3,1},{4,6},{5,7},{6,4},{7,5},{8,10},{9,11},{10,... | collective-permute-start | bytes 983048 | tf_op jit(solution)/shard_map/ppermute | solution.py:97

commit v6 on v3

--- a/solution.py
+++ b/solution.py
@@ -122,12 +122,19 @@
         precision=lax.Precision.HIGHEST,
         preferred_element_type=jnp.float32,
     )
-    grads = jnp.stack([grad_one, grad_two])
-    total = grads.size
-    levels = len(all_bits)
-    segment = grads.reshape([2] * levels + [total // devices])
-    summed = reduce_scatter_bits(segment, me, all_bits, devices)
-    grads = all_gather_bits(summed, me, all_bits, devices).reshape(grads.shape)
+    grads = jnp.concatenate([grad_one, grad_two], axis=0)
+    grad_rows = grads.shape[0] // copies
+    quarter = reduce_scatter_bits(
+        grads.reshape([2] * rep_levels + [grad_rows, feature_width]), me, rep_bits, devices
+    )
+    if grad_rows % rows == 0:
+        parts = quarter.reshape(rows, grad_rows // rows, feature_width)
+    else:
+        parts = quarter.reshape(rows, -1)
+    mine = lax.all_to_all(parts, "row", 0, 0, tiled=False).sum(axis=0)
+    spread = lax.all_to_all(jnp.broadcast_to(mine, parts.shape), "row", 0, 0, tiled=False)
+    quarter = spread.reshape(grad_rows, feature_width)
+    grads = all_gather_bits(quarter, me, rep_bits, devices).reshape(grads.shape)
 
     hidden_full = gather_rep(hidden)
     pieces_two = gather_rounds(hidden_full, rows, copies)
@@ -135,7 +142,7 @@
         local_product(pieces_two, block_index, block_count, block_values, row_index, copy_index)
     ).astype(jnp.bfloat16)
     logits = jnp.dot(agg_two, weight_two, preferred_element_type=jnp.float32).astype(jnp.bfloat16)
-    return (logits, grads[0], grads[1])
+    return (logits, grads[:feature_width], grads[feature_width:])
 
 
 def solution(mesh):

time: 96.2 us -> 92.3 us (0.959)
  starting transfers between devices: 39 us -> 44.9 us
  waiting for transfers between devices: 42.5 us -> 37.7 us
  local copies, waits for them, and re-layouts: 8.4 us -> 3.77 us
    all_to_all x0 -> x2, waiting for transfers between devices: none -> 14.6 us  [the longest x1 7.35 us: shards(): mine = lax.all_to_all(parts, 'row', 0, 0, tiled=False).sum(axis=0)]
    ppermute x9 -> x6, waiting for transfers between devices: 22.8 us -> 12.1 us  [reduce_scatter_bits(): y = keep + lax.ppermute(send, AXES, bit_pairs(devices, bit))]
    ppermute x7 -> x4, waiting for transfers between devices: 14.1 us -> 5.33 us  [all_gather_bits(): other = lax.ppermute(z, AXES, bit_pairs(devices, bit))]
    all_to_all x0 -> x2, starting transfers between devices: none -> 6.85 us  [the longest x1 3.47 us: shards(): mine = lax.all_to_all(parts, 'row', 0, 0, tiled=False).sum(axis=0)]
    squeeze x2 -> x0, local copies, waits for them, and re-layouts: 1.86 us -> none  [shards(): return (logits, grads[0], grads[1])]
    unnamed x18 -> x13, local copies, waits for them, and re-layouts: 2.81 us -> 1.69 us
    dynamic_slice x5 -> x0, local copies, waits for them, and re-layouts: 1.09 us -> none  [the longest x4 1.05 us: reduce_scatter_bits(): keep = lax.dynamic_index_in_dim(y, mine, axis, keepdims=False)]
    ppermute x9 -> x6, starting transfers between devices: 30.7 us -> 29.8 us  [reduce_scatter_bits(): y = keep + lax.ppermute(send, AXES, bit_pairs(devices, bit))]
  transfers between devices with their start and end apart: 20 -> 16, of which waited for: 12 -> 11; matrix products, arithmetic and copies ran while one was open for 4% -> 3% of each run, Pallas kernels for 0% -> 0%
where the time goes in v6:
time: 92.3 us; the launch traced here: 91.8 us
  starting transfers between devices  44.9 us (49%)
  waiting for transfers between devices  37.7 us (41%)
  local copies, waits for them, and re-layouts  3.77 us (4%)
  matrix products  2.47 us (3%)
  other arithmetic  1.96 us (2%)
  between operations  0.97 us (1%)
    ppermute x6, starting transfers between devices, reduce_scatter_bits(): y = keep + lax.ppermute(send, AXES, bit_pairs(devices, bit))  29.8 us
    ppermute x6, waiting for transfers between devices, reduce_scatter_bits(): y = keep + lax.ppermute(send, AXES, bit_pairs(devices, bit))  12.1 us
    all_to_all x1, waiting for transfers between devices, shards(): mine = lax.all_to_all(parts, 'row', 0, 0, tiled=False).sum(axis=0)  7.35 us
    all_to_all x1, waiting for transfers between devices, shards(): lax.all_to_all(jnp.broadcast_to(mine, parts.shape), 'row', 0, 0, tiled=Fa...  7.27 us
    ppermute x4, waiting for transfers between devices, gather_rounds(): pieces.append(lax.ppermute(x, AXES, pairs))  5.61 us
    ppermute x4, waiting for transfers between devices, all_gather_bits(): other = lax.ppermute(z, AXES, bit_pairs(devices, bit))  5.33 us
    ppermute x4, starting transfers between devices, gather_rounds(): pieces.append(lax.ppermute(x, AXES, pairs))  4.96 us
    all_to_all x1, starting transfers between devices, shards(): mine = lax.all_to_all(parts, 'row', 0, 0, tiled=False).sum(axis=0)  3.47 us
  transfers between devices with their start and end apart: 16, of which 11 were waited for; matrix products, arithmetic and copies ran while one was open for 3% of the time, Pallas kernels for 0%

profile of v6, /device:TPU:0, one launch (start us, length us, event | category | flops | bytes accessed | tf_op | source)
XLA Modules:
  0.0 91.8 jit_solution(10653615717436850619)
XLA Ops:
  0.6 0.0 copy-start
  0.7 1.0 %constant_dynamic-update-slice_fusion.1 = bf16[256,512]{1,0:T(8,128)(2,1)S(1)} fusion(bf16[256,256]{1,0:T(8,128)(2,1)} %param.7), kind=kLoop, calls=%fused_computation.63 | loop fusion | bytes 262144
  1.6 0.0 copy-done.1
  1.7 3.1 %collective-permute-start.1 = (bf16[256,512]{1,0:T(8,128)(2,1)S(1)}, bf16[256,512]{1,0:T(8,128)(2,1)S(1)}, u32[]{:S(2)}, u32[]{:S(2)}) collective-permute-start(bf16[256,512]{1,0:T(8,128)(2,1)S(1)} %constant_dynamic-update-slice_fusion), channel_id=1, source_target_pairs={{4,0},{12,1},{20,2},{28,3},{0,4},{8,5},{16,6},{24,7},{5,8},{13,9},... | collective-permute-start | bytes 786440 | tf_op jit(solution)/shard_map/ppermute | solution.py:46
  4.7 0.7 collective-permute-start
  5.4 0.0 copy-start.3
  5.4 0.0 copy-start.4
  5.4 0.7 copy-done.3
  6.1 0.1 compare_and_fusion
  6.2 0.1 sub.74
  6.3 5.6 %collective-permute-done.1 = bf16[256,512]{1,0:T(8,128)(2,1)S(1)} collective-permute-done((bf16[256,512]{1,0:T(8,128)(2,1)S(1)}, bf16[256,512]{1,0:T(8,128)(2,1)S(1)}, u32[]{:S(2)}, u32[]{:S(2)}) %collective-permute-start.1) | collective-permute-done | bytes 262176 | tf_op jit(solution)/shard_map/ppermute | solution.py:46
  11.9 0.1 pad_maximum_fusion
  11.9 0.6 gather_fusion
  12.6 0.4 fusion.1
  13.0 4.4 %collective-permute-start.2 = (f32[2,64,512]{2,1,0:T(8,128)S(1)}, f32[2,64,512]{2,1,0:T(8,128)S(1)}, u32[]{:S(2)}, u32[]{:S(2)}) collective-permute-start(f32[2,64,512]{2,1,0:T(8,128)S(1)} %dynamic-slice_bitcast_fusion.1), channel_id=1, source_target_pairs={{0,1},{1,0},{2,3},{3,2},{4,5},{5,4},{6,7},{7,6},{8,9},{9,8},{10,11... | collective-permute-start | bytes 786440 | tf_op jit(solution)/shard_map/ppermute | solution.py:23
  17.5 1.2 %collective-permute-done.2 = f32[2,64,512]{2,1,0:T(8,128)S(1)} collective-permute-done((f32[2,64,512]{2,1,0:T(8,128)S(1)}, f32[2,64,512]{2,1,0:T(8,128)S(1)}, u32[]{:S(2)}, u32[]{:S(2)}) %collective-permute-start.2) | collective-permute-done | bytes 262176 | tf_op jit(solution)/shard_map/ppermute | solution.py:23
  18.7 17.2 %collective-permute-start.3 = (f32[64,512]{1,0:T(8,128)S(1)}, f32[64,512]{1,0:T(8,128)S(1)}, u32[]{:S(2)}, u32[]{:S(2)}) collective-permute-start(f32[64,512]{1,0:T(8,128)S(1)} %dynamic-slice_bitcast_fusion.4), channel_id=1, source_target_pairs={{0,2},{1,3},{2,0},{3,1},{4,6},{5,7},{6,4},{7,5},{8,10},{9,11},{10,... | collective-permute-start | bytes 393224 | tf_op jit(solution)/shard_map/ppermute | solution.py:23
  35.9 3.8 %collective-permute-done.3 = f32[64,512]{1,0:T(8,128)S(1)} collective-permute-done((f32[64,512]{1,0:T(8,128)S(1)}, f32[64,512]{1,0:T(8,128)S(1)}, u32[]{:S(2)}, u32[]{:S(2)}) %collective-permute-start.3) | collective-permute-done | bytes 131104 | tf_op jit(solution)/shard_map/ppermute | solution.py:23
  39.7 0.2 fusion.23
  39.9 1.8 %collective-permute-start.4 = (bf16[64,256]{1,0:T(8,128)(2,1)S(1)}, bf16[64,256]{1,0:T(8,128)(2,1)S(1)}, u32[]{:S(2)}, u32[]{:S(2)}) collective-permute-start(bf16[64,256]{1,0:T(8,128)(2,1)S(1)} %get-tuple-element.15), channel_id=1, source_target_pairs={{0,2},{1,3},{2,0},{3,1},{4,6},{5,7},{6,4},{7,5},{8,10},{9,11},{10,... | collective-permute-start | bytes 98312 | tf_op jit(solution)/shard_map/ppermute | solution.py:30
  41.7 0.3 fusion.19
  42.1 0.3 fusion
  42.3 0.2 fusion.26
  42.6 1.3 %collective-permute-done.4 = bf16[64,256]{1,0:T(8,128)(2,1)S(1)} collective-permute-done((bf16[64,256]{1,0:T(8,128)(2,1)S(1)}, bf16[64,256]{1,0:T(8,128)(2,1)S(1)}, u32[]{:S(2)}, u32[]{:S(2)}) %collective-permute-start.4) | collective-permute-done | bytes 32800 | tf_op jit(solution)/shard_map/ppermute | solution.py:30
  43.9 0.1 collective-permute-start.5
  44.0 0.5 collective-permute-start.10
  44.6 0.7 collective-permute-done.5
  45.3 0.6 collective-permute-start.7
  45.9 0.7 collective-permute-start.6
  46.6 6.3 %collective-permute-start.11 = (f32[128,256]{1,0:T(8,128)S(1)}, f32[128,256]{1,0:T(8,128)S(1)}, u32[]{:S(2)}, u32[]{:S(2)}) collective-permute-start(f32[128,256]{1,0:T(8,128)S(1)} %dynamic-slice_bitcast_fusion.2), channel_id=1, source_target_pairs={{0,2},{1,3},{2,0},{3,1},{4,6},{5,7},{6,4},{7,5},{8,10},{9,11},{10,... | collective-permute-start | bytes 393224 | tf_op jit(solution)/shard_map/ppermute | solution.py:23
  53.0 0.6 gather_fusion.1
  53.6 6.6 %collective-permute-done.11 = f32[128,256]{1,0:T(8,128)S(1)} collective-permute-done((f32[128,256]{1,0:T(8,128)S(1)}, f32[128,256]{1,0:T(8,128)S(1)}, u32[]{:S(2)}, u32[]{:S(2)}) %collective-permute-start.11) | collective-permute-done | bytes 131104 | tf_op jit(solution)/shard_map/ppermute | solution.py:23
  60.2 0.7 bitcast_add_fusion.2
  60.9 3.5 %all-to-all-start = ((f32[8,16,256]{2,1,0:T(8,128)}), f32[8,16,256]{2,1,0:T(8,128)S(1)}, u32[]{:S(2)}, u32[]{:S(2)}) async-start(f32[8,16,256]{2,1,0:T(8,128)} %bitcast.42), calls=%async_computation | async-start | bytes 262144 | tf_op jit(solution)/shard_map/all_to_all | solution.py:134
  64.3 0.3 fusion.6
  64.7 7.3 %all-to-all-done = f32[8,16,256]{2,1,0:T(8,128)S(1)} async-done(((f32[8,16,256]{2,1,0:T(8,128)}), f32[8,16,256]{2,1,0:T(8,128)S(1)}, u32[]{:S(2)}, u32[]{:S(2)}) %all-to-all-start) | async-done | bytes 131104 | tf_op jit(solution)/shard_map/all_to_all | solution.py:134
  72.0 0.7 broadcast_in_dim.59
  72.7 3.4 %all-to-all-start.1 = ((f32[8,16,256]{2,1,0:T(8,128)}), f32[8,16,256]{2,1,0:T(8,128)S(1)}, u32[]{:S(2)}, u32[]{:S(2)}) async-start(f32[8,16,256]{2,1,0:T(8,128)} %broadcast_in_dim.59), calls=%async_computation.1 | async-start | bytes 262144 | tf_op jit(solution)/shard_map/all_to_all | solution.py:135
  76.1 0.6 collective-permute-start.8
  76.7 7.3 %all-to-all-done.1 = f32[8,16,256]{2,1,0:T(8,128)S(1)} async-done(((f32[8,16,256]{2,1,0:T(8,128)}), f32[8,16,256]{2,1,0:T(8,128)S(1)}, u32[]{:S(2)}, u32[]{:S(2)}) %all-to-all-start.1) | async-done | bytes 131104 | tf_op jit(solution)/shard_map/all_to_all | solution.py:135
  84.0 1.4 %collective-permute-start.12 = (f32[128,256]{1,0:T(8,128)S(1)}, f32[128,256]{1,0:T(8,128)S(1)}, u32[]{:S(2)}, u32[]{:S(2)}) collective-permute-start(f32[128,256]{1,0:T(8,128)S(1)} %bitcast.107), channel_id=1, source_target_pairs={{0,2},{1,3},{2,0},{3,1},{4,6},{5,7},{6,4},{7,5},{8,10},{9,11},{10,... | collective-permute-start | bytes 393224 | tf_op jit(solution)/shard_map/ppermute | solution.py:30
  85.4 0.7 collective-permute-start.9
  86.1 3.2 %collective-permute-done.12 = f32[128,256]{1,0:T(8,128)S(1)} collective-permute-done((f32[128,256]{1,0:T(8,128)S(1)}, f32[128,256]{1,0:T(8,128)S(1)}, u32[]{:S(2)}, u32[]{:S(2)}) %collective-permute-start.12) | collective-permute-done | bytes 131104 | tf_op jit(solution)/shard_map/ppermute | solution.py:30
  89.3 0.1 collective-permute-start.13
  89.4 0.6 collective-permute-done.9
  90.0 0.8 convolution_convert_fusion
  90.8 0.2 collective-permute-done.13
  91.0 0.8 pad_maximum_fusion.2
  (36 shorter events, 0.5 us)
Async XLA Ops:
  0.6 11.9 %copy-start = (bf16[1,1,2,4,128,128]{5,4,3,2,1,0:T(8,128)(2,1)S(1)}, bf16[1,1,2,4,128,128]{5,4,3,2,1,0:T(8,128)(2,1)}, u32[]{:S(2)}) copy-start(bf16[1,1,2,4,128,128]{5,4,3,2,1,0:T(8,128)(2,1)} %param.13) | copy-start | bytes 786436
  0.6 1.0 %copy-start.1 = (bf16[256,256]{1,0:T(8,128)(2,1)S(1)}, bf16[256,256]{1,0:T(8,128)(2,1)}, u32[]{:S(2)}) copy-start(bf16[256,256]{1,0:T(8,128)(2,1)} %param.8) | copy-start | bytes 393220
  1.7 10.2 %collective-permute-start.1 = (bf16[256,512]{1,0:T(8,128)(2,1)S(1)}, bf16[256,512]{1,0:T(8,128)(2,1)S(1)}, u32[]{:S(2)}, u32[]{:S(2)}) collective-permute-start(bf16[256,512]{1,0:T(8,128)(2,1)S(1)} %constant_dynamic-update-slice_fusion), channel_id=1, source_target_pairs={{4,0},{12,1},{20,2},{28,3},{0,4},{8,5},{16,6},{24,7},{5,8},{13,9},... | collective-permute-start | bytes 786440 | tf_op jit(solution)/shard_map/ppermute | solution.py:46
  4.7 7.2 %collective-permute-start = (bf16[256,512]{1,0:T(8,128)(2,1)S(1)}, bf16[256,512]{1,0:T(8,128)(2,1)S(1)}, u32[]{:S(2)}, u32[]{:S(2)}) collective-permute-start(bf16[256,512]{1,0:T(8,128)(2,1)S(1)} %constant_dynamic-update-slice_fusion), channel_id=1, source_target_pairs={{0,0},{8,1},{16,2},{24,3},{4,4},{12,5},{20,6},{28,7},{1,8},{9,9},{... | collective-permute-start | bytes 786440 | tf_op jit(solution)/shard_map/ppermute | solution.py:46
  5.4 0.7 copy-start.3
  5.4 0.7 copy-start.4
  13.0 5.6 %collective-permute-start.2 = (f32[2,64,512]{2,1,0:T(8,128)S(1)}, f32[2,64,512]{2,1,0:T(8,128)S(1)}, u32[]{:S(2)}, u32[]{:S(2)}) collective-permute-start(f32[2,64,512]{2,1,0:T(8,128)S(1)} %dynamic-slice_bitcast_fusion.1), channel_id=1, source_target_pairs={{0,1},{1,0},{2,3},{3,2},{4,5},{5,4},{6,7},{7,6},{8,9},{9,8},{10,11... | collective-permute-start | bytes 786440 | tf_op jit(solution)/shard_map/ppermute | solution.py:23
  18.7 21.0 %collective-permute-start.3 = (f32[64,512]{1,0:T(8,128)S(1)}, f32[64,512]{1,0:T(8,128)S(1)}, u32[]{:S(2)}, u32[]{:S(2)}) collective-permute-start(f32[64,512]{1,0:T(8,128)S(1)} %dynamic-slice_bitcast_fusion.4), channel_id=1, source_target_pairs={{0,2},{1,3},{2,0},{3,1},{4,6},{5,7},{6,4},{7,5},{8,10},{9,11},{10,... | collective-permute-start | bytes 393224 | tf_op jit(solution)/shard_map/ppermute | solution.py:23
  35.9 3.8 %copy-start.5 = (bf16[256,256]{1,0:T(8,128)(2,1)S(1)}, bf16[256,256]{1,0:T(8,128)(2,1)}, u32[]{:S(2)}) copy-start(bf16[256,256]{1,0:T(8,128)(2,1)} %param.9) | copy-start | bytes 393220
  39.9 2.1 %copy-start.2 = (bf16[256,256]{1,0:T(8,128)(2,1)S(1)}, bf16[256,256]{1,0:T(8,128)(2,1)}, u32[]{:S(2)}) copy-start(bf16[256,256]{1,0:T(8,128)(2,1)} %param.10) | copy-start | bytes 393220
  39.9 4.0 %collective-permute-start.4 = (bf16[64,256]{1,0:T(8,128)(2,1)S(1)}, bf16[64,256]{1,0:T(8,128)(2,1)S(1)}, u32[]{:S(2)}, u32[]{:S(2)}) collective-permute-start(bf16[64,256]{1,0:T(8,128)(2,1)S(1)} %get-tuple-element.15), channel_id=1, source_target_pairs={{0,2},{1,3},{2,0},{3,1},{4,6},{5,7},{6,4},{7,5},{8,10},{9,11},{10,... | collective-permute-start | bytes 98312 | tf_op jit(solution)/shard_map/ppermute | solution.py:30
  43.9 1.3 %collective-permute-start.5 = (bf16[2,64,256]{2,1,0:T(8,128)(2,1)S(1)}, bf16[2,64,256]{2,1,0:T(8,128)(2,1)S(1)}, u32[]{:S(2)}, u32[]{:S(2)}) collective-permute-start(bf16[2,64,256]{2,1,0:T(8,128)(2,1)S(1)} %pad_maximum_fusion.6), channel_id=1, source_target_pairs={{0,1},{1,0},{2,3},{3,2},{4,5},{5,4},{6,7},{7,6},{8,9},{9,8},{10,11... | collective-permute-start | bytes 196616 | tf_op jit(solution)/shard_map/ppermute | solution.py:30
  44.0 2.5 %collective-permute-start.10 = (f32[2,128,256]{2,1,0:T(8,128)S(1)}, f32[2,128,256]{2,1,0:T(8,128)S(1)}, u32[]{:S(2)}, u32[]{:S(2)}) collective-permute-start(f32[2,128,256]{2,1,0:T(8,128)S(1)} %dynamic-slice_bitcast_fusion), channel_id=1, source_target_pairs={{0,1},{1,0},{2,3},{3,2},{4,5},{5,4},{6,7},{7,6},{8,9},{9,8},{10,11... | collective-permute-start | bytes 786440 | tf_op jit(solution)/shard_map/ppermute | solution.py:23
  45.3 7.6 %collective-permute-start.7 = (bf16[256,256]{1,0:T(8,128)(2,1)S(1)}, bf16[256,256]{1,0:T(8,128)(2,1)S(1)}, u32[]{:S(2)}, u32[]{:S(2)}) collective-permute-start(bf16[256,256]{1,0:T(8,128)(2,1)S(1)} %bitcast.117), channel_id=1, source_target_pairs={{4,0},{12,1},{20,2},{28,3},{0,4},{8,5},{16,6},{24,7},{5,8},{13,9},... | collective-permute-start | bytes 393224 | tf_op jit(solution)/shard_map/ppermute | solution.py:46
  45.9 7.1 %collective-permute-start.6 = (bf16[256,256]{1,0:T(8,128)(2,1)S(1)}, bf16[256,256]{1,0:T(8,128)(2,1)S(1)}, u32[]{:S(2)}, u32[]{:S(2)}) collective-permute-start(bf16[256,256]{1,0:T(8,128)(2,1)S(1)} %bitcast.118), channel_id=1, source_target_pairs={{0,0},{8,1},{16,2},{24,3},{4,4},{12,5},{20,6},{28,7},{1,8},{9,9},{... | collective-permute-start | bytes 393224 | tf_op jit(solution)/shard_map/ppermute | solution.py:46
  46.6 13.5 %collective-permute-start.11 = (f32[128,256]{1,0:T(8,128)S(1)}, f32[128,256]{1,0:T(8,128)S(1)}, u32[]{:S(2)}, u32[]{:S(2)}) collective-permute-start(f32[128,256]{1,0:T(8,128)S(1)} %dynamic-slice_bitcast_fusion.2), channel_id=1, source_target_pairs={{0,2},{1,3},{2,0},{3,1},{4,6},{5,7},{6,4},{7,5},{8,10},{9,11},{10,... | collective-permute-start | bytes 393224 | tf_op jit(solution)/shard_map/ppermute | solution.py:23
  60.9 11.1 %all-to-all-start = ((f32[8,16,256]{2,1,0:T(8,128)}), f32[8,16,256]{2,1,0:T(8,128)S(1)}, u32[]{:S(2)}, u32[]{:S(2)}) async-start(f32[8,16,256]{2,1,0:T(8,128)} %bitcast.42), calls=%async_computation | async-start | bytes 262144 | tf_op jit(solution)/shard_map/all_to_all | solution.py:134
  72.7 11.3 %all-to-all-start.1 = ((f32[8,16,256]{2,1,0:T(8,128)}), f32[8,16,256]{2,1,0:T(8,128)S(1)}, u32[]{:S(2)}, u32[]{:S(2)}) async-start(f32[8,16,256]{2,1,0:T(8,128)} %broadcast_in_dim.59), calls=%async_computation.1 | async-start | bytes 262144 | tf_op jit(solution)/shard_map/all_to_all | solution.py:135
  76.1 9.3 %collective-permute-start.8 = (f32[2,64,256]{2,1,0:T(8,128)S(1)}, f32[2,64,256]{2,1,0:T(8,128)S(1)}, u32[]{:S(2)}, u32[]{:S(2)}) collective-permute-start(f32[2,64,256]{2,1,0:T(8,128)S(1)} %dynamic-slice_bitcast_fusion.3), channel_id=1, source_target_pairs={{0,1},{1,0},{2,3},{3,2},{4,5},{5,4},{6,7},{7,6},{8,9},{9,8},{10,11... | collective-permute-start | bytes 393224 | tf_op jit(solution)/shard_map/ppermute | solution.py:23
  84.0 5.3 %collective-permute-start.12 = (f32[128,256]{1,0:T(8,128)S(1)}, f32[128,256]{1,0:T(8,128)S(1)}, u32[]{:S(2)}, u32[]{:S(2)}) collective-permute-start(f32[128,256]{1,0:T(8,128)S(1)} %bitcast.107), channel_id=1, source_target_pairs={{0,2},{1,3},{2,0},{3,1},{4,6},{5,7},{6,4},{7,5},{8,10},{9,11},{10,... | collective-permute-start | bytes 393224 | tf_op jit(solution)/shard_map/ppermute | solution.py:30
  85.4 4.6 %collective-permute-start.9 = (f32[64,256]{1,0:T(8,128)S(1)}, f32[64,256]{1,0:T(8,128)S(1)}, u32[]{:S(2)}, u32[]{:S(2)}) collective-permute-start(f32[64,256]{1,0:T(8,128)S(1)} %dynamic-slice_bitcast_fusion.5), channel_id=1, source_target_pairs={{0,2},{1,3},{2,0},{3,1},{4,6},{5,7},{6,4},{7,5},{8,10},{9,11},{10,... | collective-permute-start | bytes 196616 | tf_op jit(solution)/shard_map/ppermute | solution.py:23
  89.3 1.6 %collective-permute-start.13 = (f32[2,128,256]{2,1,0:T(8,128)S(1)}, f32[2,128,256]{2,1,0:T(8,128)S(1)}, u32[]{:S(2)}, u32[]{:S(2)}) collective-permute-start(f32[2,128,256]{2,1,0:T(8,128)S(1)} %pad_maximum_fusion.4), channel_id=1, source_target_pairs={{0,1},{1,0},{2,3},{3,2},{4,5},{5,4},{6,7},{7,6},{8,9},{9,8},{10,11... | collective-permute-start | bytes 786440 | tf_op jit(solution)/shard_map/ppermute | solution.py:30

commit v7 on v6

--- a/solution.py
+++ b/solution.py
@@ -42,7 +42,8 @@
         for r in range(rows):
             for c in range(copies):
                 q = c * sections + (r + t) % sections
-                pairs.append((q * copies + r // sections, r * copies + c))
+                source = (r // sections + t + c) % copies
+                pairs.append((q * copies + source, r * copies + c))
         pieces.append(lax.ppermute(x, AXES, pairs))
     return jnp.stack(pieces)
 

time: 92.3 us -> 78.9 us (0.85)
  starting transfers between devices: 44.9 us -> 36.5 us
  waiting for transfers between devices: 37.7 us -> 32.8 us
    ppermute x6, starting transfers between devices: 29.8 us -> 13.3 us  [reduce_scatter_bits(): y = keep + lax.ppermute(send, AXES, bit_pairs(devices, bit))]
    ppermute x4, starting transfers between devices: 4.96 us -> 11.7 us  [gather_rounds(): pieces.append(lax.ppermute(x, AXES, pairs))]
    ppermute x6, waiting for transfers between devices: 12.1 us -> 8.8 us  [reduce_scatter_bits(): y = keep + lax.ppermute(send, AXES, bit_pairs(devices, bit))]
    all_to_all x1, starting transfers between devices: 3.47 us -> 6.16 us  [shards(): mine = lax.all_to_all(parts, 'row', 0, 0, tiled=False).sum(axis=0)]
    ppermute x4, starting transfers between devices: 3.32 us -> 2.01 us  [all_gather_bits(): other = lax.ppermute(z, AXES, bit_pairs(devices, bit))]
  transfers between devices with their start and end apart: 16 -> 16, of which waited for: 11 -> 11; matrix products, arithmetic and copies ran while one was open for 3% -> 4% of each run, Pallas kernels for 0% -> 0%
where the time goes in v7:
time: 78.9 us; the launch traced here: 78.5 us
  starting transfers between devices  36.5 us (46%)
  waiting for transfers between devices  32.8 us (42%)
  local copies, waits for them, and re-layouts  3.77 us (5%)
  matrix products  2.46 us (3%)
  other arithmetic  1.97 us (2%)
  between operations  0.98 us (1%)
    ppermute x6, starting transfers between devices, reduce_scatter_bits(): y = keep + lax.ppermute(send, AXES, bit_pairs(devices, bit))  13.3 us
    ppermute x4, starting transfers between devices, gather_rounds(): pieces.append(lax.ppermute(x, AXES, pairs))  11.7 us
    ppermute x6, waiting for transfers between devices, reduce_scatter_bits(): y = keep + lax.ppermute(send, AXES, bit_pairs(devices, bit))  8.8 us
    all_to_all x1, waiting for transfers between devices, shards(): lax.all_to_all(jnp.broadcast_to(mine, parts.shape), 'row', 0, 0, tiled=Fa...  7.18 us
    all_to_all x1, waiting for transfers between devices, shards(): mine = lax.all_to_all(parts, 'row', 0, 0, tiled=False).sum(axis=0)  7.02 us
    all_to_all x1, starting transfers between devices, shards(): mine = lax.all_to_all(parts, 'row', 0, 0, tiled=False).sum(axis=0)  6.16 us
    ppermute x4, waiting for transfers between devices, all_gather_bits(): other = lax.ppermute(z, AXES, bit_pairs(devices, bit))  4.98 us
    ppermute x4, waiting for transfers between devices, gather_rounds(): pieces.append(lax.ppermute(x, AXES, pairs))  4.85 us
  transfers between devices with their start and end apart: 16, of which 11 were waited for; matrix products, arithmetic and copies ran while one was open for 4% of the time, Pallas kernels for 0%

profile of v7, /device:TPU:0, one launch (start us, length us, event | category | flops | bytes accessed | tf_op | source)
XLA Modules:
  0.0 78.5 jit_solution(15146293759089623643)
XLA Ops:
  0.6 0.0 copy-start
  0.7 1.0 %constant_dynamic-update-slice_fusion.1 = bf16[256,512]{1,0:T(8,128)(2,1)S(1)} fusion(bf16[256,256]{1,0:T(8,128)(2,1)} %param.7), kind=kLoop, calls=%fused_computation.63 | loop fusion | bytes 262144
  1.6 0.0 copy-done.1
  1.7 6.1 %collective-permute-start.1 = (bf16[256,512]{1,0:T(8,128)(2,1)S(1)}, bf16[256,512]{1,0:T(8,128)(2,1)S(1)}, u32[]{:S(2)}, u32[]{:S(2)}) collective-permute-start(bf16[256,512]{1,0:T(8,128)(2,1)S(1)} %constant_dynamic-update-slice_fusion), channel_id=1, source_target_pairs={{5,0},{14,1},{23,2},{28,3},{1,4},{10,5},{19,6},{24,7},{6,8},{15,9}... | collective-permute-start | bytes 786440 | tf_op jit(solution)/shard_map/ppermute | solution.py:47
  7.8 0.7 collective-permute-start
  8.5 0.0 copy-start.4
  8.5 0.7 copy-done.3
  9.1 0.1 compare_and_fusion
  9.2 0.1 sub.74
  9.3 4.8 %collective-permute-done.1 = bf16[256,512]{1,0:T(8,128)(2,1)S(1)} collective-permute-done((bf16[256,512]{1,0:T(8,128)(2,1)S(1)}, bf16[256,512]{1,0:T(8,128)(2,1)S(1)}, u32[]{:S(2)}, u32[]{:S(2)}) %collective-permute-start.1) | collective-permute-done | bytes 262176 | tf_op jit(solution)/shard_map/ppermute | solution.py:47
  14.2 0.1 pad_maximum_fusion
  14.2 0.6 gather_fusion
  14.9 0.4 fusion.1
  15.3 3.3 %collective-permute-start.2 = (f32[2,64,512]{2,1,0:T(8,128)S(1)}, f32[2,64,512]{2,1,0:T(8,128)S(1)}, u32[]{:S(2)}, u32[]{:S(2)}) collective-permute-start(f32[2,64,512]{2,1,0:T(8,128)S(1)} %dynamic-slice_bitcast_fusion.1), channel_id=1, source_target_pairs={{0,1},{1,0},{2,3},{3,2},{4,5},{5,4},{6,7},{7,6},{8,9},{9,8},{10,11... | collective-permute-start | bytes 786440 | tf_op jit(solution)/shard_map/ppermute | solution.py:23
  18.6 1.2 %collective-permute-done.2 = f32[2,64,512]{2,1,0:T(8,128)S(1)} collective-permute-done((f32[2,64,512]{2,1,0:T(8,128)S(1)}, f32[2,64,512]{2,1,0:T(8,128)S(1)}, u32[]{:S(2)}, u32[]{:S(2)}) %collective-permute-start.2) | collective-permute-done | bytes 262176 | tf_op jit(solution)/shard_map/ppermute | solution.py:23
  19.8 3.9 %collective-permute-start.3 = (f32[64,512]{1,0:T(8,128)S(1)}, f32[64,512]{1,0:T(8,128)S(1)}, u32[]{:S(2)}, u32[]{:S(2)}) collective-permute-start(f32[64,512]{1,0:T(8,128)S(1)} %dynamic-slice_bitcast_fusion.4), channel_id=1, source_target_pairs={{0,2},{1,3},{2,0},{3,1},{4,6},{5,7},{6,4},{7,5},{8,10},{9,11},{10,... | collective-permute-start | bytes 393224 | tf_op jit(solution)/shard_map/ppermute | solution.py:23
  23.7 3.8 %collective-permute-done.3 = f32[64,512]{1,0:T(8,128)S(1)} collective-permute-done((f32[64,512]{1,0:T(8,128)S(1)}, f32[64,512]{1,0:T(8,128)S(1)}, u32[]{:S(2)}, u32[]{:S(2)}) %collective-permute-start.3) | collective-permute-done | bytes 131104 | tf_op jit(solution)/shard_map/ppermute | solution.py:23
  27.5 0.2 fusion.23
  27.7 0.0 copy-start.2
  27.7 1.8 %collective-permute-start.4 = (bf16[64,256]{1,0:T(8,128)(2,1)S(1)}, bf16[64,256]{1,0:T(8,128)(2,1)S(1)}, u32[]{:S(2)}, u32[]{:S(2)}) collective-permute-start(bf16[64,256]{1,0:T(8,128)(2,1)S(1)} %get-tuple-element.15), channel_id=1, source_target_pairs={{0,2},{1,3},{2,0},{3,1},{4,6},{5,7},{6,4},{7,5},{8,10},{9,11},{10,... | collective-permute-start | bytes 98312 | tf_op jit(solution)/shard_map/ppermute | solution.py:30
  29.5 0.3 fusion.19
  29.9 0.3 fusion
  30.1 0.2 fusion.26
  30.4 1.3 %collective-permute-done.4 = bf16[64,256]{1,0:T(8,128)(2,1)S(1)} collective-permute-done((bf16[64,256]{1,0:T(8,128)(2,1)S(1)}, bf16[64,256]{1,0:T(8,128)(2,1)S(1)}, u32[]{:S(2)}, u32[]{:S(2)}) %collective-permute-start.4) | collective-permute-done | bytes 32800 | tf_op jit(solution)/shard_map/ppermute | solution.py:30
  31.7 0.1 collective-permute-start.5
  31.8 0.5 collective-permute-start.10
  32.4 0.7 collective-permute-done.5
  33.1 4.3 %collective-permute-start.7 = (bf16[256,256]{1,0:T(8,128)(2,1)S(1)}, bf16[256,256]{1,0:T(8,128)(2,1)S(1)}, u32[]{:S(2)}, u32[]{:S(2)}) collective-permute-start(bf16[256,256]{1,0:T(8,128)(2,1)S(1)} %bitcast.117), channel_id=1, source_target_pairs={{5,0},{14,1},{23,2},{28,3},{1,4},{10,5},{19,6},{24,7},{6,8},{15,9}... | collective-permute-start | bytes 393224 | tf_op jit(solution)/shard_map/ppermute | solution.py:47
  37.4 0.7 collective-permute-start.6
  38.1 3.5 %collective-permute-start.11 = (f32[128,256]{1,0:T(8,128)S(1)}, f32[128,256]{1,0:T(8,128)S(1)}, u32[]{:S(2)}, u32[]{:S(2)}) collective-permute-start(f32[128,256]{1,0:T(8,128)S(1)} %dynamic-slice_bitcast_fusion.2), channel_id=1, source_target_pairs={{0,2},{1,3},{2,0},{3,1},{4,6},{5,7},{6,4},{7,5},{8,10},{9,11},{10,... | collective-permute-start | bytes 393224 | tf_op jit(solution)/shard_map/ppermute | solution.py:23
  41.6 0.6 gather_fusion.1
  42.2 3.3 %collective-permute-done.11 = f32[128,256]{1,0:T(8,128)S(1)} collective-permute-done((f32[128,256]{1,0:T(8,128)S(1)}, f32[128,256]{1,0:T(8,128)S(1)}, u32[]{:S(2)}, u32[]{:S(2)}) %collective-permute-start.11) | collective-permute-done | bytes 131104 | tf_op jit(solution)/shard_map/ppermute | solution.py:23
  45.5 0.7 bitcast_add_fusion.2
  46.1 6.2 %all-to-all-start = ((f32[8,16,256]{2,1,0:T(8,128)}), f32[8,16,256]{2,1,0:T(8,128)S(1)}, u32[]{:S(2)}, u32[]{:S(2)}) async-start(f32[8,16,256]{2,1,0:T(8,128)} %bitcast.42), calls=%async_computation | async-start | bytes 262144 | tf_op jit(solution)/shard_map/all_to_all | solution.py:135
  52.3 0.3 fusion.6
  52.6 7.0 %all-to-all-done = f32[8,16,256]{2,1,0:T(8,128)S(1)} async-done(((f32[8,16,256]{2,1,0:T(8,128)}), f32[8,16,256]{2,1,0:T(8,128)S(1)}, u32[]{:S(2)}, u32[]{:S(2)}) %all-to-all-start) | async-done | bytes 131104 | tf_op jit(solution)/shard_map/all_to_all | solution.py:135
  59.7 0.7 broadcast_in_dim.59
  60.3 3.4 %all-to-all-start.1 = ((f32[8,16,256]{2,1,0:T(8,128)}), f32[8,16,256]{2,1,0:T(8,128)S(1)}, u32[]{:S(2)}, u32[]{:S(2)}) async-start(f32[8,16,256]{2,1,0:T(8,128)} %broadcast_in_dim.59), calls=%async_computation.1 | async-start | bytes 262144 | tf_op jit(solution)/shard_map/all_to_all | solution.py:136
  63.7 0.1 collective-permute-start.8
  63.8 7.2 %all-to-all-done.1 = f32[8,16,256]{2,1,0:T(8,128)S(1)} async-done(((f32[8,16,256]{2,1,0:T(8,128)}), f32[8,16,256]{2,1,0:T(8,128)S(1)}, u32[]{:S(2)}, u32[]{:S(2)}) %all-to-all-start.1) | async-done | bytes 131104 | tf_op jit(solution)/shard_map/all_to_all | solution.py:136
  71.0 0.1 collective-permute-start.12
  71.1 2.0 %collective-permute-start.9 = (f32[64,256]{1,0:T(8,128)S(1)}, f32[64,256]{1,0:T(8,128)S(1)}, u32[]{:S(2)}, u32[]{:S(2)}) collective-permute-start(f32[64,256]{1,0:T(8,128)S(1)} %dynamic-slice_bitcast_fusion.5), channel_id=1, source_target_pairs={{0,2},{1,3},{2,0},{3,1},{4,6},{5,7},{6,4},{7,5},{8,10},{9,11},{10,... | collective-permute-start | bytes 196616 | tf_op jit(solution)/shard_map/ppermute | solution.py:23
  73.1 2.8 %collective-permute-done.12 = f32[128,256]{1,0:T(8,128)S(1)} collective-permute-done((f32[128,256]{1,0:T(8,128)S(1)}, f32[128,256]{1,0:T(8,128)S(1)}, u32[]{:S(2)}, u32[]{:S(2)}) %collective-permute-start.12) | collective-permute-done | bytes 131104 | tf_op jit(solution)/shard_map/ppermute | solution.py:30
  76.0 0.1 collective-permute-start.13
  76.1 0.6 collective-permute-done.9
  76.7 0.8 convolution_convert_fusion
  77.4 0.2 collective-permute-done.13
  77.7 0.8 %pad_maximum_fusion.2 = (f32[1,2,128,256]{3,2,1,0:T(8,128)}, f32[1,2,128,256]{3,2,1,0:T(8,128)}) fusion(f32[2,1,128,256]{3,2,1,0:T(8,128)S(1)} %get-tuple-element.7, f32[2,1,128,256]{3,2,1,0:T(8,128)S(1)} %get-tuple-element.8), kind=kLoop, calls=%fused_computation.22 | loop fusion | flops 131072 | bytes 1048576 | tf_op jit(solution)/shard_map/stack | solution.py:33
  (36 shorter events, 0.5 us)
Async XLA Ops:
  0.6 14.2 %copy-start = (bf16[1,1,2,4,128,128]{5,4,3,2,1,0:T(8,128)(2,1)S(1)}, bf16[1,1,2,4,128,128]{5,4,3,2,1,0:T(8,128)(2,1)}, u32[]{:S(2)}) copy-start(bf16[1,1,2,4,128,128]{5,4,3,2,1,0:T(8,128)(2,1)} %param.13) | copy-start | bytes 786436
  0.6 1.0 %copy-start.1 = (bf16[256,256]{1,0:T(8,128)(2,1)S(1)}, bf16[256,256]{1,0:T(8,128)(2,1)}, u32[]{:S(2)}) copy-start(bf16[256,256]{1,0:T(8,128)(2,1)} %param.8) | copy-start | bytes 393220
  1.7 12.5 %collective-permute-start.1 = (bf16[256,512]{1,0:T(8,128)(2,1)S(1)}, bf16[256,512]{1,0:T(8,128)(2,1)S(1)}, u32[]{:S(2)}, u32[]{:S(2)}) collective-permute-start(bf16[256,512]{1,0:T(8,128)(2,1)S(1)} %constant_dynamic-update-slice_fusion), channel_id=1, source_target_pairs={{5,0},{14,1},{23,2},{28,3},{1,4},{10,5},{19,6},{24,7},{6,8},{15,9}... | collective-permute-start | bytes 786440 | tf_op jit(solution)/shard_map/ppermute | solution.py:47
  7.8 6.4 %collective-permute-start = (bf16[256,512]{1,0:T(8,128)(2,1)S(1)}, bf16[256,512]{1,0:T(8,128)(2,1)S(1)}, u32[]{:S(2)}, u32[]{:S(2)}) collective-permute-start(bf16[256,512]{1,0:T(8,128)(2,1)S(1)} %constant_dynamic-update-slice_fusion), channel_id=1, source_target_pairs={{0,0},{9,1},{18,2},{27,3},{4,4},{13,5},{22,6},{31,7},{1,8},{10,9},... | collective-permute-start | bytes 786440 | tf_op jit(solution)/shard_map/ppermute | solution.py:47
  8.4 0.7 copy-start.3
  8.5 0.7 copy-start.4
  15.3 4.4 %collective-permute-start.2 = (f32[2,64,512]{2,1,0:T(8,128)S(1)}, f32[2,64,512]{2,1,0:T(8,128)S(1)}, u32[]{:S(2)}, u32[]{:S(2)}) collective-permute-start(f32[2,64,512]{2,1,0:T(8,128)S(1)} %dynamic-slice_bitcast_fusion.1), channel_id=1, source_target_pairs={{0,1},{1,0},{2,3},{3,2},{4,5},{5,4},{6,7},{7,6},{8,9},{9,8},{10,11... | collective-permute-start | bytes 786440 | tf_op jit(solution)/shard_map/ppermute | solution.py:23
  19.8 7.7 %collective-permute-start.3 = (f32[64,512]{1,0:T(8,128)S(1)}, f32[64,512]{1,0:T(8,128)S(1)}, u32[]{:S(2)}, u32[]{:S(2)}) collective-permute-start(f32[64,512]{1,0:T(8,128)S(1)} %dynamic-slice_bitcast_fusion.4), channel_id=1, source_target_pairs={{0,2},{1,3},{2,0},{3,1},{4,6},{5,7},{6,4},{7,5},{8,10},{9,11},{10,... | collective-permute-start | bytes 393224 | tf_op jit(solution)/shard_map/ppermute | solution.py:23
  23.7 3.8 %copy-start.5 = (bf16[256,256]{1,0:T(8,128)(2,1)S(1)}, bf16[256,256]{1,0:T(8,128)(2,1)}, u32[]{:S(2)}) copy-start(bf16[256,256]{1,0:T(8,128)(2,1)} %param.9) | copy-start | bytes 393220
  27.7 2.1 %copy-start.2 = (bf16[256,256]{1,0:T(8,128)(2,1)S(1)}, bf16[256,256]{1,0:T(8,128)(2,1)}, u32[]{:S(2)}) copy-start(bf16[256,256]{1,0:T(8,128)(2,1)} %param.10) | copy-start | bytes 393220
  27.7 4.0 %collective-permute-start.4 = (bf16[64,256]{1,0:T(8,128)(2,1)S(1)}, bf16[64,256]{1,0:T(8,128)(2,1)S(1)}, u32[]{:S(2)}, u32[]{:S(2)}) collective-permute-start(bf16[64,256]{1,0:T(8,128)(2,1)S(1)} %get-tuple-element.15), channel_id=1, source_target_pairs={{0,2},{1,3},{2,0},{3,1},{4,6},{5,7},{6,4},{7,5},{8,10},{9,11},{10,... | collective-permute-start | bytes 98312 | tf_op jit(solution)/shard_map/ppermute | solution.py:30
  31.7 1.3 %collective-permute-start.5 = (bf16[2,64,256]{2,1,0:T(8,128)(2,1)S(1)}, bf16[2,64,256]{2,1,0:T(8,128)(2,1)S(1)}, u32[]{:S(2)}, u32[]{:S(2)}) collective-permute-start(bf16[2,64,256]{2,1,0:T(8,128)(2,1)S(1)} %pad_maximum_fusion.6), channel_id=1, source_target_pairs={{0,1},{1,0},{2,3},{3,2},{4,5},{5,4},{6,7},{7,6},{8,9},{9,8},{10,11... | collective-permute-start | bytes 196616 | tf_op jit(solution)/shard_map/ppermute | solution.py:30
  31.8 6.2 %collective-permute-start.10 = (f32[2,128,256]{2,1,0:T(8,128)S(1)}, f32[2,128,256]{2,1,0:T(8,128)S(1)}, u32[]{:S(2)}, u32[]{:S(2)}) collective-permute-start(f32[2,128,256]{2,1,0:T(8,128)S(1)} %dynamic-slice_bitcast_fusion), channel_id=1, source_target_pairs={{0,1},{1,0},{2,3},{3,2},{4,5},{5,4},{6,7},{7,6},{8,9},{9,8},{10,11... | collective-permute-start | bytes 786440 | tf_op jit(solution)/shard_map/ppermute | solution.py:23
  33.1 8.5 %collective-permute-start.7 = (bf16[256,256]{1,0:T(8,128)(2,1)S(1)}, bf16[256,256]{1,0:T(8,128)(2,1)S(1)}, u32[]{:S(2)}, u32[]{:S(2)}) collective-permute-start(bf16[256,256]{1,0:T(8,128)(2,1)S(1)} %bitcast.117), channel_id=1, source_target_pairs={{5,0},{14,1},{23,2},{28,3},{1,4},{10,5},{19,6},{24,7},{6,8},{15,9}... | collective-permute-start | bytes 393224 | tf_op jit(solution)/shard_map/ppermute | solution.py:47
  37.4 4.2 %collective-permute-start.6 = (bf16[256,256]{1,0:T(8,128)(2,1)S(1)}, bf16[256,256]{1,0:T(8,128)(2,1)S(1)}, u32[]{:S(2)}, u32[]{:S(2)}) collective-permute-start(bf16[256,256]{1,0:T(8,128)(2,1)S(1)} %bitcast.118), channel_id=1, source_target_pairs={{0,0},{9,1},{18,2},{27,3},{4,4},{13,5},{22,6},{31,7},{1,8},{10,9},... | collective-permute-start | bytes 393224 | tf_op jit(solution)/shard_map/ppermute | solution.py:47
  38.1 7.4 %collective-permute-start.11 = (f32[128,256]{1,0:T(8,128)S(1)}, f32[128,256]{1,0:T(8,128)S(1)}, u32[]{:S(2)}, u32[]{:S(2)}) collective-permute-start(f32[128,256]{1,0:T(8,128)S(1)} %dynamic-slice_bitcast_fusion.2), channel_id=1, source_target_pairs={{0,2},{1,3},{2,0},{3,1},{4,6},{5,7},{6,4},{7,5},{8,10},{9,11},{10,... | collective-permute-start | bytes 393224 | tf_op jit(solution)/shard_map/ppermute | solution.py:23
  46.1 13.5 %all-to-all-start = ((f32[8,16,256]{2,1,0:T(8,128)}), f32[8,16,256]{2,1,0:T(8,128)S(1)}, u32[]{:S(2)}, u32[]{:S(2)}) async-start(f32[8,16,256]{2,1,0:T(8,128)} %bitcast.42), calls=%async_computation | async-start | bytes 262144 | tf_op jit(solution)/shard_map/all_to_all | solution.py:135
  60.3 10.7 %all-to-all-start.1 = ((f32[8,16,256]{2,1,0:T(8,128)}), f32[8,16,256]{2,1,0:T(8,128)S(1)}, u32[]{:S(2)}, u32[]{:S(2)}) async-start(f32[8,16,256]{2,1,0:T(8,128)} %broadcast_in_dim.59), calls=%async_computation.1 | async-start | bytes 262144 | tf_op jit(solution)/shard_map/all_to_all | solution.py:136
  63.7 7.3 %collective-permute-start.8 = (f32[2,64,256]{2,1,0:T(8,128)S(1)}, f32[2,64,256]{2,1,0:T(8,128)S(1)}, u32[]{:S(2)}, u32[]{:S(2)}) collective-permute-start(f32[2,64,256]{2,1,0:T(8,128)S(1)} %dynamic-slice_bitcast_fusion.3), channel_id=1, source_target_pairs={{0,1},{1,0},{2,3},{3,2},{4,5},{5,4},{6,7},{7,6},{8,9},{9,8},{10,11... | collective-permute-start | bytes 393224 | tf_op jit(solution)/shard_map/ppermute | solution.py:23
  71.0 5.0 %collective-permute-start.12 = (f32[128,256]{1,0:T(8,128)S(1)}, f32[128,256]{1,0:T(8,128)S(1)}, u32[]{:S(2)}, u32[]{:S(2)}) collective-permute-start(f32[128,256]{1,0:T(8,128)S(1)} %bitcast.107), channel_id=1, source_target_pairs={{0,2},{1,3},{2,0},{3,1},{4,6},{5,7},{6,4},{7,5},{8,10},{9,11},{10,... | collective-permute-start | bytes 393224 | tf_op jit(solution)/shard_map/ppermute | solution.py:30
  71.1 5.6 %collective-permute-start.9 = (f32[64,256]{1,0:T(8,128)S(1)}, f32[64,256]{1,0:T(8,128)S(1)}, u32[]{:S(2)}, u32[]{:S(2)}) collective-permute-start(f32[64,256]{1,0:T(8,128)S(1)} %dynamic-slice_bitcast_fusion.5), channel_id=1, source_target_pairs={{0,2},{1,3},{2,0},{3,1},{4,6},{5,7},{6,4},{7,5},{8,10},{9,11},{10,... | collective-permute-start | bytes 196616 | tf_op jit(solution)/shard_map/ppermute | solution.py:23
  76.0 1.6 %collective-permute-start.13 = (f32[2,128,256]{2,1,0:T(8,128)S(1)}, f32[2,128,256]{2,1,0:T(8,128)S(1)}, u32[]{:S(2)}, u32[]{:S(2)}) collective-permute-start(f32[2,128,256]{2,1,0:T(8,128)S(1)} %pad_maximum_fusion.4), channel_id=1, source_target_pairs={{0,1},{1,0},{2,3},{3,2},{4,5},{5,4},{6,7},{7,6},{8,9},{9,8},{10,11... | collective-permute-start | bytes 786440 | tf_op jit(solution)/shard_map/ppermute | solution.py:30

commit v8 on v7

--- a/solution.py
+++ b/solution.py
@@ -123,11 +123,14 @@
         precision=lax.Precision.HIGHEST,
         preferred_element_type=jnp.float32,
     )
+    hidden_full = gather_rep(hidden)
     grads = jnp.concatenate([grad_one, grad_two], axis=0)
     grad_rows = grads.shape[0] // copies
     quarter = reduce_scatter_bits(
         grads.reshape([2] * rep_levels + [grad_rows, feature_width]), me, rep_bits, devices
     )
+    hidden_full, quarter = lax.optimization_barrier((hidden_full, quarter))
+    pieces_two = gather_rounds(hidden_full, rows, copies)
     if grad_rows % rows == 0:
         parts = quarter.reshape(rows, grad_rows // rows, feature_width)
     else:
@@ -137,8 +140,6 @@
     quarter = spread.reshape(grad_rows, feature_width)
     grads = all_gather_bits(quarter, me, rep_bits, devices).reshape(grads.shape)
 
-    hidden_full = gather_rep(hidden)
-    pieces_two = gather_rounds(hidden_full, rows, copies)
     agg_two = reduce_rep(
         local_product(pieces_two, block_index, block_count, block_values, row_index, copy_index)
     ).astype(jnp.bfloat16)

time: 78.9 us -> 76.8 us (0.973)
  starting transfers between devices: 36.5 us -> 33.6 us
  waiting for transfers between devices: 32.8 us -> 33.6 us
    ppermute x6, starting transfers between devices: 13.3 us -> 8.99 us  [reduce_scatter_bits(): y = keep + lax.ppermute(send, AXES, bit_pairs(devices, bit))]
    ppermute x4, starting transfers between devices: 2.01 us -> 4.05 us  [all_gather_bits(): other = lax.ppermute(z, AXES, bit_pairs(devices, bit))]
    ppermute x6, waiting for transfers between devices: 8.8 us -> 9.83 us  [reduce_scatter_bits(): y = keep + lax.ppermute(send, AXES, bit_pairs(devices, bit))]
where the time goes in v8:
time: 76.8 us; the launch traced here: 76.4 us
  starting transfers between devices  33.6 us (44%)
  waiting for transfers between devices  33.6 us (44%)
  local copies, waits for them, and re-layouts  3.77 us (5%)
  matrix products  2.46 us (3%)
  other arithmetic  1.96 us (3%)
  between operations  0.99 us (1%)
    ppermute x4, starting transfers between devices, gather_rounds(): pieces.append(lax.ppermute(x, AXES, pairs))  11.6 us
    ppermute x6, waiting for transfers between devices, reduce_scatter_bits(): y = keep + lax.ppermute(send, AXES, bit_pairs(devices, bit))  9.83 us
    ppermute x6, starting transfers between devices, reduce_scatter_bits(): y = keep + lax.ppermute(send, AXES, bit_pairs(devices, bit))  8.99 us
    all_to_all x1, waiting for transfers between devices, shards(): lax.all_to_all(jnp.broadcast_to(mine, parts.shape), 'row', 0, 0, tiled=Fa...  7.18 us
    all_to_all x1, waiting for transfers between devices, shards(): mine = lax.all_to_all(parts, 'row', 0, 0, tiled=False).sum(axis=0)  6.38 us
    all_to_all x1, starting transfers between devices, shards(): mine = lax.all_to_all(parts, 'row', 0, 0, tiled=False).sum(axis=0)  5.56 us
    ppermute x4, waiting for transfers between devices, all_gather_bits(): other = lax.ppermute(z, AXES, bit_pairs(devices, bit))  5.42 us
    ppermute x4, waiting for transfers between devices, gather_rounds(): pieces.append(lax.ppermute(x, AXES, pairs))  4.85 us
  transfers between devices with their start and end apart: 16, of which 11 were waited for; matrix products, arithmetic and copies ran while one was open for 4% of the time, Pallas kernels for 0%

profile of v8, /device:TPU:0, one launch (start us, length us, event | category | flops | bytes accessed | tf_op | source)
XLA Modules:
  0.0 76.4 jit_solution(5907418065067420349)
XLA Ops:
  0.6 0.0 copy-start
  0.7 1.0 %constant_dynamic-update-slice_fusion.1 = bf16[256,512]{1,0:T(8,128)(2,1)S(1)} fusion(bf16[256,256]{1,0:T(8,128)(2,1)} %param.7), kind=kLoop, calls=%fused_computation.63 | loop fusion | bytes 262144
  1.6 0.0 copy-done.1
  1.7 6.1 %collective-permute-start.1 = (bf16[256,512]{1,0:T(8,128)(2,1)S(1)}, bf16[256,512]{1,0:T(8,128)(2,1)S(1)}, u32[]{:S(2)}, u32[]{:S(2)}) collective-permute-start(bf16[256,512]{1,0:T(8,128)(2,1)S(1)} %constant_dynamic-update-slice_fusion), channel_id=1, source_target_pairs={{5,0},{14,1},{23,2},{28,3},{1,4},{10,5},{19,6},{24,7},{6,8},{15,9}... | collective-permute-start | bytes 786440 | tf_op jit(solution)/shard_map/ppermute | solution.py:47
  7.8 0.7 collective-permute-start
  8.4 0.0 copy-start.3
  8.5 0.7 copy-done.3
  9.1 0.1 compare_and_fusion
  9.2 0.1 sub.74
  9.3 4.8 %collective-permute-done.1 = bf16[256,512]{1,0:T(8,128)(2,1)S(1)} collective-permute-done((bf16[256,512]{1,0:T(8,128)(2,1)S(1)}, bf16[256,512]{1,0:T(8,128)(2,1)S(1)}, u32[]{:S(2)}, u32[]{:S(2)}) %collective-permute-start.1) | collective-permute-done | bytes 262176 | tf_op jit(solution)/shard_map/ppermute | solution.py:47
  14.2 0.1 pad_maximum_fusion
  14.2 0.6 gather_fusion
  14.9 0.4 fusion.1
  15.3 3.3 %collective-permute-start.2 = (f32[2,64,512]{2,1,0:T(8,128)S(1)}, f32[2,64,512]{2,1,0:T(8,128)S(1)}, u32[]{:S(2)}, u32[]{:S(2)}) collective-permute-start(f32[2,64,512]{2,1,0:T(8,128)S(1)} %dynamic-slice_bitcast_fusion.1), channel_id=1, source_target_pairs={{0,1},{1,0},{2,3},{3,2},{4,5},{5,4},{6,7},{7,6},{8,9},{9,8},{10,11... | collective-permute-start | bytes 786440 | tf_op jit(solution)/shard_map/ppermute | solution.py:23
  18.6 1.2 %collective-permute-done.2 = f32[2,64,512]{2,1,0:T(8,128)S(1)} collective-permute-done((f32[2,64,512]{2,1,0:T(8,128)S(1)}, f32[2,64,512]{2,1,0:T(8,128)S(1)}, u32[]{:S(2)}, u32[]{:S(2)}) %collective-permute-start.2) | collective-permute-done | bytes 262176 | tf_op jit(solution)/shard_map/ppermute | solution.py:23
  19.8 3.9 %collective-permute-start.3 = (f32[64,512]{1,0:T(8,128)S(1)}, f32[64,512]{1,0:T(8,128)S(1)}, u32[]{:S(2)}, u32[]{:S(2)}) collective-permute-start(f32[64,512]{1,0:T(8,128)S(1)} %dynamic-slice_bitcast_fusion.4), channel_id=1, source_target_pairs={{0,2},{1,3},{2,0},{3,1},{4,6},{5,7},{6,4},{7,5},{8,10},{9,11},{10,... | collective-permute-start | bytes 393224 | tf_op jit(solution)/shard_map/ppermute | solution.py:23
  23.7 3.8 %collective-permute-done.3 = f32[64,512]{1,0:T(8,128)S(1)} collective-permute-done((f32[64,512]{1,0:T(8,128)S(1)}, f32[64,512]{1,0:T(8,128)S(1)}, u32[]{:S(2)}, u32[]{:S(2)}) %collective-permute-start.3) | collective-permute-done | bytes 131104 | tf_op jit(solution)/shard_map/ppermute | solution.py:23
  27.5 0.2 fusion.23
  27.7 0.0 copy-start.2
  27.7 1.8 %collective-permute-start.4 = (bf16[64,256]{1,0:T(8,128)(2,1)S(1)}, bf16[64,256]{1,0:T(8,128)(2,1)S(1)}, u32[]{:S(2)}, u32[]{:S(2)}) collective-permute-start(bf16[64,256]{1,0:T(8,128)(2,1)S(1)} %get-tuple-element.19), channel_id=1, source_target_pairs={{0,2},{1,3},{2,0},{3,1},{4,6},{5,7},{6,4},{7,5},{8,10},{9,11},{10,... | collective-permute-start | bytes 98312 | tf_op jit(solution)/shard_map/ppermute | solution.py:30
  29.5 0.3 fusion.19
  29.9 0.3 fusion
  30.1 0.2 fusion.26
  30.4 0.1 collective-permute-start.6
  30.5 1.2 %collective-permute-done.4 = bf16[64,256]{1,0:T(8,128)(2,1)S(1)} collective-permute-done((bf16[64,256]{1,0:T(8,128)(2,1)S(1)}, bf16[64,256]{1,0:T(8,128)(2,1)S(1)}, u32[]{:S(2)}, u32[]{:S(2)}) %collective-permute-start.4) | collective-permute-done | bytes 32800 | tf_op jit(solution)/shard_map/ppermute | solution.py:30
  31.7 0.1 collective-permute-start.5
  31.8 0.2 collective-permute-done.6
  32.1 1.6 %collective-permute-start.7 = (f32[128,256]{1,0:T(8,128)S(1)}, f32[128,256]{1,0:T(8,128)S(1)}, u32[]{:S(2)}, u32[]{:S(2)}) collective-permute-start(f32[128,256]{1,0:T(8,128)S(1)} %dynamic-slice_bitcast_fusion.3), channel_id=1, source_target_pairs={{0,2},{1,3},{2,0},{3,1},{4,6},{5,7},{6,4},{7,5},{8,10},{9,11},{10,... | collective-permute-start | bytes 393224 | tf_op jit(solution)/shard_map/ppermute | solution.py:23
  33.8 4.1 %collective-permute-done.7 = f32[128,256]{1,0:T(8,128)S(1)} collective-permute-done((f32[128,256]{1,0:T(8,128)S(1)}, f32[128,256]{1,0:T(8,128)S(1)}, u32[]{:S(2)}, u32[]{:S(2)}) %collective-permute-start.7) | collective-permute-done | bytes 131104 | tf_op jit(solution)/shard_map/ppermute | solution.py:23
  37.8 0.7 bitcast_add_fusion.3
  38.5 4.2 %collective-permute-start.9 = (bf16[256,256]{1,0:T(8,128)(2,1)S(1)}, bf16[256,256]{1,0:T(8,128)(2,1)S(1)}, u32[]{:S(2)}, u32[]{:S(2)}) collective-permute-start(bf16[256,256]{1,0:T(8,128)(2,1)S(1)} %bitcast.117), channel_id=1, source_target_pairs={{5,0},{14,1},{23,2},{28,3},{1,4},{10,5},{19,6},{24,7},{6,8},{15,9}... | collective-permute-start | bytes 393224 | tf_op jit(solution)/shard_map/ppermute | solution.py:47
  42.7 0.7 collective-permute-start.8
  43.4 5.6 %all-to-all-start = ((f32[8,16,256]{2,1,0:T(8,128)}), f32[8,16,256]{2,1,0:T(8,128)S(1)}, u32[]{:S(2)}, u32[]{:S(2)}) async-start(f32[8,16,256]{2,1,0:T(8,128)} %bitcast.42), calls=%async_computation | async-start | bytes 262144 | tf_op jit(solution)/shard_map/all_to_all | solution.py:138
  49.0 0.6 gather_fusion.1
  49.6 0.3 fusion.6
  49.9 6.4 %all-to-all-done = f32[8,16,256]{2,1,0:T(8,128)S(1)} async-done(((f32[8,16,256]{2,1,0:T(8,128)}), f32[8,16,256]{2,1,0:T(8,128)S(1)}, u32[]{:S(2)}, u32[]{:S(2)}) %all-to-all-start) | async-done | bytes 131104 | tf_op jit(solution)/shard_map/all_to_all | solution.py:138
  56.3 0.7 broadcast_in_dim.59
  57.0 3.4 %all-to-all-start.1 = ((f32[8,16,256]{2,1,0:T(8,128)}), f32[8,16,256]{2,1,0:T(8,128)S(1)}, u32[]{:S(2)}, u32[]{:S(2)}) async-start(f32[8,16,256]{2,1,0:T(8,128)} %broadcast_in_dim.59), calls=%async_computation.1 | async-start | bytes 262144 | tf_op jit(solution)/shard_map/all_to_all | solution.py:139
  60.4 0.1 collective-permute-start.10
  60.4 7.2 %all-to-all-done.1 = f32[8,16,256]{2,1,0:T(8,128)S(1)} async-done(((f32[8,16,256]{2,1,0:T(8,128)}), f32[8,16,256]{2,1,0:T(8,128)S(1)}, u32[]{:S(2)}, u32[]{:S(2)}) %all-to-all-start.1) | async-done | bytes 131104 | tf_op jit(solution)/shard_map/all_to_all | solution.py:139
  67.6 2.1 %collective-permute-start.12 = (f32[128,256]{1,0:T(8,128)S(1)}, f32[128,256]{1,0:T(8,128)S(1)}, u32[]{:S(2)}, u32[]{:S(2)}) collective-permute-start(f32[128,256]{1,0:T(8,128)S(1)} %bitcast.107), channel_id=1, source_target_pairs={{0,2},{1,3},{2,0},{3,1},{4,6},{5,7},{6,4},{7,5},{8,10},{9,11},{10,... | collective-permute-start | bytes 393224 | tf_op jit(solution)/shard_map/ppermute | solution.py:30
  69.8 0.1 collective-permute-start.11
  69.9 4.0 %collective-permute-done.12 = f32[128,256]{1,0:T(8,128)S(1)} collective-permute-done((f32[128,256]{1,0:T(8,128)S(1)}, f32[128,256]{1,0:T(8,128)S(1)}, u32[]{:S(2)}, u32[]{:S(2)}) %collective-permute-start.12) | collective-permute-done | bytes 131104 | tf_op jit(solution)/shard_map/ppermute | solution.py:30
  73.9 0.1 collective-permute-start.13
  74.0 0.6 collective-permute-done.11
  74.6 0.8 %convolution_convert_fusion = bf16[64,256]{1,0:T(8,128)(2,1)} fusion(bf16[256,256]{1,0:T(8,128)(2,1)S(1)} %copy-done.2, f32[64,256]{1,0:T(8,128)S(1)} %collective-permute-done.11, f32[2,64,256]{2,1,0:T(8,128)S(1)} %bitcast_add_fusion.2, s32[]{:T(128)S(6)} %select_n.185), kind=kOutput, calls=%fused_computation.4 | convolution fusion | flops 8437760 | bytes 294916 | tf_op jit(solution)/shard_map/dot_general | solution.py:146
  75.4 0.2 collective-permute-done.13
  75.6 0.8 %pad_maximum_fusion.2 = (f32[1,2,128,256]{3,2,1,0:T(8,128)}, f32[1,2,128,256]{3,2,1,0:T(8,128)}) fusion(f32[2,1,128,256]{3,2,1,0:T(8,128)S(1)} %get-tuple-element.11, f32[2,1,128,256]{3,2,1,0:T(8,128)S(1)} %get-tuple-element.12), kind=kLoop, calls=%fused_computation.22 | loop fusion | flops 131072 | bytes 1048576 | tf_op jit(solution)/shard_map/stack | solution.py:33
  (36 shorter events, 0.5 us)
Async XLA Ops:
  0.6 14.2 %copy-start = (bf16[1,1,2,4,128,128]{5,4,3,2,1,0:T(8,128)(2,1)S(1)}, bf16[1,1,2,4,128,128]{5,4,3,2,1,0:T(8,128)(2,1)}, u32[]{:S(2)}) copy-start(bf16[1,1,2,4,128,128]{5,4,3,2,1,0:T(8,128)(2,1)} %param.13) | copy-start | bytes 786436
  0.6 1.0 %copy-start.1 = (bf16[256,256]{1,0:T(8,128)(2,1)S(1)}, bf16[256,256]{1,0:T(8,128)(2,1)}, u32[]{:S(2)}) copy-start(bf16[256,256]{1,0:T(8,128)(2,1)} %param.8) | copy-start | bytes 393220
  1.7 12.5 %collective-permute-start.1 = (bf16[256,512]{1,0:T(8,128)(2,1)S(1)}, bf16[256,512]{1,0:T(8,128)(2,1)S(1)}, u32[]{:S(2)}, u32[]{:S(2)}) collective-permute-start(bf16[256,512]{1,0:T(8,128)(2,1)S(1)} %constant_dynamic-update-slice_fusion), channel_id=1, source_target_pairs={{5,0},{14,1},{23,2},{28,3},{1,4},{10,5},{19,6},{24,7},{6,8},{15,9}... | collective-permute-start | bytes 786440 | tf_op jit(solution)/shard_map/ppermute | solution.py:47
  7.8 6.4 %collective-permute-start = (bf16[256,512]{1,0:T(8,128)(2,1)S(1)}, bf16[256,512]{1,0:T(8,128)(2,1)S(1)}, u32[]{:S(2)}, u32[]{:S(2)}) collective-permute-start(bf16[256,512]{1,0:T(8,128)(2,1)S(1)} %constant_dynamic-update-slice_fusion), channel_id=1, source_target_pairs={{0,0},{9,1},{18,2},{27,3},{4,4},{13,5},{22,6},{31,7},{1,8},{10,9},... | collective-permute-start | bytes 786440 | tf_op jit(solution)/shard_map/ppermute | solution.py:47
  8.4 0.7 copy-start.3
  8.5 0.7 copy-start.4
  15.3 4.4 %collective-permute-start.2 = (f32[2,64,512]{2,1,0:T(8,128)S(1)}, f32[2,64,512]{2,1,0:T(8,128)S(1)}, u32[]{:S(2)}, u32[]{:S(2)}) collective-permute-start(f32[2,64,512]{2,1,0:T(8,128)S(1)} %dynamic-slice_bitcast_fusion.1), channel_id=1, source_target_pairs={{0,1},{1,0},{2,3},{3,2},{4,5},{5,4},{6,7},{7,6},{8,9},{9,8},{10,11... | collective-permute-start | bytes 786440 | tf_op jit(solution)/shard_map/ppermute | solution.py:23
  19.8 7.7 %collective-permute-start.3 = (f32[64,512]{1,0:T(8,128)S(1)}, f32[64,512]{1,0:T(8,128)S(1)}, u32[]{:S(2)}, u32[]{:S(2)}) collective-permute-start(f32[64,512]{1,0:T(8,128)S(1)} %dynamic-slice_bitcast_fusion.4), channel_id=1, source_target_pairs={{0,2},{1,3},{2,0},{3,1},{4,6},{5,7},{6,4},{7,5},{8,10},{9,11},{10,... | collective-permute-start | bytes 393224 | tf_op jit(solution)/shard_map/ppermute | solution.py:23
  23.7 3.8 %copy-start.5 = (bf16[256,256]{1,0:T(8,128)(2,1)S(1)}, bf16[256,256]{1,0:T(8,128)(2,1)}, u32[]{:S(2)}) copy-start(bf16[256,256]{1,0:T(8,128)(2,1)} %param.9) | copy-start | bytes 393220
  27.7 2.1 %copy-start.2 = (bf16[256,256]{1,0:T(8,128)(2,1)S(1)}, bf16[256,256]{1,0:T(8,128)(2,1)}, u32[]{:S(2)}) copy-start(bf16[256,256]{1,0:T(8,128)(2,1)} %param.10) | copy-start | bytes 393220
  27.7 4.0 %collective-permute-start.4 = (bf16[64,256]{1,0:T(8,128)(2,1)S(1)}, bf16[64,256]{1,0:T(8,128)(2,1)S(1)}, u32[]{:S(2)}, u32[]{:S(2)}) collective-permute-start(bf16[64,256]{1,0:T(8,128)(2,1)S(1)} %get-tuple-element.19), channel_id=1, source_target_pairs={{0,2},{1,3},{2,0},{3,1},{4,6},{5,7},{6,4},{7,5},{8,10},{9,11},{10,... | collective-permute-start | bytes 98312 | tf_op jit(solution)/shard_map/ppermute | solution.py:30
  30.4 1.6 %collective-permute-start.6 = (f32[2,128,256]{2,1,0:T(8,128)S(1)}, f32[2,128,256]{2,1,0:T(8,128)S(1)}, u32[]{:S(2)}, u32[]{:S(2)}) collective-permute-start(f32[2,128,256]{2,1,0:T(8,128)S(1)} %dynamic-slice_bitcast_fusion), channel_id=1, source_target_pairs={{0,1},{1,0},{2,3},{3,2},{4,5},{5,4},{6,7},{7,6},{8,9},{9,8},{10,11... | collective-permute-start | bytes 786440 | tf_op jit(solution)/shard_map/ppermute | solution.py:23
  31.7 2.0 %collective-permute-start.5 = (bf16[2,64,256]{2,1,0:T(8,128)(2,1)S(1)}, bf16[2,64,256]{2,1,0:T(8,128)(2,1)S(1)}, u32[]{:S(2)}, u32[]{:S(2)}) collective-permute-start(bf16[2,64,256]{2,1,0:T(8,128)(2,1)S(1)} %pad_maximum_fusion.6), channel_id=1, source_target_pairs={{0,1},{1,0},{2,3},{3,2},{4,5},{5,4},{6,7},{7,6},{8,9},{9,8},{10,11... | collective-permute-start | bytes 196616 | tf_op jit(solution)/shard_map/ppermute | solution.py:30
  32.1 5.8 %collective-permute-start.7 = (f32[128,256]{1,0:T(8,128)S(1)}, f32[128,256]{1,0:T(8,128)S(1)}, u32[]{:S(2)}, u32[]{:S(2)}) collective-permute-start(f32[128,256]{1,0:T(8,128)S(1)} %dynamic-slice_bitcast_fusion.3), channel_id=1, source_target_pairs={{0,2},{1,3},{2,0},{3,1},{4,6},{5,7},{6,4},{7,5},{8,10},{9,11},{10,... | collective-permute-start | bytes 393224 | tf_op jit(solution)/shard_map/ppermute | solution.py:23
  38.5 10.4 %collective-permute-start.9 = (bf16[256,256]{1,0:T(8,128)(2,1)S(1)}, bf16[256,256]{1,0:T(8,128)(2,1)S(1)}, u32[]{:S(2)}, u32[]{:S(2)}) collective-permute-start(bf16[256,256]{1,0:T(8,128)(2,1)S(1)} %bitcast.117), channel_id=1, source_target_pairs={{5,0},{14,1},{23,2},{28,3},{1,4},{10,5},{19,6},{24,7},{6,8},{15,9}... | collective-permute-start | bytes 393224 | tf_op jit(solution)/shard_map/ppermute | solution.py:47
  42.7 6.2 %collective-permute-start.8 = (bf16[256,256]{1,0:T(8,128)(2,1)S(1)}, bf16[256,256]{1,0:T(8,128)(2,1)S(1)}, u32[]{:S(2)}, u32[]{:S(2)}) collective-permute-start(bf16[256,256]{1,0:T(8,128)(2,1)S(1)} %bitcast.118), channel_id=1, source_target_pairs={{0,0},{9,1},{18,2},{27,3},{4,4},{13,5},{22,6},{31,7},{1,8},{10,9},... | collective-permute-start | bytes 393224 | tf_op jit(solution)/shard_map/ppermute | solution.py:47
  43.4 12.9 %all-to-all-start = ((f32[8,16,256]{2,1,0:T(8,128)}), f32[8,16,256]{2,1,0:T(8,128)S(1)}, u32[]{:S(2)}, u32[]{:S(2)}) async-start(f32[8,16,256]{2,1,0:T(8,128)} %bitcast.42), calls=%async_computation | async-start | bytes 262144 | tf_op jit(solution)/shard_map/all_to_all | solution.py:138
  57.0 10.7 %all-to-all-start.1 = ((f32[8,16,256]{2,1,0:T(8,128)}), f32[8,16,256]{2,1,0:T(8,128)S(1)}, u32[]{:S(2)}, u32[]{:S(2)}) async-start(f32[8,16,256]{2,1,0:T(8,128)} %broadcast_in_dim.59), calls=%async_computation.1 | async-start | bytes 262144 | tf_op jit(solution)/shard_map/all_to_all | solution.py:139
  60.4 9.4 %collective-permute-start.10 = (f32[2,64,256]{2,1,0:T(8,128)S(1)}, f32[2,64,256]{2,1,0:T(8,128)S(1)}, u32[]{:S(2)}, u32[]{:S(2)}) collective-permute-start(f32[2,64,256]{2,1,0:T(8,128)S(1)} %dynamic-slice_bitcast_fusion.2), channel_id=1, source_target_pairs={{0,1},{1,0},{2,3},{3,2},{4,5},{5,4},{6,7},{7,6},{8,9},{9,8},{10,11... | collective-permute-start | bytes 393224 | tf_op jit(solution)/shard_map/ppermute | solution.py:23
  67.6 6.3 %collective-permute-start.12 = (f32[128,256]{1,0:T(8,128)S(1)}, f32[128,256]{1,0:T(8,128)S(1)}, u32[]{:S(2)}, u32[]{:S(2)}) collective-permute-start(f32[128,256]{1,0:T(8,128)S(1)} %bitcast.107), channel_id=1, source_target_pairs={{0,2},{1,3},{2,0},{3,1},{4,6},{5,7},{6,4},{7,5},{8,10},{9,11},{10,... | collective-permute-start | bytes 393224 | tf_op jit(solution)/shard_map/ppermute | solution.py:30
  69.8 4.8 %collective-permute-start.11 = (f32[64,256]{1,0:T(8,128)S(1)}, f32[64,256]{1,0:T(8,128)S(1)}, u32[]{:S(2)}, u32[]{:S(2)}) collective-permute-start(f32[64,256]{1,0:T(8,128)S(1)} %dynamic-slice_bitcast_fusion.5), channel_id=1, source_target_pairs={{0,2},{1,3},{2,0},{3,1},{4,6},{5,7},{6,4},{7,5},{8,10},{9,11},{10,... | collective-permute-start | bytes 196616 | tf_op jit(solution)/shard_map/ppermute | solution.py:23
  73.9 1.6 %collective-permute-start.13 = (f32[2,128,256]{2,1,0:T(8,128)S(1)}, f32[2,128,256]{2,1,0:T(8,128)S(1)}, u32[]{:S(2)}, u32[]{:S(2)}) collective-permute-start(f32[2,128,256]{2,1,0:T(8,128)S(1)} %pad_maximum_fusion.4), channel_id=1, source_target_pairs={{0,1},{1,0},{2,3},{3,2},{4,5},{5,4},{6,7},{7,6},{8,9},{9,8},{10,11... | collective-permute-start | bytes 786440 | tf_op jit(solution)/shard_map/ppermute | solution.py:30

commit v9 on v8

--- a/solution.py
+++ b/solution.py
@@ -12,6 +12,36 @@
 
 def bit_pairs(devices, bit):
     return [(d, d ^ (1 << bit)) for d in range(devices)]
+
+
+def group_pairs(devices, mask):
+    return [(d, d ^ mask) for d in range(devices)]
+
+
+def halve(y, mine):
+    half = y.shape[0] // 2
+    keep = lax.dynamic_slice_in_dim(y, mine * half, half, 0)
+    send = lax.dynamic_slice_in_dim(y, (1 - mine) * half, half, 0)
+    return keep, send
+
+
+def join(z, other, mine, axis, stack):
+    low = jnp.where(mine == 0, z, other)
+    high = jnp.where(mine == 0, other, z)
+    if stack:
+        return jnp.stack([low, high], axis=axis)
+    return jnp.concatenate([low, high], axis=axis)
+
+
+def exchange(pieces, mask, devices, width):
+    flat = [p.reshape(-1, width) for p in pieces]
+    sizes = [f.shape[0] for f in flat]
+    got = lax.ppermute(jnp.concatenate(flat, axis=0), AXES, group_pairs(devices, mask))
+    out, at = [], 0
+    for p, n in zip(pieces, sizes):
+        out.append(got[at : at + n].reshape(p.shape))
+        at += n
+    return out
 
 
 def reduce_scatter_bits(y, me, bits, devices):
@@ -123,26 +153,34 @@
         precision=lax.Precision.HIGHEST,
         preferred_element_type=jnp.float32,
     )
-    hidden_full = gather_rep(hidden)
+    my_bit = [(me >> b) & 1 for b in range(rep_levels)]
     grads = jnp.concatenate([grad_one, grad_two], axis=0)
-    grad_rows = grads.shape[0] // copies
-    quarter = reduce_scatter_bits(
-        grads.reshape([2] * rep_levels + [grad_rows, feature_width]), me, rep_bits, devices
-    )
-    hidden_full, quarter = lax.optimization_barrier((hidden_full, quarter))
+    held = hidden.astype(jnp.float32)
+    for step, bit in enumerate(reversed(rep_bits)):
+        keep, send = halve(grads, my_bit[bit])
+        got = exchange([held, send], 1 << bit, devices, feature_width)
+        held = join(held, got[0], my_bit[bit], step, True)
+        grads = keep + got[1]
+    hidden_full = held.reshape(node_rows, feature_width).astype(jnp.bfloat16)
     pieces_two = gather_rounds(hidden_full, rows, copies)
+    grad_rows = grads.shape[0]
     if grad_rows % rows == 0:
-        parts = quarter.reshape(rows, grad_rows // rows, feature_width)
+        parts = grads.reshape(rows, grad_rows // rows, feature_width)
     else:
-        parts = quarter.reshape(rows, -1)
+        parts = grads.reshape(rows, -1)
     mine = lax.all_to_all(parts, "row", 0, 0, tiled=False).sum(axis=0)
     spread = lax.all_to_all(jnp.broadcast_to(mine, parts.shape), "row", 0, 0, tiled=False)
-    quarter = spread.reshape(grad_rows, feature_width)
-    grads = all_gather_bits(quarter, me, rep_bits, devices).reshape(grads.shape)
-
-    agg_two = reduce_rep(
-        local_product(pieces_two, block_index, block_count, block_values, row_index, copy_index)
-    ).astype(jnp.bfloat16)
+    grads = spread.reshape(grad_rows, feature_width)
+    partial_b = local_product(pieces_two, block_index, block_count, block_values, row_index, copy_index)
+    partial_b = partial_b.reshape([2] * rep_levels + [share_rows, feature_width])
+    for step, bit in enumerate(rep_bits):
+        axis = rep_levels - 1 - step
+        keep = lax.dynamic_index_in_dim(partial_b, my_bit[bit], axis, keepdims=False)
+        send = lax.dynamic_index_in_dim(partial_b, 1 - my_bit[bit], axis, keepdims=False)
+        got = exchange([send, grads], 1 << bit, devices, feature_width)
+        partial_b = keep + got[0]
+        grads = join(grads, got[1], my_bit[bit], 0, False)
+    agg_two = partial_b.astype(jnp.bfloat16)
     logits = jnp.dot(agg_two, weight_two, preferred_element_type=jnp.float32).astype(jnp.bfloat16)
     return (logits, grads[:feature_width], grads[feature_width:])
 

time: 76.8 us -> 83.9 us (1.092)
  waiting for transfers between devices: 33.6 us -> 42 us
  starting transfers between devices: 33.6 us -> 31.5 us
    ppermute x4, waiting for transfers between devices: 5.42 us -> 18.5 us  [exchange(): lax.ppermute(jnp.concatenate(flat, axis=0), AXES, group_pairs(devices, ma...]
    ppermute x6 -> x2, waiting for transfers between devices: 9.83 us -> 4.96 us  [reduce_scatter_bits(): y = keep + lax.ppermute(send, AXES, bit_pairs(devices, bit))]
    ppermute x6 -> x2, starting transfers between devices: 8.99 us -> 7.17 us  [reduce_scatter_bits(): y = keep + lax.ppermute(send, AXES, bit_pairs(devices, bit))]
    another operation x8 -> x5, other arithmetic: 0.96 us -> 0.07 us  [the longest x4 0.05 us: join(): return jnp.stack([low, high], axis=axis)]
    select_n x0 -> x2, other arithmetic: none -> 0.85 us  [the longest x1 0.82 us: join(): high = jnp.where(mine == 0, other, z)]
  transfers between devices with their start and end apart: 16 -> 12, of which waited for: 11 -> 9; matrix products, arithmetic and copies ran while one was open for 4% -> 2% of each run, Pallas kernels for 0% -> 0%
where the time goes in v9:
time: 83.9 us; the launch traced here: 83.5 us
  waiting for transfers between devices  42 us (50%)
  starting transfers between devices  31.5 us (38%)
  local copies, waits for them, and re-layouts  4.45 us (5%)
  matrix products  2.47 us (3%)
  other arithmetic  2.13 us (3%)
  between operations  0.99 us (1%)
    ppermute x4, waiting for transfers between devices, exchange(): lax.ppermute(jnp.concatenate(flat, axis=0), AXES, group_pairs(devices, ma...  18.5 us
    ppermute x4, starting transfers between devices, gather_rounds(): pieces.append(lax.ppermute(x, AXES, pairs))  11.4 us
    ppermute x2, starting transfers between devices, reduce_scatter_bits(): y = keep + lax.ppermute(send, AXES, bit_pairs(devices, bit))  7.17 us
    all_to_all x1, waiting for transfers between devices, shards(): lax.all_to_all(jnp.broadcast_to(mine, parts.shape), 'row', 0, 0, tiled=Fa...  6.93 us
    all_to_all x1, waiting for transfers between devices, shards(): mine = lax.all_to_all(parts, 'row', 0, 0, tiled=False).sum(axis=0)  6.77 us
    all_to_all x1, starting transfers between devices, shards(): mine = lax.all_to_all(parts, 'row', 0, 0, tiled=False).sum(axis=0)  5.54 us
    ppermute x2, waiting for transfers between devices, reduce_scatter_bits(): y = keep + lax.ppermute(send, AXES, bit_pairs(devices, bit))  4.96 us
    ppermute x4, waiting for transfers between devices, gather_rounds(): pieces.append(lax.ppermute(x, AXES, pairs))  4.85 us
  transfers between devices with their start and end apart: 12, of which 9 were waited for; matrix products, arithmetic and copies ran while one was open for 2% of the time, Pallas kernels for 0%

profile of v9, /device:TPU:0, one launch (start us, length us, event | category | flops | bytes accessed | tf_op | source)
XLA Modules:
  0.0 83.5 jit_solution(9608371442953827418)
XLA Ops:
  0.6 0.0 copy-start
  0.7 1.0 %constant_dynamic-update-slice_fusion.1 = bf16[256,512]{1,0:T(8,128)(2,1)S(1)} fusion(bf16[256,256]{1,0:T(8,128)(2,1)} %param.7), kind=kLoop, calls=%fused_computation.70 | loop fusion | bytes 262144
  1.6 0.0 copy-done.1
  1.7 6.1 %collective-permute-start.1 = (bf16[256,512]{1,0:T(8,128)(2,1)S(1)}, bf16[256,512]{1,0:T(8,128)(2,1)S(1)}, u32[]{:S(2)}, u32[]{:S(2)}) collective-permute-start(bf16[256,512]{1,0:T(8,128)(2,1)S(1)} %constant_dynamic-update-slice_fusion), channel_id=1, source_target_pairs={{5,0},{14,1},{23,2},{28,3},{1,4},{10,5},{19,6},{24,7},{6,8},{15,9}... | collective-permute-start | bytes 786440 | tf_op jit(solution)/shard_map/ppermute | solution.py:77
  7.8 0.7 collective-permute-start
  8.4 0.0 copy-start.3
  8.5 0.0 copy-start.4
  8.5 0.7 copy-done.3
  9.1 0.1 compare_and_fusion
  9.2 0.1 sub.74
  9.3 4.8 %collective-permute-done.1 = bf16[256,512]{1,0:T(8,128)(2,1)S(1)} collective-permute-done((bf16[256,512]{1,0:T(8,128)(2,1)S(1)}, bf16[256,512]{1,0:T(8,128)(2,1)S(1)}, u32[]{:S(2)}, u32[]{:S(2)}) %collective-permute-start.1) | collective-permute-done | bytes 262176 | tf_op jit(solution)/shard_map/ppermute | solution.py:77
  14.2 0.0 collective-permute-done
  14.2 0.1 pad_maximum_fusion
  14.2 0.6 gather_fusion
  14.9 0.4 fusion.1
  15.3 3.3 %collective-permute-start.2 = (f32[2,64,512]{2,1,0:T(8,128)S(1)}, f32[2,64,512]{2,1,0:T(8,128)S(1)}, u32[]{:S(2)}, u32[]{:S(2)}) collective-permute-start(f32[2,64,512]{2,1,0:T(8,128)S(1)} %dynamic-slice_bitcast_fusion), channel_id=1, source_target_pairs={{0,1},{1,0},{2,3},{3,2},{4,5},{5,4},{6,7},{7,6},{8,9},{9,8},{10,11... | collective-permute-start | bytes 786440 | tf_op jit(solution)/shard_map/ppermute | solution.py:53
  18.6 1.2 %collective-permute-done.2 = f32[2,64,512]{2,1,0:T(8,128)S(1)} collective-permute-done((f32[2,64,512]{2,1,0:T(8,128)S(1)}, f32[2,64,512]{2,1,0:T(8,128)S(1)}, u32[]{:S(2)}, u32[]{:S(2)}) %collective-permute-start.2) | collective-permute-done | bytes 262176 | tf_op jit(solution)/shard_map/ppermute | solution.py:53
  19.8 3.9 %collective-permute-start.3 = (f32[64,512]{1,0:T(8,128)S(1)}, f32[64,512]{1,0:T(8,128)S(1)}, u32[]{:S(2)}, u32[]{:S(2)}) collective-permute-start(f32[64,512]{1,0:T(8,128)S(1)} %dynamic-slice_bitcast_fusion.1), channel_id=1, source_target_pairs={{0,2},{1,3},{2,0},{3,1},{4,6},{5,7},{6,4},{7,5},{8,10},{9,11},{10,... | collective-permute-start | bytes 393224 | tf_op jit(solution)/shard_map/ppermute | solution.py:53
  23.7 3.8 %collective-permute-done.3 = f32[64,512]{1,0:T(8,128)S(1)} collective-permute-done((f32[64,512]{1,0:T(8,128)S(1)}, f32[64,512]{1,0:T(8,128)S(1)}, u32[]{:S(2)}, u32[]{:S(2)}) %collective-permute-start.3) | collective-permute-done | bytes 131104 | tf_op jit(solution)/shard_map/ppermute | solution.py:53
  27.5 0.0 copy-start.2
  27.5 0.2 fusion.45
  27.7 0.7 copy-done.2
  28.4 0.3 fusion
  28.7 0.2 fusion.32
  28.9 0.3 fusion.21
  29.3 0.1 fusion.15
  29.4 1.8 %collective-permute-start.4 = (f32[320,256]{1,0:T(8,128)S(1)}, f32[320,256]{1,0:T(8,128)S(1)}, u32[]{:S(2)}, u32[]{:S(2)}) collective-permute-start(f32[320,256]{1,0:T(8,128)S(1)} %pad_maximum_fusion.1), channel_id=1, source_target_pairs={{0,2},{1,3},{2,0},{3,1},{4,6},{5,7},{6,4},{7,5},{8,10},{9,11},{10,... | collective-permute-start | bytes 983048 | tf_op jit(solution)/shard_map/ppermute | solution.py:39
  31.2 7.4 %collective-permute-done.4 = f32[320,256]{1,0:T(8,128)S(1)} collective-permute-done((f32[320,256]{1,0:T(8,128)S(1)}, f32[320,256]{1,0:T(8,128)S(1)}, u32[]{:S(2)}, u32[]{:S(2)}) %collective-permute-start.4) | collective-permute-done | bytes 327712 | tf_op jit(solution)/shard_map/ppermute | solution.py:39
  38.6 0.1 fusion.14
  38.8 0.1 collective-permute-start.5
  38.9 1.5 %collective-permute-done.5 = f32[256,256]{1,0:T(8,128)S(1)} collective-permute-done((f32[256,256]{1,0:T(8,128)S(1)}, f32[256,256]{1,0:T(8,128)S(1)}, u32[]{:S(2)}, u32[]{:S(2)}) %collective-permute-start.5) | collective-permute-done | bytes 262176 | tf_op jit(solution)/shard_map/ppermute | solution.py:39
  40.5 4.0 %collective-permute-start.7 = (bf16[256,256]{1,0:T(8,128)(2,1)S(1)}, bf16[256,256]{1,0:T(8,128)(2,1)S(1)}, u32[]{:S(2)}, u32[]{:S(2)}) collective-permute-start(bf16[256,256]{1,0:T(8,128)(2,1)S(1)} %bitcast.96), channel_id=1, source_target_pairs={{5,0},{14,1},{23,2},{28,3},{1,4},{10,5},{19,6},{24,7},{6,8},{15,9}... | collective-permute-start | bytes 393224 | tf_op jit(solution)/shard_map/ppermute | solution.py:77
  44.4 0.7 collective-permute-start.6
  45.1 0.7 slice_add_fusion
  45.8 5.5 %all-to-all-start = ((f32[8,16,256]{2,1,0:T(8,128)}), f32[8,16,256]{2,1,0:T(8,128)S(1)}, u32[]{:S(2)}, u32[]{:S(2)}) async-start(f32[8,16,256]{2,1,0:T(8,128)} %bitcast.37), calls=%async_computation | async-start | bytes 262144 | tf_op jit(solution)/shard_map/all_to_all | solution.py:171
  51.3 0.0 collective-permute-done.7
  51.4 0.6 gather_fusion.1
  52.0 6.8 %all-to-all-done = f32[8,16,256]{2,1,0:T(8,128)S(1)} async-done(((f32[8,16,256]{2,1,0:T(8,128)}), f32[8,16,256]{2,1,0:T(8,128)S(1)}, u32[]{:S(2)}, u32[]{:S(2)}) %all-to-all-start) | async-done | bytes 131104 | tf_op jit(solution)/shard_map/all_to_all | solution.py:171
  58.8 0.7 broadcast_in_dim.59
  59.4 3.4 %all-to-all-start.1 = ((f32[8,16,256]{2,1,0:T(8,128)}), f32[8,16,256]{2,1,0:T(8,128)S(1)}, u32[]{:S(2)}, u32[]{:S(2)}) async-start(f32[8,16,256]{2,1,0:T(8,128)} %broadcast_in_dim.59), calls=%async_computation.1 | async-start | bytes 262144 | tf_op jit(solution)/shard_map/all_to_all | solution.py:172
  62.8 0.3 fusion.6
  63.2 6.9 %all-to-all-done.1 = f32[8,16,256]{2,1,0:T(8,128)S(1)} async-done(((f32[8,16,256]{2,1,0:T(8,128)}), f32[8,16,256]{2,1,0:T(8,128)S(1)}, u32[]{:S(2)}, u32[]{:S(2)}) %all-to-all-start.1) | async-done | bytes 131104 | tf_op jit(solution)/shard_map/all_to_all | solution.py:172
  70.1 0.1 collective-permute-start.8
  70.2 1.5 %collective-permute-done.8 = f32[256,256]{1,0:T(8,128)S(1)} collective-permute-done((f32[256,256]{1,0:T(8,128)S(1)}, f32[256,256]{1,0:T(8,128)S(1)}, u32[]{:S(2)}, u32[]{:S(2)}) %collective-permute-start.8) | collective-permute-done | bytes 262176 | tf_op jit(solution)/shard_map/ppermute | solution.py:39
  71.8 2.0 %collective-permute-start.9 = (f32[320,256]{1,0:T(8,128)S(1)}, f32[320,256]{1,0:T(8,128)S(1)}, u32[]{:S(2)}, u32[]{:S(2)}) collective-permute-start(f32[320,256]{1,0:T(8,128)S(1)} %pad_maximum_fusion.2), channel_id=1, source_target_pairs={{0,2},{1,3},{2,0},{3,1},{4,6},{5,7},{6,4},{7,5},{8,10},{9,11},{10,... | collective-permute-start | bytes 983048 | tf_op jit(solution)/shard_map/ppermute | solution.py:39
  73.9 8.0 %collective-permute-done.9 = f32[320,256]{1,0:T(8,128)S(1)} collective-permute-done((f32[320,256]{1,0:T(8,128)S(1)}, f32[320,256]{1,0:T(8,128)S(1)}, u32[]{:S(2)}, u32[]{:S(2)}) %collective-permute-start.9) | collective-permute-done | bytes 327712 | tf_op jit(solution)/shard_map/ppermute | solution.py:39
  81.9 0.8 convolution_convert_fusion
  82.6 0.8 slice_select_fusion
  (30 shorter events, 0.5 us)
Async XLA Ops:
  0.6 14.2 %copy-start = (bf16[1,1,2,4,128,128]{5,4,3,2,1,0:T(8,128)(2,1)S(1)}, bf16[1,1,2,4,128,128]{5,4,3,2,1,0:T(8,128)(2,1)}, u32[]{:S(2)}) copy-start(bf16[1,1,2,4,128,128]{5,4,3,2,1,0:T(8,128)(2,1)} %param.13) | copy-start | bytes 786436
  0.6 1.0 %copy-start.1 = (bf16[256,256]{1,0:T(8,128)(2,1)S(1)}, bf16[256,256]{1,0:T(8,128)(2,1)}, u32[]{:S(2)}) copy-start(bf16[256,256]{1,0:T(8,128)(2,1)} %param.8) | copy-start | bytes 393220
  1.7 12.5 %collective-permute-start.1 = (bf16[256,512]{1,0:T(8,128)(2,1)S(1)}, bf16[256,512]{1,0:T(8,128)(2,1)S(1)}, u32[]{:S(2)}, u32[]{:S(2)}) collective-permute-start(bf16[256,512]{1,0:T(8,128)(2,1)S(1)} %constant_dynamic-update-slice_fusion), channel_id=1, source_target_pairs={{5,0},{14,1},{23,2},{28,3},{1,4},{10,5},{19,6},{24,7},{6,8},{15,9}... | collective-permute-start | bytes 786440 | tf_op jit(solution)/shard_map/ppermute | solution.py:77
  7.8 6.4 %collective-permute-start = (bf16[256,512]{1,0:T(8,128)(2,1)S(1)}, bf16[256,512]{1,0:T(8,128)(2,1)S(1)}, u32[]{:S(2)}, u32[]{:S(2)}) collective-permute-start(bf16[256,512]{1,0:T(8,128)(2,1)S(1)} %constant_dynamic-update-slice_fusion), channel_id=1, source_target_pairs={{0,0},{9,1},{18,2},{27,3},{4,4},{13,5},{22,6},{31,7},{1,8},{10,9},... | collective-permute-start | bytes 786440 | tf_op jit(solution)/shard_map/ppermute | solution.py:77
  8.4 0.7 copy-start.3
  8.5 0.7 copy-start.4
  15.3 4.4 %collective-permute-start.2 = (f32[2,64,512]{2,1,0:T(8,128)S(1)}, f32[2,64,512]{2,1,0:T(8,128)S(1)}, u32[]{:S(2)}, u32[]{:S(2)}) collective-permute-start(f32[2,64,512]{2,1,0:T(8,128)S(1)} %dynamic-slice_bitcast_fusion), channel_id=1, source_target_pairs={{0,1},{1,0},{2,3},{3,2},{4,5},{5,4},{6,7},{7,6},{8,9},{9,8},{10,11... | collective-permute-start | bytes 786440 | tf_op jit(solution)/shard_map/ppermute | solution.py:53
  19.8 7.7 %collective-permute-start.3 = (f32[64,512]{1,0:T(8,128)S(1)}, f32[64,512]{1,0:T(8,128)S(1)}, u32[]{:S(2)}, u32[]{:S(2)}) collective-permute-start(f32[64,512]{1,0:T(8,128)S(1)} %dynamic-slice_bitcast_fusion.1), channel_id=1, source_target_pairs={{0,2},{1,3},{2,0},{3,1},{4,6},{5,7},{6,4},{7,5},{8,10},{9,11},{10,... | collective-permute-start | bytes 393224 | tf_op jit(solution)/shard_map/ppermute | solution.py:53
  23.7 3.8 %copy-start.5 = (bf16[256,256]{1,0:T(8,128)(2,1)S(1)}, bf16[256,256]{1,0:T(8,128)(2,1)}, u32[]{:S(2)}) copy-start(bf16[256,256]{1,0:T(8,128)(2,1)} %param.9) | copy-start | bytes 393220
  27.5 0.9 %copy-start.2 = (bf16[256,256]{1,0:T(8,128)(2,1)S(1)}, bf16[256,256]{1,0:T(8,128)(2,1)}, u32[]{:S(2)}) copy-start(bf16[256,256]{1,0:T(8,128)(2,1)} %param.10) | copy-start | bytes 393220
  29.4 9.2 %collective-permute-start.4 = (f32[320,256]{1,0:T(8,128)S(1)}, f32[320,256]{1,0:T(8,128)S(1)}, u32[]{:S(2)}, u32[]{:S(2)}) collective-permute-start(f32[320,256]{1,0:T(8,128)S(1)} %pad_maximum_fusion.1), channel_id=1, source_target_pairs={{0,2},{1,3},{2,0},{3,1},{4,6},{5,7},{6,4},{7,5},{8,10},{9,11},{10,... | collective-permute-start | bytes 983048 | tf_op jit(solution)/shard_map/ppermute | solution.py:39
  38.8 1.6 %collective-permute-start.5 = (f32[256,256]{1,0:T(8,128)S(1)}, f32[256,256]{1,0:T(8,128)S(1)}, u32[]{:S(2)}, u32[]{:S(2)}) collective-permute-start(f32[256,256]{1,0:T(8,128)S(1)} %pad_maximum_fusion.3), channel_id=1, source_target_pairs={{0,1},{1,0},{2,3},{3,2},{4,5},{5,4},{6,7},{7,6},{8,9},{9,8},{10,11... | collective-permute-start | bytes 786440 | tf_op jit(solution)/shard_map/ppermute | solution.py:39
  40.5 10.9 %collective-permute-start.7 = (bf16[256,256]{1,0:T(8,128)(2,1)S(1)}, bf16[256,256]{1,0:T(8,128)(2,1)S(1)}, u32[]{:S(2)}, u32[]{:S(2)}) collective-permute-start(bf16[256,256]{1,0:T(8,128)(2,1)S(1)} %bitcast.96), channel_id=1, source_target_pairs={{5,0},{14,1},{23,2},{28,3},{1,4},{10,5},{19,6},{24,7},{6,8},{15,9}... | collective-permute-start | bytes 393224 | tf_op jit(solution)/shard_map/ppermute | solution.py:77
  44.4 6.9 %collective-permute-start.6 = (bf16[256,256]{1,0:T(8,128)(2,1)S(1)}, bf16[256,256]{1,0:T(8,128)(2,1)S(1)}, u32[]{:S(2)}, u32[]{:S(2)}) collective-permute-start(bf16[256,256]{1,0:T(8,128)(2,1)S(1)} %bitcast.97), channel_id=1, source_target_pairs={{0,0},{9,1},{18,2},{27,3},{4,4},{13,5},{22,6},{31,7},{1,8},{10,9},... | collective-permute-start | bytes 393224 | tf_op jit(solution)/shard_map/ppermute | solution.py:77
  45.8 13.0 %all-to-all-start = ((f32[8,16,256]{2,1,0:T(8,128)}), f32[8,16,256]{2,1,0:T(8,128)S(1)}, u32[]{:S(2)}, u32[]{:S(2)}) async-start(f32[8,16,256]{2,1,0:T(8,128)} %bitcast.37), calls=%async_computation | async-start | bytes 262144 | tf_op jit(solution)/shard_map/all_to_all | solution.py:171
  59.4 10.7 %all-to-all-start.1 = ((f32[8,16,256]{2,1,0:T(8,128)}), f32[8,16,256]{2,1,0:T(8,128)S(1)}, u32[]{:S(2)}, u32[]{:S(2)}) async-start(f32[8,16,256]{2,1,0:T(8,128)} %broadcast_in_dim.59), calls=%async_computation.1 | async-start | bytes 262144 | tf_op jit(solution)/shard_map/all_to_all | solution.py:172
  70.1 1.6 %collective-permute-start.8 = (f32[256,256]{1,0:T(8,128)S(1)}, f32[256,256]{1,0:T(8,128)S(1)}, u32[]{:S(2)}, u32[]{:S(2)}) collective-permute-start(f32[256,256]{1,0:T(8,128)S(1)} %pad_maximum_fusion.5), channel_id=1, source_target_pairs={{0,1},{1,0},{2,3},{3,2},{4,5},{5,4},{6,7},{7,6},{8,9},{9,8},{10,11... | collective-permute-start | bytes 786440 | tf_op jit(solution)/shard_map/ppermute | solution.py:39
  71.8 10.1 %collective-permute-start.9 = (f32[320,256]{1,0:T(8,128)S(1)}, f32[320,256]{1,0:T(8,128)S(1)}, u32[]{:S(2)}, u32[]{:S(2)}) collective-permute-start(f32[320,256]{1,0:T(8,128)S(1)} %pad_maximum_fusion.2), channel_id=1, source_target_pairs={{0,2},{1,3},{2,0},{3,1},{4,6},{5,7},{6,4},{7,5},{8,10},{9,11},{10,... | collective-permute-start | bytes 983048 | tf_op jit(solution)/shard_map/ppermute | solution.py:39

commit v10 on v8

--- a/solution.py
+++ b/solution.py
@@ -42,7 +42,7 @@
         for r in range(rows):
             for c in range(copies):
                 q = c * sections + (r + t) % sections
-                source = (r // sections + t + c) % copies
+                source = (2 * c + r // sections + t) % copies
                 pairs.append((q * copies + source, r * copies + c))
         pieces.append(lax.ppermute(x, AXES, pairs))
     return jnp.stack(pieces)
@@ -129,13 +129,13 @@
     quarter = reduce_scatter_bits(
         grads.reshape([2] * rep_levels + [grad_rows, feature_width]), me, rep_bits, devices
     )
-    hidden_full, quarter = lax.optimization_barrier((hidden_full, quarter))
-    pieces_two = gather_rounds(hidden_full, rows, copies)
     if grad_rows % rows == 0:
         parts = quarter.reshape(rows, grad_rows // rows, feature_width)
     else:
         parts = quarter.reshape(rows, -1)
     mine = lax.all_to_all(parts, "row", 0, 0, tiled=False).sum(axis=0)
+    hidden_full, mine = lax.optimization_barrier((hidden_full, mine))
+    pieces_two = gather_rounds(hidden_full, rows, copies)
     spread = lax.all_to_all(jnp.broadcast_to(mine, parts.shape), "row", 0, 0, tiled=False)
     quarter = spread.reshape(grad_rows, feature_width)
     grads = all_gather_bits(quarter, me, rep_bits, devices).reshape(grads.shape)

time: 76.8 us -> 75 us (0.977)
  waiting for transfers between devices: 33.6 us -> 30.8 us
    ppermute x4, starting transfers between devices: 11.6 us -> 8.57 us  [gather_rounds(): pieces.append(lax.ppermute(x, AXES, pairs))]
    all_to_all x1, starting transfers between devices: 3.37 us -> 6.01 us  [shards(): lax.all_to_all(jnp.broadcast_to(mine, parts.shape), 'row', 0, 0, tiled=Fa...]
    ppermute x4, waiting for transfers between devices: 5.42 us -> 3.43 us  [all_gather_bits(): other = lax.ppermute(z, AXES, bit_pairs(devices, bit))]
    ppermute x6, starting transfers between devices: 8.99 us -> 10.2 us  [reduce_scatter_bits(): y = keep + lax.ppermute(send, AXES, bit_pairs(devices, bit))]
    all_to_all x1, waiting for transfers between devices: 7.18 us -> 6.27 us  [shards(): lax.all_to_all(jnp.broadcast_to(mine, parts.shape), 'row', 0, 0, tiled=Fa...]
    all_to_all x1, waiting for transfers between devices: 6.38 us -> 7.27 us  [shards(): mine = lax.all_to_all(parts, 'row', 0, 0, tiled=False).sum(axis=0)]
  transfers between devices with their start and end apart: 16 -> 16, of which waited for: 11 -> 9; matrix products, arithmetic and copies ran while one was open for 4% -> 5% of each run, Pallas kernels for 0% -> 0%
where the time goes in v10:
time: 75 us; the launch traced here: 74.6 us
  starting transfers between devices  34.1 us (45%)
  waiting for transfers between devices  30.8 us (41%)
  local copies, waits for them, and re-layouts  4.34 us (6%)
  matrix products  2.46 us (3%)
  other arithmetic  1.97 us (3%)
  between operations  0.99 us (1%)
    ppermute x6, starting transfers between devices, reduce_scatter_bits(): y = keep + lax.ppermute(send, AXES, bit_pairs(devices, bit))  10.2 us
    ppermute x6, waiting for transfers between devices, reduce_scatter_bits(): y = keep + lax.ppermute(send, AXES, bit_pairs(devices, bit))  9.34 us
    ppermute x4, starting transfers between devices, gather_rounds(): pieces.append(lax.ppermute(x, AXES, pairs))  8.57 us
    all_to_all x1, waiting for transfers between devices, shards(): mine = lax.all_to_all(parts, 'row', 0, 0, tiled=False).sum(axis=0)  7.27 us
    all_to_all x1, waiting for transfers between devices, shards(): lax.all_to_all(jnp.broadcast_to(mine, parts.shape), 'row', 0, 0, tiled=Fa...  6.27 us
    all_to_all x1, starting transfers between devices, shards(): lax.all_to_all(jnp.broadcast_to(mine, parts.shape), 'row', 0, 0, tiled=Fa...  6.01 us
    all_to_all x1, starting transfers between devices, shards(): mine = lax.all_to_all(parts, 'row', 0, 0, tiled=False).sum(axis=0)  5.65 us
    ppermute x4, waiting for transfers between devices, gather_rounds(): pieces.append(lax.ppermute(x, AXES, pairs))  4.44 us
  transfers between devices with their start and end apart: 16, of which 9 were waited for; matrix products, arithmetic and copies ran while one was open for 5% of the time, Pallas kernels for 0%

profile of v10, /device:TPU:0, one launch (start us, length us, event | category | flops | bytes accessed | tf_op | source)
XLA Modules:
  0.0 74.6 jit_solution(13750711676180797367)
XLA Ops:
  0.6 0.0 copy-start
  0.7 1.0 %constant_dynamic-update-slice_fusion.1 = bf16[256,512]{1,0:T(8,128)(2,1)S(1)} fusion(bf16[256,256]{1,0:T(8,128)(2,1)} %param.7), kind=kLoop, calls=%fused_computation.63 | loop fusion | bytes 262144
  1.6 0.0 copy-done.1
  1.7 6.1 %collective-permute-start.1 = (bf16[256,512]{1,0:T(8,128)(2,1)S(1)}, bf16[256,512]{1,0:T(8,128)(2,1)S(1)}, u32[]{:S(2)}, u32[]{:S(2)}) collective-permute-start(bf16[256,512]{1,0:T(8,128)(2,1)S(1)} %constant_dynamic-update-slice_fusion), channel_id=1, source_target_pairs={{5,0},{15,1},{21,2},{31,3},{1,4},{11,5},{17,6},{27,7},{6,8},{12,9}... | collective-permute-start | bytes 786440 | tf_op jit(solution)/shard_map/ppermute | solution.py:47
  7.8 0.7 collective-permute-start
  8.4 0.0 copy-start.3
  8.5 0.0 copy-start.4
  8.5 0.7 copy-done.3
  9.1 0.1 compare_and_fusion
  9.2 0.1 sub.74
  9.3 4.4 %collective-permute-done.1 = bf16[256,512]{1,0:T(8,128)(2,1)S(1)} collective-permute-done((bf16[256,512]{1,0:T(8,128)(2,1)S(1)}, bf16[256,512]{1,0:T(8,128)(2,1)S(1)}, u32[]{:S(2)}, u32[]{:S(2)}) %collective-permute-start.1) | collective-permute-done | bytes 262176 | tf_op jit(solution)/shard_map/ppermute | solution.py:47
  13.8 0.1 pad_maximum_fusion
  13.8 0.6 gather_fusion
  14.4 0.4 fusion.1
  14.9 4.9 %collective-permute-start.2 = (f32[2,64,512]{2,1,0:T(8,128)S(1)}, f32[2,64,512]{2,1,0:T(8,128)S(1)}, u32[]{:S(2)}, u32[]{:S(2)}) collective-permute-start(f32[2,64,512]{2,1,0:T(8,128)S(1)} %dynamic-slice_bitcast_fusion.1), channel_id=1, source_target_pairs={{0,1},{1,0},{2,3},{3,2},{4,5},{5,4},{6,7},{7,6},{8,9},{9,8},{10,11... | collective-permute-start | bytes 786440 | tf_op jit(solution)/shard_map/ppermute | solution.py:23
  19.8 1.2 %collective-permute-done.2 = f32[2,64,512]{2,1,0:T(8,128)S(1)} collective-permute-done((f32[2,64,512]{2,1,0:T(8,128)S(1)}, f32[2,64,512]{2,1,0:T(8,128)S(1)}, u32[]{:S(2)}, u32[]{:S(2)}) %collective-permute-start.2) | collective-permute-done | bytes 262176 | tf_op jit(solution)/shard_map/ppermute | solution.py:23
  21.0 3.3 %collective-permute-start.3 = (f32[64,512]{1,0:T(8,128)S(1)}, f32[64,512]{1,0:T(8,128)S(1)}, u32[]{:S(2)}, u32[]{:S(2)}) collective-permute-start(f32[64,512]{1,0:T(8,128)S(1)} %dynamic-slice_bitcast_fusion.4), channel_id=1, source_target_pairs={{0,2},{1,3},{2,0},{3,1},{4,6},{5,7},{6,4},{7,5},{8,10},{9,11},{10,... | collective-permute-start | bytes 393224 | tf_op jit(solution)/shard_map/ppermute | solution.py:23
  24.3 3.8 %collective-permute-done.3 = f32[64,512]{1,0:T(8,128)S(1)} collective-permute-done((f32[64,512]{1,0:T(8,128)S(1)}, f32[64,512]{1,0:T(8,128)S(1)}, u32[]{:S(2)}, u32[]{:S(2)}) %collective-permute-start.3) | collective-permute-done | bytes 131104 | tf_op jit(solution)/shard_map/ppermute | solution.py:23
  28.1 0.2 fusion.23
  28.3 0.0 copy-start.2
  28.3 0.3 fusion.19
  28.6 0.6 copy-done.2
  29.2 0.3 fusion
  29.5 0.2 fusion.26
  29.7 0.1 collective-permute-start.6
  29.8 1.8 %collective-permute-start.4 = (bf16[64,256]{1,0:T(8,128)(2,1)S(1)}, bf16[64,256]{1,0:T(8,128)(2,1)S(1)}, u32[]{:S(2)}, u32[]{:S(2)}) collective-permute-start(bf16[64,256]{1,0:T(8,128)(2,1)S(1)} %get-tuple-element.19), channel_id=1, source_target_pairs={{0,2},{1,3},{2,0},{3,1},{4,6},{5,7},{6,4},{7,5},{8,10},{9,11},{10,... | collective-permute-start | bytes 98312 | tf_op jit(solution)/shard_map/ppermute | solution.py:30
  31.7 1.5 %collective-permute-start.7 = (f32[128,256]{1,0:T(8,128)S(1)}, f32[128,256]{1,0:T(8,128)S(1)}, u32[]{:S(2)}, u32[]{:S(2)}) collective-permute-start(f32[128,256]{1,0:T(8,128)S(1)} %dynamic-slice_bitcast_fusion.3), channel_id=1, source_target_pairs={{0,2},{1,3},{2,0},{3,1},{4,6},{5,7},{6,4},{7,5},{8,10},{9,11},{10,... | collective-permute-start | bytes 393224 | tf_op jit(solution)/shard_map/ppermute | solution.py:23
  33.2 0.6 collective-permute-done.4
  33.8 0.1 collective-permute-start.5
  33.9 3.4 %collective-permute-done.7 = f32[128,256]{1,0:T(8,128)S(1)} collective-permute-done((f32[128,256]{1,0:T(8,128)S(1)}, f32[128,256]{1,0:T(8,128)S(1)}, u32[]{:S(2)}, u32[]{:S(2)}) %collective-permute-start.7) | collective-permute-done | bytes 131104 | tf_op jit(solution)/shard_map/ppermute | solution.py:23
  37.3 0.7 bitcast_add_fusion.3
  38.0 5.6 %all-to-all-start = ((f32[8,16,256]{2,1,0:T(8,128)}), f32[8,16,256]{2,1,0:T(8,128)S(1)}, u32[]{:S(2)}, u32[]{:S(2)}) async-start(f32[8,16,256]{2,1,0:T(8,128)} %bitcast.28), calls=%async_computation | async-start | bytes 262144 | tf_op jit(solution)/shard_map/all_to_all | solution.py:136
  43.7 7.3 %all-to-all-done = f32[8,16,256]{2,1,0:T(8,128)S(1)} async-done(((f32[8,16,256]{2,1,0:T(8,128)}), f32[8,16,256]{2,1,0:T(8,128)S(1)}, u32[]{:S(2)}, u32[]{:S(2)}) %all-to-all-start) | async-done | bytes 131104 | tf_op jit(solution)/shard_map/all_to_all | solution.py:136
  51.0 1.1 %collective-permute-start.9 = (bf16[256,256]{1,0:T(8,128)(2,1)S(1)}, bf16[256,256]{1,0:T(8,128)(2,1)S(1)}, u32[]{:S(2)}, u32[]{:S(2)}) collective-permute-start(bf16[256,256]{1,0:T(8,128)(2,1)S(1)} %bitcast.117), channel_id=1, source_target_pairs={{5,0},{15,1},{21,2},{31,3},{1,4},{11,5},{17,6},{27,7},{6,8},{12,9}... | collective-permute-start | bytes 393224 | tf_op jit(solution)/shard_map/ppermute | solution.py:47
  52.2 0.7 collective-permute-start.8
  52.8 0.7 broadcast_in_dim.59
  53.5 6.0 %all-to-all-start.1 = ((f32[8,16,256]{2,1,0:T(8,128)}), f32[8,16,256]{2,1,0:T(8,128)S(1)}, u32[]{:S(2)}, u32[]{:S(2)}) async-start(f32[8,16,256]{2,1,0:T(8,128)} %broadcast_in_dim.59), calls=%async_computation.1 | async-start | bytes 262144 | tf_op jit(solution)/shard_map/all_to_all | solution.py:139
  59.5 0.6 gather_fusion.1
  60.1 0.3 fusion.6
  60.5 0.1 collective-permute-start.10
  60.6 6.3 %all-to-all-done.1 = f32[8,16,256]{2,1,0:T(8,128)S(1)} async-done(((f32[8,16,256]{2,1,0:T(8,128)}), f32[8,16,256]{2,1,0:T(8,128)S(1)}, u32[]{:S(2)}, u32[]{:S(2)}) %all-to-all-start.1) | async-done | bytes 131104 | tf_op jit(solution)/shard_map/all_to_all | solution.py:139
  66.8 1.7 %collective-permute-start.12 = (f32[128,256]{1,0:T(8,128)S(1)}, f32[128,256]{1,0:T(8,128)S(1)}, u32[]{:S(2)}, u32[]{:S(2)}) collective-permute-start(f32[128,256]{1,0:T(8,128)S(1)} %bitcast.107), channel_id=1, source_target_pairs={{0,2},{1,3},{2,0},{3,1},{4,6},{5,7},{6,4},{7,5},{8,10},{9,11},{10,... | collective-permute-start | bytes 393224 | tf_op jit(solution)/shard_map/ppermute | solution.py:30
  68.6 0.4 collective-permute-start.11
  69.0 2.8 %collective-permute-done.12 = f32[128,256]{1,0:T(8,128)S(1)} collective-permute-done((f32[128,256]{1,0:T(8,128)S(1)}, f32[128,256]{1,0:T(8,128)S(1)}, u32[]{:S(2)}, u32[]{:S(2)}) %collective-permute-start.12) | collective-permute-done | bytes 131104 | tf_op jit(solution)/shard_map/ppermute | solution.py:30
  71.9 0.1 collective-permute-start.13
  71.9 1.0 %collective-permute-done.11 = f32[64,256]{1,0:T(8,128)S(1)} collective-permute-done((f32[64,256]{1,0:T(8,128)S(1)}, f32[64,256]{1,0:T(8,128)S(1)}, u32[]{:S(2)}, u32[]{:S(2)}) %collective-permute-start.11) | collective-permute-done | bytes 65568 | tf_op jit(solution)/shard_map/ppermute | solution.py:23
  72.9 0.8 %convolution_convert_fusion = bf16[64,256]{1,0:T(8,128)(2,1)} fusion(bf16[256,256]{1,0:T(8,128)(2,1)S(1)} %copy-done.2, f32[64,256]{1,0:T(8,128)S(1)} %collective-permute-done.11, f32[2,64,256]{2,1,0:T(8,128)S(1)} %bitcast_add_fusion.2, s32[]{:T(128)S(6)} %select_n.185), kind=kOutput, calls=%fused_computation.4 | convolution fusion | flops 8437760 | bytes 294916 | tf_op jit(solution)/shard_map/dot_general | solution.py:146
  73.7 0.8 %pad_maximum_fusion.2 = (f32[1,2,128,256]{3,2,1,0:T(8,128)}, f32[1,2,128,256]{3,2,1,0:T(8,128)}) fusion(f32[2,1,128,256]{3,2,1,0:T(8,128)S(1)} %get-tuple-element.11, f32[2,1,128,256]{3,2,1,0:T(8,128)S(1)} %get-tuple-element.12), kind=kLoop, calls=%fused_computation.22 | loop fusion | flops 131072 | bytes 1048576 | tf_op jit(solution)/shard_map/stack | solution.py:33
  (36 shorter events, 0.5 us)
Async XLA Ops:
  0.6 13.8 %copy-start = (bf16[1,1,2,4,128,128]{5,4,3,2,1,0:T(8,128)(2,1)S(1)}, bf16[1,1,2,4,128,128]{5,4,3,2,1,0:T(8,128)(2,1)}, u32[]{:S(2)}) copy-start(bf16[1,1,2,4,128,128]{5,4,3,2,1,0:T(8,128)(2,1)} %param.13) | copy-start | bytes 786436
  0.6 1.0 %copy-start.1 = (bf16[256,256]{1,0:T(8,128)(2,1)S(1)}, bf16[256,256]{1,0:T(8,128)(2,1)}, u32[]{:S(2)}) copy-start(bf16[256,256]{1,0:T(8,128)(2,1)} %param.8) | copy-start | bytes 393220
  1.7 12.1 %collective-permute-start.1 = (bf16[256,512]{1,0:T(8,128)(2,1)S(1)}, bf16[256,512]{1,0:T(8,128)(2,1)S(1)}, u32[]{:S(2)}, u32[]{:S(2)}) collective-permute-start(bf16[256,512]{1,0:T(8,128)(2,1)S(1)} %constant_dynamic-update-slice_fusion), channel_id=1, source_target_pairs={{5,0},{15,1},{21,2},{31,3},{1,4},{11,5},{17,6},{27,7},{6,8},{12,9}... | collective-permute-start | bytes 786440 | tf_op jit(solution)/shard_map/ppermute | solution.py:47
  7.8 6.0 %collective-permute-start = (bf16[256,512]{1,0:T(8,128)(2,1)S(1)}, bf16[256,512]{1,0:T(8,128)(2,1)S(1)}, u32[]{:S(2)}, u32[]{:S(2)}) collective-permute-start(bf16[256,512]{1,0:T(8,128)(2,1)S(1)} %constant_dynamic-update-slice_fusion), channel_id=1, source_target_pairs={{0,0},{10,1},{16,2},{26,3},{4,4},{14,5},{20,6},{30,7},{1,8},{11,9}... | collective-permute-start | bytes 786440 | tf_op jit(solution)/shard_map/ppermute | solution.py:47
  8.4 0.7 copy-start.3
  8.5 0.7 copy-start.4
  14.9 6.0 %collective-permute-start.2 = (f32[2,64,512]{2,1,0:T(8,128)S(1)}, f32[2,64,512]{2,1,0:T(8,128)S(1)}, u32[]{:S(2)}, u32[]{:S(2)}) collective-permute-start(f32[2,64,512]{2,1,0:T(8,128)S(1)} %dynamic-slice_bitcast_fusion.1), channel_id=1, source_target_pairs={{0,1},{1,0},{2,3},{3,2},{4,5},{5,4},{6,7},{7,6},{8,9},{9,8},{10,11... | collective-permute-start | bytes 786440 | tf_op jit(solution)/shard_map/ppermute | solution.py:23
  21.0 7.1 %collective-permute-start.3 = (f32[64,512]{1,0:T(8,128)S(1)}, f32[64,512]{1,0:T(8,128)S(1)}, u32[]{:S(2)}, u32[]{:S(2)}) collective-permute-start(f32[64,512]{1,0:T(8,128)S(1)} %dynamic-slice_bitcast_fusion.4), channel_id=1, source_target_pairs={{0,2},{1,3},{2,0},{3,1},{4,6},{5,7},{6,4},{7,5},{8,10},{9,11},{10,... | collective-permute-start | bytes 393224 | tf_op jit(solution)/shard_map/ppermute | solution.py:23
  24.3 3.8 %copy-start.5 = (bf16[256,256]{1,0:T(8,128)(2,1)S(1)}, bf16[256,256]{1,0:T(8,128)(2,1)}, u32[]{:S(2)}) copy-start(bf16[256,256]{1,0:T(8,128)(2,1)} %param.9) | copy-start | bytes 393220
  28.3 0.9 %copy-start.2 = (bf16[256,256]{1,0:T(8,128)(2,1)S(1)}, bf16[256,256]{1,0:T(8,128)(2,1)}, u32[]{:S(2)}) copy-start(bf16[256,256]{1,0:T(8,128)(2,1)} %param.10) | copy-start | bytes 393220
  29.7 1.9 %collective-permute-start.6 = (f32[2,128,256]{2,1,0:T(8,128)S(1)}, f32[2,128,256]{2,1,0:T(8,128)S(1)}, u32[]{:S(2)}, u32[]{:S(2)}) collective-permute-start(f32[2,128,256]{2,1,0:T(8,128)S(1)} %dynamic-slice_bitcast_fusion), channel_id=1, source_target_pairs={{0,1},{1,0},{2,3},{3,2},{4,5},{5,4},{6,7},{7,6},{8,9},{9,8},{10,11... | collective-permute-start | bytes 786440 | tf_op jit(solution)/shard_map/ppermute | solution.py:23
  29.8 4.0 %collective-permute-start.4 = (bf16[64,256]{1,0:T(8,128)(2,1)S(1)}, bf16[64,256]{1,0:T(8,128)(2,1)S(1)}, u32[]{:S(2)}, u32[]{:S(2)}) collective-permute-start(bf16[64,256]{1,0:T(8,128)(2,1)S(1)} %get-tuple-element.19), channel_id=1, source_target_pairs={{0,2},{1,3},{2,0},{3,1},{4,6},{5,7},{6,4},{7,5},{8,10},{9,11},{10,... | collective-permute-start | bytes 98312 | tf_op jit(solution)/shard_map/ppermute | solution.py:30
  31.7 5.6 %collective-permute-start.7 = (f32[128,256]{1,0:T(8,128)S(1)}, f32[128,256]{1,0:T(8,128)S(1)}, u32[]{:S(2)}, u32[]{:S(2)}) collective-permute-start(f32[128,256]{1,0:T(8,128)S(1)} %dynamic-slice_bitcast_fusion.3), channel_id=1, source_target_pairs={{0,2},{1,3},{2,0},{3,1},{4,6},{5,7},{6,4},{7,5},{8,10},{9,11},{10,... | collective-permute-start | bytes 393224 | tf_op jit(solution)/shard_map/ppermute | solution.py:23
  33.8 9.8 %collective-permute-start.5 = (bf16[2,64,256]{2,1,0:T(8,128)(2,1)S(1)}, bf16[2,64,256]{2,1,0:T(8,128)(2,1)S(1)}, u32[]{:S(2)}, u32[]{:S(2)}) collective-permute-start(bf16[2,64,256]{2,1,0:T(8,128)(2,1)S(1)} %pad_maximum_fusion.6), channel_id=1, source_target_pairs={{0,1},{1,0},{2,3},{3,2},{4,5},{5,4},{6,7},{7,6},{8,9},{9,8},{10,11... | collective-permute-start | bytes 196616 | tf_op jit(solution)/shard_map/ppermute | solution.py:30
  38.0 13.0 %all-to-all-start = ((f32[8,16,256]{2,1,0:T(8,128)}), f32[8,16,256]{2,1,0:T(8,128)S(1)}, u32[]{:S(2)}, u32[]{:S(2)}) async-start(f32[8,16,256]{2,1,0:T(8,128)} %bitcast.28), calls=%async_computation | async-start | bytes 262144 | tf_op jit(solution)/shard_map/all_to_all | solution.py:136
  51.0 8.5 %collective-permute-start.9 = (bf16[256,256]{1,0:T(8,128)(2,1)S(1)}, bf16[256,256]{1,0:T(8,128)(2,1)S(1)}, u32[]{:S(2)}, u32[]{:S(2)}) collective-permute-start(bf16[256,256]{1,0:T(8,128)(2,1)S(1)} %bitcast.117), channel_id=1, source_target_pairs={{5,0},{15,1},{21,2},{31,3},{1,4},{11,5},{17,6},{27,7},{6,8},{12,9}... | collective-permute-start | bytes 393224 | tf_op jit(solution)/shard_map/ppermute | solution.py:47
  52.2 7.4 %collective-permute-start.8 = (bf16[256,256]{1,0:T(8,128)(2,1)S(1)}, bf16[256,256]{1,0:T(8,128)(2,1)S(1)}, u32[]{:S(2)}, u32[]{:S(2)}) collective-permute-start(bf16[256,256]{1,0:T(8,128)(2,1)S(1)} %bitcast.118), channel_id=1, source_target_pairs={{0,0},{10,1},{16,2},{26,3},{4,4},{14,5},{20,6},{30,7},{1,8},{11,9}... | collective-permute-start | bytes 393224 | tf_op jit(solution)/shard_map/ppermute | solution.py:47
  53.5 13.4 %all-to-all-start.1 = ((f32[8,16,256]{2,1,0:T(8,128)}), f32[8,16,256]{2,1,0:T(8,128)S(1)}, u32[]{:S(2)}, u32[]{:S(2)}) async-start(f32[8,16,256]{2,1,0:T(8,128)} %broadcast_in_dim.59), calls=%async_computation.1 | async-start | bytes 262144 | tf_op jit(solution)/shard_map/all_to_all | solution.py:139
  60.5 8.1 %collective-permute-start.10 = (f32[2,64,256]{2,1,0:T(8,128)S(1)}, f32[2,64,256]{2,1,0:T(8,128)S(1)}, u32[]{:S(2)}, u32[]{:S(2)}) collective-permute-start(f32[2,64,256]{2,1,0:T(8,128)S(1)} %dynamic-slice_bitcast_fusion.2), channel_id=1, source_target_pairs={{0,1},{1,0},{2,3},{3,2},{4,5},{5,4},{6,7},{7,6},{8,9},{9,8},{10,11... | collective-permute-start | bytes 393224 | tf_op jit(solution)/shard_map/ppermute | solution.py:23
  66.8 5.0 %collective-permute-start.12 = (f32[128,256]{1,0:T(8,128)S(1)}, f32[128,256]{1,0:T(8,128)S(1)}, u32[]{:S(2)}, u32[]{:S(2)}) collective-permute-start(f32[128,256]{1,0:T(8,128)S(1)} %bitcast.107), channel_id=1, source_target_pairs={{0,2},{1,3},{2,0},{3,1},{4,6},{5,7},{6,4},{7,5},{8,10},{9,11},{10,... | collective-permute-start | bytes 393224 | tf_op jit(solution)/shard_map/ppermute | solution.py:30
  68.6 4.3 %collective-permute-start.11 = (f32[64,256]{1,0:T(8,128)S(1)}, f32[64,256]{1,0:T(8,128)S(1)}, u32[]{:S(2)}, u32[]{:S(2)}) collective-permute-start(f32[64,256]{1,0:T(8,128)S(1)} %dynamic-slice_bitcast_fusion.5), channel_id=1, source_target_pairs={{0,2},{1,3},{2,0},{3,1},{4,6},{5,7},{6,4},{7,5},{8,10},{9,11},{10,... | collective-permute-start | bytes 196616 | tf_op jit(solution)/shard_map/ppermute | solution.py:23
  71.9 1.8 %collective-permute-start.13 = (f32[2,128,256]{2,1,0:T(8,128)S(1)}, f32[2,128,256]{2,1,0:T(8,128)S(1)}, u32[]{:S(2)}, u32[]{:S(2)}) collective-permute-start(f32[2,128,256]{2,1,0:T(8,128)S(1)} %pad_maximum_fusion.4), channel_id=1, source_target_pairs={{0,1},{1,0},{2,3},{3,2},{4,5},{5,4},{6,7},{7,6},{8,9},{9,8},{10,11... | collective-permute-start | bytes 786440 | tf_op jit(solution)/shard_map/ppermute | solution.py:30

commit v11 on v10

--- a/solution.py
+++ b/solution.py
@@ -123,12 +123,13 @@
         precision=lax.Precision.HIGHEST,
         preferred_element_type=jnp.float32,
     )
-    hidden_full = gather_rep(hidden)
     grads = jnp.concatenate([grad_one, grad_two], axis=0)
     grad_rows = grads.shape[0] // copies
     quarter = reduce_scatter_bits(
         grads.reshape([2] * rep_levels + [grad_rows, feature_width]), me, rep_bits, devices
     )
+    hidden, quarter = lax.optimization_barrier((hidden, quarter))
+    hidden_full = gather_rep(hidden)
     if grad_rows % rows == 0:
         parts = quarter.reshape(rows, grad_rows // rows, feature_width)
     else:

time: 75 us -> 79.4 us (1.059)
  waiting for transfers between devices: 30.8 us -> 34.7 us
    ppermute x6, waiting for transfers between devices: 9.34 us -> 11.4 us  [reduce_scatter_bits(): y = keep + lax.ppermute(send, AXES, bit_pairs(devices, bit))]
    ppermute x4, waiting for transfers between devices: 3.43 us -> 5.01 us  [all_gather_bits(): other = lax.ppermute(z, AXES, bit_pairs(devices, bit))]
  transfers between devices with their start and end apart: 16 -> 16, of which waited for: 9 -> 10; matrix products, arithmetic and copies ran while one was open for 5% -> 3% of each run, Pallas kernels for 0% -> 0%
where the time goes in v11:
time: 79.4 us; the launch traced here: 79 us
  waiting for transfers between devices  34.7 us (44%)
  starting transfers between devices  34.6 us (44%)
  local copies, waits for them, and re-layouts  4.34 us (5%)
  matrix products  2.46 us (3%)
  other arithmetic  1.97 us (2%)
  between operations  0.98 us (1%)
    ppermute x6, waiting for transfers between devices, reduce_scatter_bits(): y = keep + lax.ppermute(send, AXES, bit_pairs(devices, bit))  11.4 us
    ppermute x6, starting transfers between devices, reduce_scatter_bits(): y = keep + lax.ppermute(send, AXES, bit_pairs(devices, bit))  10.3 us
    ppermute x4, starting transfers between devices, gather_rounds(): pieces.append(lax.ppermute(x, AXES, pairs))  8.92 us
    all_to_all x1, waiting for transfers between devices, shards(): mine = lax.all_to_all(parts, 'row', 0, 0, tiled=False).sum(axis=0)  7.56 us
    all_to_all x1, waiting for transfers between devices, shards(): lax.all_to_all(jnp.broadcast_to(mine, parts.shape), 'row', 0, 0, tiled=Fa...  6.27 us
    all_to_all x1, starting transfers between devices, shards(): mine = lax.all_to_all(parts, 'row', 0, 0, tiled=False).sum(axis=0)  5.96 us
    all_to_all x1, starting transfers between devices, shards(): lax.all_to_all(jnp.broadcast_to(mine, parts.shape), 'row', 0, 0, tiled=Fa...  5.64 us
    ppermute x4, waiting for transfers between devices, all_gather_bits(): other = lax.ppermute(z, AXES, bit_pairs(devices, bit))  5.01 us
  transfers between devices with their start and end apart: 16, of which 10 were waited for; matrix products, arithmetic and copies ran while one was open for 3% of the time, Pallas kernels for 0%

profile of v11, /device:TPU:0, one launch (start us, length us, event | category | flops | bytes accessed | tf_op | source)
XLA Modules:
  0.0 79.0 jit_solution(5860904294903519520)
XLA Ops:
  0.6 0.0 copy-start
  0.7 1.0 %constant_dynamic-update-slice_fusion.1 = bf16[256,512]{1,0:T(8,128)(2,1)S(1)} fusion(bf16[256,256]{1,0:T(8,128)(2,1)} %param.7), kind=kLoop, calls=%fused_computation.63 | loop fusion | bytes 262144
  1.6 0.0 copy-done.1
  1.7 6.1 %collective-permute-start.1 = (bf16[256,512]{1,0:T(8,128)(2,1)S(1)}, bf16[256,512]{1,0:T(8,128)(2,1)S(1)}, u32[]{:S(2)}, u32[]{:S(2)}) collective-permute-start(bf16[256,512]{1,0:T(8,128)(2,1)S(1)} %constant_dynamic-update-slice_fusion), channel_id=1, source_target_pairs={{5,0},{15,1},{21,2},{31,3},{1,4},{11,5},{17,6},{27,7},{6,8},{12,9}... | collective-permute-start | bytes 786440 | tf_op jit(solution)/shard_map/ppermute | solution.py:47
  7.8 0.7 collective-permute-start
  8.4 0.0 copy-start.3
  8.5 0.0 copy-start.4
  8.5 0.7 copy-done.3
  9.1 0.1 compare_and_fusion
  9.2 0.1 sub.74
  9.3 4.4 %collective-permute-done.1 = bf16[256,512]{1,0:T(8,128)(2,1)S(1)} collective-permute-done((bf16[256,512]{1,0:T(8,128)(2,1)S(1)}, bf16[256,512]{1,0:T(8,128)(2,1)S(1)}, u32[]{:S(2)}, u32[]{:S(2)}) %collective-permute-start.1) | collective-permute-done | bytes 262176 | tf_op jit(solution)/shard_map/ppermute | solution.py:47
  13.8 0.1 pad_maximum_fusion
  13.8 0.6 gather_fusion
  14.4 0.4 fusion.1
  14.9 4.9 %collective-permute-start.2 = (f32[2,64,512]{2,1,0:T(8,128)S(1)}, f32[2,64,512]{2,1,0:T(8,128)S(1)}, u32[]{:S(2)}, u32[]{:S(2)}) collective-permute-start(f32[2,64,512]{2,1,0:T(8,128)S(1)} %dynamic-slice_bitcast_fusion.1), channel_id=1, source_target_pairs={{0,1},{1,0},{2,3},{3,2},{4,5},{5,4},{6,7},{7,6},{8,9},{9,8},{10,11... | collective-permute-start | bytes 786440 | tf_op jit(solution)/shard_map/ppermute | solution.py:23
  19.8 1.2 %collective-permute-done.2 = f32[2,64,512]{2,1,0:T(8,128)S(1)} collective-permute-done((f32[2,64,512]{2,1,0:T(8,128)S(1)}, f32[2,64,512]{2,1,0:T(8,128)S(1)}, u32[]{:S(2)}, u32[]{:S(2)}) %collective-permute-start.2) | collective-permute-done | bytes 262176 | tf_op jit(solution)/shard_map/ppermute | solution.py:23
  21.0 3.3 %collective-permute-start.3 = (f32[64,512]{1,0:T(8,128)S(1)}, f32[64,512]{1,0:T(8,128)S(1)}, u32[]{:S(2)}, u32[]{:S(2)}) collective-permute-start(f32[64,512]{1,0:T(8,128)S(1)} %dynamic-slice_bitcast_fusion.4), channel_id=1, source_target_pairs={{0,2},{1,3},{2,0},{3,1},{4,6},{5,7},{6,4},{7,5},{8,10},{9,11},{10,... | collective-permute-start | bytes 393224 | tf_op jit(solution)/shard_map/ppermute | solution.py:23
  24.3 3.8 %collective-permute-done.3 = f32[64,512]{1,0:T(8,128)S(1)} collective-permute-done((f32[64,512]{1,0:T(8,128)S(1)}, f32[64,512]{1,0:T(8,128)S(1)}, u32[]{:S(2)}, u32[]{:S(2)}) %collective-permute-start.3) | collective-permute-done | bytes 131104 | tf_op jit(solution)/shard_map/ppermute | solution.py:23
  28.1 0.2 fusion.23
  28.3 0.3 fusion.19
  28.6 0.6 copy-done.2
  29.2 0.3 fusion
  29.5 0.2 fusion.26
  29.7 0.1 collective-permute-start.4
  29.8 1.5 %collective-permute-done.4 = f32[2,128,256]{2,1,0:T(8,128)S(1)} collective-permute-done((f32[2,128,256]{2,1,0:T(8,128)S(1)}, f32[2,128,256]{2,1,0:T(8,128)S(1)}, u32[]{:S(2)}, u32[]{:S(2)}) %collective-permute-start.4) | collective-permute-done | bytes 262176 | tf_op jit(solution)/shard_map/ppermute | solution.py:23
  31.4 1.8 %collective-permute-start.5 = (f32[128,256]{1,0:T(8,128)S(1)}, f32[128,256]{1,0:T(8,128)S(1)}, u32[]{:S(2)}, u32[]{:S(2)}) collective-permute-start(f32[128,256]{1,0:T(8,128)S(1)} %dynamic-slice_bitcast_fusion.3), channel_id=1, source_target_pairs={{0,2},{1,3},{2,0},{3,1},{4,6},{5,7},{6,4},{7,5},{8,10},{9,11},{10,... | collective-permute-start | bytes 393224 | tf_op jit(solution)/shard_map/ppermute | solution.py:23
  33.2 3.8 %collective-permute-done.5 = f32[128,256]{1,0:T(8,128)S(1)} collective-permute-done((f32[128,256]{1,0:T(8,128)S(1)}, f32[128,256]{1,0:T(8,128)S(1)}, u32[]{:S(2)}, u32[]{:S(2)}) %collective-permute-start.5) | collective-permute-done | bytes 131104 | tf_op jit(solution)/shard_map/ppermute | solution.py:23
  37.0 0.7 bitcast_add_fusion.3
  37.7 1.7 %collective-permute-start.6 = (bf16[64,256]{1,0:T(8,128)(2,1)S(1)}, bf16[64,256]{1,0:T(8,128)(2,1)S(1)}, u32[]{:S(2)}, u32[]{:S(2)}) collective-permute-start(bf16[64,256]{1,0:T(8,128)(2,1)S(1)} %get-tuple-element.7), channel_id=1, source_target_pairs={{0,2},{1,3},{2,0},{3,1},{4,6},{5,7},{6,4},{7,5},{8,10},{9,11},{10,... | collective-permute-start | bytes 98312 | tf_op jit(solution)/shard_map/ppermute | solution.py:30
  39.4 2.2 %collective-permute-done.6 = bf16[64,256]{1,0:T(8,128)(2,1)S(1)} collective-permute-done((bf16[64,256]{1,0:T(8,128)(2,1)S(1)}, bf16[64,256]{1,0:T(8,128)(2,1)S(1)}, u32[]{:S(2)}, u32[]{:S(2)}) %collective-permute-start.6) | collective-permute-done | bytes 32800 | tf_op jit(solution)/shard_map/ppermute | solution.py:30
  41.6 0.1 collective-permute-start.7
  41.7 6.0 %all-to-all-start = ((f32[8,16,256]{2,1,0:T(8,128)}), f32[8,16,256]{2,1,0:T(8,128)S(1)}, u32[]{:S(2)}, u32[]{:S(2)}) async-start(f32[8,16,256]{2,1,0:T(8,128)} %bitcast.28), calls=%async_computation | async-start | bytes 262144 | tf_op jit(solution)/shard_map/all_to_all | solution.py:137
  47.8 7.6 %all-to-all-done = f32[8,16,256]{2,1,0:T(8,128)S(1)} async-done(((f32[8,16,256]{2,1,0:T(8,128)}), f32[8,16,256]{2,1,0:T(8,128)S(1)}, u32[]{:S(2)}, u32[]{:S(2)}) %all-to-all-start) | async-done | bytes 131104 | tf_op jit(solution)/shard_map/all_to_all | solution.py:137
  55.3 1.5 %collective-permute-start.9 = (bf16[256,256]{1,0:T(8,128)(2,1)S(1)}, bf16[256,256]{1,0:T(8,128)(2,1)S(1)}, u32[]{:S(2)}, u32[]{:S(2)}) collective-permute-start(bf16[256,256]{1,0:T(8,128)(2,1)S(1)} %bitcast.117), channel_id=1, source_target_pairs={{5,0},{15,1},{21,2},{31,3},{1,4},{11,5},{17,6},{27,7},{6,8},{12,9}... | collective-permute-start | bytes 393224 | tf_op jit(solution)/shard_map/ppermute | solution.py:47
  56.8 0.7 collective-permute-start.8
  57.5 0.7 broadcast_in_dim.59
  58.2 5.6 %all-to-all-start.1 = ((f32[8,16,256]{2,1,0:T(8,128)}), f32[8,16,256]{2,1,0:T(8,128)S(1)}, u32[]{:S(2)}, u32[]{:S(2)}) async-start(f32[8,16,256]{2,1,0:T(8,128)} %broadcast_in_dim.59), calls=%async_computation.1 | async-start | bytes 262144 | tf_op jit(solution)/shard_map/all_to_all | solution.py:140
  63.9 0.6 gather_fusion.1
  64.4 0.3 fusion.6
  64.8 0.1 collective-permute-start.10
  64.9 6.3 %all-to-all-done.1 = f32[8,16,256]{2,1,0:T(8,128)S(1)} async-done(((f32[8,16,256]{2,1,0:T(8,128)}), f32[8,16,256]{2,1,0:T(8,128)S(1)}, u32[]{:S(2)}, u32[]{:S(2)}) %all-to-all-start.1) | async-done | bytes 131104 | tf_op jit(solution)/shard_map/all_to_all | solution.py:140
  71.1 1.8 %collective-permute-start.12 = (f32[128,256]{1,0:T(8,128)S(1)}, f32[128,256]{1,0:T(8,128)S(1)}, u32[]{:S(2)}, u32[]{:S(2)}) collective-permute-start(f32[128,256]{1,0:T(8,128)S(1)} %bitcast.107), channel_id=1, source_target_pairs={{0,2},{1,3},{2,0},{3,1},{4,6},{5,7},{6,4},{7,5},{8,10},{9,11},{10,... | collective-permute-start | bytes 393224 | tf_op jit(solution)/shard_map/ppermute | solution.py:30
  73.0 0.3 collective-permute-start.11
  73.3 2.8 %collective-permute-done.12 = f32[128,256]{1,0:T(8,128)S(1)} collective-permute-done((f32[128,256]{1,0:T(8,128)S(1)}, f32[128,256]{1,0:T(8,128)S(1)}, u32[]{:S(2)}, u32[]{:S(2)}) %collective-permute-start.12) | collective-permute-done | bytes 131104 | tf_op jit(solution)/shard_map/ppermute | solution.py:30
  76.2 0.1 collective-permute-start.13
  76.2 1.1 %collective-permute-done.11 = f32[64,256]{1,0:T(8,128)S(1)} collective-permute-done((f32[64,256]{1,0:T(8,128)S(1)}, f32[64,256]{1,0:T(8,128)S(1)}, u32[]{:S(2)}, u32[]{:S(2)}) %collective-permute-start.11) | collective-permute-done | bytes 65568 | tf_op jit(solution)/shard_map/ppermute | solution.py:23
  77.4 0.8 convolution_convert_fusion
  78.2 0.8 %pad_maximum_fusion.2 = (f32[1,2,128,256]{3,2,1,0:T(8,128)}, f32[1,2,128,256]{3,2,1,0:T(8,128)}) fusion(f32[2,1,128,256]{3,2,1,0:T(8,128)S(1)} %get-tuple-element.15, f32[2,1,128,256]{3,2,1,0:T(8,128)S(1)} %get-tuple-element.16), kind=kLoop, calls=%fused_computation.22 | loop fusion | flops 131072 | bytes 1048576 | tf_op jit(solution)/shard_map/stack | solution.py:33
  (36 shorter events, 0.5 us)
Async XLA Ops:
  0.6 13.8 %copy-start = (bf16[1,1,2,4,128,128]{5,4,3,2,1,0:T(8,128)(2,1)S(1)}, bf16[1,1,2,4,128,128]{5,4,3,2,1,0:T(8,128)(2,1)}, u32[]{:S(2)}) copy-start(bf16[1,1,2,4,128,128]{5,4,3,2,1,0:T(8,128)(2,1)} %param.13) | copy-start | bytes 786436
  0.6 1.0 %copy-start.1 = (bf16[256,256]{1,0:T(8,128)(2,1)S(1)}, bf16[256,256]{1,0:T(8,128)(2,1)}, u32[]{:S(2)}) copy-start(bf16[256,256]{1,0:T(8,128)(2,1)} %param.8) | copy-start | bytes 393220
  1.7 12.1 %collective-permute-start.1 = (bf16[256,512]{1,0:T(8,128)(2,1)S(1)}, bf16[256,512]{1,0:T(8,128)(2,1)S(1)}, u32[]{:S(2)}, u32[]{:S(2)}) collective-permute-start(bf16[256,512]{1,0:T(8,128)(2,1)S(1)} %constant_dynamic-update-slice_fusion), channel_id=1, source_target_pairs={{5,0},{15,1},{21,2},{31,3},{1,4},{11,5},{17,6},{27,7},{6,8},{12,9}... | collective-permute-start | bytes 786440 | tf_op jit(solution)/shard_map/ppermute | solution.py:47
  7.8 6.0 %collective-permute-start = (bf16[256,512]{1,0:T(8,128)(2,1)S(1)}, bf16[256,512]{1,0:T(8,128)(2,1)S(1)}, u32[]{:S(2)}, u32[]{:S(2)}) collective-permute-start(bf16[256,512]{1,0:T(8,128)(2,1)S(1)} %constant_dynamic-update-slice_fusion), channel_id=1, source_target_pairs={{0,0},{10,1},{16,2},{26,3},{4,4},{14,5},{20,6},{30,7},{1,8},{11,9}... | collective-permute-start | bytes 786440 | tf_op jit(solution)/shard_map/ppermute | solution.py:47
  8.4 0.7 copy-start.3
  8.5 0.7 copy-start.4
  14.9 6.0 %collective-permute-start.2 = (f32[2,64,512]{2,1,0:T(8,128)S(1)}, f32[2,64,512]{2,1,0:T(8,128)S(1)}, u32[]{:S(2)}, u32[]{:S(2)}) collective-permute-start(f32[2,64,512]{2,1,0:T(8,128)S(1)} %dynamic-slice_bitcast_fusion.1), channel_id=1, source_target_pairs={{0,1},{1,0},{2,3},{3,2},{4,5},{5,4},{6,7},{7,6},{8,9},{9,8},{10,11... | collective-permute-start | bytes 786440 | tf_op jit(solution)/shard_map/ppermute | solution.py:23
  21.0 7.1 %collective-permute-start.3 = (f32[64,512]{1,0:T(8,128)S(1)}, f32[64,512]{1,0:T(8,128)S(1)}, u32[]{:S(2)}, u32[]{:S(2)}) collective-permute-start(f32[64,512]{1,0:T(8,128)S(1)} %dynamic-slice_bitcast_fusion.4), channel_id=1, source_target_pairs={{0,2},{1,3},{2,0},{3,1},{4,6},{5,7},{6,4},{7,5},{8,10},{9,11},{10,... | collective-permute-start | bytes 393224 | tf_op jit(solution)/shard_map/ppermute | solution.py:23
  24.3 3.8 %copy-start.5 = (bf16[256,256]{1,0:T(8,128)(2,1)S(1)}, bf16[256,256]{1,0:T(8,128)(2,1)}, u32[]{:S(2)}) copy-start(bf16[256,256]{1,0:T(8,128)(2,1)} %param.9) | copy-start | bytes 393220
  28.3 0.9 %copy-start.2 = (bf16[256,256]{1,0:T(8,128)(2,1)S(1)}, bf16[256,256]{1,0:T(8,128)(2,1)}, u32[]{:S(2)}) copy-start(bf16[256,256]{1,0:T(8,128)(2,1)} %param.10) | copy-start | bytes 393220
  29.7 1.6 %collective-permute-start.4 = (f32[2,128,256]{2,1,0:T(8,128)S(1)}, f32[2,128,256]{2,1,0:T(8,128)S(1)}, u32[]{:S(2)}, u32[]{:S(2)}) collective-permute-start(f32[2,128,256]{2,1,0:T(8,128)S(1)} %dynamic-slice_bitcast_fusion), channel_id=1, source_target_pairs={{0,1},{1,0},{2,3},{3,2},{4,5},{5,4},{6,7},{7,6},{8,9},{9,8},{10,11... | collective-permute-start | bytes 786440 | tf_op jit(solution)/shard_map/ppermute | solution.py:23
  31.4 5.6 %collective-permute-start.5 = (f32[128,256]{1,0:T(8,128)S(1)}, f32[128,256]{1,0:T(8,128)S(1)}, u32[]{:S(2)}, u32[]{:S(2)}) collective-permute-start(f32[128,256]{1,0:T(8,128)S(1)} %dynamic-slice_bitcast_fusion.3), channel_id=1, source_target_pairs={{0,2},{1,3},{2,0},{3,1},{4,6},{5,7},{6,4},{7,5},{8,10},{9,11},{10,... | collective-permute-start | bytes 393224 | tf_op jit(solution)/shard_map/ppermute | solution.py:23
  37.7 3.9 %collective-permute-start.6 = (bf16[64,256]{1,0:T(8,128)(2,1)S(1)}, bf16[64,256]{1,0:T(8,128)(2,1)S(1)}, u32[]{:S(2)}, u32[]{:S(2)}) collective-permute-start(bf16[64,256]{1,0:T(8,128)(2,1)S(1)} %get-tuple-element.7), channel_id=1, source_target_pairs={{0,2},{1,3},{2,0},{3,1},{4,6},{5,7},{6,4},{7,5},{8,10},{9,11},{10,... | collective-permute-start | bytes 98312 | tf_op jit(solution)/shard_map/ppermute | solution.py:30
  41.6 6.0 %collective-permute-start.7 = (bf16[2,64,256]{2,1,0:T(8,128)(2,1)S(1)}, bf16[2,64,256]{2,1,0:T(8,128)(2,1)S(1)}, u32[]{:S(2)}, u32[]{:S(2)}) collective-permute-start(bf16[2,64,256]{2,1,0:T(8,128)(2,1)S(1)} %pad_maximum_fusion.6), channel_id=1, source_target_pairs={{0,1},{1,0},{2,3},{3,2},{4,5},{5,4},{6,7},{7,6},{8,9},{9,8},{10,11... | collective-permute-start | bytes 196616 | tf_op jit(solution)/shard_map/ppermute | solution.py:30
  41.7 13.6 %all-to-all-start = ((f32[8,16,256]{2,1,0:T(8,128)}), f32[8,16,256]{2,1,0:T(8,128)S(1)}, u32[]{:S(2)}, u32[]{:S(2)}) async-start(f32[8,16,256]{2,1,0:T(8,128)} %bitcast.28), calls=%async_computation | async-start | bytes 262144 | tf_op jit(solution)/shard_map/all_to_all | solution.py:137
  55.3 8.5 %collective-permute-start.9 = (bf16[256,256]{1,0:T(8,128)(2,1)S(1)}, bf16[256,256]{1,0:T(8,128)(2,1)S(1)}, u32[]{:S(2)}, u32[]{:S(2)}) collective-permute-start(bf16[256,256]{1,0:T(8,128)(2,1)S(1)} %bitcast.117), channel_id=1, source_target_pairs={{5,0},{15,1},{21,2},{31,3},{1,4},{11,5},{17,6},{27,7},{6,8},{12,9}... | collective-permute-start | bytes 393224 | tf_op jit(solution)/shard_map/ppermute | solution.py:47
  56.8 7.0 %collective-permute-start.8 = (bf16[256,256]{1,0:T(8,128)(2,1)S(1)}, bf16[256,256]{1,0:T(8,128)(2,1)S(1)}, u32[]{:S(2)}, u32[]{:S(2)}) collective-permute-start(bf16[256,256]{1,0:T(8,128)(2,1)S(1)} %bitcast.118), channel_id=1, source_target_pairs={{0,0},{10,1},{16,2},{26,3},{4,4},{14,5},{20,6},{30,7},{1,8},{11,9}... | collective-permute-start | bytes 393224 | tf_op jit(solution)/shard_map/ppermute | solution.py:47
  58.2 13.0 %all-to-all-start.1 = ((f32[8,16,256]{2,1,0:T(8,128)}), f32[8,16,256]{2,1,0:T(8,128)S(1)}, u32[]{:S(2)}, u32[]{:S(2)}) async-start(f32[8,16,256]{2,1,0:T(8,128)} %broadcast_in_dim.59), calls=%async_computation.1 | async-start | bytes 262144 | tf_op jit(solution)/shard_map/all_to_all | solution.py:140
  64.8 8.2 %collective-permute-start.10 = (f32[2,64,256]{2,1,0:T(8,128)S(1)}, f32[2,64,256]{2,1,0:T(8,128)S(1)}, u32[]{:S(2)}, u32[]{:S(2)}) collective-permute-start(f32[2,64,256]{2,1,0:T(8,128)S(1)} %dynamic-slice_bitcast_fusion.2), channel_id=1, source_target_pairs={{0,1},{1,0},{2,3},{3,2},{4,5},{5,4},{6,7},{7,6},{8,9},{9,8},{10,11... | collective-permute-start | bytes 393224 | tf_op jit(solution)/shard_map/ppermute | solution.py:23
  71.1 5.0 %collective-permute-start.12 = (f32[128,256]{1,0:T(8,128)S(1)}, f32[128,256]{1,0:T(8,128)S(1)}, u32[]{:S(2)}, u32[]{:S(2)}) collective-permute-start(f32[128,256]{1,0:T(8,128)S(1)} %bitcast.107), channel_id=1, source_target_pairs={{0,2},{1,3},{2,0},{3,1},{4,6},{5,7},{6,4},{7,5},{8,10},{9,11},{10,... | collective-permute-start | bytes 393224 | tf_op jit(solution)/shard_map/ppermute | solution.py:30
  73.0 4.3 %collective-permute-start.11 = (f32[64,256]{1,0:T(8,128)S(1)}, f32[64,256]{1,0:T(8,128)S(1)}, u32[]{:S(2)}, u32[]{:S(2)}) collective-permute-start(f32[64,256]{1,0:T(8,128)S(1)} %dynamic-slice_bitcast_fusion.5), channel_id=1, source_target_pairs={{0,2},{1,3},{2,0},{3,1},{4,6},{5,7},{6,4},{7,5},{8,10},{9,11},{10,... | collective-permute-start | bytes 196616 | tf_op jit(solution)/shard_map/ppermute | solution.py:23
  76.2 2.0 %collective-permute-start.13 = (f32[2,128,256]{2,1,0:T(8,128)S(1)}, f32[2,128,256]{2,1,0:T(8,128)S(1)}, u32[]{:S(2)}, u32[]{:S(2)}) collective-permute-start(f32[2,128,256]{2,1,0:T(8,128)S(1)} %pad_maximum_fusion.4), channel_id=1, source_target_pairs={{0,1},{1,0},{2,3},{3,2},{4,5},{5,4},{6,7},{7,6},{8,9},{9,8},{10,11... | collective-permute-start | bytes 786440 | tf_op jit(solution)/shard_map/ppermute | solution.py:30

commit v12 on v10

--- a/solution.py
+++ b/solution.py
@@ -93,37 +93,45 @@
     def gather_rep(z):
         return all_gather_bits(z, me, rep_bits, devices).reshape(node_rows, z.shape[-1])
 
-    stage_in = jnp.concatenate([features, cotangent], axis=1)
-    pieces = gather_rounds(stage_in, rows, copies)
-    both = reduce_rep(
-        local_product(pieces, block_index, block_count, block_values, row_index, copy_index)
+    feature_pieces = gather_rounds(features, rows, copies)
+    feature_pieces, cotangent_in = lax.optimization_barrier((feature_pieces, cotangent))
+    cotangent_pieces = gather_rounds(cotangent_in, rows, copies)
+    agg_sum = local_product(
+        feature_pieces, block_index, block_count, block_values, row_index, copy_index
     )
-    agg_one = both[:, :feature_width].astype(jnp.bfloat16)
-    spread_cotangent = both[:, feature_width:]
-    carried = lax.dot_general(
-        spread_cotangent,
+    for bit in rep_bits:
+        agg_sum = agg_sum + lax.ppermute(agg_sum, AXES, bit_pairs(devices, bit))
+    agg_one = agg_sum.astype(jnp.bfloat16)
+    pre_one = jnp.dot(agg_one, weight_one, preferred_element_type=jnp.float32)
+    hidden = jax.nn.silu(pre_one).astype(jnp.bfloat16)
+    gate_value = jax.nn.sigmoid(pre_one)
+    slope = gate_value + pre_one * gate_value * (1.0 - gate_value)
+    spread_share = local_product(
+        cotangent_pieces, block_index, block_count, block_values, row_index, copy_index
+    )
+    carried_share = lax.dot_general(
+        spread_share,
         weight_two.astype(jnp.float32),
         (((1,), (1,)), ((), ())),
         precision=lax.Precision.HIGHEST,
         preferred_element_type=jnp.float32,
     )
-    pre_one = jnp.dot(agg_one, weight_one, preferred_element_type=jnp.float32)
-    hidden = jax.nn.silu(pre_one).astype(jnp.bfloat16)
-    gate_value = jax.nn.sigmoid(pre_one)
-    pre_grad = (carried * (gate_value + pre_one * gate_value * (1.0 - gate_value))).astype(
-        jnp.bfloat16
-    )
+    pre_grad_share = carried_share * slope
     grad_one = lax.dot_general(
-        agg_one, pre_grad, (((0,), (0,)), ((), ())), preferred_element_type=jnp.float32
-    )
-    grad_two = lax.dot_general(
-        hidden.astype(jnp.float32),
-        spread_cotangent,
+        agg_one.astype(jnp.float32),
+        pre_grad_share,
         (((0,), (0,)), ((), ())),
         precision=lax.Precision.HIGHEST,
         preferred_element_type=jnp.float32,
     )
-    hidden_full = gather_rep(hidden)
+    grad_two = lax.dot_general(
+        hidden.astype(jnp.float32),
+        spread_share,
+        (((0,), (0,)), ((), ())),
+        precision=lax.Precision.HIGHEST,
+        preferred_element_type=jnp.float32,
+    )
+    hidden_full = hidden
     grads = jnp.concatenate([grad_one, grad_two], axis=0)
     grad_rows = grads.shape[0] // copies
     quarter = reduce_scatter_bits(

time: 75 us -> 81.8 us (1.091)
  blocking collectives: 0 us -> 11.7 us
  waiting for transfers between devices: 30.8 us -> 25.8 us
    all_to_all x0 -> x1, blocking collectives: none -> 11.7 us  [shards(): mine = lax.all_to_all(parts, 'row', 0, 0, tiled=False).sum(axis=0)]
    ppermute x4 -> x6, starting transfers between devices: 8.57 us -> 16.5 us  [gather_rounds(): pieces.append(lax.ppermute(x, AXES, pairs))]
    ppermute x6 -> x4, starting transfers between devices: 10.2 us -> 2.33 us  [reduce_scatter_bits(): y = keep + lax.ppermute(send, AXES, bit_pairs(devices, bit))]
    ppermute x0 -> x2, waiting for transfers between devices: none -> 7.64 us  [shards(): agg_sum = agg_sum + lax.ppermute(agg_sum, AXES, bit_pairs(devices, bit))]
    all_to_all x1 -> x0, waiting for transfers between devices: 7.27 us -> none  [shards(): mine = lax.all_to_all(parts, 'row', 0, 0, tiled=False).sum(axis=0)]
    ppermute x0 -> x2, starting transfers between devices: none -> 7.2 us  [shards(): agg_sum = agg_sum + lax.ppermute(agg_sum, AXES, bit_pairs(devices, bit))]
    all_to_all x1 -> x0, starting transfers between devices: 5.65 us -> none  [shards(): mine = lax.all_to_all(parts, 'row', 0, 0, tiled=False).sum(axis=0)]
    ppermute x6 -> x4, waiting for transfers between devices: 9.34 us -> 6.3 us  [reduce_scatter_bits(): y = keep + lax.ppermute(send, AXES, bit_pairs(devices, bit))]
  transfers between devices with their start and end apart: 16 -> 15, of which waited for: 9 -> 9; matrix products, arithmetic and copies ran while one was open for 5% -> 4% of each run, Pallas kernels for 0% -> 0%
where the time goes in v12:
time: 81.8 us; the launch traced here: 81.5 us
  starting transfers between devices  33.8 us (41%)
  waiting for transfers between devices  25.8 us (32%)
  blocking collectives  11.7 us (14%)
  local copies, waits for them, and re-layouts  4.72 us (6%)
  matrix products  2.87 us (4%)
  other arithmetic  1.55 us (2%)
  between operations  0.95 us (1%)
    ppermute x6, starting transfers between devices, gather_rounds(): pieces.append(lax.ppermute(x, AXES, pairs))  16.5 us
    all_to_all x1, blocking collectives, shards(): mine = lax.all_to_all(parts, 'row', 0, 0, tiled=False).sum(axis=0)  11.7 us
    ppermute x2, waiting for transfers between devices, shards(): agg_sum = agg_sum + lax.ppermute(agg_sum, AXES, bit_pairs(devices, bit))  7.64 us
    ppermute x2, starting transfers between devices, shards(): agg_sum = agg_sum + lax.ppermute(agg_sum, AXES, bit_pairs(devices, bit))  7.2 us
    ppermute x4, waiting for transfers between devices, reduce_scatter_bits(): y = keep + lax.ppermute(send, AXES, bit_pairs(devices, bit))  6.3 us
    all_to_all x1, waiting for transfers between devices, shards(): lax.all_to_all(jnp.broadcast_to(mine, parts.shape), 'row', 0, 0, tiled=Fa...  6.16 us
    all_to_all x1, starting transfers between devices, shards(): lax.all_to_all(jnp.broadcast_to(mine, parts.shape), 'row', 0, 0, tiled=Fa...  6.01 us
    ppermute x6, waiting for transfers between devices, gather_rounds(): pieces.append(lax.ppermute(x, AXES, pairs))  2.91 us
  transfers between devices with their start and end apart: 15, of which 9 were waited for; matrix products, arithmetic and copies ran while one was open for 4% of the time, Pallas kernels for 0%

profile of v12, /device:TPU:0, one launch (start us, length us, event | category | flops | bytes accessed | tf_op | source)
XLA Modules:
  0.0 81.5 jit_solution(16480188550874734528)
XLA Ops:
  0.6 0.0 copy-start
  0.6 6.1 %collective-permute-start.1 = (bf16[256,256]{1,0:T(8,128)(2,1)}, bf16[256,256]{1,0:T(8,128)(2,1)S(1)}, u32[]{:S(2)}, u32[]{:S(2)}) collective-permute-start(bf16[256,256]{1,0:T(8,128)(2,1)} %param.9), channel_id=1, source_target_pairs={{5,0},{15,1},{21,2},{31,3},{1,4},{11,5},{17,6},{27,7},{6,8},{12,9}... | collective-permute-start | bytes 393224 | tf_op jit(solution)/shard_map/ppermute | solution.py:47
  6.7 1.6 %collective-permute-start = (bf16[256,256]{1,0:T(8,128)(2,1)}, bf16[256,256]{1,0:T(8,128)(2,1)S(1)}, u32[]{:S(2)}, u32[]{:S(2)}) collective-permute-start(bf16[256,256]{1,0:T(8,128)(2,1)} %param.9), channel_id=1, source_target_pairs={{0,0},{10,1},{16,2},{26,3},{4,4},{14,5},{20,6},{30,7},{1,8},{11,9}... | collective-permute-start | bytes 393224 | tf_op jit(solution)/shard_map/ppermute | solution.py:47
  8.3 0.7 copy-done.2
  9.0 0.1 sub.44
  9.1 1.1 %collective-permute-done.1 = bf16[256,256]{1,0:T(8,128)(2,1)S(1)} collective-permute-done((bf16[256,256]{1,0:T(8,128)(2,1)}, bf16[256,256]{1,0:T(8,128)(2,1)S(1)}, u32[]{:S(2)}, u32[]{:S(2)}) %collective-permute-start.1) | collective-permute-done | bytes 131104 | tf_op jit(solution)/shard_map/ppermute | solution.py:47
  10.3 0.9 %copy-done.3 = bf16[256,256]{1,0:T(8,128)(2,1)S(1)} copy-done((bf16[256,256]{1,0:T(8,128)(2,1)S(1)}, bf16[256,256]{1,0:T(8,128)(2,1)}, u32[]{:S(2)}) %copy-start.3) | copy-done | bytes 131096
  11.1 6.4 %collective-permute-start.5 = (bf16[256,256]{1,0:T(8,128)(2,1)S(1)}, bf16[256,256]{1,0:T(8,128)(2,1)S(1)}, u32[]{:S(2)}, u32[]{:S(2)}) collective-permute-start(bf16[256,256]{1,0:T(8,128)(2,1)S(1)} %copy-done.3), channel_id=1, source_target_pairs={{5,0},{15,1},{21,2},{31,3},{1,4},{11,5},{17,6},{27,7},{6,8},{12,9}... | collective-permute-start | bytes 393224 | tf_op jit(solution)/shard_map/ppermute | solution.py:47
  17.5 0.7 collective-permute-start.4
  18.2 0.1 iota_compare_fusion
  18.3 0.6 gather_fusion
  18.9 1.8 %collective-permute-done.5 = bf16[256,256]{1,0:T(8,128)(2,1)S(1)} collective-permute-done((bf16[256,256]{1,0:T(8,128)(2,1)S(1)}, bf16[256,256]{1,0:T(8,128)(2,1)S(1)}, u32[]{:S(2)}, u32[]{:S(2)}) %collective-permute-start.5) | collective-permute-done | bytes 131104 | tf_op jit(solution)/shard_map/ppermute | solution.py:47
  20.6 0.6 gather_fusion.1
  21.2 0.2 broadcast_select_fusion
  21.4 0.3 fusion.4
  21.7 2.8 %collective-permute-start.2 = (f32[256,256]{1,0:T(8,128)S(1)}, f32[256,256]{1,0:T(8,128)S(1)}, u32[]{:S(2)}, u32[]{:S(2)}) collective-permute-start(f32[256,256]{1,0:T(8,128)S(1)} %bitcast.94), channel_id=1, source_target_pairs={{0,1},{1,0},{2,3},{3,2},{4,5},{5,4},{6,7},{7,6},{8,9},{9,8},{10,11... | collective-permute-start | bytes 786440 | tf_op jit(solution)/shard_map/ppermute | solution.py:103
  24.6 1.2 %collective-permute-done.2 = f32[256,256]{1,0:T(8,128)S(1)} collective-permute-done((f32[256,256]{1,0:T(8,128)S(1)}, f32[256,256]{1,0:T(8,128)S(1)}, u32[]{:S(2)}, u32[]{:S(2)}) %collective-permute-start.2) | collective-permute-done | bytes 262176 | tf_op jit(solution)/shard_map/ppermute | solution.py:103
  25.8 4.4 %collective-permute-start.3 = (f32[256,256]{1,0:T(8,128)S(1)}, f32[256,256]{1,0:T(8,128)S(1)}, u32[]{:S(2)}, u32[]{:S(2)}) collective-permute-start(f32[256,256]{1,0:T(8,128)S(1)} %bitcast_add_fusion.4), channel_id=1, source_target_pairs={{0,2},{1,3},{2,0},{3,1},{4,6},{5,7},{6,4},{7,5},{8,10},{9,11},{10,... | collective-permute-start | bytes 786440 | tf_op jit(solution)/shard_map/ppermute | solution.py:103
  30.1 0.3 fusion.2
  30.4 0.0 copy-start.4
  30.4 6.5 %collective-permute-done.3 = f32[256,256]{1,0:T(8,128)S(1)} collective-permute-done((f32[256,256]{1,0:T(8,128)S(1)}, f32[256,256]{1,0:T(8,128)S(1)}, u32[]{:S(2)}, u32[]{:S(2)}) %collective-permute-start.3) | collective-permute-done | bytes 262176 | tf_op jit(solution)/shard_map/ppermute | solution.py:103
  37.0 0.2 fusion.17
  37.2 0.0 copy-start.1
  37.2 0.3 fusion.28
  37.5 0.6 copy-done.1
  38.1 0.3 convolution_multiply_fusion
  38.5 0.3 fusion.27
  38.9 0.1 collective-permute-start.6
  38.9 1.5 %collective-permute-done.6 = f32[2,128,256]{2,1,0:T(8,128)S(1)} collective-permute-done((f32[2,128,256]{2,1,0:T(8,128)S(1)}, f32[2,128,256]{2,1,0:T(8,128)S(1)}, u32[]{:S(2)}, u32[]{:S(2)}) %collective-permute-start.6) | collective-permute-done | bytes 262176 | tf_op jit(solution)/shard_map/ppermute | solution.py:23
  40.5 1.8 %collective-permute-start.7 = (f32[128,256]{1,0:T(8,128)S(1)}, f32[128,256]{1,0:T(8,128)S(1)}, u32[]{:S(2)}, u32[]{:S(2)}) collective-permute-start(f32[128,256]{1,0:T(8,128)S(1)} %dynamic-slice_bitcast_fusion.2), channel_id=1, source_target_pairs={{0,2},{1,3},{2,0},{3,1},{4,6},{5,7},{6,4},{7,5},{8,10},{9,11},{10,... | collective-permute-start | bytes 393224 | tf_op jit(solution)/shard_map/ppermute | solution.py:23
  42.3 3.8 %collective-permute-done.7 = f32[128,256]{1,0:T(8,128)S(1)} collective-permute-done((f32[128,256]{1,0:T(8,128)S(1)}, f32[128,256]{1,0:T(8,128)S(1)}, u32[]{:S(2)}, u32[]{:S(2)}) %collective-permute-start.7) | collective-permute-done | bytes 131104 | tf_op jit(solution)/shard_map/ppermute | solution.py:23
  46.1 11.7 %all_to_all.10 = f32[8,16,256]{2,1,0:T(8,128)S(1)} all-to-all(f32[8,16,256]{2,1,0:T(8,128)S(1)} %bitcast.92), channel_id=1, replica_groups=mesh['row'=8,'rep'=4] {'row'}, dimensions={0} | all-to-all | bytes 262144 | tf_op jit(solution)/shard_map/all_to_all | solution.py:144
  57.9 1.1 %collective-permute-start.9 = (bf16[256,256]{1,0:T(8,128)(2,1)S(1)}, bf16[256,256]{1,0:T(8,128)(2,1)S(1)}, u32[]{:S(2)}, u32[]{:S(2)}) collective-permute-start(bf16[256,256]{1,0:T(8,128)(2,1)S(1)} %get-tuple-element.10), channel_id=1, source_target_pairs={{5,0},{15,1},{21,2},{31,3},{1,4},{11,5},{17,6},{27,7},{6,8},{12,9}... | collective-permute-start | bytes 393224 | tf_op jit(solution)/shard_map/ppermute | solution.py:47
  59.0 0.7 collective-permute-start.8
  59.7 0.7 broadcast_in_dim.40
  60.4 6.0 %all-to-all-start.1 = ((f32[8,16,256]{2,1,0:T(8,128)}), f32[8,16,256]{2,1,0:T(8,128)S(1)}, u32[]{:S(2)}, u32[]{:S(2)}) async-start(f32[8,16,256]{2,1,0:T(8,128)} %broadcast_in_dim.40), calls=%async_computation.1 | async-start | bytes 262144 | tf_op jit(solution)/shard_map/all_to_all | solution.py:147
  66.4 0.6 gather_fusion.2
  67.0 0.1 broadcast_select_fusion.2
  67.1 0.3 fusion
  67.5 0.1 collective-permute-start.10
  67.6 6.2 %all-to-all-done.1 = f32[8,16,256]{2,1,0:T(8,128)S(1)} async-done(((f32[8,16,256]{2,1,0:T(8,128)}), f32[8,16,256]{2,1,0:T(8,128)S(1)}, u32[]{:S(2)}, u32[]{:S(2)}) %all-to-all-start.1) | async-done | bytes 131104 | tf_op jit(solution)/shard_map/all_to_all | solution.py:147
  73.7 1.7 %collective-permute-start.12 = (f32[128,256]{1,0:T(8,128)S(1)}, f32[128,256]{1,0:T(8,128)S(1)}, u32[]{:S(2)}, u32[]{:S(2)}) collective-permute-start(f32[128,256]{1,0:T(8,128)S(1)} %bitcast.91), channel_id=1, source_target_pairs={{0,2},{1,3},{2,0},{3,1},{4,6},{5,7},{6,4},{7,5},{8,10},{9,11},{10,... | collective-permute-start | bytes 393224 | tf_op jit(solution)/shard_map/ppermute | solution.py:30
  75.5 0.4 collective-permute-start.11
  75.9 2.8 %collective-permute-done.12 = f32[128,256]{1,0:T(8,128)S(1)} collective-permute-done((f32[128,256]{1,0:T(8,128)S(1)}, f32[128,256]{1,0:T(8,128)S(1)}, u32[]{:S(2)}, u32[]{:S(2)}) %collective-permute-start.12) | collective-permute-done | bytes 131104 | tf_op jit(solution)/shard_map/ppermute | solution.py:30
  78.7 0.1 collective-permute-start.13
  78.8 1.0 %collective-permute-done.11 = f32[64,256]{1,0:T(8,128)S(1)} collective-permute-done((f32[64,256]{1,0:T(8,128)S(1)}, f32[64,256]{1,0:T(8,128)S(1)}, u32[]{:S(2)}, u32[]{:S(2)}) %collective-permute-start.11) | collective-permute-done | bytes 65568 | tf_op jit(solution)/shard_map/ppermute | solution.py:23
  79.8 0.8 convolution_convert_fusion
  80.6 0.8 %pad_maximum_fusion.1 = (f32[1,2,128,256]{3,2,1,0:T(8,128)}, f32[1,2,128,256]{3,2,1,0:T(8,128)}) fusion(f32[2,1,128,256]{3,2,1,0:T(8,128)S(1)} %get-tuple-element.16, f32[2,1,128,256]{3,2,1,0:T(8,128)S(1)} %get-tuple-element.17), kind=kLoop, calls=%fused_computation.21 | loop fusion | flops 131072 | bytes 1048576 | tf_op jit(solution)/shard_map/stack | solution.py:33
  (32 shorter events, 0.5 us)
Async XLA Ops:
  0.6 20.8 %copy-start = (bf16[1,1,2,4,128,128]{5,4,3,2,1,0:T(8,128)(2,1)S(1)}, bf16[1,1,2,4,128,128]{5,4,3,2,1,0:T(8,128)(2,1)}, u32[]{:S(2)}) copy-start(bf16[1,1,2,4,128,128]{5,4,3,2,1,0:T(8,128)(2,1)} %param.15) | copy-start | bytes 786436
  0.6 9.6 %collective-permute-start.1 = (bf16[256,256]{1,0:T(8,128)(2,1)}, bf16[256,256]{1,0:T(8,128)(2,1)S(1)}, u32[]{:S(2)}, u32[]{:S(2)}) collective-permute-start(bf16[256,256]{1,0:T(8,128)(2,1)} %param.9), channel_id=1, source_target_pairs={{5,0},{15,1},{21,2},{31,3},{1,4},{11,5},{17,6},{27,7},{6,8},{12,9}... | collective-permute-start | bytes 393224 | tf_op jit(solution)/shard_map/ppermute | solution.py:47
  6.7 3.5 %collective-permute-start = (bf16[256,256]{1,0:T(8,128)(2,1)}, bf16[256,256]{1,0:T(8,128)(2,1)S(1)}, u32[]{:S(2)}, u32[]{:S(2)}) collective-permute-start(bf16[256,256]{1,0:T(8,128)(2,1)} %param.9), channel_id=1, source_target_pairs={{0,0},{10,1},{16,2},{26,3},{4,4},{14,5},{20,6},{30,7},{1,8},{11,9}... | collective-permute-start | bytes 393224 | tf_op jit(solution)/shard_map/ppermute | solution.py:47
  8.3 0.7 copy-start.2
  10.2 0.9 %copy-start.3 = (bf16[256,256]{1,0:T(8,128)(2,1)S(1)}, bf16[256,256]{1,0:T(8,128)(2,1)}, u32[]{:S(2)}) copy-start(bf16[256,256]{1,0:T(8,128)(2,1)} %param.10) | copy-start | bytes 393220
  11.1 7.0 %copy-start.5 = (s32[1,1,2]{2,1,0:T(1,128)S(1)}, s32[1,1,2]{2,1,0:T(1,128)}, u32[]{:S(2)}) copy-start(s32[1,1,2]{2,1,0:T(1,128)} %param.14) | copy-start | bytes 28
  11.1 9.5 %collective-permute-start.5 = (bf16[256,256]{1,0:T(8,128)(2,1)S(1)}, bf16[256,256]{1,0:T(8,128)(2,1)S(1)}, u32[]{:S(2)}, u32[]{:S(2)}) collective-permute-start(bf16[256,256]{1,0:T(8,128)(2,1)S(1)} %copy-done.3), channel_id=1, source_target_pairs={{5,0},{15,1},{21,2},{31,3},{1,4},{11,5},{17,6},{27,7},{6,8},{12,9}... | collective-permute-start | bytes 393224 | tf_op jit(solution)/shard_map/ppermute | solution.py:47
  17.5 3.1 %collective-permute-start.4 = (bf16[256,256]{1,0:T(8,128)(2,1)S(1)}, bf16[256,256]{1,0:T(8,128)(2,1)S(1)}, u32[]{:S(2)}, u32[]{:S(2)}) collective-permute-start(bf16[256,256]{1,0:T(8,128)(2,1)S(1)} %copy-done.3), channel_id=1, source_target_pairs={{0,0},{10,1},{16,2},{26,3},{4,4},{14,5},{20,6},{30,7},{1,8},{11,9}... | collective-permute-start | bytes 393224 | tf_op jit(solution)/shard_map/ppermute | solution.py:47
  21.7 4.0 %collective-permute-start.2 = (f32[256,256]{1,0:T(8,128)S(1)}, f32[256,256]{1,0:T(8,128)S(1)}, u32[]{:S(2)}, u32[]{:S(2)}) collective-permute-start(f32[256,256]{1,0:T(8,128)S(1)} %bitcast.94), channel_id=1, source_target_pairs={{0,1},{1,0},{2,3},{3,2},{4,5},{5,4},{6,7},{7,6},{8,9},{9,8},{10,11... | collective-permute-start | bytes 786440 | tf_op jit(solution)/shard_map/ppermute | solution.py:103
  25.8 11.2 %collective-permute-start.3 = (f32[256,256]{1,0:T(8,128)S(1)}, f32[256,256]{1,0:T(8,128)S(1)}, u32[]{:S(2)}, u32[]{:S(2)}) collective-permute-start(f32[256,256]{1,0:T(8,128)S(1)} %bitcast_add_fusion.4), channel_id=1, source_target_pairs={{0,2},{1,3},{2,0},{3,1},{4,6},{5,7},{6,4},{7,5},{8,10},{9,11},{10,... | collective-permute-start | bytes 786440 | tf_op jit(solution)/shard_map/ppermute | solution.py:103
  30.4 6.5 %copy-start.4 = (bf16[256,256]{1,0:T(8,128)(2,1)S(1)}, bf16[256,256]{1,0:T(8,128)(2,1)}, u32[]{:S(2)}) copy-start(bf16[256,256]{1,0:T(8,128)(2,1)} %param.11) | copy-start | bytes 393220
  37.2 0.9 %copy-start.1 = (bf16[256,256]{1,0:T(8,128)(2,1)S(1)}, bf16[256,256]{1,0:T(8,128)(2,1)}, u32[]{:S(2)}) copy-start(bf16[256,256]{1,0:T(8,128)(2,1)} %param.12) | copy-start | bytes 393220
  38.9 1.6 %collective-permute-start.6 = (f32[2,128,256]{2,1,0:T(8,128)S(1)}, f32[2,128,256]{2,1,0:T(8,128)S(1)}, u32[]{:S(2)}, u32[]{:S(2)}) collective-permute-start(f32[2,128,256]{2,1,0:T(8,128)S(1)} %dynamic-slice_bitcast_fusion), channel_id=1, source_target_pairs={{0,1},{1,0},{2,3},{3,2},{4,5},{5,4},{6,7},{7,6},{8,9},{9,8},{10,11... | collective-permute-start | bytes 786440 | tf_op jit(solution)/shard_map/ppermute | solution.py:23
  40.5 5.6 %collective-permute-start.7 = (f32[128,256]{1,0:T(8,128)S(1)}, f32[128,256]{1,0:T(8,128)S(1)}, u32[]{:S(2)}, u32[]{:S(2)}) collective-permute-start(f32[128,256]{1,0:T(8,128)S(1)} %dynamic-slice_bitcast_fusion.2), channel_id=1, source_target_pairs={{0,2},{1,3},{2,0},{3,1},{4,6},{5,7},{6,4},{7,5},{8,10},{9,11},{10,... | collective-permute-start | bytes 393224 | tf_op jit(solution)/shard_map/ppermute | solution.py:23
  57.9 8.5 %collective-permute-start.9 = (bf16[256,256]{1,0:T(8,128)(2,1)S(1)}, bf16[256,256]{1,0:T(8,128)(2,1)S(1)}, u32[]{:S(2)}, u32[]{:S(2)}) collective-permute-start(bf16[256,256]{1,0:T(8,128)(2,1)S(1)} %get-tuple-element.10), channel_id=1, source_target_pairs={{5,0},{15,1},{21,2},{31,3},{1,4},{11,5},{17,6},{27,7},{6,8},{12,9}... | collective-permute-start | bytes 393224 | tf_op jit(solution)/shard_map/ppermute | solution.py:47
  59.0 7.4 %collective-permute-start.8 = (bf16[256,256]{1,0:T(8,128)(2,1)S(1)}, bf16[256,256]{1,0:T(8,128)(2,1)S(1)}, u32[]{:S(2)}, u32[]{:S(2)}) collective-permute-start(bf16[256,256]{1,0:T(8,128)(2,1)S(1)} %get-tuple-element.10), channel_id=1, source_target_pairs={{0,0},{10,1},{16,2},{26,3},{4,4},{14,5},{20,6},{30,7},{1,8},{11,9}... | collective-permute-start | bytes 393224 | tf_op jit(solution)/shard_map/ppermute | solution.py:47
  60.4 13.4 %all-to-all-start.1 = ((f32[8,16,256]{2,1,0:T(8,128)}), f32[8,16,256]{2,1,0:T(8,128)S(1)}, u32[]{:S(2)}, u32[]{:S(2)}) async-start(f32[8,16,256]{2,1,0:T(8,128)} %broadcast_in_dim.40), calls=%async_computation.1 | async-start | bytes 262144 | tf_op jit(solution)/shard_map/all_to_all | solution.py:147
  67.5 8.0 %collective-permute-start.10 = (f32[2,64,256]{2,1,0:T(8,128)S(1)}, f32[2,64,256]{2,1,0:T(8,128)S(1)}, u32[]{:S(2)}, u32[]{:S(2)}) collective-permute-start(f32[2,64,256]{2,1,0:T(8,128)S(1)} %dynamic-slice_bitcast_fusion.1), channel_id=1, source_target_pairs={{0,1},{1,0},{2,3},{3,2},{4,5},{5,4},{6,7},{7,6},{8,9},{9,8},{10,11... | collective-permute-start | bytes 393224 | tf_op jit(solution)/shard_map/ppermute | solution.py:23
  73.7 5.0 %collective-permute-start.12 = (f32[128,256]{1,0:T(8,128)S(1)}, f32[128,256]{1,0:T(8,128)S(1)}, u32[]{:S(2)}, u32[]{:S(2)}) collective-permute-start(f32[128,256]{1,0:T(8,128)S(1)} %bitcast.91), channel_id=1, source_target_pairs={{0,2},{1,3},{2,0},{3,1},{4,6},{5,7},{6,4},{7,5},{8,10},{9,11},{10,... | collective-permute-start | bytes 393224 | tf_op jit(solution)/shard_map/ppermute | solution.py:30
  75.5 4.3 %collective-permute-start.11 = (f32[64,256]{1,0:T(8,128)S(1)}, f32[64,256]{1,0:T(8,128)S(1)}, u32[]{:S(2)}, u32[]{:S(2)}) collective-permute-start(f32[64,256]{1,0:T(8,128)S(1)} %dynamic-slice_bitcast_fusion.3), channel_id=1, source_target_pairs={{0,2},{1,3},{2,0},{3,1},{4,6},{5,7},{6,4},{7,5},{8,10},{9,11},{10,... | collective-permute-start | bytes 196616 | tf_op jit(solution)/shard_map/ppermute | solution.py:23
  78.7 1.8 %collective-permute-start.13 = (f32[2,128,256]{2,1,0:T(8,128)S(1)}, f32[2,128,256]{2,1,0:T(8,128)S(1)}, u32[]{:S(2)}, u32[]{:S(2)}) collective-permute-start(f32[2,128,256]{2,1,0:T(8,128)S(1)} %pad_maximum_fusion.5), channel_id=1, source_target_pairs={{0,1},{1,0},{2,3},{3,2},{4,5},{5,4},{6,7},{7,6},{8,9},{9,8},{10,11... | collective-permute-start | bytes 786440 | tf_op jit(solution)/shard_map/ppermute | solution.py:30

commit v13 on v12

--- a/solution.py
+++ b/solution.py
@@ -94,20 +94,23 @@
         return all_gather_bits(z, me, rep_bits, devices).reshape(node_rows, z.shape[-1])
 
     feature_pieces = gather_rounds(features, rows, copies)
-    feature_pieces, cotangent_in = lax.optimization_barrier((feature_pieces, cotangent))
-    cotangent_pieces = gather_rounds(cotangent_in, rows, copies)
     agg_sum = local_product(
         feature_pieces, block_index, block_count, block_values, row_index, copy_index
     )
-    for bit in rep_bits:
+    for step, bit in enumerate(rep_bits):
         agg_sum = agg_sum + lax.ppermute(agg_sum, AXES, bit_pairs(devices, bit))
+        if step == 0:
+            agg_sum, cotangent_in, late_values = lax.optimization_barrier(
+                (agg_sum, cotangent, block_values)
+            )
+            cotangent_pieces = gather_rounds(cotangent_in, rows, copies)
     agg_one = agg_sum.astype(jnp.bfloat16)
     pre_one = jnp.dot(agg_one, weight_one, preferred_element_type=jnp.float32)
     hidden = jax.nn.silu(pre_one).astype(jnp.bfloat16)
     gate_value = jax.nn.sigmoid(pre_one)
     slope = gate_value + pre_one * gate_value * (1.0 - gate_value)
     spread_share = local_product(
-        cotangent_pieces, block_index, block_count, block_values, row_index, copy_index
+        cotangent_pieces, block_index, block_count, late_values, row_index, copy_index
     )
     carried_share = lax.dot_general(
         spread_share,

time: 81.8 us -> 77 us (0.941)
  starting transfers between devices: 33.8 us -> 30.8 us
  waiting for transfers between devices: 25.8 us -> 23.9 us
    ppermute x6, waiting for transfers between devices: 2.91 us -> 0.42 us  [gather_rounds(): pieces.append(lax.ppermute(x, AXES, pairs))]
    ppermute x6, starting transfers between devices: 16.5 us -> 14.6 us  [gather_rounds(): pieces.append(lax.ppermute(x, AXES, pairs))]
    ppermute x2, starting transfers between devices: 7.2 us -> 5.66 us  [shards(): agg_sum = agg_sum + lax.ppermute(agg_sum, AXES, bit_pairs(devices, bit))]
  transfers between devices with their start and end apart: 15 -> 15, of which waited for: 9 -> 8; matrix products, arithmetic and copies ran while one was open for 4% -> 5% of each run, Pallas kernels for 0% -> 0%
where the time goes in v13:
time: 77 us; the launch traced here: 76.7 us
  starting transfers between devices  30.8 us (40%)
  waiting for transfers between devices  23.9 us (31%)
  blocking collectives  11.9 us (15%)
  local copies, waits for them, and re-layouts  4.58 us (6%)
  matrix products  2.87 us (4%)
  other arithmetic  1.62 us (2%)
  between operations  0.97 us (1%)
    ppermute x6, starting transfers between devices, gather_rounds(): pieces.append(lax.ppermute(x, AXES, pairs))  14.6 us
    all_to_all x1, blocking collectives, shards(): mine = lax.all_to_all(parts, 'row', 0, 0, tiled=False).sum(axis=0)  11.9 us
    ppermute x2, waiting for transfers between devices, shards(): agg_sum = agg_sum + lax.ppermute(agg_sum, AXES, bit_pairs(devices, bit))  8.28 us
    ppermute x4, waiting for transfers between devices, reduce_scatter_bits(): y = keep + lax.ppermute(send, AXES, bit_pairs(devices, bit))  6.2 us
    all_to_all x1, waiting for transfers between devices, shards(): lax.all_to_all(jnp.broadcast_to(mine, parts.shape), 'row', 0, 0, tiled=Fa...  6.16 us
    all_to_all x1, starting transfers between devices, shards(): lax.all_to_all(jnp.broadcast_to(mine, parts.shape), 'row', 0, 0, tiled=Fa...  6.01 us
    ppermute x2, starting transfers between devices, shards(): agg_sum = agg_sum + lax.ppermute(agg_sum, AXES, bit_pairs(devices, bit))  5.66 us
    ppermute x2, waiting for transfers between devices, all_gather_bits(): other = lax.ppermute(z, AXES, bit_pairs(devices, bit))  2.83 us
  transfers between devices with their start and end apart: 15, of which 8 were waited for; matrix products, arithmetic and copies ran while one was open for 5% of the time, Pallas kernels for 0%

profile of v13, /device:TPU:0, one launch (start us, length us, event | category | flops | bytes accessed | tf_op | source)
XLA Modules:
  0.0 76.7 jit_solution(7406213471800068813)
XLA Ops:
  0.6 0.0 copy-start
  0.6 6.1 %collective-permute-start.1 = (bf16[256,256]{1,0:T(8,128)(2,1)}, bf16[256,256]{1,0:T(8,128)(2,1)S(1)}, u32[]{:S(2)}, u32[]{:S(2)}) collective-permute-start(bf16[256,256]{1,0:T(8,128)(2,1)} %param.9), channel_id=1, source_target_pairs={{5,0},{15,1},{21,2},{31,3},{1,4},{11,5},{17,6},{27,7},{6,8},{12,9}... | collective-permute-start | bytes 393224 | tf_op jit(solution)/shard_map/ppermute | solution.py:47
  6.7 1.6 %collective-permute-start = (bf16[256,256]{1,0:T(8,128)(2,1)}, bf16[256,256]{1,0:T(8,128)(2,1)S(1)}, u32[]{:S(2)}, u32[]{:S(2)}) collective-permute-start(bf16[256,256]{1,0:T(8,128)(2,1)} %param.9), channel_id=1, source_target_pairs={{0,0},{10,1},{16,2},{26,3},{4,4},{14,5},{20,6},{30,7},{1,8},{11,9}... | collective-permute-start | bytes 393224 | tf_op jit(solution)/shard_map/ppermute | solution.py:47
  8.3 0.7 copy-done.2
  9.0 0.1 sub.44
  9.1 0.6 copy-done.5
  9.7 0.1 iota_compare_fusion
  9.8 0.4 collective-permute-done.1
  10.3 0.6 gather_fusion
  10.9 0.1 broadcast_select_fusion.1
  11.0 0.3 fusion.4
  11.3 0.0 copy-start.3
  11.3 2.3 %collective-permute-start.2 = (f32[256,256]{1,0:T(8,128)S(1)}, f32[256,256]{1,0:T(8,128)S(1)}, u32[]{:S(2)}, u32[]{:S(2)}) collective-permute-start(f32[256,256]{1,0:T(8,128)S(1)} %bitcast.93), channel_id=1, source_target_pairs={{0,1},{1,0},{2,3},{3,2},{4,5},{5,4},{6,7},{7,6},{8,9},{9,8},{10,11... | collective-permute-start | bytes 786440 | tf_op jit(solution)/shard_map/ppermute | solution.py:101
  13.6 1.2 %collective-permute-done.2 = f32[256,256]{1,0:T(8,128)S(1)} collective-permute-done((f32[256,256]{1,0:T(8,128)S(1)}, f32[256,256]{1,0:T(8,128)S(1)}, u32[]{:S(2)}, u32[]{:S(2)}) %collective-permute-start.2) | collective-permute-done | bytes 262176 | tf_op jit(solution)/shard_map/ppermute | solution.py:101
  14.9 4.5 %collective-permute-start.5 = (bf16[256,256]{1,0:T(8,128)(2,1)S(1)}, bf16[256,256]{1,0:T(8,128)(2,1)S(1)}, u32[]{:S(2)}, u32[]{:S(2)}) collective-permute-start(bf16[256,256]{1,0:T(8,128)(2,1)S(1)} %copy-done.3), channel_id=1, source_target_pairs={{5,0},{15,1},{21,2},{31,3},{1,4},{11,5},{17,6},{27,7},{6,8},{12,9}... | collective-permute-start | bytes 393224 | tf_op jit(solution)/shard_map/ppermute | solution.py:47
  19.4 0.7 collective-permute-start.4
  20.1 3.3 %collective-permute-start.3 = (f32[256,256]{1,0:T(8,128)S(1)}, f32[256,256]{1,0:T(8,128)S(1)}, u32[]{:S(2)}, u32[]{:S(2)}) collective-permute-start(f32[256,256]{1,0:T(8,128)S(1)} %bitcast_add_fusion.4), channel_id=1, source_target_pairs={{0,2},{1,3},{2,0},{3,1},{4,6},{5,7},{6,4},{7,5},{8,10},{9,11},{10,... | collective-permute-start | bytes 786440 | tf_op jit(solution)/shard_map/ppermute | solution.py:101
  23.4 0.6 gather_fusion.1
  24.0 0.1 broadcast_select_fusion
  24.1 0.3 fusion.2
  24.4 0.0 copy-start.4
  24.4 7.1 %collective-permute-done.3 = f32[256,256]{1,0:T(8,128)S(1)} collective-permute-done((f32[256,256]{1,0:T(8,128)S(1)}, f32[256,256]{1,0:T(8,128)S(1)}, u32[]{:S(2)}, u32[]{:S(2)}) %collective-permute-start.3) | collective-permute-done | bytes 262176 | tf_op jit(solution)/shard_map/ppermute | solution.py:101
  31.6 0.2 fusion.17
  31.9 0.7 copy-done.1
  32.5 0.3 convolution_multiply_fusion
  32.9 0.3 fusion.27
  33.2 0.3 fusion.28
  33.6 0.2 collective-permute-start.6
  33.8 1.4 %collective-permute-done.6 = f32[2,128,256]{2,1,0:T(8,128)S(1)} collective-permute-done((f32[2,128,256]{2,1,0:T(8,128)S(1)}, f32[2,128,256]{2,1,0:T(8,128)S(1)}, u32[]{:S(2)}, u32[]{:S(2)}) %collective-permute-start.6) | collective-permute-done | bytes 262176 | tf_op jit(solution)/shard_map/ppermute | solution.py:23
  35.3 2.1 %collective-permute-start.7 = (f32[128,256]{1,0:T(8,128)S(1)}, f32[128,256]{1,0:T(8,128)S(1)}, u32[]{:S(2)}, u32[]{:S(2)}) collective-permute-start(f32[128,256]{1,0:T(8,128)S(1)} %dynamic-slice_bitcast_fusion.2), channel_id=1, source_target_pairs={{0,2},{1,3},{2,0},{3,1},{4,6},{5,7},{6,4},{7,5},{8,10},{9,11},{10,... | collective-permute-start | bytes 393224 | tf_op jit(solution)/shard_map/ppermute | solution.py:23
  37.3 3.8 %collective-permute-done.7 = f32[128,256]{1,0:T(8,128)S(1)} collective-permute-done((f32[128,256]{1,0:T(8,128)S(1)}, f32[128,256]{1,0:T(8,128)S(1)}, u32[]{:S(2)}, u32[]{:S(2)}) %collective-permute-start.7) | collective-permute-done | bytes 131104 | tf_op jit(solution)/shard_map/ppermute | solution.py:23
  41.2 11.9 %all_to_all.10 = f32[8,16,256]{2,1,0:T(8,128)S(1)} all-to-all(f32[8,16,256]{2,1,0:T(8,128)S(1)} %bitcast.89), channel_id=1, replica_groups=mesh['row'=8,'rep'=4] {'row'}, dimensions={0} | all-to-all | bytes 262144 | tf_op jit(solution)/shard_map/all_to_all | solution.py:147
  53.1 1.1 %collective-permute-start.9 = (bf16[256,256]{1,0:T(8,128)(2,1)S(1)}, bf16[256,256]{1,0:T(8,128)(2,1)S(1)}, u32[]{:S(2)}, u32[]{:S(2)}) collective-permute-start(bf16[256,256]{1,0:T(8,128)(2,1)S(1)} %get-tuple-element.12), channel_id=1, source_target_pairs={{5,0},{15,1},{21,2},{31,3},{1,4},{11,5},{17,6},{27,7},{6,8},{12,9}... | collective-permute-start | bytes 393224 | tf_op jit(solution)/shard_map/ppermute | solution.py:47
  54.2 0.7 collective-permute-start.8
  54.9 0.7 broadcast_in_dim.40
  55.6 6.0 %all-to-all-start.1 = ((f32[8,16,256]{2,1,0:T(8,128)}), f32[8,16,256]{2,1,0:T(8,128)S(1)}, u32[]{:S(2)}, u32[]{:S(2)}) async-start(f32[8,16,256]{2,1,0:T(8,128)} %broadcast_in_dim.40), calls=%async_computation.1 | async-start | bytes 262144 | tf_op jit(solution)/shard_map/all_to_all | solution.py:150
  61.6 0.6 gather_fusion.2
  62.2 0.1 broadcast_select_fusion.2
  62.3 0.3 fusion
  62.7 0.1 collective-permute-start.10
  62.8 6.2 %all-to-all-done.1 = f32[8,16,256]{2,1,0:T(8,128)S(1)} async-done(((f32[8,16,256]{2,1,0:T(8,128)}), f32[8,16,256]{2,1,0:T(8,128)S(1)}, u32[]{:S(2)}, u32[]{:S(2)}) %all-to-all-start.1) | async-done | bytes 131104 | tf_op jit(solution)/shard_map/all_to_all | solution.py:150
  68.9 1.7 %collective-permute-start.12 = (f32[128,256]{1,0:T(8,128)S(1)}, f32[128,256]{1,0:T(8,128)S(1)}, u32[]{:S(2)}, u32[]{:S(2)}) collective-permute-start(f32[128,256]{1,0:T(8,128)S(1)} %bitcast.88), channel_id=1, source_target_pairs={{0,2},{1,3},{2,0},{3,1},{4,6},{5,7},{6,4},{7,5},{8,10},{9,11},{10,... | collective-permute-start | bytes 393224 | tf_op jit(solution)/shard_map/ppermute | solution.py:30
  70.7 0.4 collective-permute-start.11
  71.1 2.8 %collective-permute-done.12 = f32[128,256]{1,0:T(8,128)S(1)} collective-permute-done((f32[128,256]{1,0:T(8,128)S(1)}, f32[128,256]{1,0:T(8,128)S(1)}, u32[]{:S(2)}, u32[]{:S(2)}) %collective-permute-start.12) | collective-permute-done | bytes 131104 | tf_op jit(solution)/shard_map/ppermute | solution.py:30
  73.9 0.1 collective-permute-start.13
  74.0 1.0 %collective-permute-done.11 = f32[64,256]{1,0:T(8,128)S(1)} collective-permute-done((f32[64,256]{1,0:T(8,128)S(1)}, f32[64,256]{1,0:T(8,128)S(1)}, u32[]{:S(2)}, u32[]{:S(2)}) %collective-permute-start.11) | collective-permute-done | bytes 65568 | tf_op jit(solution)/shard_map/ppermute | solution.py:23
  75.0 0.8 %convolution_convert_fusion = bf16[64,256]{1,0:T(8,128)(2,1)} fusion(bf16[256,256]{1,0:T(8,128)(2,1)S(1)} %copy-done.1, f32[64,256]{1,0:T(8,128)S(1)} %collective-permute-done.11, f32[2,64,256]{2,1,0:T(8,128)S(1)} %bitcast_add_fusion.1, s32[]{:T(128)S(6)} %select_n.97), kind=kOutput, calls=%fused_computation.4 | convolution fusion | flops 8437760 | bytes 294916 | tf_op jit(solution)/shard_map/dot_general | solution.py:157
  75.8 0.8 %pad_maximum_fusion.1 = (f32[1,2,128,256]{3,2,1,0:T(8,128)}, f32[1,2,128,256]{3,2,1,0:T(8,128)}) fusion(f32[2,1,128,256]{3,2,1,0:T(8,128)S(1)} %get-tuple-element.18, f32[2,1,128,256]{3,2,1,0:T(8,128)S(1)} %get-tuple-element.19), kind=kLoop, calls=%fused_computation.21 | loop fusion | flops 131072 | bytes 1048576 | tf_op jit(solution)/shard_map/stack | solution.py:33
  (33 shorter events, 0.5 us)
Async XLA Ops:
  0.6 10.3 %copy-start = (bf16[1,1,2,4,128,128]{5,4,3,2,1,0:T(8,128)(2,1)S(1)}, bf16[1,1,2,4,128,128]{5,4,3,2,1,0:T(8,128)(2,1)}, u32[]{:S(2)}) copy-start(bf16[1,1,2,4,128,128]{5,4,3,2,1,0:T(8,128)(2,1)} %param.15) | copy-start | bytes 786436
  0.6 9.6 %collective-permute-start.1 = (bf16[256,256]{1,0:T(8,128)(2,1)}, bf16[256,256]{1,0:T(8,128)(2,1)S(1)}, u32[]{:S(2)}, u32[]{:S(2)}) collective-permute-start(bf16[256,256]{1,0:T(8,128)(2,1)} %param.9), channel_id=1, source_target_pairs={{5,0},{15,1},{21,2},{31,3},{1,4},{11,5},{17,6},{27,7},{6,8},{12,9}... | collective-permute-start | bytes 393224 | tf_op jit(solution)/shard_map/ppermute | solution.py:47
  6.7 3.5 %collective-permute-start = (bf16[256,256]{1,0:T(8,128)(2,1)}, bf16[256,256]{1,0:T(8,128)(2,1)S(1)}, u32[]{:S(2)}, u32[]{:S(2)}) collective-permute-start(bf16[256,256]{1,0:T(8,128)(2,1)} %param.9), channel_id=1, source_target_pairs={{0,0},{10,1},{16,2},{26,3},{4,4},{14,5},{20,6},{30,7},{1,8},{11,9}... | collective-permute-start | bytes 393224 | tf_op jit(solution)/shard_map/ppermute | solution.py:47
  8.3 0.7 copy-start.2
  9.1 0.7 copy-start.5
  11.3 3.6 %copy-start.3 = (bf16[256,256]{1,0:T(8,128)(2,1)S(1)}, bf16[256,256]{1,0:T(8,128)(2,1)}, u32[]{:S(2)}) copy-start(bf16[256,256]{1,0:T(8,128)(2,1)} %param.10) | copy-start | bytes 393220
  11.3 3.5 %collective-permute-start.2 = (f32[256,256]{1,0:T(8,128)S(1)}, f32[256,256]{1,0:T(8,128)S(1)}, u32[]{:S(2)}, u32[]{:S(2)}) collective-permute-start(f32[256,256]{1,0:T(8,128)S(1)} %bitcast.93), channel_id=1, source_target_pairs={{0,1},{1,0},{2,3},{3,2},{4,5},{5,4},{6,7},{7,6},{8,9},{9,8},{10,11... | collective-permute-start | bytes 786440 | tf_op jit(solution)/shard_map/ppermute | solution.py:101
  14.9 8.5 %collective-permute-start.5 = (bf16[256,256]{1,0:T(8,128)(2,1)S(1)}, bf16[256,256]{1,0:T(8,128)(2,1)S(1)}, u32[]{:S(2)}, u32[]{:S(2)}) collective-permute-start(bf16[256,256]{1,0:T(8,128)(2,1)S(1)} %copy-done.3), channel_id=1, source_target_pairs={{5,0},{15,1},{21,2},{31,3},{1,4},{11,5},{17,6},{27,7},{6,8},{12,9}... | collective-permute-start | bytes 393224 | tf_op jit(solution)/shard_map/ppermute | solution.py:47
  19.4 4.0 %collective-permute-start.4 = (bf16[256,256]{1,0:T(8,128)(2,1)S(1)}, bf16[256,256]{1,0:T(8,128)(2,1)S(1)}, u32[]{:S(2)}, u32[]{:S(2)}) collective-permute-start(bf16[256,256]{1,0:T(8,128)(2,1)S(1)} %copy-done.3), channel_id=1, source_target_pairs={{0,0},{10,1},{16,2},{26,3},{4,4},{14,5},{20,6},{30,7},{1,8},{11,9}... | collective-permute-start | bytes 393224 | tf_op jit(solution)/shard_map/ppermute | solution.py:47
  20.1 11.5 %collective-permute-start.3 = (f32[256,256]{1,0:T(8,128)S(1)}, f32[256,256]{1,0:T(8,128)S(1)}, u32[]{:S(2)}, u32[]{:S(2)}) collective-permute-start(f32[256,256]{1,0:T(8,128)S(1)} %bitcast_add_fusion.4), channel_id=1, source_target_pairs={{0,2},{1,3},{2,0},{3,1},{4,6},{5,7},{6,4},{7,5},{8,10},{9,11},{10,... | collective-permute-start | bytes 786440 | tf_op jit(solution)/shard_map/ppermute | solution.py:101
  24.4 7.2 %copy-start.4 = (bf16[256,256]{1,0:T(8,128)(2,1)S(1)}, bf16[256,256]{1,0:T(8,128)(2,1)}, u32[]{:S(2)}) copy-start(bf16[256,256]{1,0:T(8,128)(2,1)} %param.11) | copy-start | bytes 393220
  31.6 0.9 %copy-start.1 = (bf16[256,256]{1,0:T(8,128)(2,1)S(1)}, bf16[256,256]{1,0:T(8,128)(2,1)}, u32[]{:S(2)}) copy-start(bf16[256,256]{1,0:T(8,128)(2,1)} %param.12) | copy-start | bytes 393220
  33.6 1.6 %collective-permute-start.6 = (f32[2,128,256]{2,1,0:T(8,128)S(1)}, f32[2,128,256]{2,1,0:T(8,128)S(1)}, u32[]{:S(2)}, u32[]{:S(2)}) collective-permute-start(f32[2,128,256]{2,1,0:T(8,128)S(1)} %dynamic-slice_bitcast_fusion), channel_id=1, source_target_pairs={{0,1},{1,0},{2,3},{3,2},{4,5},{5,4},{6,7},{7,6},{8,9},{9,8},{10,11... | collective-permute-start | bytes 786440 | tf_op jit(solution)/shard_map/ppermute | solution.py:23
  35.3 5.9 %collective-permute-start.7 = (f32[128,256]{1,0:T(8,128)S(1)}, f32[128,256]{1,0:T(8,128)S(1)}, u32[]{:S(2)}, u32[]{:S(2)}) collective-permute-start(f32[128,256]{1,0:T(8,128)S(1)} %dynamic-slice_bitcast_fusion.2), channel_id=1, source_target_pairs={{0,2},{1,3},{2,0},{3,1},{4,6},{5,7},{6,4},{7,5},{8,10},{9,11},{10,... | collective-permute-start | bytes 393224 | tf_op jit(solution)/shard_map/ppermute | solution.py:23
  53.1 8.5 %collective-permute-start.9 = (bf16[256,256]{1,0:T(8,128)(2,1)S(1)}, bf16[256,256]{1,0:T(8,128)(2,1)S(1)}, u32[]{:S(2)}, u32[]{:S(2)}) collective-permute-start(bf16[256,256]{1,0:T(8,128)(2,1)S(1)} %get-tuple-element.12), channel_id=1, source_target_pairs={{5,0},{15,1},{21,2},{31,3},{1,4},{11,5},{17,6},{27,7},{6,8},{12,9}... | collective-permute-start | bytes 393224 | tf_op jit(solution)/shard_map/ppermute | solution.py:47
  54.2 7.4 %collective-permute-start.8 = (bf16[256,256]{1,0:T(8,128)(2,1)S(1)}, bf16[256,256]{1,0:T(8,128)(2,1)S(1)}, u32[]{:S(2)}, u32[]{:S(2)}) collective-permute-start(bf16[256,256]{1,0:T(8,128)(2,1)S(1)} %get-tuple-element.12), channel_id=1, source_target_pairs={{0,0},{10,1},{16,2},{26,3},{4,4},{14,5},{20,6},{30,7},{1,8},{11,9}... | collective-permute-start | bytes 393224 | tf_op jit(solution)/shard_map/ppermute | solution.py:47
  55.6 13.4 %all-to-all-start.1 = ((f32[8,16,256]{2,1,0:T(8,128)}), f32[8,16,256]{2,1,0:T(8,128)S(1)}, u32[]{:S(2)}, u32[]{:S(2)}) async-start(f32[8,16,256]{2,1,0:T(8,128)} %broadcast_in_dim.40), calls=%async_computation.1 | async-start | bytes 262144 | tf_op jit(solution)/shard_map/all_to_all | solution.py:150
  62.7 8.0 %collective-permute-start.10 = (f32[2,64,256]{2,1,0:T(8,128)S(1)}, f32[2,64,256]{2,1,0:T(8,128)S(1)}, u32[]{:S(2)}, u32[]{:S(2)}) collective-permute-start(f32[2,64,256]{2,1,0:T(8,128)S(1)} %dynamic-slice_bitcast_fusion.1), channel_id=1, source_target_pairs={{0,1},{1,0},{2,3},{3,2},{4,5},{5,4},{6,7},{7,6},{8,9},{9,8},{10,11... | collective-permute-start | bytes 393224 | tf_op jit(solution)/shard_map/ppermute | solution.py:23
  68.9 5.0 %collective-permute-start.12 = (f32[128,256]{1,0:T(8,128)S(1)}, f32[128,256]{1,0:T(8,128)S(1)}, u32[]{:S(2)}, u32[]{:S(2)}) collective-permute-start(f32[128,256]{1,0:T(8,128)S(1)} %bitcast.88), channel_id=1, source_target_pairs={{0,2},{1,3},{2,0},{3,1},{4,6},{5,7},{6,4},{7,5},{8,10},{9,11},{10,... | collective-permute-start | bytes 393224 | tf_op jit(solution)/shard_map/ppermute | solution.py:30
  70.7 4.3 %collective-permute-start.11 = (f32[64,256]{1,0:T(8,128)S(1)}, f32[64,256]{1,0:T(8,128)S(1)}, u32[]{:S(2)}, u32[]{:S(2)}) collective-permute-start(f32[64,256]{1,0:T(8,128)S(1)} %dynamic-slice_bitcast_fusion.3), channel_id=1, source_target_pairs={{0,2},{1,3},{2,0},{3,1},{4,6},{5,7},{6,4},{7,5},{8,10},{9,11},{10,... | collective-permute-start | bytes 196616 | tf_op jit(solution)/shard_map/ppermute | solution.py:23
  73.9 1.8 %collective-permute-start.13 = (f32[2,128,256]{2,1,0:T(8,128)S(1)}, f32[2,128,256]{2,1,0:T(8,128)S(1)}, u32[]{:S(2)}, u32[]{:S(2)}) collective-permute-start(f32[2,128,256]{2,1,0:T(8,128)S(1)} %pad_maximum_fusion.5), channel_id=1, source_target_pairs={{0,1},{1,0},{2,3},{3,2},{4,5},{5,4},{6,7},{7,6},{8,9},{9,8},{10,11... | collective-permute-start | bytes 786440 | tf_op jit(solution)/shard_map/ppermute | solution.py:30

commit v14 on v13

--- a/solution.py
+++ b/solution.py
@@ -97,14 +97,19 @@
     agg_sum = local_product(
         feature_pieces, block_index, block_count, block_values, row_index, copy_index
     )
+    agg_sum = agg_sum.reshape([2] * rep_levels + [share_rows, feature_width])
     for step, bit in enumerate(rep_bits):
-        agg_sum = agg_sum + lax.ppermute(agg_sum, AXES, bit_pairs(devices, bit))
+        axis = rep_levels - 1 - step
+        mine = (me >> bit) & 1
+        keep = lax.dynamic_index_in_dim(agg_sum, mine, axis, keepdims=False)
+        send = lax.dynamic_index_in_dim(agg_sum, 1 - mine, axis, keepdims=False)
+        agg_sum = keep + lax.ppermute(send, AXES, bit_pairs(devices, bit))
         if step == 0:
             agg_sum, cotangent_in, late_values = lax.optimization_barrier(
                 (agg_sum, cotangent, block_values)
             )
             cotangent_pieces = gather_rounds(cotangent_in, rows, copies)
-    agg_one = agg_sum.astype(jnp.bfloat16)
+    agg_one = gather_rep(agg_sum.astype(jnp.bfloat16))
     pre_one = jnp.dot(agg_one, weight_one, preferred_element_type=jnp.float32)
     hidden = jax.nn.silu(pre_one).astype(jnp.bfloat16)
     gate_value = jax.nn.sigmoid(pre_one)

time: 77 us -> 79.2 us (1.029)
  starting transfers between devices: 30.8 us -> 33.5 us
  waiting for transfers between devices: 23.9 us -> 22.7 us
  local copies, waits for them, and re-layouts: 4.58 us -> 5.48 us
    ppermute x2, waiting for transfers between devices: 8.28 us -> 3.39 us  [shards(): agg_sum = keep + lax.ppermute(send, AXES, bit_pairs(devices, bit))]
    ppermute x6, starting transfers between devices: 14.6 us -> 10.5 us  [gather_rounds(): pieces.append(lax.ppermute(x, AXES, pairs))]
    ppermute x4, starting transfers between devices: 2.71 us -> 5.99 us  [reduce_scatter_bits(): y = keep + lax.ppermute(send, AXES, bit_pairs(devices, bit))]
    ppermute x6, waiting for transfers between devices: 0.42 us -> 3.3 us  [gather_rounds(): pieces.append(lax.ppermute(x, AXES, pairs))]
    ppermute x2 -> x4, starting transfers between devices: 1.78 us -> 4.31 us  [all_gather_bits(): other = lax.ppermute(z, AXES, bit_pairs(devices, bit))]
    ppermute x2 -> x4, waiting for transfers between devices: 2.83 us -> 3.88 us  [all_gather_bits(): other = lax.ppermute(z, AXES, bit_pairs(devices, bit))]
    ppermute x2, starting transfers between devices: 5.66 us -> 6.69 us  [shards(): agg_sum = keep + lax.ppermute(send, AXES, bit_pairs(devices, bit))]
    unnamed x12, local copies, waits for them, and re-layouts: 2.01 us -> 2.88 us
  transfers between devices with their start and end apart: 15 -> 17, of which waited for: 8 -> 10; matrix products, arithmetic and copies ran while one was open for 5% -> 5% of each run, Pallas kernels for 0% -> 0%
where the time goes in v14:
time: 79.2 us; the launch traced here: 78.8 us
  starting transfers between devices  33.5 us (42%)
  waiting for transfers between devices  22.7 us (29%)
  blocking collectives  11.7 us (15%)
  local copies, waits for them, and re-layouts  5.48 us (7%)
  matrix products  2.87 us (4%)
  other arithmetic  1.63 us (2%)
  between operations  0.97 us (1%)
    all_to_all x1, blocking collectives, shards(): mine = lax.all_to_all(parts, 'row', 0, 0, tiled=False).sum(axis=0)  11.7 us
    ppermute x6, starting transfers between devices, gather_rounds(): pieces.append(lax.ppermute(x, AXES, pairs))  10.5 us
    ppermute x2, starting transfers between devices, shards(): agg_sum = keep + lax.ppermute(send, AXES, bit_pairs(devices, bit))  6.69 us
    all_to_all x1, waiting for transfers between devices, shards(): lax.all_to_all(jnp.broadcast_to(mine, parts.shape), 'row', 0, 0, tiled=Fa...  6.17 us
    all_to_all x1, starting transfers between devices, shards(): lax.all_to_all(jnp.broadcast_to(mine, parts.shape), 'row', 0, 0, tiled=Fa...  6.01 us
    ppermute x4, starting transfers between devices, reduce_scatter_bits(): y = keep + lax.ppermute(send, AXES, bit_pairs(devices, bit))  5.99 us
    ppermute x4, waiting for transfers between devices, reduce_scatter_bits(): y = keep + lax.ppermute(send, AXES, bit_pairs(devices, bit))  5.95 us
    ppermute x4, starting transfers between devices, all_gather_bits(): other = lax.ppermute(z, AXES, bit_pairs(devices, bit))  4.31 us
  transfers between devices with their start and end apart: 17, of which 10 were waited for; matrix products, arithmetic and copies ran while one was open for 5% of the time, Pallas kernels for 0%

profile of v14, /device:TPU:0, one launch (start us, length us, event | category | flops | bytes accessed | tf_op | source)
XLA Modules:
  0.0 78.8 jit_solution(3241510990616041744)
XLA Ops:
  0.6 6.1 %collective-permute-start.1 = (bf16[256,256]{1,0:T(8,128)(2,1)}, bf16[256,256]{1,0:T(8,128)(2,1)S(1)}, u32[]{:S(2)}, u32[]{:S(2)}) collective-permute-start(bf16[256,256]{1,0:T(8,128)(2,1)} %param.9), channel_id=1, source_target_pairs={{5,0},{15,1},{21,2},{31,3},{1,4},{11,5},{17,6},{27,7},{6,8},{12,9}... | collective-permute-start | bytes 393224 | tf_op jit(solution)/shard_map/ppermute | solution.py:47
  6.7 1.6 %collective-permute-start = (bf16[256,256]{1,0:T(8,128)(2,1)}, bf16[256,256]{1,0:T(8,128)(2,1)S(1)}, u32[]{:S(2)}, u32[]{:S(2)}) collective-permute-start(bf16[256,256]{1,0:T(8,128)(2,1)} %param.9), channel_id=1, source_target_pairs={{0,0},{10,1},{16,2},{26,3},{4,4},{14,5},{20,6},{30,7},{1,8},{11,9}... | collective-permute-start | bytes 393224 | tf_op jit(solution)/shard_map/ppermute | solution.py:47
  8.3 0.7 copy-done.2
  9.0 0.1 sub.46
  9.1 0.6 copy-done.5
  9.7 0.1 iota_compare_fusion
  9.8 0.4 collective-permute-done.1
  10.3 0.6 gather_fusion
  10.9 0.1 broadcast_select_fusion.1
  11.0 0.3 fusion.4
  11.3 2.3 %collective-permute-start.2 = (f32[2,64,256]{2,1,0:T(8,128)S(1)}, f32[2,64,256]{2,1,0:T(8,128)S(1)}, u32[]{:S(2)}, u32[]{:S(2)}) collective-permute-start(f32[2,64,256]{2,1,0:T(8,128)S(1)} %dynamic-slice_bitcast_fusion.3), channel_id=1, source_target_pairs={{0,1},{1,0},{2,3},{3,2},{4,5},{5,4},{6,7},{7,6},{8,9},{9,8},{10,11... | collective-permute-start | bytes 393224 | tf_op jit(solution)/shard_map/ppermute | solution.py:106
  13.7 1.0 %collective-permute-done.2 = f32[2,64,256]{2,1,0:T(8,128)S(1)} collective-permute-done((f32[2,64,256]{2,1,0:T(8,128)S(1)}, f32[2,64,256]{2,1,0:T(8,128)S(1)}, u32[]{:S(2)}, u32[]{:S(2)}) %collective-permute-start.2) | collective-permute-done | bytes 131104 | tf_op jit(solution)/shard_map/ppermute | solution.py:106
  14.7 4.3 %collective-permute-start.3 = (f32[64,256]{1,0:T(8,128)S(1)}, f32[64,256]{1,0:T(8,128)S(1)}, u32[]{:S(2)}, u32[]{:S(2)}) collective-permute-start(f32[64,256]{1,0:T(8,128)S(1)} %dynamic-slice_bitcast_fusion.5), channel_id=1, source_target_pairs={{0,2},{1,3},{2,0},{3,1},{4,6},{5,7},{6,4},{7,5},{8,10},{9,11},{10,... | collective-permute-start | bytes 196616 | tf_op jit(solution)/shard_map/ppermute | solution.py:106
  19.0 2.4 %collective-permute-done.3 = f32[64,256]{1,0:T(8,128)S(1)} collective-permute-done((f32[64,256]{1,0:T(8,128)S(1)}, f32[64,256]{1,0:T(8,128)S(1)}, u32[]{:S(2)}, u32[]{:S(2)}) %collective-permute-start.3) | collective-permute-done | bytes 65568 | tf_op jit(solution)/shard_map/ppermute | solution.py:106
  21.5 1.9 %collective-permute-start.4 = (bf16[64,256]{1,0:T(8,128)(2,1)S(1)}, bf16[64,256]{1,0:T(8,128)(2,1)S(1)}, u32[]{:S(2)}, u32[]{:S(2)}) collective-permute-start(bf16[64,256]{1,0:T(8,128)(2,1)S(1)} %fusion.19), channel_id=1, source_target_pairs={{0,2},{1,3},{2,0},{3,1},{4,6},{5,7},{6,4},{7,5},{8,10},{9,11},{10,... | collective-permute-start | bytes 98312 | tf_op jit(solution)/shard_map/ppermute | solution.py:30
  23.4 0.3 collective-permute-start.7
  23.7 0.7 collective-permute-start.6
  24.4 1.0 %collective-permute-done.4 = bf16[64,256]{1,0:T(8,128)(2,1)S(1)} collective-permute-done((bf16[64,256]{1,0:T(8,128)(2,1)S(1)}, bf16[64,256]{1,0:T(8,128)(2,1)S(1)}, u32[]{:S(2)}, u32[]{:S(2)}) %collective-permute-start.4) | collective-permute-done | bytes 32800 | tf_op jit(solution)/shard_map/ppermute | solution.py:30
  25.5 0.6 collective-permute-start.5
  26.1 2.9 %collective-permute-done.7 = bf16[256,256]{1,0:T(8,128)(2,1)S(1)} collective-permute-done((bf16[256,256]{1,0:T(8,128)(2,1)S(1)}, bf16[256,256]{1,0:T(8,128)(2,1)S(1)}, u32[]{:S(2)}, u32[]{:S(2)}) %collective-permute-start.7) | collective-permute-done | bytes 131104 | tf_op jit(solution)/shard_map/ppermute | solution.py:47
  29.0 0.6 gather_fusion.1
  29.6 0.1 broadcast_select_fusion
  29.7 0.3 fusion.2
  30.1 0.9 %copy-done.4 = bf16[256,256]{1,0:T(8,128)(2,1)S(1)} copy-done((bf16[256,256]{1,0:T(8,128)(2,1)S(1)}, bf16[256,256]{1,0:T(8,128)(2,1)}, u32[]{:S(2)}) %copy-start.4) | copy-done | bytes 131096
  31.0 0.2 fusion.17
  31.2 0.7 copy-done.1
  31.9 0.3 convolution_multiply_fusion
  32.2 0.3 fusion.28
  32.5 0.3 fusion.29
  32.9 2.3 %collective-permute-start.8 = (f32[2,128,256]{2,1,0:T(8,128)S(1)}, f32[2,128,256]{2,1,0:T(8,128)S(1)}, u32[]{:S(2)}, u32[]{:S(2)}) collective-permute-start(f32[2,128,256]{2,1,0:T(8,128)S(1)} %dynamic-slice_bitcast_fusion), channel_id=1, source_target_pairs={{0,1},{1,0},{2,3},{3,2},{4,5},{5,4},{6,7},{7,6},{8,9},{9,8},{10,11... | collective-permute-start | bytes 786440 | tf_op jit(solution)/shard_map/ppermute | solution.py:23
  35.2 1.2 %collective-permute-done.8 = f32[2,128,256]{2,1,0:T(8,128)S(1)} collective-permute-done((f32[2,128,256]{2,1,0:T(8,128)S(1)}, f32[2,128,256]{2,1,0:T(8,128)S(1)}, u32[]{:S(2)}, u32[]{:S(2)}) %collective-permute-start.8) | collective-permute-done | bytes 262176 | tf_op jit(solution)/shard_map/ppermute | solution.py:23
  36.4 3.2 %collective-permute-start.9 = (f32[128,256]{1,0:T(8,128)S(1)}, f32[128,256]{1,0:T(8,128)S(1)}, u32[]{:S(2)}, u32[]{:S(2)}) collective-permute-start(f32[128,256]{1,0:T(8,128)S(1)} %dynamic-slice_bitcast_fusion.2), channel_id=1, source_target_pairs={{0,2},{1,3},{2,0},{3,1},{4,6},{5,7},{6,4},{7,5},{8,10},{9,11},{10,... | collective-permute-start | bytes 393224 | tf_op jit(solution)/shard_map/ppermute | solution.py:23
  39.7 3.8 %collective-permute-done.9 = f32[128,256]{1,0:T(8,128)S(1)} collective-permute-done((f32[128,256]{1,0:T(8,128)S(1)}, f32[128,256]{1,0:T(8,128)S(1)}, u32[]{:S(2)}, u32[]{:S(2)}) %collective-permute-start.9) | collective-permute-done | bytes 131104 | tf_op jit(solution)/shard_map/ppermute | solution.py:23
  43.5 11.7 %all_to_all.10 = f32[8,16,256]{2,1,0:T(8,128)S(1)} all-to-all(f32[8,16,256]{2,1,0:T(8,128)S(1)} %bitcast.111), channel_id=1, replica_groups=mesh['row'=8,'rep'=4] {'row'}, dimensions={0} | all-to-all | bytes 262144 | tf_op jit(solution)/shard_map/all_to_all | solution.py:152
  55.2 1.1 %collective-permute-start.11 = (bf16[256,256]{1,0:T(8,128)(2,1)S(1)}, bf16[256,256]{1,0:T(8,128)(2,1)S(1)}, u32[]{:S(2)}, u32[]{:S(2)}) collective-permute-start(bf16[256,256]{1,0:T(8,128)(2,1)S(1)} %get-tuple-element.12), channel_id=1, source_target_pairs={{5,0},{15,1},{21,2},{31,3},{1,4},{11,5},{17,6},{27,7},{6,8},{12,9}... | collective-permute-start | bytes 393224 | tf_op jit(solution)/shard_map/ppermute | solution.py:47
  56.4 0.7 collective-permute-start.10
  57.1 0.7 broadcast_in_dim.40
  57.7 6.0 %all-to-all-start.1 = ((f32[8,16,256]{2,1,0:T(8,128)}), f32[8,16,256]{2,1,0:T(8,128)S(1)}, u32[]{:S(2)}, u32[]{:S(2)}) async-start(f32[8,16,256]{2,1,0:T(8,128)} %broadcast_in_dim.40), calls=%async_computation.1 | async-start | bytes 262144 | tf_op jit(solution)/shard_map/all_to_all | solution.py:155
  63.8 0.6 gather_fusion.2
  64.4 0.1 broadcast_select_fusion.2
  64.5 0.3 fusion
  64.9 6.2 %all-to-all-done.1 = f32[8,16,256]{2,1,0:T(8,128)S(1)} async-done(((f32[8,16,256]{2,1,0:T(8,128)}), f32[8,16,256]{2,1,0:T(8,128)S(1)}, u32[]{:S(2)}, u32[]{:S(2)}) %all-to-all-start.1) | async-done | bytes 131104 | tf_op jit(solution)/shard_map/all_to_all | solution.py:155
  71.1 1.7 %collective-permute-start.14 = (f32[128,256]{1,0:T(8,128)S(1)}, f32[128,256]{1,0:T(8,128)S(1)}, u32[]{:S(2)}, u32[]{:S(2)}) collective-permute-start(f32[128,256]{1,0:T(8,128)S(1)} %bitcast.108), channel_id=1, source_target_pairs={{0,2},{1,3},{2,0},{3,1},{4,6},{5,7},{6,4},{7,5},{8,10},{9,11},{10,... | collective-permute-start | bytes 393224 | tf_op jit(solution)/shard_map/ppermute | solution.py:30
  72.8 0.4 collective-permute-start.13
  73.2 2.8 %collective-permute-done.14 = f32[128,256]{1,0:T(8,128)S(1)} collective-permute-done((f32[128,256]{1,0:T(8,128)S(1)}, f32[128,256]{1,0:T(8,128)S(1)}, u32[]{:S(2)}, u32[]{:S(2)}) %collective-permute-start.14) | collective-permute-done | bytes 131104 | tf_op jit(solution)/shard_map/ppermute | solution.py:30
  76.2 1.0 %collective-permute-done.13 = f32[64,256]{1,0:T(8,128)S(1)} collective-permute-done((f32[64,256]{1,0:T(8,128)S(1)}, f32[64,256]{1,0:T(8,128)S(1)}, u32[]{:S(2)}, u32[]{:S(2)}) %collective-permute-start.13) | collective-permute-done | bytes 65568 | tf_op jit(solution)/shard_map/ppermute | solution.py:23
  77.2 0.8 convolution_convert_fusion
  78.0 0.8 %pad_maximum_fusion.1 = (f32[1,2,128,256]{3,2,1,0:T(8,128)}, f32[1,2,128,256]{3,2,1,0:T(8,128)}) fusion(f32[2,1,128,256]{3,2,1,0:T(8,128)S(1)} %get-tuple-element.18, f32[2,1,128,256]{3,2,1,0:T(8,128)S(1)} %get-tuple-element.19), kind=kLoop, calls=%fused_computation.21 | loop fusion | flops 131072 | bytes 1048576 | tf_op jit(solution)/shard_map/stack | solution.py:33
  (43 shorter events, 0.7 us)
Async XLA Ops:
  0.6 10.3 %copy-start = (bf16[1,1,2,4,128,128]{5,4,3,2,1,0:T(8,128)(2,1)S(1)}, bf16[1,1,2,4,128,128]{5,4,3,2,1,0:T(8,128)(2,1)}, u32[]{:S(2)}) copy-start(bf16[1,1,2,4,128,128]{5,4,3,2,1,0:T(8,128)(2,1)} %param.15) | copy-start | bytes 786436
  0.6 9.6 %collective-permute-start.1 = (bf16[256,256]{1,0:T(8,128)(2,1)}, bf16[256,256]{1,0:T(8,128)(2,1)S(1)}, u32[]{:S(2)}, u32[]{:S(2)}) collective-permute-start(bf16[256,256]{1,0:T(8,128)(2,1)} %param.9), channel_id=1, source_target_pairs={{5,0},{15,1},{21,2},{31,3},{1,4},{11,5},{17,6},{27,7},{6,8},{12,9}... | collective-permute-start | bytes 393224 | tf_op jit(solution)/shard_map/ppermute | solution.py:47
  6.7 3.5 %collective-permute-start = (bf16[256,256]{1,0:T(8,128)(2,1)}, bf16[256,256]{1,0:T(8,128)(2,1)S(1)}, u32[]{:S(2)}, u32[]{:S(2)}) collective-permute-start(bf16[256,256]{1,0:T(8,128)(2,1)} %param.9), channel_id=1, source_target_pairs={{0,0},{10,1},{16,2},{26,3},{4,4},{14,5},{20,6},{30,7},{1,8},{11,9}... | collective-permute-start | bytes 393224 | tf_op jit(solution)/shard_map/ppermute | solution.py:47
  8.3 0.7 copy-start.2
  9.1 0.7 copy-start.5
  11.3 3.3 %collective-permute-start.2 = (f32[2,64,256]{2,1,0:T(8,128)S(1)}, f32[2,64,256]{2,1,0:T(8,128)S(1)}, u32[]{:S(2)}, u32[]{:S(2)}) collective-permute-start(f32[2,64,256]{2,1,0:T(8,128)S(1)} %dynamic-slice_bitcast_fusion.3), channel_id=1, source_target_pairs={{0,1},{1,0},{2,3},{3,2},{4,5},{5,4},{6,7},{7,6},{8,9},{9,8},{10,11... | collective-permute-start | bytes 393224 | tf_op jit(solution)/shard_map/ppermute | solution.py:106
  14.7 8.7 %copy-start.3 = (bf16[256,256]{1,0:T(8,128)(2,1)S(1)}, bf16[256,256]{1,0:T(8,128)(2,1)}, u32[]{:S(2)}) copy-start(bf16[256,256]{1,0:T(8,128)(2,1)} %param.10) | copy-start | bytes 393220
  14.7 6.8 %collective-permute-start.3 = (f32[64,256]{1,0:T(8,128)S(1)}, f32[64,256]{1,0:T(8,128)S(1)}, u32[]{:S(2)}, u32[]{:S(2)}) collective-permute-start(f32[64,256]{1,0:T(8,128)S(1)} %dynamic-slice_bitcast_fusion.5), channel_id=1, source_target_pairs={{0,2},{1,3},{2,0},{3,1},{4,6},{5,7},{6,4},{7,5},{8,10},{9,11},{10,... | collective-permute-start | bytes 196616 | tf_op jit(solution)/shard_map/ppermute | solution.py:106
  21.5 4.0 %collective-permute-start.4 = (bf16[64,256]{1,0:T(8,128)(2,1)S(1)}, bf16[64,256]{1,0:T(8,128)(2,1)S(1)}, u32[]{:S(2)}, u32[]{:S(2)}) collective-permute-start(bf16[64,256]{1,0:T(8,128)(2,1)S(1)} %fusion.19), channel_id=1, source_target_pairs={{0,2},{1,3},{2,0},{3,1},{4,6},{5,7},{6,4},{7,5},{8,10},{9,11},{10,... | collective-permute-start | bytes 98312 | tf_op jit(solution)/shard_map/ppermute | solution.py:30
  23.4 5.6 %collective-permute-start.7 = (bf16[256,256]{1,0:T(8,128)(2,1)S(1)}, bf16[256,256]{1,0:T(8,128)(2,1)S(1)}, u32[]{:S(2)}, u32[]{:S(2)}) collective-permute-start(bf16[256,256]{1,0:T(8,128)(2,1)S(1)} %copy-done.3), channel_id=1, source_target_pairs={{5,0},{15,1},{21,2},{31,3},{1,4},{11,5},{17,6},{27,7},{6,8},{12,9}... | collective-permute-start | bytes 393224 | tf_op jit(solution)/shard_map/ppermute | solution.py:47
  23.7 5.2 %collective-permute-start.6 = (bf16[256,256]{1,0:T(8,128)(2,1)S(1)}, bf16[256,256]{1,0:T(8,128)(2,1)S(1)}, u32[]{:S(2)}, u32[]{:S(2)}) collective-permute-start(bf16[256,256]{1,0:T(8,128)(2,1)S(1)} %copy-done.3), channel_id=1, source_target_pairs={{0,0},{10,1},{16,2},{26,3},{4,4},{14,5},{20,6},{30,7},{1,8},{11,9}... | collective-permute-start | bytes 393224 | tf_op jit(solution)/shard_map/ppermute | solution.py:47
  25.5 4.5 %collective-permute-start.5 = (bf16[2,64,256]{2,1,0:T(8,128)(2,1)S(1)}, bf16[2,64,256]{2,1,0:T(8,128)(2,1)S(1)}, u32[]{:S(2)}, u32[]{:S(2)}) collective-permute-start(bf16[2,64,256]{2,1,0:T(8,128)(2,1)S(1)} %pad_maximum_fusion.7), channel_id=1, source_target_pairs={{0,1},{1,0},{2,3},{3,2},{4,5},{5,4},{6,7},{7,6},{8,9},{9,8},{10,11... | collective-permute-start | bytes 196616 | tf_op jit(solution)/shard_map/ppermute | solution.py:30
  30.1 0.9 %copy-start.4 = (bf16[256,256]{1,0:T(8,128)(2,1)S(1)}, bf16[256,256]{1,0:T(8,128)(2,1)}, u32[]{:S(2)}) copy-start(bf16[256,256]{1,0:T(8,128)(2,1)} %param.11) | copy-start | bytes 393220
  31.0 0.9 %copy-start.1 = (bf16[256,256]{1,0:T(8,128)(2,1)S(1)}, bf16[256,256]{1,0:T(8,128)(2,1)}, u32[]{:S(2)}) copy-start(bf16[256,256]{1,0:T(8,128)(2,1)} %param.12) | copy-start | bytes 393220
  32.9 3.5 %collective-permute-start.8 = (f32[2,128,256]{2,1,0:T(8,128)S(1)}, f32[2,128,256]{2,1,0:T(8,128)S(1)}, u32[]{:S(2)}, u32[]{:S(2)}) collective-permute-start(f32[2,128,256]{2,1,0:T(8,128)S(1)} %dynamic-slice_bitcast_fusion), channel_id=1, source_target_pairs={{0,1},{1,0},{2,3},{3,2},{4,5},{5,4},{6,7},{7,6},{8,9},{9,8},{10,11... | collective-permute-start | bytes 786440 | tf_op jit(solution)/shard_map/ppermute | solution.py:23
  36.4 7.0 %collective-permute-start.9 = (f32[128,256]{1,0:T(8,128)S(1)}, f32[128,256]{1,0:T(8,128)S(1)}, u32[]{:S(2)}, u32[]{:S(2)}) collective-permute-start(f32[128,256]{1,0:T(8,128)S(1)} %dynamic-slice_bitcast_fusion.2), channel_id=1, source_target_pairs={{0,2},{1,3},{2,0},{3,1},{4,6},{5,7},{6,4},{7,5},{8,10},{9,11},{10,... | collective-permute-start | bytes 393224 | tf_op jit(solution)/shard_map/ppermute | solution.py:23
  55.2 8.5 %collective-permute-start.11 = (bf16[256,256]{1,0:T(8,128)(2,1)S(1)}, bf16[256,256]{1,0:T(8,128)(2,1)S(1)}, u32[]{:S(2)}, u32[]{:S(2)}) collective-permute-start(bf16[256,256]{1,0:T(8,128)(2,1)S(1)} %get-tuple-element.12), channel_id=1, source_target_pairs={{5,0},{15,1},{21,2},{31,3},{1,4},{11,5},{17,6},{27,7},{6,8},{12,9}... | collective-permute-start | bytes 393224 | tf_op jit(solution)/shard_map/ppermute | solution.py:47
  56.4 7.4 %collective-permute-start.10 = (bf16[256,256]{1,0:T(8,128)(2,1)S(1)}, bf16[256,256]{1,0:T(8,128)(2,1)S(1)}, u32[]{:S(2)}, u32[]{:S(2)}) collective-permute-start(bf16[256,256]{1,0:T(8,128)(2,1)S(1)} %get-tuple-element.12), channel_id=1, source_target_pairs={{0,0},{10,1},{16,2},{26,3},{4,4},{14,5},{20,6},{30,7},{1,8},{11,9}... | collective-permute-start | bytes 393224 | tf_op jit(solution)/shard_map/ppermute | solution.py:47
  57.7 13.4 %all-to-all-start.1 = ((f32[8,16,256]{2,1,0:T(8,128)}), f32[8,16,256]{2,1,0:T(8,128)S(1)}, u32[]{:S(2)}, u32[]{:S(2)}) async-start(f32[8,16,256]{2,1,0:T(8,128)} %broadcast_in_dim.40), calls=%async_computation.1 | async-start | bytes 262144 | tf_op jit(solution)/shard_map/all_to_all | solution.py:155
  64.8 8.0 %collective-permute-start.12 = (f32[2,64,256]{2,1,0:T(8,128)S(1)}, f32[2,64,256]{2,1,0:T(8,128)S(1)}, u32[]{:S(2)}, u32[]{:S(2)}) collective-permute-start(f32[2,64,256]{2,1,0:T(8,128)S(1)} %dynamic-slice_bitcast_fusion.1), channel_id=1, source_target_pairs={{0,1},{1,0},{2,3},{3,2},{4,5},{5,4},{6,7},{7,6},{8,9},{9,8},{10,11... | collective-permute-start | bytes 393224 | tf_op jit(solution)/shard_map/ppermute | solution.py:23
  71.1 5.0 %collective-permute-start.14 = (f32[128,256]{1,0:T(8,128)S(1)}, f32[128,256]{1,0:T(8,128)S(1)}, u32[]{:S(2)}, u32[]{:S(2)}) collective-permute-start(f32[128,256]{1,0:T(8,128)S(1)} %bitcast.108), channel_id=1, source_target_pairs={{0,2},{1,3},{2,0},{3,1},{4,6},{5,7},{6,4},{7,5},{8,10},{9,11},{10,... | collective-permute-start | bytes 393224 | tf_op jit(solution)/shard_map/ppermute | solution.py:30
  72.8 4.3 %collective-permute-start.13 = (f32[64,256]{1,0:T(8,128)S(1)}, f32[64,256]{1,0:T(8,128)S(1)}, u32[]{:S(2)}, u32[]{:S(2)}) collective-permute-start(f32[64,256]{1,0:T(8,128)S(1)} %dynamic-slice_bitcast_fusion.4), channel_id=1, source_target_pairs={{0,2},{1,3},{2,0},{3,1},{4,6},{5,7},{6,4},{7,5},{8,10},{9,11},{10,... | collective-permute-start | bytes 196616 | tf_op jit(solution)/shard_map/ppermute | solution.py:23
  76.1 1.8 %collective-permute-start.15 = (f32[2,128,256]{2,1,0:T(8,128)S(1)}, f32[2,128,256]{2,1,0:T(8,128)S(1)}, u32[]{:S(2)}, u32[]{:S(2)}) collective-permute-start(f32[2,128,256]{2,1,0:T(8,128)S(1)} %pad_maximum_fusion.5), channel_id=1, source_target_pairs={{0,1},{1,0},{2,3},{3,2},{4,5},{5,4},{6,7},{7,6},{8,9},{9,8},{10,11... | collective-permute-start | bytes 786440 | tf_op jit(solution)/shard_map/ppermute | solution.py:30

commit v15 on v10

--- a/solution.py
+++ b/solution.py
@@ -123,7 +123,6 @@
         precision=lax.Precision.HIGHEST,
         preferred_element_type=jnp.float32,
     )
-    hidden_full = gather_rep(hidden)
     grads = jnp.concatenate([grad_one, grad_two], axis=0)
     grad_rows = grads.shape[0] // copies
     quarter = reduce_scatter_bits(
@@ -134,7 +133,8 @@
     else:
         parts = quarter.reshape(rows, -1)
     mine = lax.all_to_all(parts, "row", 0, 0, tiled=False).sum(axis=0)
-    hidden_full, mine = lax.optimization_barrier((hidden_full, mine))
+    hidden, mine = lax.optimization_barrier((hidden, mine))
+    hidden_full = gather_rep(hidden)
     pieces_two = gather_rounds(hidden_full, rows, copies)
     spread = lax.all_to_all(jnp.broadcast_to(mine, parts.shape), "row", 0, 0, tiled=False)
     quarter = spread.reshape(grad_rows, feature_width)

time: 75 us -> 79.4 us (1.059)
  blocking collectives: 0 us -> 13.1 us
  starting transfers between devices: 34.1 us -> 27.3 us
  waiting for transfers between devices: 30.8 us -> 29.7 us
    all_to_all x0 -> x1, blocking collectives: none -> 13.1 us  [shards(): mine = lax.all_to_all(parts, 'row', 0, 0, tiled=False).sum(axis=0)]
    all_to_all x1 -> x0, waiting for transfers between devices: 7.27 us -> none  [shards(): mine = lax.all_to_all(parts, 'row', 0, 0, tiled=False).sum(axis=0)]
    all_to_all x1 -> x0, starting transfers between devices: 5.65 us -> none  [shards(): mine = lax.all_to_all(parts, 'row', 0, 0, tiled=False).sum(axis=0)]
    ppermute x4, waiting for transfers between devices: 3.43 us -> 7.73 us  [all_gather_bits(): other = lax.ppermute(z, AXES, bit_pairs(devices, bit))]
    ppermute x6, waiting for transfers between devices: 9.34 us -> 11.2 us  [reduce_scatter_bits(): y = keep + lax.ppermute(send, AXES, bit_pairs(devices, bit))]
    ppermute x4, starting transfers between devices: 3.66 us -> 2.2 us  [all_gather_bits(): other = lax.ppermute(z, AXES, bit_pairs(devices, bit))]
  transfers between devices with their start and end apart: 16 -> 15, of which waited for: 9 -> 10; matrix products, arithmetic and copies ran while one was open for 5% -> 3% of each run, Pallas kernels for 0% -> 0%
where the time goes in v15:
time: 79.4 us; the launch traced here: 79.1 us
  waiting for transfers between devices  29.7 us (37%)
  starting transfers between devices  27.3 us (34%)
  blocking collectives  13.1 us (16%)
  local copies, waits for them, and re-layouts  4.34 us (5%)
  matrix products  2.46 us (3%)
  other arithmetic  1.31 us (2%)
  between operations  0.98 us (1%)
    all_to_all x1, blocking collectives, shards(): mine = lax.all_to_all(parts, 'row', 0, 0, tiled=False).sum(axis=0)  13.1 us
    ppermute x6, waiting for transfers between devices, reduce_scatter_bits(): y = keep + lax.ppermute(send, AXES, bit_pairs(devices, bit))  11.2 us
    ppermute x6, starting transfers between devices, reduce_scatter_bits(): y = keep + lax.ppermute(send, AXES, bit_pairs(devices, bit))  10.5 us
    ppermute x4, starting transfers between devices, gather_rounds(): pieces.append(lax.ppermute(x, AXES, pairs))  8.57 us
    ppermute x4, waiting for transfers between devices, all_gather_bits(): other = lax.ppermute(z, AXES, bit_pairs(devices, bit))  7.73 us
    all_to_all x1, waiting for transfers between devices, shards(): lax.all_to_all(jnp.broadcast_to(mine, parts.shape), 'row', 0, 0, tiled=Fa...  6.27 us
    all_to_all x1, starting transfers between devices, shards(): lax.all_to_all(jnp.broadcast_to(mine, parts.shape), 'row', 0, 0, tiled=Fa...  6.01 us
    ppermute x4, waiting for transfers between devices, gather_rounds(): pieces.append(lax.ppermute(x, AXES, pairs))  4.44 us
  transfers between devices with their start and end apart: 15, of which 10 were waited for; matrix products, arithmetic and copies ran while one was open for 3% of the time, Pallas kernels for 0%

profile of v15, /device:TPU:0, one launch (start us, length us, event | category | flops | bytes accessed | tf_op | source)
XLA Modules:
  0.0 79.1 jit_solution(2513507186145913428)
XLA Ops:
  0.6 0.0 copy-start
  0.7 1.0 %constant_dynamic-update-slice_fusion.1 = bf16[256,512]{1,0:T(8,128)(2,1)S(1)} fusion(bf16[256,256]{1,0:T(8,128)(2,1)} %param.7), kind=kLoop, calls=%fused_computation.63 | loop fusion | bytes 262144
  1.6 0.0 copy-done.1
  1.7 6.1 %collective-permute-start.1 = (bf16[256,512]{1,0:T(8,128)(2,1)S(1)}, bf16[256,512]{1,0:T(8,128)(2,1)S(1)}, u32[]{:S(2)}, u32[]{:S(2)}) collective-permute-start(bf16[256,512]{1,0:T(8,128)(2,1)S(1)} %constant_dynamic-update-slice_fusion), channel_id=1, source_target_pairs={{5,0},{15,1},{21,2},{31,3},{1,4},{11,5},{17,6},{27,7},{6,8},{12,9}... | collective-permute-start | bytes 786440 | tf_op jit(solution)/shard_map/ppermute | solution.py:47
  7.8 0.7 collective-permute-start
  8.4 0.0 copy-start.3
  8.5 0.0 copy-start.4
  8.5 0.7 copy-done.3
  9.1 0.1 compare_and_fusion
  9.2 0.1 sub.74
  9.3 4.4 %collective-permute-done.1 = bf16[256,512]{1,0:T(8,128)(2,1)S(1)} collective-permute-done((bf16[256,512]{1,0:T(8,128)(2,1)S(1)}, bf16[256,512]{1,0:T(8,128)(2,1)S(1)}, u32[]{:S(2)}, u32[]{:S(2)}) %collective-permute-start.1) | collective-permute-done | bytes 262176 | tf_op jit(solution)/shard_map/ppermute | solution.py:47
  13.8 0.1 pad_maximum_fusion
  13.8 0.6 gather_fusion
  14.4 0.4 fusion.1
  14.9 4.9 %collective-permute-start.2 = (f32[2,64,512]{2,1,0:T(8,128)S(1)}, f32[2,64,512]{2,1,0:T(8,128)S(1)}, u32[]{:S(2)}, u32[]{:S(2)}) collective-permute-start(f32[2,64,512]{2,1,0:T(8,128)S(1)} %dynamic-slice_bitcast_fusion.1), channel_id=1, source_target_pairs={{0,1},{1,0},{2,3},{3,2},{4,5},{5,4},{6,7},{7,6},{8,9},{9,8},{10,11... | collective-permute-start | bytes 786440 | tf_op jit(solution)/shard_map/ppermute | solution.py:23
  19.8 1.2 %collective-permute-done.2 = f32[2,64,512]{2,1,0:T(8,128)S(1)} collective-permute-done((f32[2,64,512]{2,1,0:T(8,128)S(1)}, f32[2,64,512]{2,1,0:T(8,128)S(1)}, u32[]{:S(2)}, u32[]{:S(2)}) %collective-permute-start.2) | collective-permute-done | bytes 262176 | tf_op jit(solution)/shard_map/ppermute | solution.py:23
  21.0 3.3 %collective-permute-start.3 = (f32[64,512]{1,0:T(8,128)S(1)}, f32[64,512]{1,0:T(8,128)S(1)}, u32[]{:S(2)}, u32[]{:S(2)}) collective-permute-start(f32[64,512]{1,0:T(8,128)S(1)} %dynamic-slice_bitcast_fusion.4), channel_id=1, source_target_pairs={{0,2},{1,3},{2,0},{3,1},{4,6},{5,7},{6,4},{7,5},{8,10},{9,11},{10,... | collective-permute-start | bytes 393224 | tf_op jit(solution)/shard_map/ppermute | solution.py:23
  24.3 3.8 %collective-permute-done.3 = f32[64,512]{1,0:T(8,128)S(1)} collective-permute-done((f32[64,512]{1,0:T(8,128)S(1)}, f32[64,512]{1,0:T(8,128)S(1)}, u32[]{:S(2)}, u32[]{:S(2)}) %collective-permute-start.3) | collective-permute-done | bytes 131104 | tf_op jit(solution)/shard_map/ppermute | solution.py:23
  28.1 0.2 fusion.23
  28.3 0.0 copy-start.2
  28.3 0.3 fusion.19
  28.6 0.6 copy-done.2
  29.2 0.3 fusion
  29.5 0.2 fusion.26
  29.7 0.1 collective-permute-start.4
  29.8 1.5 %collective-permute-done.4 = f32[2,128,256]{2,1,0:T(8,128)S(1)} collective-permute-done((f32[2,128,256]{2,1,0:T(8,128)S(1)}, f32[2,128,256]{2,1,0:T(8,128)S(1)}, u32[]{:S(2)}, u32[]{:S(2)}) %collective-permute-start.4) | collective-permute-done | bytes 262176 | tf_op jit(solution)/shard_map/ppermute | solution.py:23
  31.4 1.8 %collective-permute-start.5 = (f32[128,256]{1,0:T(8,128)S(1)}, f32[128,256]{1,0:T(8,128)S(1)}, u32[]{:S(2)}, u32[]{:S(2)}) collective-permute-start(f32[128,256]{1,0:T(8,128)S(1)} %dynamic-slice_bitcast_fusion.3), channel_id=1, source_target_pairs={{0,2},{1,3},{2,0},{3,1},{4,6},{5,7},{6,4},{7,5},{8,10},{9,11},{10,... | collective-permute-start | bytes 393224 | tf_op jit(solution)/shard_map/ppermute | solution.py:23
  33.2 3.8 %collective-permute-done.5 = f32[128,256]{1,0:T(8,128)S(1)} collective-permute-done((f32[128,256]{1,0:T(8,128)S(1)}, f32[128,256]{1,0:T(8,128)S(1)}, u32[]{:S(2)}, u32[]{:S(2)}) %collective-permute-start.5) | collective-permute-done | bytes 131104 | tf_op jit(solution)/shard_map/ppermute | solution.py:23
  37.0 13.1 %all_to_all.10 = f32[8,16,256]{2,1,0:T(8,128)S(1)} all-to-all(f32[8,16,256]{2,1,0:T(8,128)S(1)} %bitcast.110), channel_id=1, replica_groups=mesh['row'=8,'rep'=4] {'row'}, dimensions={0} | all-to-all | bytes 262144 | tf_op jit(solution)/shard_map/all_to_all | solution.py:135
  50.1 0.4 collective-permute-start.6
  50.5 3.6 %collective-permute-done.6 = bf16[64,256]{1,0:T(8,128)(2,1)S(1)} collective-permute-done((bf16[64,256]{1,0:T(8,128)(2,1)S(1)}, bf16[64,256]{1,0:T(8,128)(2,1)S(1)}, u32[]{:S(2)}, u32[]{:S(2)}) %collective-permute-start.6) | collective-permute-done | bytes 32800 | tf_op jit(solution)/shard_map/ppermute | solution.py:30
  54.2 0.1 collective-permute-start.7
  54.2 1.2 %collective-permute-done.7 = bf16[2,64,256]{2,1,0:T(8,128)(2,1)S(1)} collective-permute-done((bf16[2,64,256]{2,1,0:T(8,128)(2,1)S(1)}, bf16[2,64,256]{2,1,0:T(8,128)(2,1)S(1)}, u32[]{:S(2)}, u32[]{:S(2)}) %collective-permute-start.7) | collective-permute-done | bytes 65568 | tf_op jit(solution)/shard_map/ppermute | solution.py:30
  55.5 1.1 %collective-permute-start.9 = (bf16[256,256]{1,0:T(8,128)(2,1)S(1)}, bf16[256,256]{1,0:T(8,128)(2,1)S(1)}, u32[]{:S(2)}, u32[]{:S(2)}) collective-permute-start(bf16[256,256]{1,0:T(8,128)(2,1)S(1)} %bitcast.118), channel_id=1, source_target_pairs={{5,0},{15,1},{21,2},{31,3},{1,4},{11,5},{17,6},{27,7},{6,8},{12,9}... | collective-permute-start | bytes 393224 | tf_op jit(solution)/shard_map/ppermute | solution.py:47
  56.7 0.7 collective-permute-start.8
  57.3 0.7 broadcast_in_dim.59
  58.0 6.0 %all-to-all-start.1 = ((f32[8,16,256]{2,1,0:T(8,128)}), f32[8,16,256]{2,1,0:T(8,128)S(1)}, u32[]{:S(2)}, u32[]{:S(2)}) async-start(f32[8,16,256]{2,1,0:T(8,128)} %broadcast_in_dim.59), calls=%async_computation.1 | async-start | bytes 262144 | tf_op jit(solution)/shard_map/all_to_all | solution.py:139
  64.1 0.6 gather_fusion.1
  64.7 0.3 fusion.6
  65.0 0.1 collective-permute-start.10
  65.1 6.3 %all-to-all-done.1 = f32[8,16,256]{2,1,0:T(8,128)S(1)} async-done(((f32[8,16,256]{2,1,0:T(8,128)}), f32[8,16,256]{2,1,0:T(8,128)S(1)}, u32[]{:S(2)}, u32[]{:S(2)}) %all-to-all-start.1) | async-done | bytes 131104 | tf_op jit(solution)/shard_map/all_to_all | solution.py:139
  71.4 1.7 %collective-permute-start.12 = (f32[128,256]{1,0:T(8,128)S(1)}, f32[128,256]{1,0:T(8,128)S(1)}, u32[]{:S(2)}, u32[]{:S(2)}) collective-permute-start(f32[128,256]{1,0:T(8,128)S(1)} %bitcast.107), channel_id=1, source_target_pairs={{0,2},{1,3},{2,0},{3,1},{4,6},{5,7},{6,4},{7,5},{8,10},{9,11},{10,... | collective-permute-start | bytes 393224 | tf_op jit(solution)/shard_map/ppermute | solution.py:30
  73.1 0.4 collective-permute-start.11
  73.5 2.9 %collective-permute-done.12 = f32[128,256]{1,0:T(8,128)S(1)} collective-permute-done((f32[128,256]{1,0:T(8,128)S(1)}, f32[128,256]{1,0:T(8,128)S(1)}, u32[]{:S(2)}, u32[]{:S(2)}) %collective-permute-start.12) | collective-permute-done | bytes 131104 | tf_op jit(solution)/shard_map/ppermute | solution.py:30
  76.4 0.1 collective-permute-start.13
  76.5 1.0 %collective-permute-done.11 = f32[64,256]{1,0:T(8,128)S(1)} collective-permute-done((f32[64,256]{1,0:T(8,128)S(1)}, f32[64,256]{1,0:T(8,128)S(1)}, u32[]{:S(2)}, u32[]{:S(2)}) %collective-permute-start.11) | collective-permute-done | bytes 65568 | tf_op jit(solution)/shard_map/ppermute | solution.py:23
  77.5 0.8 convolution_convert_fusion
  78.3 0.8 %pad_maximum_fusion.2 = (f32[1,2,128,256]{3,2,1,0:T(8,128)}, f32[1,2,128,256]{3,2,1,0:T(8,128)}) fusion(f32[2,1,128,256]{3,2,1,0:T(8,128)S(1)} %get-tuple-element.11, f32[2,1,128,256]{3,2,1,0:T(8,128)S(1)} %get-tuple-element.12), kind=kLoop, calls=%fused_computation.22 | loop fusion | flops 131072 | bytes 1048576 | tf_op jit(solution)/shard_map/stack | solution.py:33
  (35 shorter events, 0.5 us)
Async XLA Ops:
  0.6 13.8 %copy-start = (bf16[1,1,2,4,128,128]{5,4,3,2,1,0:T(8,128)(2,1)S(1)}, bf16[1,1,2,4,128,128]{5,4,3,2,1,0:T(8,128)(2,1)}, u32[]{:S(2)}) copy-start(bf16[1,1,2,4,128,128]{5,4,3,2,1,0:T(8,128)(2,1)} %param.13) | copy-start | bytes 786436
  0.6 1.0 %copy-start.1 = (bf16[256,256]{1,0:T(8,128)(2,1)S(1)}, bf16[256,256]{1,0:T(8,128)(2,1)}, u32[]{:S(2)}) copy-start(bf16[256,256]{1,0:T(8,128)(2,1)} %param.8) | copy-start | bytes 393220
  1.7 12.1 %collective-permute-start.1 = (bf16[256,512]{1,0:T(8,128)(2,1)S(1)}, bf16[256,512]{1,0:T(8,128)(2,1)S(1)}, u32[]{:S(2)}, u32[]{:S(2)}) collective-permute-start(bf16[256,512]{1,0:T(8,128)(2,1)S(1)} %constant_dynamic-update-slice_fusion), channel_id=1, source_target_pairs={{5,0},{15,1},{21,2},{31,3},{1,4},{11,5},{17,6},{27,7},{6,8},{12,9}... | collective-permute-start | bytes 786440 | tf_op jit(solution)/shard_map/ppermute | solution.py:47
  7.8 6.0 %collective-permute-start = (bf16[256,512]{1,0:T(8,128)(2,1)S(1)}, bf16[256,512]{1,0:T(8,128)(2,1)S(1)}, u32[]{:S(2)}, u32[]{:S(2)}) collective-permute-start(bf16[256,512]{1,0:T(8,128)(2,1)S(1)} %constant_dynamic-update-slice_fusion), channel_id=1, source_target_pairs={{0,0},{10,1},{16,2},{26,3},{4,4},{14,5},{20,6},{30,7},{1,8},{11,9}... | collective-permute-start | bytes 786440 | tf_op jit(solution)/shard_map/ppermute | solution.py:47
  8.4 0.7 copy-start.3
  8.5 0.7 copy-start.4
  14.9 6.0 %collective-permute-start.2 = (f32[2,64,512]{2,1,0:T(8,128)S(1)}, f32[2,64,512]{2,1,0:T(8,128)S(1)}, u32[]{:S(2)}, u32[]{:S(2)}) collective-permute-start(f32[2,64,512]{2,1,0:T(8,128)S(1)} %dynamic-slice_bitcast_fusion.1), channel_id=1, source_target_pairs={{0,1},{1,0},{2,3},{3,2},{4,5},{5,4},{6,7},{7,6},{8,9},{9,8},{10,11... | collective-permute-start | bytes 786440 | tf_op jit(solution)/shard_map/ppermute | solution.py:23
  21.0 7.1 %collective-permute-start.3 = (f32[64,512]{1,0:T(8,128)S(1)}, f32[64,512]{1,0:T(8,128)S(1)}, u32[]{:S(2)}, u32[]{:S(2)}) collective-permute-start(f32[64,512]{1,0:T(8,128)S(1)} %dynamic-slice_bitcast_fusion.4), channel_id=1, source_target_pairs={{0,2},{1,3},{2,0},{3,1},{4,6},{5,7},{6,4},{7,5},{8,10},{9,11},{10,... | collective-permute-start | bytes 393224 | tf_op jit(solution)/shard_map/ppermute | solution.py:23
  24.3 3.8 %copy-start.5 = (bf16[256,256]{1,0:T(8,128)(2,1)S(1)}, bf16[256,256]{1,0:T(8,128)(2,1)}, u32[]{:S(2)}) copy-start(bf16[256,256]{1,0:T(8,128)(2,1)} %param.9) | copy-start | bytes 393220
  28.3 0.9 %copy-start.2 = (bf16[256,256]{1,0:T(8,128)(2,1)S(1)}, bf16[256,256]{1,0:T(8,128)(2,1)}, u32[]{:S(2)}) copy-start(bf16[256,256]{1,0:T(8,128)(2,1)} %param.10) | copy-start | bytes 393220
  29.7 1.6 %collective-permute-start.4 = (f32[2,128,256]{2,1,0:T(8,128)S(1)}, f32[2,128,256]{2,1,0:T(8,128)S(1)}, u32[]{:S(2)}, u32[]{:S(2)}) collective-permute-start(f32[2,128,256]{2,1,0:T(8,128)S(1)} %dynamic-slice_bitcast_fusion), channel_id=1, source_target_pairs={{0,1},{1,0},{2,3},{3,2},{4,5},{5,4},{6,7},{7,6},{8,9},{9,8},{10,11... | collective-permute-start | bytes 786440 | tf_op jit(solution)/shard_map/ppermute | solution.py:23
  31.4 5.6 %collective-permute-start.5 = (f32[128,256]{1,0:T(8,128)S(1)}, f32[128,256]{1,0:T(8,128)S(1)}, u32[]{:S(2)}, u32[]{:S(2)}) collective-permute-start(f32[128,256]{1,0:T(8,128)S(1)} %dynamic-slice_bitcast_fusion.3), channel_id=1, source_target_pairs={{0,2},{1,3},{2,0},{3,1},{4,6},{5,7},{6,4},{7,5},{8,10},{9,11},{10,... | collective-permute-start | bytes 393224 | tf_op jit(solution)/shard_map/ppermute | solution.py:23
  50.1 4.0 %collective-permute-start.6 = (bf16[64,256]{1,0:T(8,128)(2,1)S(1)}, bf16[64,256]{1,0:T(8,128)(2,1)S(1)}, u32[]{:S(2)}, u32[]{:S(2)}) collective-permute-start(bf16[64,256]{1,0:T(8,128)(2,1)S(1)} %get-tuple-element.5), channel_id=1, source_target_pairs={{0,2},{1,3},{2,0},{3,1},{4,6},{5,7},{6,4},{7,5},{8,10},{9,11},{10,... | collective-permute-start | bytes 98312 | tf_op jit(solution)/shard_map/ppermute | solution.py:30
  54.2 1.3 %collective-permute-start.7 = (bf16[2,64,256]{2,1,0:T(8,128)(2,1)S(1)}, bf16[2,64,256]{2,1,0:T(8,128)(2,1)S(1)}, u32[]{:S(2)}, u32[]{:S(2)}) collective-permute-start(bf16[2,64,256]{2,1,0:T(8,128)(2,1)S(1)} %pad_maximum_fusion.6), channel_id=1, source_target_pairs={{0,1},{1,0},{2,3},{3,2},{4,5},{5,4},{6,7},{7,6},{8,9},{9,8},{10,11... | collective-permute-start | bytes 196616 | tf_op jit(solution)/shard_map/ppermute | solution.py:30
  55.5 8.5 %collective-permute-start.9 = (bf16[256,256]{1,0:T(8,128)(2,1)S(1)}, bf16[256,256]{1,0:T(8,128)(2,1)S(1)}, u32[]{:S(2)}, u32[]{:S(2)}) collective-permute-start(bf16[256,256]{1,0:T(8,128)(2,1)S(1)} %bitcast.118), channel_id=1, source_target_pairs={{5,0},{15,1},{21,2},{31,3},{1,4},{11,5},{17,6},{27,7},{6,8},{12,9}... | collective-permute-start | bytes 393224 | tf_op jit(solution)/shard_map/ppermute | solution.py:47
  56.7 7.4 %collective-permute-start.8 = (bf16[256,256]{1,0:T(8,128)(2,1)S(1)}, bf16[256,256]{1,0:T(8,128)(2,1)S(1)}, u32[]{:S(2)}, u32[]{:S(2)}) collective-permute-start(bf16[256,256]{1,0:T(8,128)(2,1)S(1)} %bitcast.119), channel_id=1, source_target_pairs={{0,0},{10,1},{16,2},{26,3},{4,4},{14,5},{20,6},{30,7},{1,8},{11,9}... | collective-permute-start | bytes 393224 | tf_op jit(solution)/shard_map/ppermute | solution.py:47
  58.0 13.4 %all-to-all-start.1 = ((f32[8,16,256]{2,1,0:T(8,128)}), f32[8,16,256]{2,1,0:T(8,128)S(1)}, u32[]{:S(2)}, u32[]{:S(2)}) async-start(f32[8,16,256]{2,1,0:T(8,128)} %broadcast_in_dim.59), calls=%async_computation.1 | async-start | bytes 262144 | tf_op jit(solution)/shard_map/all_to_all | solution.py:139
  65.0 8.1 %collective-permute-start.10 = (f32[2,64,256]{2,1,0:T(8,128)S(1)}, f32[2,64,256]{2,1,0:T(8,128)S(1)}, u32[]{:S(2)}, u32[]{:S(2)}) collective-permute-start(f32[2,64,256]{2,1,0:T(8,128)S(1)} %dynamic-slice_bitcast_fusion.2), channel_id=1, source_target_pairs={{0,1},{1,0},{2,3},{3,2},{4,5},{5,4},{6,7},{7,6},{8,9},{9,8},{10,11... | collective-permute-start | bytes 393224 | tf_op jit(solution)/shard_map/ppermute | solution.py:23
  71.4 5.0 %collective-permute-start.12 = (f32[128,256]{1,0:T(8,128)S(1)}, f32[128,256]{1,0:T(8,128)S(1)}, u32[]{:S(2)}, u32[]{:S(2)}) collective-permute-start(f32[128,256]{1,0:T(8,128)S(1)} %bitcast.107), channel_id=1, source_target_pairs={{0,2},{1,3},{2,0},{3,1},{4,6},{5,7},{6,4},{7,5},{8,10},{9,11},{10,... | collective-permute-start | bytes 393224 | tf_op jit(solution)/shard_map/ppermute | solution.py:30
  73.1 4.3 %collective-permute-start.11 = (f32[64,256]{1,0:T(8,128)S(1)}, f32[64,256]{1,0:T(8,128)S(1)}, u32[]{:S(2)}, u32[]{:S(2)}) collective-permute-start(f32[64,256]{1,0:T(8,128)S(1)} %dynamic-slice_bitcast_fusion.5), channel_id=1, source_target_pairs={{0,2},{1,3},{2,0},{3,1},{4,6},{5,7},{6,4},{7,5},{8,10},{9,11},{10,... | collective-permute-start | bytes 196616 | tf_op jit(solution)/shard_map/ppermute | solution.py:23
  76.4 1.8 %collective-permute-start.13 = (f32[2,128,256]{2,1,0:T(8,128)S(1)}, f32[2,128,256]{2,1,0:T(8,128)S(1)}, u32[]{:S(2)}, u32[]{:S(2)}) collective-permute-start(f32[2,128,256]{2,1,0:T(8,128)S(1)} %pad_maximum_fusion.4), channel_id=1, source_target_pairs={{0,1},{1,0},{2,3},{3,2},{4,5},{5,4},{6,7},{7,6},{8,9},{9,8},{10,11... | collective-permute-start | bytes 786440 | tf_op jit(solution)/shard_map/ppermute | solution.py:30

commit v16 on v10

--- a/solution.py
+++ b/solution.py
@@ -48,27 +48,32 @@
     return jnp.stack(pieces)
 
 
-def local_product(pieces, block_index, block_count, block_values, row_index, copy_index):
-    sections = pieces.shape[0]
+def panel_blocks(block_index, block_count, block_values, row_index, copy_index, sections):
     block_rows = block_values.shape[2]
     slot_count = block_values.shape[3]
-    block_side = block_values.shape[-1]
-    width = pieces.shape[-1]
-    panels = pieces.reshape(sections * block_rows, block_side, width)
     local = block_index[0, 0] - copy_index * slot_count
     shard = local // block_rows
     arrival = (shard - row_index) % sections
     columns = arrival * block_rows + local % block_rows
     live_slots = jnp.arange(slot_count, dtype=jnp.int32)[None, :] < block_count[0, 0][:, None]
-    picked = jnp.take(panels, columns.reshape(-1), axis=0).reshape(
-        block_rows, slot_count, block_side, width
+    panel_ids = jnp.arange(sections * block_rows, dtype=jnp.int32)
+    onehot = (columns[:, :, None] == panel_ids[None, None, :]) & live_slots[:, :, None]
+    placed = jnp.einsum(
+        "asp,asxy->axpy",
+        onehot.astype(block_values.dtype),
+        block_values[0, 0],
+        preferred_element_type=jnp.float32,
     )
-    picked = jnp.where(live_slots[:, :, None, None], picked, jnp.zeros((), picked.dtype))
+    return placed.astype(block_values.dtype)
+
+
+def local_product(pieces, placed):
+    sections = pieces.shape[0]
+    block_rows, block_side = placed.shape[0], placed.shape[1]
+    width = pieces.shape[-1]
+    panels = pieces.reshape(sections * block_rows, block_side, width)
     partial_value = lax.dot_general(
-        block_values[0, 0],
-        picked,
-        (((1, 3), (1, 2)), ((0,), (0,))),
-        preferred_element_type=jnp.float32,
+        placed, panels, (((2, 3), (0, 1)), ((), ())), preferred_element_type=jnp.float32
     )
     return partial_value.reshape(block_rows * block_side, width)
 
@@ -93,10 +98,13 @@
     def gather_rep(z):
         return all_gather_bits(z, me, rep_bits, devices).reshape(node_rows, z.shape[-1])
 
+    placed = panel_blocks(
+        block_index, block_count, block_values, row_index, copy_index, rows // copies
+    )
     stage_in = jnp.concatenate([features, cotangent], axis=1)
     pieces = gather_rounds(stage_in, rows, copies)
     both = reduce_rep(
-        local_product(pieces, block_index, block_count, block_values, row_index, copy_index)
+        local_product(pieces, placed)
     )
     agg_one = both[:, :feature_width].astype(jnp.bfloat16)
     spread_cotangent = both[:, feature_width:]
@@ -141,7 +149,7 @@
     grads = all_gather_bits(quarter, me, rep_bits, devices).reshape(grads.shape)
 
     agg_two = reduce_rep(
-        local_product(pieces_two, block_index, block_count, block_values, row_index, copy_index)
+        local_product(pieces_two, placed)
     ).astype(jnp.bfloat16)
     logits = jnp.dot(agg_two, weight_two, preferred_element_type=jnp.float32).astype(jnp.bfloat16)
     return (logits, grads[:feature_width], grads[feature_width:])

time: 75 us -> 75.9 us (1.012)
  starting transfers between devices: 34.1 us -> 37.1 us
  waiting for transfers between devices: 30.8 us -> 29 us
    ppermute x6, starting transfers between devices: 10.2 us -> 14.1 us  [reduce_scatter_bits(): y = keep + lax.ppermute(send, AXES, bit_pairs(devices, bit))]
    ppermute x4, starting transfers between devices: 8.57 us -> 11.9 us  [gather_rounds(): pieces.append(lax.ppermute(x, AXES, pairs))]
    all_to_all x1, starting transfers between devices: 6.01 us -> 3.37 us  [shards(): lax.all_to_all(jnp.broadcast_to(mine, parts.shape), 'row', 0, 0, tiled=Fa...]
    ppermute x4, waiting for transfers between devices: 4.44 us -> 2.2 us  [gather_rounds(): pieces.append(lax.ppermute(x, AXES, pairs))]
    ppermute x4, waiting for transfers between devices: 3.43 us -> 4.85 us  [all_gather_bits(): other = lax.ppermute(z, AXES, bit_pairs(devices, bit))]
    gather x2 -> x0, local copies, waits for them, and re-layouts: 1.19 us -> none  [local_product(): jnp.take(panels, columns.reshape(-1), axis=0)]
    all_to_all x1, waiting for transfers between devices: 6.27 us -> 5.2 us  [shards(): lax.all_to_all(jnp.broadcast_to(mine, parts.shape), 'row', 0, 0, tiled=Fa...]
    all_to_all x1, starting transfers between devices: 5.65 us -> 4.74 us  [shards(): mine = lax.all_to_all(parts, 'row', 0, 0, tiled=False).sum(axis=0)]
  transfers between devices with their start and end apart: 16 -> 16, of which waited for: 9 -> 9; matrix products, arithmetic and copies ran while one was open for 5% -> 4% of each run, Pallas kernels for 0% -> 0%
where the time goes in v16:
time: 75.9 us; the launch traced here: 75.4 us
  starting transfers between devices  37.1 us (49%)
  waiting for transfers between devices  29 us (38%)
  local copies, waits for them, and re-layouts  3.86 us (5%)
  matrix products  2.55 us (3%)
  other arithmetic  1.95 us (3%)
  between operations  0.97 us (1%)
    ppermute x6, starting transfers between devices, reduce_scatter_bits(): y = keep + lax.ppermute(send, AXES, bit_pairs(devices, bit))  14.1 us
    ppermute x4, starting transfers between devices, gather_rounds(): pieces.append(lax.ppermute(x, AXES, pairs))  11.9 us
    ppermute x6, waiting for transfers between devices, reduce_scatter_bits(): y = keep + lax.ppermute(send, AXES, bit_pairs(devices, bit))  9.48 us
    all_to_all x1, waiting for transfers between devices, shards(): mine = lax.all_to_all(parts, 'row', 0, 0, tiled=False).sum(axis=0)  7.27 us
    all_to_all x1, waiting for transfers between devices, shards(): lax.all_to_all(jnp.broadcast_to(mine, parts.shape), 'row', 0, 0, tiled=Fa...  5.2 us
    ppermute x4, waiting for transfers between devices, all_gather_bits(): other = lax.ppermute(z, AXES, bit_pairs(devices, bit))  4.85 us
    all_to_all x1, starting transfers between devices, shards(): mine = lax.all_to_all(parts, 'row', 0, 0, tiled=False).sum(axis=0)  4.74 us
    all_to_all x1, starting transfers between devices, shards(): lax.all_to_all(jnp.broadcast_to(mine, parts.shape), 'row', 0, 0, tiled=Fa...  3.37 us
  transfers between devices with their start and end apart: 16, of which 9 were waited for; matrix products, arithmetic and copies ran while one was open for 4% of the time, Pallas kernels for 0%

profile of v16, /device:TPU:0, one launch (start us, length us, event | category | flops | bytes accessed | tf_op | source)
XLA Modules:
  0.0 75.4 jit_solution(11684593991455280867)
XLA Ops:
  0.6 0.0 copy-start
  0.7 1.0 %constant_dynamic-update-slice_fusion.1 = bf16[256,512]{1,0:T(8,128)(2,1)S(1)} fusion(bf16[256,256]{1,0:T(8,128)(2,1)} %param.7), kind=kLoop, calls=%fused_computation.50 | loop fusion | bytes 262144
  1.6 0.0 copy-done.1
  1.7 0.7 collective-permute-start
  2.4 8.1 %collective-permute-start.1 = (bf16[256,512]{1,0:T(8,128)(2,1)S(1)}, bf16[256,512]{1,0:T(8,128)(2,1)S(1)}, u32[]{:S(2)}, u32[]{:S(2)}) collective-permute-start(bf16[256,512]{1,0:T(8,128)(2,1)S(1)} %constant_dynamic-update-slice_fusion), channel_id=1, source_target_pairs={{5,0},{15,1},{21,2},{31,3},{1,4},{11,5},{17,6},{27,7},{6,8},{12,9}... | collective-permute-start | bytes 786440 | tf_op jit(solution)/shard_map/ppermute | solution.py:47
  10.5 0.7 copy-done.3
  11.2 0.6 copy-done.5
  11.9 0.1 iota_compare_fusion.1
  11.9 0.3 convolution_convert_fusion
  12.2 2.2 %collective-permute-done.1 = bf16[256,512]{1,0:T(8,128)(2,1)S(1)} collective-permute-done((bf16[256,512]{1,0:T(8,128)(2,1)S(1)}, bf16[256,512]{1,0:T(8,128)(2,1)S(1)}, u32[]{:S(2)}, u32[]{:S(2)}) %collective-permute-start.1) | collective-permute-done | bytes 262176 | tf_op jit(solution)/shard_map/ppermute | solution.py:47
  14.4 0.1 pad_maximum_fusion
  14.5 0.3 convolution_bitcast_fusion
  14.8 6.7 %collective-permute-start.2 = (f32[2,64,512]{2,1,0:T(8,128)S(1)}, f32[2,64,512]{2,1,0:T(8,128)S(1)}, u32[]{:S(2)}, u32[]{:S(2)}) collective-permute-start(f32[2,64,512]{2,1,0:T(8,128)S(1)} %dynamic-slice_bitcast_fusion.1), channel_id=1, source_target_pairs={{0,1},{1,0},{2,3},{3,2},{4,5},{5,4},{6,7},{7,6},{8,9},{9,8},{10,11... | collective-permute-start | bytes 786440 | tf_op jit(solution)/shard_map/ppermute | solution.py:23
  21.6 1.2 %collective-permute-done.2 = f32[2,64,512]{2,1,0:T(8,128)S(1)} collective-permute-done((f32[2,64,512]{2,1,0:T(8,128)S(1)}, f32[2,64,512]{2,1,0:T(8,128)S(1)}, u32[]{:S(2)}, u32[]{:S(2)}) %collective-permute-start.2) | collective-permute-done | bytes 262176 | tf_op jit(solution)/shard_map/ppermute | solution.py:23
  22.8 3.0 %collective-permute-start.3 = (f32[64,512]{1,0:T(8,128)S(1)}, f32[64,512]{1,0:T(8,128)S(1)}, u32[]{:S(2)}, u32[]{:S(2)}) collective-permute-start(f32[64,512]{1,0:T(8,128)S(1)} %dynamic-slice_bitcast_fusion.4), channel_id=1, source_target_pairs={{0,2},{1,3},{2,0},{3,1},{4,6},{5,7},{6,4},{7,5},{8,10},{9,11},{10,... | collective-permute-start | bytes 393224 | tf_op jit(solution)/shard_map/ppermute | solution.py:23
  25.7 3.8 %collective-permute-done.3 = f32[64,512]{1,0:T(8,128)S(1)} collective-permute-done((f32[64,512]{1,0:T(8,128)S(1)}, f32[64,512]{1,0:T(8,128)S(1)}, u32[]{:S(2)}, u32[]{:S(2)}) %collective-permute-start.3) | collective-permute-done | bytes 131104 | tf_op jit(solution)/shard_map/ppermute | solution.py:23
  29.6 0.0 copy-start.2
  29.6 0.2 fusion.10
  29.8 0.7 copy-done.2
  30.5 0.3 fusion
  30.8 0.2 fusion.13
  31.0 0.3 fusion.6
  31.4 0.1 collective-permute-start.6
  31.5 1.8 %collective-permute-start.4 = (bf16[64,256]{1,0:T(8,128)(2,1)S(1)}, bf16[64,256]{1,0:T(8,128)(2,1)S(1)}, u32[]{:S(2)}, u32[]{:S(2)}) collective-permute-start(bf16[64,256]{1,0:T(8,128)(2,1)S(1)} %get-tuple-element.17), channel_id=1, source_target_pairs={{0,2},{1,3},{2,0},{3,1},{4,6},{5,7},{6,4},{7,5},{8,10},{9,11},{10,... | collective-permute-start | bytes 98312 | tf_op jit(solution)/shard_map/ppermute | solution.py:30
  33.3 1.5 %collective-permute-start.7 = (f32[128,256]{1,0:T(8,128)S(1)}, f32[128,256]{1,0:T(8,128)S(1)}, u32[]{:S(2)}, u32[]{:S(2)}) collective-permute-start(f32[128,256]{1,0:T(8,128)S(1)} %dynamic-slice_bitcast_fusion.3), channel_id=1, source_target_pairs={{0,2},{1,3},{2,0},{3,1},{4,6},{5,7},{6,4},{7,5},{8,10},{9,11},{10,... | collective-permute-start | bytes 393224 | tf_op jit(solution)/shard_map/ppermute | solution.py:23
  34.8 0.6 collective-permute-done.4
  35.5 0.1 collective-permute-start.5
  35.5 3.4 %collective-permute-done.7 = f32[128,256]{1,0:T(8,128)S(1)} collective-permute-done((f32[128,256]{1,0:T(8,128)S(1)}, f32[128,256]{1,0:T(8,128)S(1)}, u32[]{:S(2)}, u32[]{:S(2)}) %collective-permute-start.7) | collective-permute-done | bytes 131104 | tf_op jit(solution)/shard_map/ppermute | solution.py:23
  38.9 0.7 bitcast_add_fusion.3
  39.6 4.7 %all-to-all-start = ((f32[8,16,256]{2,1,0:T(8,128)}), f32[8,16,256]{2,1,0:T(8,128)S(1)}, u32[]{:S(2)}, u32[]{:S(2)}) async-start(f32[8,16,256]{2,1,0:T(8,128)} %bitcast.29), calls=%async_computation | async-start | bytes 262144 | tf_op jit(solution)/shard_map/all_to_all | solution.py:144
  44.3 0.0 collective-permute-done.5
  44.4 7.3 %all-to-all-done = f32[8,16,256]{2,1,0:T(8,128)S(1)} async-done(((f32[8,16,256]{2,1,0:T(8,128)}), f32[8,16,256]{2,1,0:T(8,128)S(1)}, u32[]{:S(2)}, u32[]{:S(2)}) %all-to-all-start) | async-done | bytes 131104 | tf_op jit(solution)/shard_map/all_to_all | solution.py:144
  51.7 0.7 collective-permute-start.8
  52.4 2.4 %collective-permute-start.9 = (bf16[256,256]{1,0:T(8,128)(2,1)S(1)}, bf16[256,256]{1,0:T(8,128)(2,1)S(1)}, u32[]{:S(2)}, u32[]{:S(2)}) collective-permute-start(bf16[256,256]{1,0:T(8,128)(2,1)S(1)} %bitcast.117), channel_id=1, source_target_pairs={{5,0},{15,1},{21,2},{31,3},{1,4},{11,5},{17,6},{27,7},{6,8},{12,9}... | collective-permute-start | bytes 393224 | tf_op jit(solution)/shard_map/ppermute | solution.py:47
  54.8 0.7 broadcast_in_dim.2
  55.4 3.4 %all-to-all-start.1 = ((f32[8,16,256]{2,1,0:T(8,128)}), f32[8,16,256]{2,1,0:T(8,128)S(1)}, u32[]{:S(2)}, u32[]{:S(2)}) async-start(f32[8,16,256]{2,1,0:T(8,128)} %broadcast_in_dim.2), calls=%async_computation.1 | async-start | bytes 262144 | tf_op jit(solution)/shard_map/all_to_all | solution.py:147
  58.8 0.0 collective-permute-done.9
  58.9 0.2 convolution_bitcast_fusion.1
  59.1 1.8 %collective-permute-start.10 = (f32[2,64,256]{2,1,0:T(8,128)S(1)}, f32[2,64,256]{2,1,0:T(8,128)S(1)}, u32[]{:S(2)}, u32[]{:S(2)}) collective-permute-start(f32[2,64,256]{2,1,0:T(8,128)S(1)} %dynamic-slice_bitcast_fusion.2), channel_id=1, source_target_pairs={{0,1},{1,0},{2,3},{3,2},{4,5},{5,4},{6,7},{7,6},{8,9},{9,8},{10,11... | collective-permute-start | bytes 393224 | tf_op jit(solution)/shard_map/ppermute | solution.py:23
  61.0 5.2 %all-to-all-done.1 = f32[8,16,256]{2,1,0:T(8,128)S(1)} async-done(((f32[8,16,256]{2,1,0:T(8,128)}), f32[8,16,256]{2,1,0:T(8,128)S(1)}, u32[]{:S(2)}, u32[]{:S(2)}) %all-to-all-start.1) | async-done | bytes 131104 | tf_op jit(solution)/shard_map/all_to_all | solution.py:147
  66.1 1.1 %collective-permute-start.12 = (f32[128,256]{1,0:T(8,128)S(1)}, f32[128,256]{1,0:T(8,128)S(1)}, u32[]{:S(2)}, u32[]{:S(2)}) collective-permute-start(f32[128,256]{1,0:T(8,128)S(1)} %bitcast.111), channel_id=1, source_target_pairs={{0,2},{1,3},{2,0},{3,1},{4,6},{5,7},{6,4},{7,5},{8,10},{9,11},{10,... | collective-permute-start | bytes 393224 | tf_op jit(solution)/shard_map/ppermute | solution.py:30
  67.2 0.0 collective-permute-done.10
  67.3 1.0 %collective-permute-start.11 = (f32[64,256]{1,0:T(8,128)S(1)}, f32[64,256]{1,0:T(8,128)S(1)}, u32[]{:S(2)}, u32[]{:S(2)}) collective-permute-start(f32[64,256]{1,0:T(8,128)S(1)} %dynamic-slice_bitcast_fusion.5), channel_id=1, source_target_pairs={{0,2},{1,3},{2,0},{3,1},{4,6},{5,7},{6,4},{7,5},{8,10},{9,11},{10,... | collective-permute-start | bytes 196616 | tf_op jit(solution)/shard_map/ppermute | solution.py:23
  68.3 4.2 %collective-permute-done.12 = f32[128,256]{1,0:T(8,128)S(1)} collective-permute-done((f32[128,256]{1,0:T(8,128)S(1)}, f32[128,256]{1,0:T(8,128)S(1)}, u32[]{:S(2)}, u32[]{:S(2)}) %collective-permute-start.12) | collective-permute-done | bytes 131104 | tf_op jit(solution)/shard_map/ppermute | solution.py:30
  72.6 0.1 collective-permute-start.13
  72.7 1.1 %collective-permute-done.11 = f32[64,256]{1,0:T(8,128)S(1)} collective-permute-done((f32[64,256]{1,0:T(8,128)S(1)}, f32[64,256]{1,0:T(8,128)S(1)}, u32[]{:S(2)}, u32[]{:S(2)}) %collective-permute-start.11) | collective-permute-done | bytes 65568 | tf_op jit(solution)/shard_map/ppermute | solution.py:23
  73.8 0.8 %convolution_convert_fusion.1 = bf16[64,256]{1,0:T(8,128)(2,1)} fusion(bf16[256,256]{1,0:T(8,128)(2,1)S(1)} %copy-done.2, f32[64,256]{1,0:T(8,128)S(1)} %collective-permute-done.11, f32[2,64,256]{2,1,0:T(8,128)S(1)} %bitcast_add_fusion.2, s32[]{:T(128)S(6)} %select_n.109), kind=kOutput, calls=%fused_computation.5 | convolution fusion | flops 8437760 | bytes 294916 | tf_op jit(solution)/shard_map/dot_general | solution.py:154
  74.6 0.8 %pad_maximum_fusion.2 = (f32[1,2,128,256]{3,2,1,0:T(8,128)}, f32[1,2,128,256]{3,2,1,0:T(8,128)}) fusion(f32[2,1,128,256]{3,2,1,0:T(8,128)S(1)} %get-tuple-element.9, f32[2,1,128,256]{3,2,1,0:T(8,128)S(1)} %get-tuple-element.10), kind=kLoop, calls=%fused_computation.11 | loop fusion | flops 131072 | bytes 1048576 | tf_op jit(solution)/shard_map/stack | solution.py:33
  (33 shorter events, 0.5 us)
Async XLA Ops:
  0.6 11.3 %copy-start = (bf16[1,1,2,4,128,128]{5,4,3,2,1,0:T(8,128)(2,1)S(1)}, bf16[1,1,2,4,128,128]{5,4,3,2,1,0:T(8,128)(2,1)}, u32[]{:S(2)}) copy-start(bf16[1,1,2,4,128,128]{5,4,3,2,1,0:T(8,128)(2,1)} %param.13) | copy-start | bytes 786436
  0.6 1.0 %copy-start.1 = (bf16[256,256]{1,0:T(8,128)(2,1)S(1)}, bf16[256,256]{1,0:T(8,128)(2,1)}, u32[]{:S(2)}) copy-start(bf16[256,256]{1,0:T(8,128)(2,1)} %param.8) | copy-start | bytes 393220
  1.7 10.6 %collective-permute-start = (bf16[256,512]{1,0:T(8,128)(2,1)S(1)}, bf16[256,512]{1,0:T(8,128)(2,1)S(1)}, u32[]{:S(2)}, u32[]{:S(2)}) collective-permute-start(bf16[256,512]{1,0:T(8,128)(2,1)S(1)} %constant_dynamic-update-slice_fusion), channel_id=1, source_target_pairs={{0,0},{10,1},{16,2},{26,3},{4,4},{14,5},{20,6},{30,7},{1,8},{11,9}... | collective-permute-start | bytes 786440 | tf_op jit(solution)/shard_map/ppermute | solution.py:47
  2.4 12.1 %collective-permute-start.1 = (bf16[256,512]{1,0:T(8,128)(2,1)S(1)}, bf16[256,512]{1,0:T(8,128)(2,1)S(1)}, u32[]{:S(2)}, u32[]{:S(2)}) collective-permute-start(bf16[256,512]{1,0:T(8,128)(2,1)S(1)} %constant_dynamic-update-slice_fusion), channel_id=1, source_target_pairs={{5,0},{15,1},{21,2},{31,3},{1,4},{11,5},{17,6},{27,7},{6,8},{12,9}... | collective-permute-start | bytes 786440 | tf_op jit(solution)/shard_map/ppermute | solution.py:47
  10.5 0.7 copy-start.3
  11.2 0.7 copy-start.5
  14.8 7.9 %collective-permute-start.2 = (f32[2,64,512]{2,1,0:T(8,128)S(1)}, f32[2,64,512]{2,1,0:T(8,128)S(1)}, u32[]{:S(2)}, u32[]{:S(2)}) collective-permute-start(f32[2,64,512]{2,1,0:T(8,128)S(1)} %dynamic-slice_bitcast_fusion.1), channel_id=1, source_target_pairs={{0,1},{1,0},{2,3},{3,2},{4,5},{5,4},{6,7},{7,6},{8,9},{9,8},{10,11... | collective-permute-start | bytes 786440 | tf_op jit(solution)/shard_map/ppermute | solution.py:23
  22.8 6.8 %collective-permute-start.3 = (f32[64,512]{1,0:T(8,128)S(1)}, f32[64,512]{1,0:T(8,128)S(1)}, u32[]{:S(2)}, u32[]{:S(2)}) collective-permute-start(f32[64,512]{1,0:T(8,128)S(1)} %dynamic-slice_bitcast_fusion.4), channel_id=1, source_target_pairs={{0,2},{1,3},{2,0},{3,1},{4,6},{5,7},{6,4},{7,5},{8,10},{9,11},{10,... | collective-permute-start | bytes 393224 | tf_op jit(solution)/shard_map/ppermute | solution.py:23
  25.7 3.8 %copy-start.4 = (bf16[256,256]{1,0:T(8,128)(2,1)S(1)}, bf16[256,256]{1,0:T(8,128)(2,1)}, u32[]{:S(2)}) copy-start(bf16[256,256]{1,0:T(8,128)(2,1)} %param.9) | copy-start | bytes 393220
  29.6 0.9 %copy-start.2 = (bf16[256,256]{1,0:T(8,128)(2,1)S(1)}, bf16[256,256]{1,0:T(8,128)(2,1)}, u32[]{:S(2)}) copy-start(bf16[256,256]{1,0:T(8,128)(2,1)} %param.10) | copy-start | bytes 393220
  31.4 1.9 %collective-permute-start.6 = (f32[2,128,256]{2,1,0:T(8,128)S(1)}, f32[2,128,256]{2,1,0:T(8,128)S(1)}, u32[]{:S(2)}, u32[]{:S(2)}) collective-permute-start(f32[2,128,256]{2,1,0:T(8,128)S(1)} %dynamic-slice_bitcast_fusion), channel_id=1, source_target_pairs={{0,1},{1,0},{2,3},{3,2},{4,5},{5,4},{6,7},{7,6},{8,9},{9,8},{10,11... | collective-permute-start | bytes 786440 | tf_op jit(solution)/shard_map/ppermute | solution.py:23
  31.5 4.0 %collective-permute-start.4 = (bf16[64,256]{1,0:T(8,128)(2,1)S(1)}, bf16[64,256]{1,0:T(8,128)(2,1)S(1)}, u32[]{:S(2)}, u32[]{:S(2)}) collective-permute-start(bf16[64,256]{1,0:T(8,128)(2,1)S(1)} %get-tuple-element.17), channel_id=1, source_target_pairs={{0,2},{1,3},{2,0},{3,1},{4,6},{5,7},{6,4},{7,5},{8,10},{9,11},{10,... | collective-permute-start | bytes 98312 | tf_op jit(solution)/shard_map/ppermute | solution.py:30
  33.3 5.6 %collective-permute-start.7 = (f32[128,256]{1,0:T(8,128)S(1)}, f32[128,256]{1,0:T(8,128)S(1)}, u32[]{:S(2)}, u32[]{:S(2)}) collective-permute-start(f32[128,256]{1,0:T(8,128)S(1)} %dynamic-slice_bitcast_fusion.3), channel_id=1, source_target_pairs={{0,2},{1,3},{2,0},{3,1},{4,6},{5,7},{6,4},{7,5},{8,10},{9,11},{10,... | collective-permute-start | bytes 393224 | tf_op jit(solution)/shard_map/ppermute | solution.py:23
  35.5 8.9 %collective-permute-start.5 = (bf16[2,64,256]{2,1,0:T(8,128)(2,1)S(1)}, bf16[2,64,256]{2,1,0:T(8,128)(2,1)S(1)}, u32[]{:S(2)}, u32[]{:S(2)}) collective-permute-start(bf16[2,64,256]{2,1,0:T(8,128)(2,1)S(1)} %pad_maximum_fusion.6), channel_id=1, source_target_pairs={{0,1},{1,0},{2,3},{3,2},{4,5},{5,4},{6,7},{7,6},{8,9},{9,8},{10,11... | collective-permute-start | bytes 196616 | tf_op jit(solution)/shard_map/ppermute | solution.py:30
  39.6 12.1 %all-to-all-start = ((f32[8,16,256]{2,1,0:T(8,128)}), f32[8,16,256]{2,1,0:T(8,128)S(1)}, u32[]{:S(2)}, u32[]{:S(2)}) async-start(f32[8,16,256]{2,1,0:T(8,128)} %bitcast.29), calls=%async_computation | async-start | bytes 262144 | tf_op jit(solution)/shard_map/all_to_all | solution.py:144
  51.7 7.1 %collective-permute-start.8 = (bf16[256,256]{1,0:T(8,128)(2,1)S(1)}, bf16[256,256]{1,0:T(8,128)(2,1)S(1)}, u32[]{:S(2)}, u32[]{:S(2)}) collective-permute-start(bf16[256,256]{1,0:T(8,128)(2,1)S(1)} %bitcast.116), channel_id=1, source_target_pairs={{0,0},{10,1},{16,2},{26,3},{4,4},{14,5},{20,6},{30,7},{1,8},{11,9}... | collective-permute-start | bytes 393224 | tf_op jit(solution)/shard_map/ppermute | solution.py:47
  52.4 6.5 %collective-permute-start.9 = (bf16[256,256]{1,0:T(8,128)(2,1)S(1)}, bf16[256,256]{1,0:T(8,128)(2,1)S(1)}, u32[]{:S(2)}, u32[]{:S(2)}) collective-permute-start(bf16[256,256]{1,0:T(8,128)(2,1)S(1)} %bitcast.117), channel_id=1, source_target_pairs={{5,0},{15,1},{21,2},{31,3},{1,4},{11,5},{17,6},{27,7},{6,8},{12,9}... | collective-permute-start | bytes 393224 | tf_op jit(solution)/shard_map/ppermute | solution.py:47
  55.4 10.7 %all-to-all-start.1 = ((f32[8,16,256]{2,1,0:T(8,128)}), f32[8,16,256]{2,1,0:T(8,128)S(1)}, u32[]{:S(2)}, u32[]{:S(2)}) async-start(f32[8,16,256]{2,1,0:T(8,128)} %broadcast_in_dim.2), calls=%async_computation.1 | async-start | bytes 262144 | tf_op jit(solution)/shard_map/all_to_all | solution.py:147
  59.1 8.1 %collective-permute-start.10 = (f32[2,64,256]{2,1,0:T(8,128)S(1)}, f32[2,64,256]{2,1,0:T(8,128)S(1)}, u32[]{:S(2)}, u32[]{:S(2)}) collective-permute-start(f32[2,64,256]{2,1,0:T(8,128)S(1)} %dynamic-slice_bitcast_fusion.2), channel_id=1, source_target_pairs={{0,1},{1,0},{2,3},{3,2},{4,5},{5,4},{6,7},{7,6},{8,9},{9,8},{10,11... | collective-permute-start | bytes 393224 | tf_op jit(solution)/shard_map/ppermute | solution.py:23
  66.1 6.4 %collective-permute-start.12 = (f32[128,256]{1,0:T(8,128)S(1)}, f32[128,256]{1,0:T(8,128)S(1)}, u32[]{:S(2)}, u32[]{:S(2)}) collective-permute-start(f32[128,256]{1,0:T(8,128)S(1)} %bitcast.111), channel_id=1, source_target_pairs={{0,2},{1,3},{2,0},{3,1},{4,6},{5,7},{6,4},{7,5},{8,10},{9,11},{10,... | collective-permute-start | bytes 393224 | tf_op jit(solution)/shard_map/ppermute | solution.py:30
  67.3 6.5 %collective-permute-start.11 = (f32[64,256]{1,0:T(8,128)S(1)}, f32[64,256]{1,0:T(8,128)S(1)}, u32[]{:S(2)}, u32[]{:S(2)}) collective-permute-start(f32[64,256]{1,0:T(8,128)S(1)} %dynamic-slice_bitcast_fusion.5), channel_id=1, source_target_pairs={{0,2},{1,3},{2,0},{3,1},{4,6},{5,7},{6,4},{7,5},{8,10},{9,11},{10,... | collective-permute-start | bytes 196616 | tf_op jit(solution)/shard_map/ppermute | solution.py:23
  72.6 2.0 %collective-permute-start.13 = (f32[2,128,256]{2,1,0:T(8,128)S(1)}, f32[2,128,256]{2,1,0:T(8,128)S(1)}, u32[]{:S(2)}, u32[]{:S(2)}) collective-permute-start(f32[2,128,256]{2,1,0:T(8,128)S(1)} %pad_maximum_fusion.4), channel_id=1, source_target_pairs={{0,1},{1,0},{2,3},{3,2},{4,5},{5,4},{6,7},{7,6},{8,9},{9,8},{10,11... | collective-permute-start | bytes 786440 | tf_op jit(solution)/shard_map/ppermute | solution.py:30
